TPU v7x, 32 devices: a whole 2x2x4 slice. The times are simulated.
32 devices in a mesh: ctx: 8 (over y, x, core), head: 4 (over z).
Axes of the slice: x: 2, y: 2, z: 4, core: 2. Of those that a mesh axis runs over, the one named last changes fastest.
Arguments:
- queries: bfloat16 [4096, 4096], P(('ctx', 'head')), may hold values from -42 to 42
- keys: bfloat16 [4096, 1024], P(('ctx', 'head')), may hold values from -4 to 4
- values: bfloat16 [4096, 1024], P(('ctx', 'head')), may hold values from -6 to 6
- out_grad: bfloat16 [4096, 4096], P(('ctx', 'head')), may hold values from -6 to 6
- beacon_pos: int32 [8, 64], P('ctx'), may hold values from 0 to 511, as said below
Outputs:
- attended: bfloat16 [4096, 4096], P(('ctx', 'head'))
- query_grad: bfloat16 [4096, 4096], P(('ctx', 'head'))
- key_grad: bfloat16 [4096, 1024], P(('ctx', 'head'))
- value_grad: bfloat16 [4096, 1024], P(('ctx', 'head'))
Inputs may be any that keep to these rules, and one draw needn't show every extreme that they name: `beacon_pos`: row c holds 64 distinct positions in increasing order, the first equal to 0 and the last equal to 511.
All inputs are finite; a program needn't handle non-finite values.
Results may differ from a plain program's by a relative error of at most 0.029.
Values may be sent and summed in bfloat16 or wider, within the bound.
No kernel may reach another device: no remote copies, remote signals or barrier semaphores. Data moves between devices by JAX's collectives and lax.ppermute only.
A program may use at most 128 MiB of HBM per device.

v0:
```python
import jax
import jax.numpy as jnp
from jax import lax
from jax.sharding import PartitionSpec as P

HD = 128


NEG_FILL = -1e30


def local(queries, keys, values, out_grad, beacon_pos):
    query_rows, key_rows, value_rows, grad_rows = (
        lax.all_to_all(queries, "head", split_axis=1, concat_axis=0, tiled=True),
        lax.all_to_all(keys, "head", split_axis=1, concat_axis=0, tiled=True),
        lax.all_to_all(values, "head", split_axis=1, concat_axis=0, tiled=True),
        lax.all_to_all(out_grad, "head", split_axis=1, concat_axis=0, tiled=True),
    )
    window = query_rows.shape[0]
    kv_local = key_rows.shape[1] // HD
    group_size = query_rows.shape[1] // HD // kv_local
    scaling = HD ** (-0.5)
    query_head_rows = query_rows.reshape(window, kv_local, group_size, HD)
    head_gradients = grad_rows.reshape(window, kv_local, group_size, HD)
    key_heads = key_rows.reshape(window, kv_local, HD)
    value_heads = value_rows.reshape(window, kv_local, HD)
    positions = beacon_pos[0]
    beacon_keys, beacon_values = (
        lax.all_gather(key_rows[positions], "ctx", axis=0, tiled=True),
        lax.all_gather(value_rows[positions], "ctx", axis=0, tiled=True),
    )
    beacon_total = beacon_keys.shape[0]
    per_shard = positions.shape[0]
    beacon_key_heads = beacon_keys.reshape(beacon_total, kv_local, HD)
    beacon_value_heads = beacon_values.reshape(beacon_total, kv_local, HD)
    owners = jnp.arange(beacon_total, dtype=jnp.int32) // per_shard
    shard_id = lax.axis_index("ctx")
    block_rows = min(beacon_total, 512)
    block_count = beacon_total // block_rows
    causal = jnp.arange(window)[:, None] >= jnp.arange(window)[None, :]
    local_scores = (
        jnp.einsum("wkgd,vkd->kgwv", query_head_rows, key_heads, preferred_element_type=jnp.float32)
        * scaling
    )
    local_scores = jnp.where(causal, local_scores, NEG_FILL)

    def beacon_scores(block_index):
        start = block_index * block_rows
        key_tile_block = lax.dynamic_slice_in_dim(beacon_key_heads, start, block_rows, 0)
        value_tile_block = lax.dynamic_slice_in_dim(beacon_value_heads, start, block_rows, 0)
        seen = lax.dynamic_slice_in_dim(owners, start, block_rows, 0) < shard_id
        scores = (
            jnp.einsum(
                "jahm,pam->ahjp",
                query_head_rows,
                key_tile_block,
                preferred_element_type=jnp.float32,
            )
            * scaling
        )
        return (jnp.where(seen, scores, NEG_FILL), key_tile_block, value_tile_block, start)

    row_max = jnp.max(local_scores, axis=-1)
    row_sum = jnp.sum(jnp.exp(local_scores - row_max[..., None]), axis=-1)

    def gather_stats(block_index, stats):
        old_max, old_sum = stats
        scores = beacon_scores(block_index)[0]
        new_max = jnp.maximum(old_max, jnp.max(scores, axis=-1))
        updated_sum = old_sum * jnp.exp(old_max - new_max) + jnp.sum(
            jnp.exp(scores - new_max[..., None]), axis=-1
        )
        return (new_max, updated_sum)

    row_max, row_sum = lax.fori_loop(0, block_count, gather_stats, (row_max, row_sum))

    def normalize(scores):
        return jnp.exp(scores - row_max[..., None]) / row_sum[..., None]

    local_probs = normalize(local_scores)
    local_probs_low = local_probs.astype(jnp.bfloat16)
    attended = jnp.einsum(
        "kgwv,vkd->wkgd", local_probs_low, value_heads, preferred_element_type=jnp.float32
    )

    def add_values(block_index, running):
        scores, key_tile_block, value_tile_block, start = beacon_scores(block_index)
        reduced_probability = normalize(scores).astype(jnp.bfloat16)
        return running + jnp.einsum(
            "lupa,alx->plux",
            reduced_probability,
            value_tile_block,
            preferred_element_type=jnp.float32,
        )

    attended = lax.fori_loop(0, block_count, add_values, attended).astype(jnp.bfloat16)
    row_dot = jnp.einsum(
        "wkgd,wkgd->kgw", head_gradients, attended, preferred_element_type=jnp.float32
    )[..., None]
    local_dprob = jnp.einsum(
        "wkgd,vkd->kgwv", head_gradients, value_heads, preferred_element_type=jnp.float32
    )
    local_grad_scores = (local_probs * (local_dprob - row_dot)).astype(jnp.bfloat16)
    query_grad = jnp.einsum(
        "kgwv,vkd->wkgd", local_grad_scores, key_heads, preferred_element_type=jnp.float32
    )
    key_grad = (
        jnp.einsum(
            "kgwv,wkgd->vkd", local_grad_scores, query_head_rows, preferred_element_type=jnp.float32
        )
        * scaling
    )
    value_grad = jnp.einsum(
        "kgwv,wkgd->vkd", local_probs_low, head_gradients, preferred_element_type=jnp.float32
    )

    def add_grads(block_index, carried):
        query_count_total, key_buffer, value_buffer = carried
        scores, key_tile_block, value_tile_block, start = beacon_scores(block_index)
        probabilities = normalize(scores)
        reduced_probability = probabilities.astype(jnp.bfloat16)
        dprob = jnp.einsum(
            "jahm,pam->ahjp", head_gradients, value_tile_block, preferred_element_type=jnp.float32
        )
        score_gradient = (probabilities * (dprob - row_dot)).astype(jnp.bfloat16)
        query_count_total = query_count_total + jnp.einsum(
            "lupa,alx->plux", score_gradient, key_tile_block, preferred_element_type=jnp.float32
        )
        key_part = (
            jnp.einsum(
                "ecxr,xecz->rez",
                score_gradient,
                query_head_rows,
                preferred_element_type=jnp.float32,
            )
            * scaling
        )
        value_part = jnp.einsum(
            "ecxr,xecz->rez",
            reduced_probability,
            head_gradients,
            preferred_element_type=jnp.float32,
        )
        key_buffer = lax.dynamic_update_slice_in_dim(key_buffer, key_part, start, 0)
        value_buffer = lax.dynamic_update_slice_in_dim(value_buffer, value_part, start, 0)
        return (query_count_total, key_buffer, value_buffer)

    empty_buffer = jnp.zeros((beacon_total, kv_local, HD), jnp.float32)
    query_grad, key_buffer, value_buffer = lax.fori_loop(
        0, block_count, add_grads, (query_grad, empty_buffer, empty_buffer)
    )
    query_grad = (query_grad * scaling).astype(jnp.bfloat16)
    own_keys, own_values = (
        lax.psum_scatter(
            key_buffer.astype(jnp.bfloat16), "ctx", scatter_dimension=0, tiled=True
        ).astype(jnp.float32),
        lax.psum_scatter(
            value_buffer.astype(jnp.bfloat16), "ctx", scatter_dimension=0, tiled=True
        ).astype(jnp.float32),
    )
    key_grad = key_grad.at[positions].add(own_keys)
    value_grad = value_grad.at[positions].add(own_values)
    attended_out = attended.reshape(window, group_size * kv_local * HD)
    query_out = query_grad.reshape(window, group_size * kv_local * HD)
    key_out = key_grad.astype(jnp.bfloat16).reshape(window, kv_local * HD)
    value_out = value_grad.astype(jnp.bfloat16).reshape(window, kv_local * HD)
    return (
        lax.all_to_all(attended_out, "head", split_axis=0, concat_axis=1, tiled=True),
        lax.all_to_all(query_out, "head", split_axis=0, concat_axis=1, tiled=True),
        lax.all_to_all(key_out, "head", split_axis=0, concat_axis=1, tiled=True),
        lax.all_to_all(value_out, "head", split_axis=0, concat_axis=1, tiled=True),
    )


def solution(mesh):
    in_specs = (
        P(("ctx", "head"), None),
        P(("ctx", "head"), None),
        P(("ctx", "head"), None),
        P(("ctx", "head"), None),
        P("ctx", None),
    )
    out_specs = (
        P(("ctx", "head"), None),
        P(("ctx", "head"), None),
        P(("ctx", "head"), None),
        P(("ctx", "head"), None),
    )
    return jax.shard_map(local, mesh=mesh, in_specs=in_specs, out_specs=out_specs, check_vma=False)
```

profile of v0, /device:TPU:10, one launch (start us, length us, event | category | flops | bytes accessed | tf_op | source)
XLA Modules:
  0.0 281.1 jit_solution(10834364162672158835)
XLA Ops:
  8.8 5.3 %all-to-all-start = ((bf16[128,4,256]{2,0,1:T(8,128)(2,1)}), bf16[128,4,256]{2,0,1:T(8,128)(2,1)S(1)}, u32[]{:S(2)}, u32[]{:S(2)}) async-start(bf16[128,4,256]{2,0,1:T(8,128)(2,1)} %bitcast.156), calls=%async_computation | async-start | bytes 524288 | tf_op jit(solution)/shard_map/all_to_all | solution.py:15
  15.8 5.4 %all-to-all-done = bf16[128,4,256]{2,0,1:T(8,128)(2,1)S(1)} async-done(((bf16[128,4,256]{2,0,1:T(8,128)(2,1)}), bf16[128,4,256]{2,0,1:T(8,128)(2,1)S(1)}, u32[]{:S(2)}, u32[]{:S(2)}) %all-to-all-start) | async-done | bytes 262176 | tf_op jit(solution)/shard_map/all_to_all | solution.py:15
  21.2 5.2 %all-to-all-start.2 = ((bf16[128,4,256]{2,0,1:T(8,128)(2,1)}), bf16[128,4,256]{2,0,1:T(8,128)(2,1)S(1)}, u32[]{:S(2)}, u32[]{:S(2)}) async-start(bf16[128,4,256]{2,0,1:T(8,128)(2,1)} %bitcast.155), calls=%async_computation.2 | async-start | bytes 524288 | tf_op jit(solution)/shard_map/all_to_all | solution.py:16
  28.7 4.0 %all-to-all-done.2 = bf16[128,4,256]{2,0,1:T(8,128)(2,1)S(1)} async-done(((bf16[128,4,256]{2,0,1:T(8,128)(2,1)}), bf16[128,4,256]{2,0,1:T(8,128)(2,1)S(1)}, u32[]{:S(2)}, u32[]{:S(2)}) %all-to-all-start.2) | async-done | bytes 262176 | tf_op jit(solution)/shard_map/all_to_all | solution.py:16
  32.7 4.3 %all-to-all-start.1 = ((bf16[128,4,1024]{2,0,1:T(8,128)(2,1)}), bf16[128,4,1024]{2,0,1:T(8,128)(2,1)S(1)}, u32[]{:S(2)}, u32[]{:S(2)}) async-start(bf16[128,4,1024]{2,0,1:T(8,128)(2,1)} %bitcast.154), calls=%async_computation.1 | async-start | bytes 2097152 | tf_op jit(solution)/shard_map/all_to_all | solution.py:14
  39.3 17.4 %all-to-all-done.1 = bf16[128,4,1024]{2,0,1:T(8,128)(2,1)S(1)} async-done(((bf16[128,4,1024]{2,0,1:T(8,128)(2,1)}), bf16[128,4,1024]{2,0,1:T(8,128)(2,1)S(1)}, u32[]{:S(2)}, u32[]{:S(2)}) %all-to-all-start.1) | async-done | bytes 1048608 | tf_op jit(solution)/shard_map/all_to_all | solution.py:14
  56.7 6.8 %all-to-all-start.4 = ((bf16[128,4,1024]{2,0,1:T(8,128)(2,1)}), bf16[128,4,1024]{2,0,1:T(8,128)(2,1)S(1)}, u32[]{:S(2)}, u32[]{:S(2)}) async-start(bf16[128,4,1024]{2,0,1:T(8,128)(2,1)} %bitcast.153), calls=%async_computation.4 | async-start | bytes 2097152 | tf_op jit(solution)/shard_map/all_to_all | solution.py:17
  65.0 9.3 %all-gather = bf16[512,256]{1,0:T(8,128)(2,1)S(1)} all-gather(bf16[64,256]{1,0:T(8,128)(2,1)S(1)} %gather_fusion), channel_id=2, replica_groups=mesh['ctx'=8,'head'=4] {'ctx'}, dimensions={0}, use_global_device_ids=true | all-gather | bytes 294912 | tf_op jit(solution)/shard_map/all_gather | solution.py:29
  75.9 8.3 %all-gather.1 = bf16[512,256]{1,0:T(8,128)(2,1)S(1)} all-gather(bf16[64,256]{1,0:T(8,128)(2,1)S(1)} %gather_fusion.1), channel_id=3, replica_groups=mesh['ctx'=8,'head'=4] {'ctx'}, dimensions={0}, use_global_device_ids=true | all-gather | bytes 294912 | tf_op jit(solution)/shard_map/all_gather | solution.py:30
  103.0 5.3 %fusion.13 = f32[2,128,4,512]{1,3,2,0:T(8,128)S(1)} fusion(bf16[512,2,128,1]{0,2,3,1:T(8,128)(2,1)S(1)} %bitcast.174, f32[2,4,512,512]{2,3,1,0:T(8,128)} %copy-done), kind=kOutput, calls=%fused_computation.28 | convolution fusion | flops 538968064 | bytes 10747904 | tf_op jit(solution)/shard_map/while/body/eval_jaxpr/lupa,alx->plux/dot_general | solution.py:89
  108.8 4.0 %bitcast_convert_fusion = (f32[2,4,512,128]{3,2,1,0:T(8,128)S(1)}, bf16[512,2,4,128]{3,0,2,1:T(8,128)(2,1)}) fusion(f32[2,128,4,512]{1,3,2,0:T(8,128)S(1)} %fusion.13, bf16[512,2,128,1]{2,1,0,3:T(2,128)(2,1)S(1)} %bitcast.184, f32[2,4,512]{2,1,0:T(4,128)S(1)} %bitcast.190, f32[2,4,512]{2,1,0:T(4,128)S(1)} %max.11, f32[2,512,512,4]{2,1,3,0:T(8,128)S(1)} %copy-done.2, ...), kind=kOutput, calls=%fused_computation.47 | convolution fusion | flops 548929536 | bytes 14188544 | tf_op jit(solution)/shard_map/kgwv,vkd->wkgd/dot_general | solution.py:82
  115.0 6.8 %fusion.3 = bf16[2,4,512,512]{2,3,1,0:T(8,128)(2,1)} fusion(f32[2,4,512]{2,1,0:T(4,128)S(1)} %copy.112, bf16[512,2,4,128]{3,2,1,0:T(4,128)(2,1)S(1)} %reshape.114, bf16[512,2,128,1]{2,1,0,3:T(2,128)(2,1)} %bitcast.183, f32[2,4,512]{2,1,0:T(4,128)S(1)} %bitcast.191, f32[2,4,512]{2,1,0:T(4,128)S(1)} %max.11, f32[2,512,512,4]{2,1,3,0:T(8,128)} %copy-done.1, ...), kind=kOutput, calls=%fused_computation.9 | convolution fusion | flops 551550976 | bytes 14204928 | tf_op jit(solution)/shard_map/wkgd,vkd->kgwv/dot_general | solution.py:100
  121.8 6.7 %fusion.1 = bf16[2,4,512,512]{2,3,1,0:T(8,128)(2,1)} fusion(f32[2,4,512,512]{2,3,1,0:T(8,128)} %copy-done, f32[2,4,512]{2,1,0:T(4,128)S(1)} %copy.112, bf16[512,2,128,1]{0,2,3,1:T(8,128)(2,1)S(1)} %bitcast.175, bf16[512,2,4,128]{3,2,1,0:T(4,128)(2,1)S(1)} %reshape.114), kind=kOutput, calls=%fused_computation.6 | convolution fusion | flops 543162368 | bytes 13910016 | tf_op jit(solution)/shard_map/while/body/eval_jaxpr/jahm,pam->ahjp/dot_general | solution.py:122
  129.0 4.1 %fusion.37 = bf16[512,2,128]{2,0,1:T(8,128)(2,1)} fusion(bf16[2,4,512,512]{2,3,1,0:T(8,128)(2,1)} %fusion.1, bf16[512,2,4,128]{3,2,1,0:T(4,128)(2,1)S(1)} %reshape.110), kind=kOutput, calls=%fused_computation.44 | convolution fusion | flops 537133056 | bytes 5505024 | tf_op jit(solution)/shard_map/while/body/eval_jaxpr/ecxr,xecz->rez/dot_general | solution.py:130
  133.2 30.0 %reduce-scatter.5.cloned.1.call-done = bf16[64,2,128]{2,0,1:T(8,128)(2,1)} async-done(((bf16[512,2,128]{2,0,1:T(8,128)(2,1)}), bf16[64,2,128]{2,0,1:T(8,128)(2,1)}) %reduce-scatter.5.cloned.1.call-update) | async-done | bytes 32784 | tf_op jit(solution)/shard_map/reduce_scatter | solution.py:157
  167.8 5.1 %all-to-all-start.7 = ((bf16[4,128,256]{2,1,0:T(8,128)(2,1)}), bf16[4,128,256]{2,1,0:T(8,128)(2,1)}, u32[]{:S(2)}, u32[]{:S(2)}) async-start(bf16[4,128,256]{2,1,0:T(8,128)(2,1)} %all_to_all.134), calls=%async_computation.9 | async-start | bytes 524288 | tf_op jit(solution)/shard_map/all_to_all | solution.py:171
  172.9 3.6 %fusion.28 = f32[512,2,128]{2,0,1:T(8,128)S(1)} fusion(bf16[2,4,512,512]{2,3,1,0:T(8,128)(2,1)} %fusion.3, bf16[512,2,4,128]{3,2,1,0:T(4,128)(2,1)S(1)} %reshape.110), kind=kOutput, calls=%fused_computation.39 | convolution fusion | flops 537001984 | bytes 5767168 | tf_op jit(solution)/shard_map/kgwv,wkgd->vkd/dot_general | solution.py:108
  178.8 21.9 %reduce-scatter.3.cloned.1.call-done = bf16[64,2,128]{2,0,1:T(8,128)(2,1)} async-done(((bf16[512,2,128]{2,0,1:T(8,128)(2,1)}), bf16[64,2,128]{2,0,1:T(8,128)(2,1)}) %reduce-scatter.3.cloned.1.call-update) | async-done | bytes 32784 | tf_op jit(solution)/shard_map/reduce_scatter | solution.py:154
  205.3 5.3 %all-to-all-start.6 = ((bf16[4,128,256]{2,1,0:T(8,128)(2,1)}), bf16[4,128,256]{2,1,0:T(8,128)(2,1)}, u32[]{:S(2)}, u32[]{:S(2)}) async-start(bf16[4,128,256]{2,1,0:T(8,128)(2,1)} %all_to_all.130), calls=%async_computation.7 | async-start | bytes 524288 | tf_op jit(solution)/shard_map/all_to_all | solution.py:170
  210.5 3.9 %fusion.9 = bf16[512,2,4,128]{3,0,2,1:T(8,128)(2,1)S(1)} fusion(f32[2,4,512,128]{3,2,1,0:T(8,128)S(1)} %fusion.50, bf16[512,2,128,1]{0,2,3,1:T(8,128)(2,1)S(1)} %bitcast.173, bf16[2,4,512,512]{2,3,1,0:T(8,128)(2,1)} %fusion.1), kind=kOutput, calls=%fused_computation.22 | convolution fusion | flops 538443776 | bytes 7602176 | tf_op jit(solution)/shard_map/while/body/eval_jaxpr/lupa,alx->plux/dot_general | solution.py:126
  217.3 5.3 %all-to-all-start.5 = ((bf16[4,128,1024]{2,1,0:T(8,128)(2,1)}), bf16[4,128,1024]{2,1,0:T(8,128)(2,1)S(1)}, u32[]{:S(2)}, u32[]{:S(2)}) async-start(bf16[4,128,1024]{2,1,0:T(8,128)(2,1)} %all_to_all.126), calls=%async_computation.5 | async-start | bytes 2097152 | tf_op jit(solution)/shard_map/all_to_all | solution.py:169
  225.0 18.6 %all-to-all-done.5 = bf16[4,128,1024]{2,1,0:T(8,128)(2,1)S(1)} async-done(((bf16[4,128,1024]{2,1,0:T(8,128)(2,1)}), bf16[4,128,1024]{2,1,0:T(8,128)(2,1)S(1)}, u32[]{:S(2)}, u32[]{:S(2)}) %all-to-all-start.5) | async-done | bytes 1048608 | tf_op jit(solution)/shard_map/all_to_all | solution.py:169
  243.6 6.8 %all-to-all-start.3 = ((bf16[4,128,1024]{2,1,0:T(8,128)(2,1)}), bf16[4,128,1024]{2,1,0:T(8,128)(2,1)S(1)}, u32[]{:S(2)}, u32[]{:S(2)}) async-start(bf16[4,128,1024]{2,1,0:T(8,128)(2,1)} %all_to_all.119), calls=%async_computation.3 | async-start | bytes 2097152 | tf_op jit(solution)/shard_map/all_to_all | solution.py:168
  255.6 16.6 %all-to-all-done.3 = bf16[4,128,1024]{2,1,0:T(8,128)(2,1)S(1)} async-done(((bf16[4,128,1024]{2,1,0:T(8,128)(2,1)}), bf16[4,128,1024]{2,1,0:T(8,128)(2,1)S(1)}, u32[]{:S(2)}, u32[]{:S(2)}) %all-to-all-start.3) | async-done | bytes 1048608 | tf_op jit(solution)/shard_map/all_to_all | solution.py:168
  (77 shorter events, 56.8 us)
Async XLA Ops:
  7.2 56.3 %copy-start.10 = (s32[1,64]{1,0:T(1,128)S(1)}, s32[1,64]{1,0:T(1,128)}, u32[]{:S(2)}) copy-start(s32[1,64]{1,0:T(1,128)} %param.9) | copy-start | bytes 772
  8.8 12.4 %all-to-all-start = ((bf16[128,4,256]{2,0,1:T(8,128)(2,1)}), bf16[128,4,256]{2,0,1:T(8,128)(2,1)S(1)}, u32[]{:S(2)}, u32[]{:S(2)}) async-start(bf16[128,4,256]{2,0,1:T(8,128)(2,1)} %bitcast.156), calls=%async_computation | async-start | bytes 524288 | tf_op jit(solution)/shard_map/all_to_all | solution.py:15
  21.2 11.5 %all-to-all-start.2 = ((bf16[128,4,256]{2,0,1:T(8,128)(2,1)}), bf16[128,4,256]{2,0,1:T(8,128)(2,1)S(1)}, u32[]{:S(2)}, u32[]{:S(2)}) async-start(bf16[128,4,256]{2,0,1:T(8,128)(2,1)} %bitcast.155), calls=%async_computation.2 | async-start | bytes 524288 | tf_op jit(solution)/shard_map/all_to_all | solution.py:16
  32.7 24.0 %all-to-all-start.1 = ((bf16[128,4,1024]{2,0,1:T(8,128)(2,1)}), bf16[128,4,1024]{2,0,1:T(8,128)(2,1)S(1)}, u32[]{:S(2)}, u32[]{:S(2)}) async-start(bf16[128,4,1024]{2,0,1:T(8,128)(2,1)} %bitcast.154), calls=%async_computation.1 | async-start | bytes 2097152 | tf_op jit(solution)/shard_map/all_to_all | solution.py:14
  56.7 29.9 %all-to-all-start.4 = ((bf16[128,4,1024]{2,0,1:T(8,128)(2,1)}), bf16[128,4,1024]{2,0,1:T(8,128)(2,1)S(1)}, u32[]{:S(2)}, u32[]{:S(2)}) async-start(bf16[128,4,1024]{2,0,1:T(8,128)(2,1)} %bitcast.153), calls=%async_computation.4 | async-start | bytes 2097152 | tf_op jit(solution)/shard_map/all_to_all | solution.py:17
  63.5 99.7 %reduce-scatter.5.cloned.1.call-start = ((), (), s32[]{:S(2)}) async-start(), calls=%async_computation.11 | async-start | bytes 294912 | tf_op jit(solution)/shard_map/reduce_scatter | solution.py:157
  87.4 2.2 copy-start.5
  87.4 2.2 copy-start.6
  91.3 6.1 %copy-start.1 = (f32[2,512,512,4]{2,1,3,0:T(8,128)}, f32[2,512,512,4]{2,1,3,0:T(8,128)S(1)}, u32[]{:S(2)}) copy-start(f32[2,512,512,4]{2,1,3,0:T(8,128)S(1)} %get-tuple-element.77) | copy-start | bytes 25165828
  97.5 3.6 %copy-start = (f32[2,4,512,512]{2,3,1,0:T(8,128)}, f32[2,4,512,512]{2,3,1,0:T(8,128)S(1)}, u32[]{:S(2)}) copy-start(f32[2,4,512,512]{2,3,1,0:T(8,128)S(1)} %fusion.6) | copy-start | bytes 25165828
  101.0 2.0 copy-start.4
  101.0 7.3 %copy-start.9 = (bf16[512,2,128]{2,1,0:T(2,128)(2,1)S(1)}, bf16[512,2,128]{2,1,0:T(2,128)(2,1)}, u32[]{:S(2)}) copy-start(bf16[512,2,128]{2,1,0:T(2,128)(2,1)} %reshape.112) | copy-start | bytes 786436
  103.0 5.8 %copy-start.2 = (f32[2,512,512,4]{2,1,3,0:T(8,128)S(1)}, f32[2,512,512,4]{2,1,3,0:T(8,128)}, u32[]{:S(2)}) copy-start(f32[2,512,512,4]{2,1,3,0:T(8,128)} %copy-done.1) | copy-start | bytes 25165828
  121.8 6.8 %copy-start.8 = (f32[512,2,128]{2,0,1:T(8,128)S(1)}, f32[512,2,128]{2,0,1:T(8,128)}, u32[]{:S(2)}) copy-start(f32[512,2,128]{2,0,1:T(8,128)} %fusion.21) | copy-start | bytes 1572868
  128.5 72.1 %reduce-scatter.3.cloned.1.call-start = ((), (), s32[]{:S(2)}) async-start(), calls=%async_computation.10 | async-start | bytes 294912 | tf_op jit(solution)/shard_map/reduce_scatter | solution.py:154
  167.8 37.5 %all-to-all-start.7 = ((bf16[4,128,256]{2,1,0:T(8,128)(2,1)}), bf16[4,128,256]{2,1,0:T(8,128)(2,1)}, u32[]{:S(2)}, u32[]{:S(2)}) async-start(bf16[4,128,256]{2,1,0:T(8,128)(2,1)} %all_to_all.134), calls=%async_computation.9 | async-start | bytes 524288 | tf_op jit(solution)/shard_map/all_to_all | solution.py:171
  172.9 4.0 %copy-start.3 = (bf16[2,4,512,512]{2,3,1,0:T(8,128)(2,1)S(1)}, bf16[2,4,512,512]{2,3,1,0:T(8,128)(2,1)}, u32[]{:S(2)}) copy-start(bf16[2,4,512,512]{2,3,1,0:T(8,128)(2,1)} %fusion.3) | copy-start | bytes 12582916
  205.3 17.3 %copy-start.7 = (bf16[512,2,4,128]{3,0,2,1:T(8,128)(2,1)S(1)}, bf16[512,2,4,128]{3,0,2,1:T(8,128)(2,1)}, u32[]{:S(2)}) copy-start(bf16[512,2,4,128]{3,0,2,1:T(8,128)(2,1)} %get-tuple-element.81) | copy-start | bytes 3145732
  205.3 12.0 %all-to-all-start.6 = ((bf16[4,128,256]{2,1,0:T(8,128)(2,1)}), bf16[4,128,256]{2,1,0:T(8,128)(2,1)}, u32[]{:S(2)}, u32[]{:S(2)}) async-start(bf16[4,128,256]{2,1,0:T(8,128)(2,1)} %all_to_all.130), calls=%async_computation.7 | async-start | bytes 524288 | tf_op jit(solution)/shard_map/all_to_all | solution.py:170
  217.3 26.3 %all-to-all-start.5 = ((bf16[4,128,1024]{2,1,0:T(8,128)(2,1)}), bf16[4,128,1024]{2,1,0:T(8,128)(2,1)S(1)}, u32[]{:S(2)}, u32[]{:S(2)}) async-start(bf16[4,128,1024]{2,1,0:T(8,128)(2,1)} %all_to_all.126), calls=%async_computation.5 | async-start | bytes 2097152 | tf_op jit(solution)/shard_map/all_to_all | solution.py:169
  243.6 28.7 %all-to-all-start.3 = ((bf16[4,128,1024]{2,1,0:T(8,128)(2,1)}), bf16[4,128,1024]{2,1,0:T(8,128)(2,1)S(1)}, u32[]{:S(2)}, u32[]{:S(2)}) async-start(bf16[4,128,1024]{2,1,0:T(8,128)(2,1)} %all_to_all.119), calls=%async_computation.3 | async-start | bytes 2097152 | tf_op jit(solution)/shard_map/all_to_all | solution.py:168
Sparse Core Ops, SparseCore 0:
  128.7 34.4 reduce-scatter.4
  167.1 33.5 reduce-scatter.2
where the time goes:
time: 286 us; the launch traced here: 281 us
  waiting for transfers between devices  114 us (40%)
  matrix products  45.5 us (16%)
  starting transfers between devices  44.1 us (15%)
  local copies, waits for them, and re-layouts  30.2 us (11%)
  blocking collectives  17.7 us (6%)
  other arithmetic  14.8 us (5%)
  between operations  14.3 us (5%)
    reduce_scatter x1, waiting for transfers between devices, local(): lax.psum_scatter(value_buffer.astype(jnp.bfloat16), 'ctx', scatter_dimens...  30 us
    reduce_scatter x1, waiting for transfers between devices, local(): lax.psum_scatter(key_buffer.astype(jnp.bfloat16), 'ctx', scatter_dimensio...  21.9 us
    all_to_all x1, waiting for transfers between devices, local(): lax.all_to_all(query_out, 'head', split_axis=0, concat_axis=1, tiled=True)  18.6 us
    all_to_all x1, waiting for transfers between devices, local(): lax.all_to_all(queries, 'head', split_axis=1, concat_axis=0, tiled=True)  17.4 us
    all_to_all x1, waiting for transfers between devices, local(): lax.all_to_all(attended_out, 'head', split_axis=0, concat_axis=1, tiled=T...  16.6 us
    all_gather x1, blocking collectives, local(): lax.all_gather(key_rows[positions], 'ctx', axis=0, tiled=True)  9.32 us
    all_gather x1, blocking collectives, local(): lax.all_gather(value_rows[positions], 'ctx', axis=0, tiled=True)  8.34 us
    dot_general x1, matrix products, local(): jnp.einsum('wkgd,vkd->kgwv', head_gradients, value_heads, preferred_eleme...  6.77 us
  transfers between devices with their start and end apart: 10, of which 8 were waited for; matrix products, arithmetic and copies ran while one was open for 14% of the time, Pallas kernels for 0%

commit v1 on v0

v1 whole, which is shorter than its diff:
```python
import jax
import jax.numpy as jnp
from jax import lax
from jax.sharding import PartitionSpec as P

HD = 128


NEG_FILL = -1e30


def local(queries, keys, values, out_grad, beacon_pos):
    rows = queries.shape[0]
    kv_width = keys.shape[1]
    kv_heads = kv_width // HD
    group_size = queries.shape[1] // HD // kv_heads
    scaling = HD ** (-0.5)
    head_id = lax.axis_index("head")
    shard_id = lax.axis_index("ctx")

    kv_rows = jnp.concatenate([keys, values], axis=1)
    kv_window = lax.all_gather(kv_rows, "head", axis=0, tiled=True)
    window = kv_window.shape[0]
    positions = beacon_pos[0]
    per_shard = positions.shape[0]
    kv_beacons = lax.all_gather(kv_window[positions], "ctx", axis=0, tiled=True)
    beacon_total = kv_beacons.shape[0]
    kv_all = jnp.concatenate([kv_window, kv_beacons], axis=0)
    key_count = window + beacon_total
    key_heads = kv_all[:, :kv_width].reshape(key_count, kv_heads, HD).transpose(1, 0, 2)
    value_heads = kv_all[:, kv_width:].reshape(key_count, kv_heads, HD).transpose(1, 0, 2)

    query_heads = queries.reshape(rows, kv_heads, group_size, HD).transpose(1, 2, 0, 3)
    grad_heads = out_grad.reshape(rows, kv_heads, group_size, HD).transpose(1, 2, 0, 3)

    query_pos = head_id * rows + jnp.arange(rows)
    causal = query_pos[:, None] >= jnp.arange(window)[None, :]
    owners = jnp.arange(beacon_total, dtype=jnp.int32) // per_shard
    seen = jnp.broadcast_to((owners < shard_id)[None, :], (rows, beacon_total))
    visible = jnp.concatenate([causal, seen], axis=1)

    def per_head(inputs):
        q_part, g_part, k_part, v_part = inputs
        scores = jnp.einsum("grd,kd->grk", q_part, k_part, preferred_element_type=jnp.float32) * scaling
        scores = jnp.where(visible, scores, NEG_FILL)
        row_max = jnp.max(scores, axis=-1, keepdims=True)
        weights = jnp.exp(scores - row_max)
        probs = weights / jnp.sum(weights, axis=-1, keepdims=True)
        probs_low = probs.astype(jnp.bfloat16)
        attended = jnp.einsum(
            "grk,kd->grd", probs_low, v_part, preferred_element_type=jnp.float32
        ).astype(jnp.bfloat16)
        row_dot = jnp.sum(
            g_part.astype(jnp.float32) * attended.astype(jnp.float32), axis=-1, keepdims=True
        )
        dprob = jnp.einsum("grd,kd->grk", g_part, v_part, preferred_element_type=jnp.float32)
        grad_scores = (probs * (dprob - row_dot)).astype(jnp.bfloat16)
        query_grad = (
            jnp.einsum("grk,kd->grd", grad_scores, k_part, preferred_element_type=jnp.float32)
            * scaling
        ).astype(jnp.bfloat16)
        key_grad = (
            jnp.einsum("grk,grd->kd", grad_scores, q_part, preferred_element_type=jnp.float32)
            * scaling
        )
        value_grad = jnp.einsum("grk,grd->kd", probs_low, g_part, preferred_element_type=jnp.float32)
        return attended, query_grad, key_grad, value_grad

    attended, query_grad, key_grad, value_grad = lax.map(
        per_head, (query_heads, grad_heads, key_heads, value_heads)
    )
    attended_out = attended.transpose(2, 0, 1, 3).reshape(rows, -1)
    query_out = query_grad.transpose(2, 0, 1, 3).reshape(rows, -1)
    kv_grads = jnp.concatenate(
        [
            key_grad.transpose(1, 0, 2).reshape(key_count, kv_width),
            value_grad.transpose(1, 0, 2).reshape(key_count, kv_width),
        ],
        axis=1,
    )
    own_beacons = lax.psum_scatter(
        kv_grads[window:].astype(jnp.bfloat16), "ctx", scatter_dimension=0, tiled=True
    ).astype(jnp.float32)
    window_grads = kv_grads[:window].at[positions].add(own_beacons)
    own_grads = lax.psum_scatter(
        window_grads.astype(jnp.bfloat16), "head", scatter_dimension=0, tiled=True
    )
    return attended_out, query_out, own_grads[:, :kv_width], own_grads[:, kv_width:]


def solution(mesh):
    in_specs = (
        P(("ctx", "head"), None),
        P(("ctx", "head"), None),
        P(("ctx", "head"), None),
        P(("ctx", "head"), None),
        P("ctx", None),
    )
    out_specs = (
        P(("ctx", "head"), None),
        P(("ctx", "head"), None),
        P(("ctx", "head"), None),
        P(("ctx", "head"), None),
    )
    return jax.shard_map(local, mesh=mesh, in_specs=in_specs, out_specs=out_specs, check_vma=False)
```

time: 286 us -> 346 us (1.21)
  matrix products: 45.5 us -> 122 us
  starting transfers between devices: 44.1 us -> 0.16 us
  waiting for transfers between devices: 114 us -> 142 us
  blocking collectives: 17.7 us -> 0 us
  local copies, waits for them, and re-layouts: 30.2 us -> 42.7 us
  other arithmetic: 14.8 us -> 20.1 us
    all_gather x0 -> x2, waiting for transfers between devices: none -> 68.3 us  [the longest x1 45.8 us: local(): kv_window = lax.all_gather(kv_rows, 'head', axis=0, tiled=True)]
    all_to_all x8 -> x0, waiting for transfers between devices: 62.5 us -> none  [the longest x1 18.6 us: local(): lax.all_to_all(query_out, 'head', split_axis=0, concat_axis=1, tiled=True)]
    dot_general x12 -> x40, matrix products: 45.5 us -> 96 us  [the longest x8 26.8 us: per_head(): jnp.einsum('grk,grd->kd', probs_low, g_part, preferred_element_type=jnp.f...]
    all_to_all x8 -> x0, starting transfers between devices: 44 us -> none  [the longest x1 6.76 us: local(): lax.all_to_all(out_grad, 'head', split_axis=1, concat_axis=0, tiled=True)]
    sub x0 -> x8, matrix products: none -> 25.6 us  [per_head(): weights = jnp.exp(scores - row_max)]
    reduce_scatter x2, waiting for transfers between devices: 51.9 us -> 73.5 us  [the longest x1 36.9 us: local(): lax.psum_scatter(window_grads.astype(jnp.bfloat16), 'head', scatter_dimen...]
    all_gather x2 -> x0, blocking collectives: 17.7 us -> none  [the longest x1 9.32 us: local(): lax.all_gather(key_rows[positions], 'ctx', axis=0, tiled=True)]
    all_to_all x12 -> x0, local copies, waits for them, and re-layouts: 17.4 us -> none  [the longest x2 2.55 us: local(): lax.all_to_all(value_out, 'head', split_axis=0, concat_axis=1, tiled=True)]
  transfers between devices with their start and end apart: 10 -> 4, of which waited for: 8 -> 4; matrix products, arithmetic and copies ran while one was open for 14% -> 4% of each run, Pallas kernels for 0% -> 0%
where the time goes in v1:
time: 346 us; the launch traced here: 340 us
  waiting for transfers between devices  142 us (41%)
  matrix products  122 us (35%)
  local copies, waits for them, and re-layouts  42.7 us (12%)
  other arithmetic  20.1 us (6%)
  between operations  13.9 us (4%)
    all_gather x1, waiting for transfers between devices, local(): kv_window = lax.all_gather(kv_rows, 'head', axis=0, tiled=True)  45.8 us
    reduce_scatter x1, waiting for transfers between devices, local(): lax.psum_scatter(window_grads.astype(jnp.bfloat16), 'head', scatter_dimen...  36.9 us
    reduce_scatter x1, waiting for transfers between devices, local(): lax.psum_scatter(kv_grads[window:].astype(jnp.bfloat16), 'ctx', scatter_d...  36.6 us
    dot_general x8, matrix products, per_head(): jnp.einsum('grk,grd->kd', probs_low, g_part, preferred_element_type=jnp.f...  26.8 us
    sub x8, matrix products, per_head(): weights = jnp.exp(scores - row_max)  25.6 us
    dot_general x8, matrix products, per_head(): jnp.einsum('grk,kd->grd', probs_low, v_part, preferred_element_type=jnp.f...  24.7 us
    all_gather x1, waiting for transfers between devices, local(): kv_beacons = lax.all_gather(kv_window[positions], 'ctx', axis=0, tiled=True)  22.5 us
    dot_general x8, matrix products, per_head(): jnp.einsum('grd,kd->grk', g_part, v_part, preferred_element_type=jnp.floa...  17.9 us
  transfers between devices with their start and end apart: 4, of which 4 were waited for; matrix products, arithmetic and copies ran while one was open for 4% of the time, Pallas kernels for 0%

profile of v1, /device:TPU:10, one launch (start us, length us, event | category | flops | bytes accessed | tf_op | source)
XLA Modules:
  0.0 340.3 jit_solution(13346720008451056820)
XLA Ops:
  9.8 45.8 %all-gather.4.cloned.1.call-done = bf16[512,2048]{1,0:T(8,128)(2,1)} async-done(((bf16[128,2048]{1,0:T(8,128)(2,1)}), bf16[512,2048]{1,0:T(8,128)(2,1)}) %all-gather.4.cloned.1.call-update) | async-done | bytes 2097168 | tf_op jit(solution)/shard_map/all_gather | solution.py:22
  55.6 3.5 %gather_fusion = bf16[64,2048]{1,0:T(8,128)(2,1)} fusion(bf16[512,2048]{1,0:T(8,128)(2,1)} %all-gather.4.cloned.1.call-done, s32[1024]{0:T(1024)S(1)} %pad_clamp_fusion), kind=kCustom, calls=%fused_computation | custom fusion | bytes 524544 | tf_op jit(solution)/shard_map/gather | solution.py:26
  65.1 22.5 %all-gather.6.cloned.1.call-done = bf16[512,2048]{1,0:T(8,128)(2,1)} async-done(((bf16[64,2048]{1,0:T(8,128)(2,1)}), bf16[512,2048]{1,0:T(8,128)(2,1)}) %all-gather.6.cloned.1.call-update) | async-done | bytes 2097168 | tf_op jit(solution)/shard_map/all_gather | solution.py:26
  90.7 4.5 %fusion.86 = (bf16[1024,1024]{1,0:T(8,128)(2,1)}, bf16[128,8,8,128]{3,2,1,0:T(8,128)(2,1)S(1)}) fusion(bf16[1024,2048]{1,0:T(8,128)(2,1)} %constant_dynamic-update-slice_fusion), kind=kLoop, calls=%fused_computation.78 | loop fusion | bytes 8388608 | tf_op jit(solution)/shard_map/slice | solution.py:31
  95.2 3.9 %copy.43 = bf16[1024,1024]{0,1:T(8,128)(2,1)} copy(bf16[1024,1024]{1,0:T(8,128)(2,1)} %get-tuple-element.107) | data formatting | bytes 4194304 | tf_op jit(solution)/shard_map/reshape | solution.py:31
  100.8 129.3 %while.16 = (s32[]{:T(128)}, bf16[8,4,128,128]{2,3,1,0:T(8,128)(2,1)}, bf16[8,4,128,128]{3,2,1,0:T(8,128)(2,1)}, f32[8,1024,128]{2,1,0:T(8,128)}, f32[8,1024,128...) while((s32[]{:T(128)}, ...), condition=%wide.region_4.5_spmd, body=%wide.region_0.4_spmd.sunk | while | flops 1083772416 | bytes 11817081 | solution.py:69
  113.6 3.3 fusion.127
  116.9 3.2 fusion.124
  129.7 3.4 fusion.127
  133.1 3.2 fusion.124
  145.9 3.3 fusion.127
  162.1 3.4 fusion.127
  178.3 3.4 fusion.127
  181.6 3.2 fusion.124
  194.4 3.4 fusion.127
  210.6 3.3 fusion.127
  213.9 3.2 fusion.124
  226.7 3.4 fusion.127
  234.1 3.2 copy-done
  239.1 4.7 %slice.29 = f32[512,2048]{1,0:T(8,128)} slice(f32[1024,2048]{1,0:T(8,128)} %copy-done), slice={[0:512], [0:2048]} | slice | bytes 8388608 | tf_op jit(solution)/shard_map/slice | solution.py:84
  243.8 36.6 %reduce-scatter.3.cloned.1.call-done = bf16[64,2048]{1,0:T(8,128)(2,1)} async-done(((bf16[512,2048]{1,0:T(8,128)(2,1)}), bf16[64,2048]{1,0:T(8,128)(2,1)}) %reduce-scatter.3.cloned.1.call-update) | async-done | bytes 262160 | tf_op jit(solution)/shard_map/reduce_scatter | solution.py:81
  280.4 5.9 %scatter_custom_fusion = f32[512,2048]{1,0:T(8,128)} fusion(f32[512,2048]{1,0:T(8,128)} %slice.29, s32[64]{0:T(128)S(1)} %fusion.76, bf16[64,2048]{1,0:T(8,128)(2,1)} %reduce-scatter.3.cloned.1.call-done), kind=kCustom, calls=%fused_computation.59 | custom fusion | flops 262144 | bytes 4456448 | tf_op jit(solution)/shard_map/scatter-add | solution.py:84
  286.3 3.9 %convert_element_type.26 = bf16[512,2048]{1,0:T(8,128)(2,1)} convert(f32[512,2048]{1,0:T(8,128)} %scatter_custom_fusion) | non-fusion elementwise | flops 1048576 | bytes 6291456 | tf_op jit(solution)/shard_map/convert_element_type | solution.py:86
  295.1 36.9 %reduce-scatter.5.cloned.1.call-done = bf16[128,2048]{1,0:T(8,128)(2,1)} async-done(((bf16[512,2048]{1,0:T(8,128)(2,1)}), bf16[128,2048]{1,0:T(8,128)(2,1)}) %reduce-scatter.5.cloned.1.call-update) | async-done | bytes 524304 | tf_op jit(solution)/shard_map/reduce_scatter | solution.py:85
  (85 shorter events, 115.4 us)
Async XLA Ops:
  7.2 48.5 %all-gather.4.cloned.1.call-start = ((), (), s32[]{:S(2)}) async-start(), calls=%async_computation.2 | async-start | bytes 2621440 | tf_op jit(solution)/shard_map/all_gather | solution.py:22
  9.1 78.5 %all-gather.6.cloned.1.call-start = ((), (), s32[]{:S(2)}) async-start(), calls=%async_computation.5 | async-start | bytes 2359296 | tf_op jit(solution)/shard_map/all_gather | solution.py:26
  59.2 221.1 %reduce-scatter.3.cloned.1.call-start = ((), (), s32[]{:S(2)}) async-start(), calls=%async_computation.3 | async-start | bytes 2359296 | tf_op jit(solution)/shard_map/reduce_scatter | solution.py:81
  59.3 4.2 %copy-start.1 = (bf16[512,2048]{1,0:T(8,128)(2,1)S(1)}, bf16[512,2048]{1,0:T(8,128)(2,1)}, u32[]{:S(2)}) copy-start(bf16[512,2048]{1,0:T(8,128)(2,1)} %all-gather.4.cloned.1.call-done) | copy-start | bytes 6291460
  230.1 3.4 %copy-start.2 = (f32[8,1024,128]{2,1,0:T(8,128)S(1)}, f32[8,1024,128]{2,1,0:T(8,128)}, u32[]{:S(2)}) copy-start(f32[8,1024,128]{2,1,0:T(8,128)} %get-tuple-element.62) | copy-start | bytes 12582916
  234.1 3.2 copy-start
  239.0 92.9 %reduce-scatter.5.cloned.1.call-start = ((), (), s32[]{:S(2)}) async-start(), calls=%async_computation.4 | async-start | bytes 2621440 | tf_op jit(solution)/shard_map/reduce_scatter | solution.py:85
  290.1 1.2 copy-start.4
  290.1 2.5 copy-start.3
Sparse Core Ops, SparseCore 0:
  10.1 45.4 all-gather.3
  59.3 28.2 all-gather.5
  239.2 41.1 reduce-scatter.2
  290.3 41.6 reduce-scatter.4

commit v2 on v1

v2 whole, which is shorter than its diff:
```python
import functools
import jax
import jax.numpy as jnp
from jax import lax
from jax.experimental import pallas as pl
from jax.experimental.pallas import tpu as pltpu
from jax.sharding import PartitionSpec as P

HD = 128


NEG_FILL = -1e30


def attention_kernel(
    ids_ref, q_ref, g_ref, k_ref, v_ref, att_ref, dq_ref, dk_ref, dv_ref, *, rows, window, per_shard, group_size
):
    scaling = HD ** (-0.5)
    head_id = ids_ref[0]
    shard_id = ids_ref[1]
    key_count = k_ref.shape[0]
    k = k_ref[...]
    v = v_ref[...]
    row = lax.broadcasted_iota(jnp.int32, (rows, key_count), 0) + head_id * rows
    col = lax.broadcasted_iota(jnp.int32, (rows, key_count), 1)
    in_window = col < window
    visible = (in_window & (row >= col)) | (
        jnp.logical_not(in_window) & (col < window + shard_id * per_shard)
    )
    nt = (((1,), (1,)), ((), ()))
    tn = (((0,), (0,)), ((), ()))
    dk_acc = jnp.zeros((key_count, HD), jnp.float32)
    dv_acc = jnp.zeros((key_count, HD), jnp.float32)
    for g in range(group_size):
        cols = slice(g * HD, (g + 1) * HD)
        q = q_ref[:, cols]
        do = g_ref[:, cols]
        scores = lax.dot_general(q, k, nt, preferred_element_type=jnp.float32) * scaling
        scores = jnp.where(visible, scores, NEG_FILL)
        row_max = jnp.max(scores, axis=1, keepdims=True)
        weights = jnp.exp(scores - row_max)
        probs = weights / jnp.sum(weights, axis=1, keepdims=True)
        probs_low = probs.astype(jnp.bfloat16)
        attended = jnp.dot(probs_low, v, preferred_element_type=jnp.float32).astype(jnp.bfloat16)
        att_ref[:, cols] = attended
        row_dot = jnp.sum(do.astype(jnp.float32) * attended.astype(jnp.float32), axis=1, keepdims=True)
        dprob = lax.dot_general(do, v, nt, preferred_element_type=jnp.float32)
        grad_scores = (probs * (dprob - row_dot)).astype(jnp.bfloat16)
        dq_ref[:, cols] = (
            jnp.dot(grad_scores, k, preferred_element_type=jnp.float32) * scaling
        ).astype(jnp.bfloat16)
        dk_acc = dk_acc + lax.dot_general(grad_scores, q, tn, preferred_element_type=jnp.float32)
        dv_acc = dv_acc + lax.dot_general(probs_low, do, tn, preferred_element_type=jnp.float32)
    dk_ref[...] = dk_acc * scaling
    dv_ref[...] = dv_acc


def attend_all(ids, queries, out_grad, kv_all, window, per_shard):
    rows, q_width = queries.shape
    key_count, kv_double = kv_all.shape
    kv_heads = kv_double // 2 // HD
    group_size = q_width // HD // kv_heads
    kernel = functools.partial(
        attention_kernel, rows=rows, window=window, per_shard=per_shard, group_size=group_size
    )
    qblock = pl.BlockSpec((rows, group_size * HD), lambda h, ids: (0, h))
    kblock = pl.BlockSpec((key_count, HD), lambda h, ids: (0, h))
    vblock = pl.BlockSpec((key_count, HD), lambda h, ids: (0, h + kv_heads))
    return pl.pallas_call(
        kernel,
        grid_spec=pltpu.PrefetchScalarGridSpec(
            num_scalar_prefetch=1,
            grid=(kv_heads,),
            in_specs=[qblock, qblock, kblock, vblock],
            out_specs=[qblock, qblock, kblock, kblock],
        ),
        out_shape=[
            jax.ShapeDtypeStruct((rows, q_width), jnp.bfloat16),
            jax.ShapeDtypeStruct((rows, q_width), jnp.bfloat16),
            jax.ShapeDtypeStruct((key_count, kv_heads * HD), jnp.float32),
            jax.ShapeDtypeStruct((key_count, kv_heads * HD), jnp.float32),
        ],
    )(ids, queries, out_grad, kv_all, kv_all)


def local(queries, keys, values, out_grad, beacon_pos):
    rows = queries.shape[0]
    kv_width = keys.shape[1]
    head_id = lax.axis_index("head")
    shard_id = lax.axis_index("ctx")

    kv_rows = jnp.concatenate([keys, values], axis=1)
    kv_window = lax.all_gather(kv_rows, "head", axis=0, tiled=True)
    window = kv_window.shape[0]
    positions = beacon_pos[0]
    per_shard = positions.shape[0]
    kv_beacons = lax.all_gather(kv_window[positions], "ctx", axis=0, tiled=True)
    kv_all = jnp.concatenate([kv_window, kv_beacons], axis=0)
    ids = jnp.stack([head_id, shard_id]).astype(jnp.int32)
    attended_out, query_out, key_grad, value_grad = attend_all(
        ids, queries, out_grad, kv_all, window, per_shard
    )
    kv_grads = jnp.concatenate([key_grad, value_grad], axis=1)
    own_beacons = lax.psum_scatter(
        kv_grads[window:].astype(jnp.bfloat16), "ctx", scatter_dimension=0, tiled=True
    ).astype(jnp.float32)
    window_grads = kv_grads[:window].at[positions].add(own_beacons)
    own_grads = lax.psum_scatter(
        window_grads.astype(jnp.bfloat16), "head", scatter_dimension=0, tiled=True
    )
    return attended_out, query_out, own_grads[:, :kv_width], own_grads[:, kv_width:]


def solution(mesh):
    in_specs = (
        P(("ctx", "head"), None),
        P(("ctx", "head"), None),
        P(("ctx", "head"), None),
        P(("ctx", "head"), None),
        P("ctx", None),
    )
    out_specs = (
        P(("ctx", "head"), None),
        P(("ctx", "head"), None),
        P(("ctx", "head"), None),
        P(("ctx", "head"), None),
    )
    return jax.shard_map(local, mesh=mesh, in_specs=in_specs, out_specs=out_specs, check_vma=False)
```

time: 346 us -> 239 us (0.69)
  matrix products: 122 us -> 0 us
  Pallas kernels: 0 us -> 31.9 us
  local copies, waits for them, and re-layouts: 42.7 us -> 18.9 us
  waiting for transfers between devices: 142 us -> 152 us
    dot_general x40 -> x0, matrix products: 96 us -> none  [the longest x8 26.8 us: per_head(): jnp.einsum('grk,grd->kd', probs_low, g_part, preferred_element_type=jnp.f...]
    pallas_call x0 -> x1, Pallas kernels: none -> 31.9 us  [attend_all(): pl.pallas_call(kernel, grid_spec=pltpu.PrefetchScalarGridSpec(num_scalar_...]
    sub x8 -> x0, matrix products: 25.6 us -> none  [per_head(): weights = jnp.exp(scores - row_max)]
    reshape x4 -> x0, local copies, waits for them, and re-layouts: 8.52 us -> none  [the longest x1 3.93 us: local(): kv_all[:, kv_width:].reshape(key_count, kv_heads, HD).transpose(1, 0, 2)]
    reduce_sum x8 -> x0, other arithmetic: 7.63 us -> none  [per_head(): jnp.sum(g_part.astype(jnp.float32) * attended.astype(jnp.float32), axis=-...]
    unnamed x14 -> x5, local copies, waits for them, and re-layouts: 13.4 us -> 6.67 us
    all_gather x1, waiting for transfers between devices: 22.5 us -> 27.7 us  [local(): kv_beacons = lax.all_gather(kv_window[positions], 'ctx', axis=0, tiled=True)]
    reduce_scatter x1, waiting for transfers between devices: 36.9 us -> 41.8 us  [local(): lax.psum_scatter(window_grads.astype(jnp.bfloat16), 'head', scatter_dimen...]
  transfers between devices with their start and end apart: 4 -> 4, of which waited for: 4 -> 4; matrix products, arithmetic and copies ran while one was open for 4% -> 3% of each run, Pallas kernels for 0% -> 0%
where the time goes in v2:
time: 239 us; the launch traced here: 234 us
  waiting for transfers between devices  152 us (64%)
  Pallas kernels  31.9 us (13%)
  local copies, waits for them, and re-layouts  18.9 us (8%)
  other arithmetic  17.7 us (7%)
  between operations  13.8 us (6%)
    all_gather x1, waiting for transfers between devices, local(): kv_window = lax.all_gather(kv_rows, 'head', axis=0, tiled=True)  45.8 us
    reduce_scatter x1, waiting for transfers between devices, local(): lax.psum_scatter(window_grads.astype(jnp.bfloat16), 'head', scatter_dimen...  41.8 us
    reduce_scatter x1, waiting for transfers between devices, local(): lax.psum_scatter(kv_grads[window:].astype(jnp.bfloat16), 'ctx', scatter_d...  36.6 us
    pallas_call x1, Pallas kernels, attend_all(): pl.pallas_call(kernel, grid_spec=pltpu.PrefetchScalarGridSpec(num_scalar_...  31.9 us
    all_gather x1, waiting for transfers between devices, local(): kv_beacons = lax.all_gather(kv_window[positions], 'ctx', axis=0, tiled=True)  27.7 us
    unnamed x5, local copies, waits for them, and re-layouts  6.67 us
    scatter-add x1, other arithmetic, local(): window_grads = kv_grads[:window].at[positions].add(own_beacons)  5.91 us
  transfers between devices with their start and end apart: 4, of which 4 were waited for; matrix products, arithmetic and copies ran while one was open for 3% of the time, Pallas kernels for 0%

profile of v2, /device:TPU:10, one launch (start us, length us, event | category | flops | bytes accessed | tf_op | source)
XLA Modules:
  0.0 234.4 jit_solution(14902707552132354666)
XLA Ops:
  7.2 0.0 all-gather.4.cloned.1.call-start
  7.2 1.9 pad_maximum_fusion.1
  9.1 0.0 all-gather.6.cloned.1.call-start
  9.2 0.7 fusion.2
  9.8 45.8 %all-gather.4.cloned.1.call-done = bf16[512,2048]{1,0:T(8,128)(2,1)} async-done(((bf16[128,2048]{1,0:T(8,128)(2,1)}), bf16[512,2048]{1,0:T(8,128)(2,1)}) %all-gather.4.cloned.1.call-update) | async-done | bytes 2097168 | tf_op jit(solution)/shard_map/all_gather | solution.py:93
  55.6 3.5 %gather_fusion = bf16[64,2048]{1,0:T(8,128)(2,1)} fusion(bf16[512,2048]{1,0:T(8,128)(2,1)} %all-gather.4.cloned.1.call-done, s32[1024]{0:T(1024)S(1)} %pad_clamp_fusion), kind=kCustom, calls=%fused_computation | custom fusion | bytes 524544 | tf_op jit(solution)/shard_map/gather | solution.py:97
  59.2 0.0 all-gather.6.cloned.1.call-update
  59.2 0.0 reduce-scatter.3.cloned.1.call-start
  59.3 0.6 pad_add_fusion.ids_ref
  59.9 27.7 %all-gather.6.cloned.1.call-done = bf16[512,2048]{1,0:T(8,128)(2,1)} async-done(((bf16[64,2048]{1,0:T(8,128)(2,1)}), bf16[512,2048]{1,0:T(8,128)(2,1)}) %all-gather.6.cloned.1.call-update) | async-done | bytes 2097168 | tf_op jit(solution)/shard_map/all_gather | solution.py:97
  87.6 4.7 %pad_maximum_fusion.k_ref.v_ref = bf16[1024,2048]{1,0:T(8,128)(2,1)} fusion(bf16[512,2048]{1,0:T(8,128)(2,1)} %all-gather.6.cloned.1.call-done, bf16[512,2048]{1,0:T(8,128)(2,1)} %all-gather.4.cloned.1.call-done), kind=kLoop, calls=%fused_computation.3 | loop fusion | flops 8388608 | bytes 8388608 | tf_op jit(solution)/shard_map/concatenate | solution.py:98
  92.3 31.9 %shard_map.84 = (bf16[128,4096]{1,0:T(8,128)(2,1)}, bf16[128,4096]{1,0:T(8,128)(2,1)}, f32[1024,1024]{1,0:T(8,128)}, f32[1024,1024]{1,0:T(8,128)}) custom-call(s32[2]{0:T(128)} %pad_add_fusion.ids_ref, bf16[128,4096]{1,0:T(8,128)(2,1)} %q_ref.1, bf16[128,4096]{1,0:T(8,128)(2,1)} %g_ref.1, bf16[1024,2048]{1,0:T(8,128)(2,1)} %pad_maximum_fusion.k_ref.v_ref, ...), custom_call_target="tpu_custom_call" | custom-call | tf_op jit(solution)/shard_map/pallas_call | solution.py:69
  124.2 2.7 %constant_dynamic-update-slice_fusion.1 = f32[1024,2048]{1,0:T(8,128)S(1)} fusion(f32[1024,1024]{1,0:T(8,128)} %get-tuple-element.10), kind=kLoop, calls=%fused_computation.9 | loop fusion | bytes 8388608
  126.9 0.8 copy-done.1
  127.7 0.6 constant_dynamic-update-slice_fusion
  128.2 3.2 %copy-done = f32[1024,2048]{1,0:T(8,128)} copy-done((f32[1024,2048]{1,0:T(8,128)}, f32[1024,2048]{1,0:T(8,128)S(1)}, u32[]{:S(2)}) %copy-start) | copy-done | bytes 8388632
  131.5 1.6 slice.24
  133.1 0.0 reduce-scatter.5.cloned.1.call-start
  133.2 4.6 %slice.19 = f32[512,2048]{1,0:T(8,128)} slice(f32[1024,2048]{1,0:T(8,128)} %copy-done), slice={[0:512], [0:2048]} | slice | bytes 8388608 | tf_op jit(solution)/shard_map/slice | solution.py:107
  137.8 36.6 %reduce-scatter.3.cloned.1.call-done = bf16[64,2048]{1,0:T(8,128)(2,1)} async-done(((bf16[512,2048]{1,0:T(8,128)(2,1)}), bf16[64,2048]{1,0:T(8,128)(2,1)}) %reduce-scatter.3.cloned.1.call-update) | async-done | bytes 262160 | tf_op jit(solution)/shard_map/reduce_scatter | solution.py:104
  174.5 5.9 %scatter_custom_fusion = f32[512,2048]{1,0:T(8,128)} fusion(f32[512,2048]{1,0:T(8,128)} %slice.19, s32[64]{0:T(128)S(1)} %fusion.2, bf16[64,2048]{1,0:T(8,128)(2,1)} %reduce-scatter.3.cloned.1.call-done), kind=kCustom, calls=%fused_computation.5 | custom fusion | flops 262144 | bytes 4456448 | tf_op jit(solution)/shard_map/scatter-add | solution.py:107
  180.4 3.9 %convert_element_type.8 = bf16[512,2048]{1,0:T(8,128)(2,1)} convert(f32[512,2048]{1,0:T(8,128)} %scatter_custom_fusion) | non-fusion elementwise | flops 1048576 | bytes 6291456 | tf_op jit(solution)/shard_map/convert_element_type | solution.py:109
  184.3 41.8 %reduce-scatter.5.cloned.1.call-done = bf16[128,2048]{1,0:T(8,128)(2,1)} async-done(((bf16[512,2048]{1,0:T(8,128)(2,1)}), bf16[128,2048]{1,0:T(8,128)(2,1)}) %reduce-scatter.5.cloned.1.call-update) | async-done | bytes 524304 | tf_op jit(solution)/shard_map/reduce_scatter | solution.py:108
  226.1 1.9 fusion.3
  (6 shorter events, 0.1 us)
Async XLA Ops:
  7.2 48.5 %all-gather.4.cloned.1.call-start = ((), (), s32[]{:S(2)}) async-start(), calls=%async_computation.2 | async-start | bytes 2621440 | tf_op jit(solution)/shard_map/all_gather | solution.py:93
  9.1 78.5 %all-gather.6.cloned.1.call-start = ((), (), s32[]{:S(2)}) async-start(), calls=%async_computation.5 | async-start | bytes 2359296 | tf_op jit(solution)/shard_map/all_gather | solution.py:97
  59.2 115.3 %reduce-scatter.3.cloned.1.call-start = ((), (), s32[]{:S(2)}) async-start(), calls=%async_computation.3 | async-start | bytes 2359296 | tf_op jit(solution)/shard_map/reduce_scatter | solution.py:104
  124.2 3.4 %copy-start.1 = (f32[1024,1024]{1,0:T(8,128)S(1)}, f32[1024,1024]{1,0:T(8,128)}, u32[]{:S(2)}) copy-start(f32[1024,1024]{1,0:T(8,128)} %get-tuple-element.11) | copy-start | bytes 12582916
  128.2 3.2 %copy-start = (f32[1024,2048]{1,0:T(8,128)}, f32[1024,2048]{1,0:T(8,128)S(1)}, u32[]{:S(2)}) copy-start(f32[1024,2048]{1,0:T(8,128)S(1)} %constant_dynamic-update-slice_fusion) | copy-start | bytes 25165828
  133.1 92.9 %reduce-scatter.5.cloned.1.call-start = ((), (), s32[]{:S(2)}) async-start(), calls=%async_computation.4 | async-start | bytes 2621440 | tf_op jit(solution)/shard_map/reduce_scatter | solution.py:108
Sparse Core Ops, SparseCore 0:
  10.1 45.4 all-gather.3
  59.3 28.2 all-gather.5
  133.3 41.1 reduce-scatter.2
  184.4 41.6 reduce-scatter.4

commit v3 on v2

--- a/solution.py
+++ b/solution.py
@@ -83,31 +83,68 @@
     )(ids, queries, out_grad, kv_all, kv_all)
 
 
-def local(queries, keys, values, out_grad, beacon_pos):
+def head_gather(block, axis, count):
+    index = lax.axis_index(axis)
+    from_left, from_right = [block], [block]
+    for step in range(1, count):
+        from_left.append(
+            lax.ppermute(from_left[-1], axis, [(j, j + 1) for j in range(step - 1, count - 1)])
+        )
+        from_right.append(
+            lax.ppermute(from_right[-1], axis, [(j + 1, j) for j in range(count - step)])
+        )
+    pieces = jnp.stack(from_left + from_right[1:])
+    order = jnp.arange(count)
+    pick = jnp.where(order <= index, index - order, count - 1 + order - index)
+    return pieces[pick].reshape((count * block.shape[0],) + block.shape[1:])
+
+
+def head_reduce(partials, axis, count):
+    index = lax.axis_index(axis)
+    rows = partials.shape[0] // count
+
+    def block_of(target):
+        return lax.dynamic_slice_in_dim(partials, jnp.clip(target, 0, count - 1) * rows, rows, 0)
+
+    left = jnp.zeros((rows, partials.shape[1]), jnp.bfloat16)
+    right = jnp.zeros((rows, partials.shape[1]), jnp.bfloat16)
+    for step in range(1, count):
+        send_left = (block_of(index + step - count) + left.astype(jnp.float32)).astype(jnp.bfloat16)
+        send_right = (block_of(index - step + count) + right.astype(jnp.float32)).astype(jnp.bfloat16)
+        left = lax.ppermute(send_left, axis, [(j, j - 1) for j in range(max(1, count - step), count)])
+        right = lax.ppermute(send_right, axis, [(j, j + 1) for j in range(0, min(step, count - 1))])
+    return block_of(index) + left.astype(jnp.float32) + right.astype(jnp.float32)
+
+
+def local(queries, keys, values, out_grad, beacon_pos, *, heads_axis, ctx_axis):
     rows = queries.shape[0]
     kv_width = keys.shape[1]
     head_id = lax.axis_index("head")
     shard_id = lax.axis_index("ctx")
 
     kv_rows = jnp.concatenate([keys, values], axis=1)
-    kv_window = lax.all_gather(kv_rows, "head", axis=0, tiled=True)
+    kv_window = head_gather(kv_rows, "head", heads_axis)
     window = kv_window.shape[0]
     positions = beacon_pos[0]
     per_shard = positions.shape[0]
-    kv_beacons = lax.all_gather(kv_window[positions], "ctx", axis=0, tiled=True)
+    own_beacon_rows = kv_window[positions]
+    kv_beacons = lax.all_to_all(
+        jnp.broadcast_to(own_beacon_rows[None], (ctx_axis,) + own_beacon_rows.shape),
+        "ctx", 0, 0, tiled=True,
+    ).reshape(ctx_axis * per_shard, 2 * kv_width)
     kv_all = jnp.concatenate([kv_window, kv_beacons], axis=0)
     ids = jnp.stack([head_id, shard_id]).astype(jnp.int32)
     attended_out, query_out, key_grad, value_grad = attend_all(
         ids, queries, out_grad, kv_all, window, per_shard
     )
     kv_grads = jnp.concatenate([key_grad, value_grad], axis=1)
-    own_beacons = lax.psum_scatter(
-        kv_grads[window:].astype(jnp.bfloat16), "ctx", scatter_dimension=0, tiled=True
-    ).astype(jnp.float32)
+    beacon_parts = lax.all_to_all(
+        kv_grads[window:].astype(jnp.bfloat16).reshape(ctx_axis, per_shard, 2 * kv_width),
+        "ctx", 0, 0, tiled=True,
+    )
+    own_beacons = jnp.sum(beacon_parts.astype(jnp.float32), axis=0)
     window_grads = kv_grads[:window].at[positions].add(own_beacons)
-    own_grads = lax.psum_scatter(
-        window_grads.astype(jnp.bfloat16), "head", scatter_dimension=0, tiled=True
-    )
+    own_grads = head_reduce(window_grads, "head", heads_axis).astype(jnp.bfloat16)
     return attended_out, query_out, own_grads[:, :kv_width], own_grads[:, kv_width:]
 
 
@@ -125,4 +162,5 @@
         P(("ctx", "head"), None),
         P(("ctx", "head"), None),
     )
-    return jax.shard_map(local, mesh=mesh, in_specs=in_specs, out_specs=out_specs, check_vma=False)
+    body = functools.partial(local, heads_axis=mesh.shape["head"], ctx_axis=mesh.shape["ctx"])
+    return jax.shard_map(body, mesh=mesh, in_specs=in_specs, out_specs=out_specs, check_vma=False)

time: 239 us -> 233 us (0.975); the launches traced: 234 us -> 232 us
  starting transfers between devices: 0.16 us -> 36.5 us
  waiting for transfers between devices: 152 us -> 117 us
  between operations: 13.8 us -> 0.89 us
  local copies, waits for them, and re-layouts: 18.9 us -> 29 us
    reduce_scatter x2 -> x0, waiting for transfers between devices: 78.4 us -> none  [the longest x1 41.8 us: local(): lax.psum_scatter(window_grads.astype(jnp.bfloat16), 'head', scatter_dimen...]
    all_gather x2 -> x0, waiting for transfers between devices: 73.5 us -> none  [the longest x1 45.8 us: local(): kv_window = lax.all_gather(kv_rows, 'head', axis=0, tiled=True)]
    ppermute x0 -> x12, waiting for transfers between devices: none -> 71.9 us  [the longest x3 30.7 us: head_reduce(): lax.ppermute(send_right, axis, [(j, j + 1) for j in range(0, min(step, co...]
    all_to_all x0 -> x2, waiting for transfers between devices: none -> 45.1 us  [the longest x1 24.6 us: local(): lax.all_to_all(jnp.broadcast_to(own_beacon_rows[None], (ctx_axis,) + own_...]
    ppermute x0 -> x12, starting transfers between devices: none -> 26.7 us  [the longest x3 8.27 us: head_reduce(): lax.ppermute(send_right, axis, [(j, j + 1) for j in range(0, min(step, co...]
    all_to_all x0 -> x2, starting transfers between devices: none -> 9.79 us  [the longest x1 5.03 us: local(): lax.all_to_all(kv_grads[window:].astype(jnp.bfloat16).reshape(ctx_axis, p...]
    unnamed x5 -> x12, local copies, waits for them, and re-layouts: 6.67 us -> 12.7 us
    convert_element_type x1 -> x4, other arithmetic: 3.86 us -> 5.9 us  [the longest x2 3.16 us: head_reduce(): (block_of(index + step - count) + left.astype(jnp.float32)).astype(jnp.bf...]
  transfers between devices with their start and end apart: 4 -> 14, of which waited for: 4 -> 10; matrix products, arithmetic and copies ran while one was open for 3% -> 6% of each run, Pallas kernels for 0% -> 0%
where the time goes in v3:
time: 233 us; the launch traced here: 232 us
  waiting for transfers between devices  117 us (50%)
  starting transfers between devices  36.5 us (16%)
  Pallas kernels  31.9 us (14%)
  local copies, waits for them, and re-layouts  29 us (12%)
  other arithmetic  17.2 us (7%)
    pallas_call x1, Pallas kernels, attend_all(): pl.pallas_call(kernel, grid_spec=pltpu.PrefetchScalarGridSpec(num_scalar_...  31.9 us
    ppermute x3, waiting for transfers between devices, head_reduce(): lax.ppermute(send_right, axis, [(j, j + 1) for j in range(0, min(step, co...  30.7 us
    all_to_all x1, waiting for transfers between devices, local(): lax.all_to_all(jnp.broadcast_to(own_beacon_rows[None], (ctx_axis,) + own_...  24.6 us
    all_to_all x1, waiting for transfers between devices, local(): lax.all_to_all(kv_grads[window:].astype(jnp.bfloat16).reshape(ctx_axis, p...  20.5 us
    ppermute x3, waiting for transfers between devices, head_gather(): lax.ppermute(from_left[-1], axis, [(j, j + 1) for j in range(step - 1, co...  16.5 us
    ppermute x3, waiting for transfers between devices, head_reduce(): lax.ppermute(send_left, axis, [(j, j - 1) for j in range(max(1, count - s...  15.3 us
    unnamed x12, local copies, waits for them, and re-layouts  12.7 us
    ppermute x3, waiting for transfers between devices, head_gather(): lax.ppermute(from_right[-1], axis, [(j + 1, j) for j in range(count - ste...  9.36 us
  transfers between devices with their start and end apart: 14, of which 10 were waited for; matrix products, arithmetic and copies ran while one was open for 6% of the time, Pallas kernels for 0%

profile of v3, /device:TPU:10, one launch (start us, length us, event | category | flops | bytes accessed | tf_op | source)
XLA Modules:
  0.0 232.3 jit_solution(18015641689347213038)
XLA Ops:
  2.6 3.5 %collective-permute-start = (bf16[128,2048]{1,0:T(8,128)(2,1)S(1)}, bf16[128,2048]{1,0:T(8,128)(2,1)S(1)}, u32[]{:S(2)}, u32[]{:S(2)}) collective-permute-start(bf16[128,2048]{1,0:T(8,128)(2,1)S(1)} %constant_dynamic-update-slice_fusion), channel_id=1, source_target_pairs={{0,1},{1,2},{2,3},{4,5},{5,6},{6,7},{8,9},{9,10},{10,11},{12,13},{... | collective-permute-start | bytes 1572872 | tf_op jit(solution)/shard_map/ppermute | solution.py:91
  6.1 2.4 %collective-permute-start.3 = (bf16[128,2048]{1,0:T(8,128)(2,1)S(1)}, bf16[128,2048]{1,0:T(8,128)(2,1)S(1)}, u32[]{:S(2)}, u32[]{:S(2)}) collective-permute-start(bf16[128,2048]{1,0:T(8,128)(2,1)S(1)} %constant_dynamic-update-slice_fusion), channel_id=1, source_target_pairs={{1,0},{2,1},{3,2},{5,4},{6,5},{7,6},{9,8},{10,9},{11,10},{13,12},{... | collective-permute-start | bytes 1572872 | tf_op jit(solution)/shard_map/ppermute | solution.py:94
  9.1 9.0 %collective-permute-done = bf16[128,2048]{1,0:T(8,128)(2,1)S(1)} collective-permute-done((bf16[128,2048]{1,0:T(8,128)(2,1)S(1)}, bf16[128,2048]{1,0:T(8,128)(2,1)S(1)}, u32[]{:S(2)}, u32[]{:S(2)}) %collective-permute-start) | collective-permute-done | bytes 524320 | tf_op jit(solution)/shard_map/ppermute | solution.py:91
  18.1 3.5 %collective-permute-start.1 = (bf16[128,2048]{1,0:T(8,128)(2,1)S(1)}, bf16[128,2048]{1,0:T(8,128)(2,1)S(1)}, u32[]{:S(2)}, u32[]{:S(2)}) collective-permute-start(bf16[128,2048]{1,0:T(8,128)(2,1)S(1)} %collective-permute-done), channel_id=1, source_target_pairs={{1,2},{2,3},{5,6},{6,7},{9,10},{10,11},{13,14},{14,15},{17,18},{18... | collective-permute-start | bytes 1572872 | tf_op jit(solution)/shard_map/ppermute | solution.py:91
  24.4 7.5 %collective-permute-done.1 = bf16[128,2048]{1,0:T(8,128)(2,1)S(1)} collective-permute-done((bf16[128,2048]{1,0:T(8,128)(2,1)S(1)}, bf16[128,2048]{1,0:T(8,128)(2,1)S(1)}, u32[]{:S(2)}, u32[]{:S(2)}) %collective-permute-start.1) | collective-permute-done | bytes 524320 | tf_op jit(solution)/shard_map/ppermute | solution.py:91
  33.4 3.4 %collective-permute-done.4 = bf16[128,2048]{1,0:T(8,128)(2,1)S(1)} collective-permute-done((bf16[128,2048]{1,0:T(8,128)(2,1)S(1)}, bf16[128,2048]{1,0:T(8,128)(2,1)S(1)}, u32[]{:S(2)}, u32[]{:S(2)}) %collective-permute-start.4) | collective-permute-done | bytes 524320 | tf_op jit(solution)/shard_map/ppermute | solution.py:94
  42.5 5.9 %collective-permute-done.5 = bf16[128,2048]{1,0:T(8,128)(2,1)S(1)} collective-permute-done((bf16[128,2048]{1,0:T(8,128)(2,1)S(1)}, bf16[128,2048]{1,0:T(8,128)(2,1)S(1)}, u32[]{:S(2)}, u32[]{:S(2)}) %collective-permute-start.5) | collective-permute-done | bytes 524320 | tf_op jit(solution)/shard_map/ppermute | solution.py:94
  49.3 2.7 %gather_fusion = bf16[4,128,2048]{2,1,0:T(8,128)(2,1)S(1)} fusion(bf16[7,128,2048]{2,1,0:T(8,128)(2,1)} %bitcast_dynamic-update-slice_fusion, s32[1024]{0:T(1024)S(1)} %pad_clamp_fusion.1), kind=kCustom, calls=%fused_computation | custom fusion | bytes 4194320 | tf_op jit(solution)/shard_map/gather | solution.py:99
  54.3 4.8 %all-to-all-start = ((bf16[8,64,2048]{2,1,0:T(8,128)(2,1)}), bf16[8,64,2048]{2,1,0:T(8,128)(2,1)}, u32[]{:S(2)}, u32[]{:S(2)}) async-start(bf16[8,64,2048]{2,1,0:T(8,128)(2,1)} %broadcast_in_dim.2), calls=%async_computation | async-start | bytes 4194304 | tf_op jit(solution)/shard_map/all_to_all | solution.py:131
  59.7 24.6 %all-to-all-done = bf16[8,64,2048]{2,1,0:T(8,128)(2,1)} async-done(((bf16[8,64,2048]{2,1,0:T(8,128)(2,1)}), bf16[8,64,2048]{2,1,0:T(8,128)(2,1)}, u32[]{:S(2)}, u32[]{:S(2)}) %all-to-all-start) | async-done | bytes 2097184 | tf_op jit(solution)/shard_map/all_to_all | solution.py:131
  84.3 4.1 %pad_maximum_fusion.k_ref.v_ref = bf16[1024,2048]{1,0:T(8,128)(2,1)} fusion(bf16[512,2048]{1,0:T(8,128)(2,1)} %bitcast.13, bf16[512,2048]{1,0:T(8,128)(2,1)S(1)} %bitcast.26), kind=kLoop, calls=%fused_computation.4 | loop fusion | flops 8388608 | bytes 8388608 | tf_op jit(solution)/shard_map/concatenate | solution.py:135
  88.5 31.9 %shard_map.84 = (bf16[128,4096]{1,0:T(8,128)(2,1)}, bf16[128,4096]{1,0:T(8,128)(2,1)}, f32[1024,1024]{1,0:T(8,128)}, f32[1024,1024]{1,0:T(8,128)}) custom-call(s32[2]{0:T(128)} %pad_add_fusion.ids_ref, bf16[128,4096]{1,0:T(8,128)(2,1)} %q_ref.1, bf16[128,4096]{1,0:T(8,128)(2,1)} %g_ref.1, bf16[1024,2048]{1,0:T(8,128)(2,1)} %pad_maximum_fusion.k_ref.v_ref, ...), custom_call_target="tpu_custom_call" | custom-call | tf_op jit(solution)/shard_map/pallas_call | solution.py:69
  120.3 2.7 %constant_dynamic-update-slice_fusion.3 = f32[1024,2048]{1,0:T(8,128)S(1)} fusion(f32[1024,1024]{1,0:T(8,128)} %get-tuple-element.10), kind=kLoop, calls=%fused_computation.23 | loop fusion | bytes 8388608
  124.4 3.2 %copy-done = f32[1024,2048]{1,0:T(8,128)} copy-done((f32[1024,2048]{1,0:T(8,128)}, f32[1024,2048]{1,0:T(8,128)S(1)}, u32[]{:S(2)}) %copy-start) | copy-done | bytes 8388632
  129.3 5.0 %all-to-all-start.1 = ((bf16[8,64,2048]{2,1,0:T(8,128)(2,1)}), bf16[8,64,2048]{2,1,0:T(8,128)(2,1)S(1)}, u32[]{:S(2)}, u32[]{:S(2)}) async-start(bf16[8,64,2048]{2,1,0:T(8,128)(2,1)} %bitcast.27), calls=%async_computation.1 | async-start | bytes 4194304 | tf_op jit(solution)/shard_map/all_to_all | solution.py:141
  134.3 4.7 %slice.21 = f32[512,2048]{1,0:T(8,128)} slice(f32[1024,2048]{1,0:T(8,128)} %copy-done), slice={[0:512], [0:2048]} | slice | bytes 8388608 | tf_op jit(solution)/shard_map/slice | solution.py:146
  139.0 20.5 %all-to-all-done.1 = bf16[8,64,2048]{2,1,0:T(8,128)(2,1)S(1)} async-done(((bf16[8,64,2048]{2,1,0:T(8,128)(2,1)}), bf16[8,64,2048]{2,1,0:T(8,128)(2,1)S(1)}, u32[]{:S(2)}, u32[]{:S(2)}) %all-to-all-start.1) | async-done | bytes 2097184 | tf_op jit(solution)/shard_map/all_to_all | solution.py:141
  159.8 5.5 %scatter_fusion = f32[512,2048]{1,0:T(8,128)} fusion(f32[512,2048]{1,0:T(8,128)} %slice.21, s32[64]{0:T(128)S(1)} %fusion, f32[64,2048]{1,0:T(8,128)S(1)} %convert_reduce_fusion), kind=kCustom, calls=%fused_computation.2 | custom fusion | flops 131072 | bytes 1573120 | tf_op jit(solution)/shard_map/scatter-add | solution.py:146
  171.6 11.9 %collective-permute-done.9 = bf16[128,2048]{1,0:T(8,128)(2,1)S(1)} collective-permute-done((bf16[128,2048]{1,0:T(8,128)(2,1)S(1)}, bf16[128,2048]{1,0:T(8,128)(2,1)S(1)}, u32[]{:S(2)}, u32[]{:S(2)}) %collective-permute-start.9) | collective-permute-done | bytes 524320 | tf_op jit(solution)/shard_map/ppermute | solution.py:115
  183.6 15.3 %collective-permute-done.7 = bf16[128,2048]{1,0:T(8,128)(2,1)S(1)} collective-permute-done((bf16[128,2048]{1,0:T(8,128)(2,1)S(1)}, bf16[128,2048]{1,0:T(8,128)(2,1)S(1)}, u32[]{:S(2)}, u32[]{:S(2)}) %collective-permute-start.7) | collective-permute-done | bytes 524320 | tf_op jit(solution)/shard_map/ppermute | solution.py:114
  200.8 3.6 %collective-permute-start.10 = (bf16[128,2048]{1,0:T(8,128)(2,1)S(1)}, bf16[128,2048]{1,0:T(8,128)(2,1)S(1)}, u32[]{:S(2)}, u32[]{:S(2)}) collective-permute-start(bf16[128,2048]{1,0:T(8,128)(2,1)S(1)} %get-tuple-element.13), channel_id=1, source_target_pairs={{0,1},{1,2},{4,5},{5,6},{8,9},{9,10},{12,13},{13,14},{16,17},{17,1... | collective-permute-start | bytes 1572872 | tf_op jit(solution)/shard_map/ppermute | solution.py:115
  206.6 8.6 %collective-permute-done.10 = bf16[128,2048]{1,0:T(8,128)(2,1)S(1)} collective-permute-done((bf16[128,2048]{1,0:T(8,128)(2,1)S(1)}, bf16[128,2048]{1,0:T(8,128)(2,1)S(1)}, u32[]{:S(2)}, u32[]{:S(2)}) %collective-permute-start.10) | collective-permute-done | bytes 524320 | tf_op jit(solution)/shard_map/ppermute | solution.py:115
  216.6 3.3 %collective-permute-start.11 = (bf16[128,2048]{1,0:T(8,128)(2,1)S(1)}, bf16[128,2048]{1,0:T(8,128)(2,1)S(1)}, u32[]{:S(2)}, u32[]{:S(2)}) collective-permute-start(bf16[128,2048]{1,0:T(8,128)(2,1)S(1)} %add_convert_fusion.1), channel_id=1, source_target_pairs={{0,1},{1,2},{2,3},{4,5},{5,6},{6,7},{8,9},{9,10},{10,11},{12,13},{... | collective-permute-start | bytes 1572872 | tf_op jit(solution)/shard_map/ppermute | solution.py:115
  219.9 10.2 %collective-permute-done.11 = bf16[128,2048]{1,0:T(8,128)(2,1)S(1)} collective-permute-done((bf16[128,2048]{1,0:T(8,128)(2,1)S(1)}, bf16[128,2048]{1,0:T(8,128)(2,1)S(1)}, u32[]{:S(2)}, u32[]{:S(2)}) %collective-permute-start.11) | collective-permute-done | bytes 524320 | tf_op jit(solution)/shard_map/ppermute | solution.py:115
  (39 shorter events, 33.6 us)
Async XLA Ops:
  2.6 15.6 %collective-permute-start = (bf16[128,2048]{1,0:T(8,128)(2,1)S(1)}, bf16[128,2048]{1,0:T(8,128)(2,1)S(1)}, u32[]{:S(2)}, u32[]{:S(2)}) collective-permute-start(bf16[128,2048]{1,0:T(8,128)(2,1)S(1)} %constant_dynamic-update-slice_fusion), channel_id=1, source_target_pairs={{0,1},{1,2},{2,3},{4,5},{5,6},{6,7},{8,9},{9,10},{10,11},{12,13},{... | collective-permute-start | bytes 1572872 | tf_op jit(solution)/shard_map/ppermute | solution.py:91
  6.1 16.4 %collective-permute-start.3 = (bf16[128,2048]{1,0:T(8,128)(2,1)S(1)}, bf16[128,2048]{1,0:T(8,128)(2,1)S(1)}, u32[]{:S(2)}, u32[]{:S(2)}) collective-permute-start(bf16[128,2048]{1,0:T(8,128)(2,1)S(1)} %constant_dynamic-update-slice_fusion), channel_id=1, source_target_pairs={{1,0},{2,1},{3,2},{5,4},{6,5},{7,6},{9,8},{10,9},{11,10},{13,12},{... | collective-permute-start | bytes 1572872 | tf_op jit(solution)/shard_map/ppermute | solution.py:94
  18.1 13.8 %collective-permute-start.1 = (bf16[128,2048]{1,0:T(8,128)(2,1)S(1)}, bf16[128,2048]{1,0:T(8,128)(2,1)S(1)}, u32[]{:S(2)}, u32[]{:S(2)}) collective-permute-start(bf16[128,2048]{1,0:T(8,128)(2,1)S(1)} %collective-permute-done), channel_id=1, source_target_pairs={{1,2},{2,3},{5,6},{6,7},{9,10},{10,11},{13,14},{14,15},{17,18},{18... | collective-permute-start | bytes 1572872 | tf_op jit(solution)/shard_map/ppermute | solution.py:91
  22.5 14.4 %collective-permute-start.4 = (bf16[128,2048]{1,0:T(8,128)(2,1)S(1)}, bf16[128,2048]{1,0:T(8,128)(2,1)S(1)}, u32[]{:S(2)}, u32[]{:S(2)}) collective-permute-start(bf16[128,2048]{1,0:T(8,128)(2,1)S(1)} %collective-permute-done.3), channel_id=1, source_target_pairs={{1,0},{2,1},{5,4},{6,5},{9,8},{10,9},{13,12},{14,13},{17,16},{18,1... | collective-permute-start | bytes 1572872 | tf_op jit(solution)/shard_map/ppermute | solution.py:94
  31.9 8.1 %collective-permute-start.2 = (bf16[128,2048]{1,0:T(8,128)(2,1)S(1)}, bf16[128,2048]{1,0:T(8,128)(2,1)S(1)}, u32[]{:S(2)}, u32[]{:S(2)}) collective-permute-start(bf16[128,2048]{1,0:T(8,128)(2,1)S(1)} %collective-permute-done.1), channel_id=1, source_target_pairs={{2,3},{6,7},{10,11},{14,15},{18,19},{22,23},{26,27},{30,31}} | collective-permute-start | bytes 1572872 | tf_op jit(solution)/shard_map/ppermute | solution.py:91
  36.9 11.6 %collective-permute-start.5 = (bf16[128,2048]{1,0:T(8,128)(2,1)S(1)}, bf16[128,2048]{1,0:T(8,128)(2,1)S(1)}, u32[]{:S(2)}, u32[]{:S(2)}) collective-permute-start(bf16[128,2048]{1,0:T(8,128)(2,1)S(1)} %collective-permute-done.4), channel_id=1, source_target_pairs={{1,0},{5,4},{9,8},{13,12},{17,16},{21,20},{25,24},{29,28}} | collective-permute-start | bytes 1572872 | tf_op jit(solution)/shard_map/ppermute | solution.py:94
  54.3 30.0 %all-to-all-start = ((bf16[8,64,2048]{2,1,0:T(8,128)(2,1)}), bf16[8,64,2048]{2,1,0:T(8,128)(2,1)}, u32[]{:S(2)}, u32[]{:S(2)}) async-start(bf16[8,64,2048]{2,1,0:T(8,128)(2,1)} %broadcast_in_dim.2), calls=%async_computation | async-start | bytes 4194304 | tf_op jit(solution)/shard_map/all_to_all | solution.py:131
  120.3 3.4 %copy-start.1 = (f32[1024,1024]{1,0:T(8,128)S(1)}, f32[1024,1024]{1,0:T(8,128)}, u32[]{:S(2)}) copy-start(f32[1024,1024]{1,0:T(8,128)} %get-tuple-element.11) | copy-start | bytes 12582916
  124.4 3.2 %copy-start = (f32[1024,2048]{1,0:T(8,128)}, f32[1024,2048]{1,0:T(8,128)S(1)}, u32[]{:S(2)}) copy-start(f32[1024,2048]{1,0:T(8,128)S(1)} %constant_dynamic-update-slice_fusion.2) | copy-start | bytes 25165828
  129.3 30.2 %all-to-all-start.1 = ((bf16[8,64,2048]{2,1,0:T(8,128)(2,1)}), bf16[8,64,2048]{2,1,0:T(8,128)(2,1)S(1)}, u32[]{:S(2)}, u32[]{:S(2)}) async-start(bf16[8,64,2048]{2,1,0:T(8,128)(2,1)} %bitcast.27), calls=%async_computation.1 | async-start | bytes 4194304 | tf_op jit(solution)/shard_map/all_to_all | solution.py:141
  167.0 2.0 collective-permute-start.6
  167.7 15.9 %collective-permute-start.9 = (bf16[128,2048]{1,0:T(8,128)(2,1)S(1)}, bf16[128,2048]{1,0:T(8,128)(2,1)S(1)}, u32[]{:S(2)}, u32[]{:S(2)}) collective-permute-start(bf16[128,2048]{1,0:T(8,128)(2,1)S(1)} %get-tuple-element.15), channel_id=1, source_target_pairs={{0,1},{4,5},{8,9},{12,13},{16,17},{20,21},{24,25},{28,29}} | collective-permute-start | bytes 1572872 | tf_op jit(solution)/shard_map/ppermute | solution.py:115
  170.3 28.6 %collective-permute-start.7 = (bf16[128,2048]{1,0:T(8,128)(2,1)S(1)}, bf16[128,2048]{1,0:T(8,128)(2,1)S(1)}, u32[]{:S(2)}, u32[]{:S(2)}) collective-permute-start(bf16[128,2048]{1,0:T(8,128)(2,1)S(1)} %add_convert_fusion.4), channel_id=1, source_target_pairs={{2,1},{3,2},{6,5},{7,6},{10,9},{11,10},{14,13},{15,14},{18,17},{19... | collective-permute-start | bytes 1572872 | tf_op jit(solution)/shard_map/ppermute | solution.py:114
  200.8 14.5 %collective-permute-start.10 = (bf16[128,2048]{1,0:T(8,128)(2,1)S(1)}, bf16[128,2048]{1,0:T(8,128)(2,1)S(1)}, u32[]{:S(2)}, u32[]{:S(2)}) collective-permute-start(bf16[128,2048]{1,0:T(8,128)(2,1)S(1)} %get-tuple-element.13), channel_id=1, source_target_pairs={{0,1},{1,2},{4,5},{5,6},{8,9},{9,10},{12,13},{13,14},{16,17},{17,1... | collective-permute-start | bytes 1572872 | tf_op jit(solution)/shard_map/ppermute | solution.py:115
  204.4 15.5 %collective-permute-start.8 = (bf16[128,2048]{1,0:T(8,128)(2,1)S(1)}, bf16[128,2048]{1,0:T(8,128)(2,1)S(1)}, u32[]{:S(2)}, u32[]{:S(2)}) collective-permute-start(bf16[128,2048]{1,0:T(8,128)(2,1)S(1)} %get-tuple-element.12), channel_id=1, source_target_pairs={{1,0},{2,1},{3,2},{5,4},{6,5},{7,6},{9,8},{10,9},{11,10},{13,12},{... | collective-permute-start | bytes 1572872 | tf_op jit(solution)/shard_map/ppermute | solution.py:114
  216.6 13.5 %collective-permute-start.11 = (bf16[128,2048]{1,0:T(8,128)(2,1)S(1)}, bf16[128,2048]{1,0:T(8,128)(2,1)S(1)}, u32[]{:S(2)}, u32[]{:S(2)}) collective-permute-start(bf16[128,2048]{1,0:T(8,128)(2,1)S(1)} %add_convert_fusion.1), channel_id=1, source_target_pairs={{0,1},{1,2},{2,3},{4,5},{5,6},{6,7},{8,9},{9,10},{10,11},{12,13},{... | collective-permute-start | bytes 1572872 | tf_op jit(solution)/shard_map/ppermute | solution.py:115

commit v4 on v3

--- a/solution.py
+++ b/solution.py
@@ -116,24 +116,18 @@
     return block_of(index) + left.astype(jnp.float32) + right.astype(jnp.float32)
 
 
-def local(queries, keys, values, out_grad, beacon_pos, *, heads_axis, ctx_axis):
-    rows = queries.shape[0]
+def local_part(queries, keys, values, out_grad, positions, ids, heads_axis, ctx_axis):
     kv_width = keys.shape[1]
-    head_id = lax.axis_index("head")
-    shard_id = lax.axis_index("ctx")
-
+    per_shard = positions.shape[0]
     kv_rows = jnp.concatenate([keys, values], axis=1)
     kv_window = head_gather(kv_rows, "head", heads_axis)
     window = kv_window.shape[0]
-    positions = beacon_pos[0]
-    per_shard = positions.shape[0]
     own_beacon_rows = kv_window[positions]
     kv_beacons = lax.all_to_all(
         jnp.broadcast_to(own_beacon_rows[None], (ctx_axis,) + own_beacon_rows.shape),
         "ctx", 0, 0, tiled=True,
     ).reshape(ctx_axis * per_shard, 2 * kv_width)
     kv_all = jnp.concatenate([kv_window, kv_beacons], axis=0)
-    ids = jnp.stack([head_id, shard_id]).astype(jnp.int32)
     attended_out, query_out, key_grad, value_grad = attend_all(
         ids, queries, out_grad, kv_all, window, per_shard
     )
@@ -146,6 +140,26 @@
     window_grads = kv_grads[:window].at[positions].add(own_beacons)
     own_grads = head_reduce(window_grads, "head", heads_axis).astype(jnp.bfloat16)
     return attended_out, query_out, own_grads[:, :kv_width], own_grads[:, kv_width:]
+
+
+def local(queries, keys, values, out_grad, beacon_pos, *, heads_axis, ctx_axis, parts):
+    head_id = lax.axis_index("head")
+    shard_id = lax.axis_index("ctx")
+    ids = jnp.stack([head_id, shard_id]).astype(jnp.int32)
+    positions = beacon_pos[0]
+    q_cols = queries.shape[1] // parts
+    kv_cols = keys.shape[1] // parts
+    results = []
+    for part in range(parts):
+        qs = slice(part * q_cols, (part + 1) * q_cols)
+        ks = slice(part * kv_cols, (part + 1) * kv_cols)
+        results.append(
+            local_part(
+                queries[:, qs], keys[:, ks], values[:, ks], out_grad[:, qs],
+                positions, ids, heads_axis, ctx_axis,
+            )
+        )
+    return tuple(jnp.concatenate(outs, axis=1) for outs in zip(*results))
 
 
 def solution(mesh):
@@ -162,5 +176,5 @@
         P(("ctx", "head"), None),
         P(("ctx", "head"), None),
     )
-    body = functools.partial(local, heads_axis=mesh.shape["head"], ctx_axis=mesh.shape["ctx"])
+    body = functools.partial(local, heads_axis=mesh.shape["head"], ctx_axis=mesh.shape["ctx"], parts=2)
     return jax.shard_map(body, mesh=mesh, in_specs=in_specs, out_specs=out_specs, check_vma=False)

time: 233 us -> 199 us (0.85)
  waiting for transfers between devices: 117 us -> 25.2 us
  starting transfers between devices: 36.5 us -> 74.3 us
  local copies, waits for them, and re-layouts: 29 us -> 39.6 us
  other arithmetic: 17.2 us -> 21.8 us
  Pallas kernels: 31.9 us -> 34.8 us
    all_to_all x2 -> x4, waiting for transfers between devices: 45.1 us -> 9.11 us  [the longest x2 6.27 us: local_part(): lax.all_to_all(jnp.broadcast_to(own_beacon_rows[None], (ctx_axis,) + own_...]
    ppermute x3 -> x6, waiting for transfers between devices: 30.7 us -> 10.3 us  [head_reduce(): lax.ppermute(send_right, axis, [(j, j + 1) for j in range(0, min(step, co...]
    ppermute x3 -> x6, waiting for transfers between devices: 16.5 us -> 0.02 us  [head_gather(): lax.ppermute(from_left[-1], axis, [(j, j + 1) for j in range(step - 1, co...]
    ppermute x3 -> x6, waiting for transfers between devices: 15.3 us -> 3.56 us  [head_reduce(): lax.ppermute(send_left, axis, [(j, j - 1) for j in range(max(1, count - s...]
    ppermute x3 -> x6, starting transfers between devices: 4.22 us -> 13.2 us  [head_reduce(): lax.ppermute(send_left, axis, [(j, j - 1) for j in range(max(1, count - s...]
    ppermute x3 -> x6, starting transfers between devices: 6.51 us -> 15.3 us  [head_gather(): lax.ppermute(from_right[-1], axis, [(j + 1, j) for j in range(count - ste...]
    ppermute x3 -> x6, starting transfers between devices: 7.67 us -> 16.4 us  [head_gather(): lax.ppermute(from_left[-1], axis, [(j, j + 1) for j in range(step - 1, co...]
    all_to_all x2 -> x4, starting transfers between devices: 9.79 us -> 18.3 us  [the longest x2 9.88 us: local_part(): lax.all_to_all(jnp.broadcast_to(own_beacon_rows[None], (ctx_axis,) + own_...]
  transfers between devices with their start and end apart: 14 -> 28, of which waited for: 10 -> 8; matrix products, arithmetic and copies ran while one was open for 6% -> 27% of each run, Pallas kernels for 0% -> 18%
where the time goes in v4:
time: 199 us; the launch traced here: 197 us
  starting transfers between devices  74.3 us (37%)
  local copies, waits for them, and re-layouts  39.6 us (20%)
  Pallas kernels  34.8 us (17%)
  waiting for transfers between devices  25.2 us (13%)
  other arithmetic  21.8 us (11%)
    pallas_call x2, Pallas kernels, attend_all(): pl.pallas_call(kernel, grid_spec=pltpu.PrefetchScalarGridSpec(num_scalar_...  34.8 us
    ppermute x6, starting transfers between devices, head_gather(): lax.ppermute(from_left[-1], axis, [(j, j + 1) for j in range(step - 1, co...  16.4 us
    unnamed x36, local copies, waits for them, and re-layouts  15.3 us
    ppermute x6, starting transfers between devices, head_gather(): lax.ppermute(from_right[-1], axis, [(j + 1, j) for j in range(count - ste...  15.3 us
    ppermute x6, starting transfers between devices, head_reduce(): lax.ppermute(send_left, axis, [(j, j - 1) for j in range(max(1, count - s...  13.2 us
    ppermute x6, starting transfers between devices, head_reduce(): lax.ppermute(send_right, axis, [(j, j + 1) for j in range(0, min(step, co...  11.1 us
    ppermute x6, waiting for transfers between devices, head_reduce(): lax.ppermute(send_right, axis, [(j, j + 1) for j in range(0, min(step, co...  10.3 us
    all_to_all x2, starting transfers between devices, local_part(): lax.all_to_all(jnp.broadcast_to(own_beacon_rows[None], (ctx_axis,) + own_...  9.88 us
  transfers between devices with their start and end apart: 28, of which 8 were waited for; matrix products, arithmetic and copies ran while one was open for 27% of the time, Pallas kernels for 18%

profile of v4, /device:TPU:10, one launch (start us, length us, event | category | flops | bytes accessed | tf_op | source)
XLA Modules:
  0.0 196.9 jit_solution(3799903428802208764)
XLA Ops:
  2.7 3.5 %collective-permute-start = (bf16[128,1024]{1,0:T(8,128)(2,1)S(1)}, bf16[128,1024]{1,0:T(8,128)(2,1)S(1)}, u32[]{:S(2)}, u32[]{:S(2)}) collective-permute-start(bf16[128,1024]{1,0:T(8,128)(2,1)S(1)} %pad_maximum_fusion.4), channel_id=1, source_target_pairs={{0,1},{1,2},{2,3},{4,5},{5,6},{6,7},{8,9},{9,10},{10,11},{12,13},{... | collective-permute-start | bytes 786440 | tf_op jit(solution)/shard_map/ppermute | solution.py:91
  8.6 3.5 %collective-permute-start.6 = (bf16[128,1024]{1,0:T(8,128)(2,1)S(1)}, bf16[128,1024]{1,0:T(8,128)(2,1)S(1)}, u32[]{:S(2)}, u32[]{:S(2)}) collective-permute-start(bf16[128,1024]{1,0:T(8,128)(2,1)S(1)} %pad_maximum_fusion.5), channel_id=1, source_target_pairs={{0,1},{1,2},{2,3},{4,5},{5,6},{6,7},{8,9},{9,10},{10,11},{12,13},{... | collective-permute-start | bytes 786440 | tf_op jit(solution)/shard_map/ppermute | solution.py:91
  15.8 3.5 %collective-permute-start.1 = (bf16[128,1024]{1,0:T(8,128)(2,1)S(1)}, bf16[128,1024]{1,0:T(8,128)(2,1)S(1)}, u32[]{:S(2)}, u32[]{:S(2)}) collective-permute-start(bf16[128,1024]{1,0:T(8,128)(2,1)S(1)} %collective-permute-done), channel_id=1, source_target_pairs={{1,2},{2,3},{5,6},{6,7},{9,10},{10,11},{13,14},{14,15},{17,18},{18... | collective-permute-start | bytes 786440 | tf_op jit(solution)/shard_map/ppermute | solution.py:91
  22.0 3.9 %collective-permute-start.7 = (bf16[128,1024]{1,0:T(8,128)(2,1)S(1)}, bf16[128,1024]{1,0:T(8,128)(2,1)S(1)}, u32[]{:S(2)}, u32[]{:S(2)}) collective-permute-start(bf16[128,1024]{1,0:T(8,128)(2,1)S(1)} %collective-permute-done.6), channel_id=1, source_target_pairs={{1,2},{2,3},{5,6},{6,7},{9,10},{10,11},{13,14},{14,15},{17,18},{18... | collective-permute-start | bytes 786440 | tf_op jit(solution)/shard_map/ppermute | solution.py:91
  34.6 5.1 %collective-permute-start.11 = (bf16[128,1024]{1,0:T(8,128)(2,1)S(1)}, bf16[128,1024]{1,0:T(8,128)(2,1)}, u32[]{:S(2)}, u32[]{:S(2)}) collective-permute-start(bf16[128,1024]{1,0:T(8,128)(2,1)S(1)} %collective-permute-done.10), channel_id=1, source_target_pairs={{1,0},{5,4},{9,8},{13,12},{17,16},{21,20},{25,24},{29,28}} | collective-permute-start | bytes 786440 | tf_op jit(solution)/shard_map/ppermute | solution.py:94
  46.6 4.3 %all-to-all-start = ((bf16[8,64,1024]{2,1,0:T(8,128)(2,1)}), bf16[8,64,1024]{2,1,0:T(8,128)(2,1)S(1)}, u32[]{:S(2)}, u32[]{:S(2)}) async-start(bf16[8,64,1024]{2,1,0:T(8,128)(2,1)} %broadcast_in_dim.4), calls=%async_computation | async-start | bytes 2097152 | tf_op jit(solution)/shard_map/all_to_all | solution.py:126
  58.5 6.3 %all-to-all-done = bf16[8,64,1024]{2,1,0:T(8,128)(2,1)S(1)} async-done(((bf16[8,64,1024]{2,1,0:T(8,128)(2,1)}), bf16[8,64,1024]{2,1,0:T(8,128)(2,1)S(1)}, u32[]{:S(2)}, u32[]{:S(2)}) %all-to-all-start) | async-done | bytes 1048608 | tf_op jit(solution)/shard_map/all_to_all | solution.py:126
  65.8 5.6 %all-to-all-start.1 = ((bf16[8,64,1024]{2,1,0:T(8,128)(2,1)}), bf16[8,64,1024]{2,1,0:T(8,128)(2,1)}, u32[]{:S(2)}, u32[]{:S(2)}) async-start(bf16[8,64,1024]{2,1,0:T(8,128)(2,1)} %broadcast_in_dim.5), calls=%async_computation.1 | async-start | bytes 2097152 | tf_op jit(solution)/shard_map/all_to_all | solution.py:126
  71.5 2.9 %fusion.2 = (bf16[128,2048]{1,0:T(8,128)(2,1)}, bf16[128,2048]{1,0:T(8,128)(2,1)}, bf16[128,2048]{1,0:T(8,128)(2,1)}, bf16[128,2048]{1,0:T(8,128)(2,1)}) fusion(bf16[128,4096]{1,0:T(8,128)(2,1)} %param.8, bf16[128,4096]{1,0:T(8,128)(2,1)} %param.5), kind=kLoop, calls=%fused_computation.58 | loop fusion | bytes 4194304 | tf_op jit(solution)/shard_map/slice | solution.py:158
  75.9 17.4 %shard_map.84 = (bf16[128,2048]{1,0:T(8,128)(2,1)}, bf16[128,2048]{1,0:T(8,128)(2,1)}, f32[1024,512]{1,0:T(8,128)}, f32[1024,512]{1,0:T(8,128)}) custom-call(s32[2]{0:T(128)} %pad_add_fusion.ids_ref, bf16[128,2048]{1,0:T(8,128)(2,1)} %get-tuple-element.43.q_ref, bf16[128,2048]{1,0:T(8,128)(2,1)} %get-tuple-element.28.g_ref, ...), custom_call_target="tpu_custom_call" | custom-call | tf_op jit(solution)/shard_map/pallas_call | solution.py:69
  98.9 4.2 %all-to-all-start.2 = ((bf16[8,64,1024]{2,1,0:T(8,128)(2,1)}), bf16[8,64,1024]{2,1,0:T(8,128)(2,1)S(1)}, u32[]{:S(2)}, u32[]{:S(2)}) async-start(bf16[8,64,1024]{2,1,0:T(8,128)(2,1)} %bitcast.23), calls=%async_computation.2 | async-start | bytes 2097152 | tf_op jit(solution)/shard_map/all_to_all | solution.py:135
  103.1 2.8 %pad_maximum_fusion.1.k_ref.v_ref = bf16[1024,1024]{1,0:T(8,128)(2,1)} fusion(bf16[512,1024]{1,0:T(8,128)(2,1)} %bitcast.22, bf16[512,1024]{1,0:T(8,128)(2,1)S(1)} %bitcast.45), kind=kLoop, calls=%fused_computation.9 | loop fusion | flops 4194304 | bytes 4194304 | tf_op jit(solution)/shard_map/concatenate | solution.py:130
  105.9 17.4 %shard_map.85 = (bf16[128,2048]{1,0:T(8,128)(2,1)}, bf16[128,2048]{1,0:T(8,128)(2,1)}, f32[1024,512]{1,0:T(8,128)}, f32[1024,512]{1,0:T(8,128)}) custom-call(s32[2]{0:T(128)} %pad_add_fusion.ids_ref, bf16[128,2048]{1,0:T(8,128)(2,1)} %get-tuple-element.42.q_ref, bf16[128,2048]{1,0:T(8,128)(2,1)} %get-tuple-element.29.g_ref, ...), custom_call_target="tpu_custom_call" | custom-call | tf_op jit(solution)/shard_map/pallas_call | solution.py:69
  128.9 4.2 %all-to-all-start.3 = ((bf16[8,64,1024]{2,1,0:T(8,128)(2,1)}), bf16[8,64,1024]{2,1,0:T(8,128)(2,1)}, u32[]{:S(2)}, u32[]{:S(2)}) async-start(bf16[8,64,1024]{2,1,0:T(8,128)(2,1)} %bitcast.24), calls=%async_computation.3 | async-start | bytes 2097152 | tf_op jit(solution)/shard_map/all_to_all | solution.py:135
  133.1 3.3 %slice.74 = f32[512,1024]{1,0:T(8,128)} slice(f32[1024,1024]{1,0:T(8,128)} %copy-done.1), slice={[0:512], [0:1024]} | slice | bytes 4194304 | tf_op jit(solution)/shard_map/slice | solution.py:140
  136.9 4.0 %scatter_fusion = f32[512,1024]{1,0:T(8,128)} fusion(f32[512,1024]{1,0:T(8,128)} %slice.74, s32[64]{0:T(128)S(1)} %fusion, f32[64,1024]{1,0:T(8,128)S(1)} %convert_reduce_fusion.1), kind=kCustom, calls=%fused_computation.4 | custom fusion | flops 65536 | bytes 786688 | tf_op jit(solution)/shard_map/scatter-add | solution.py:140
  144.3 2.8 %all-to-all-done.3 = bf16[8,64,1024]{2,1,0:T(8,128)(2,1)} async-done(((bf16[8,64,1024]{2,1,0:T(8,128)(2,1)}), bf16[8,64,1024]{2,1,0:T(8,128)(2,1)}, u32[]{:S(2)}, u32[]{:S(2)}) %all-to-all-start.3) | async-done | bytes 1048608 | tf_op jit(solution)/shard_map/all_to_all | solution.py:135
  161.0 2.9 %collective-permute-done.15 = bf16[128,1024]{1,0:T(8,128)(2,1)} collective-permute-done((bf16[128,1024]{1,0:T(8,128)(2,1)}, bf16[128,1024]{1,0:T(8,128)(2,1)}, u32[]{:S(2)}, u32[]{:S(2)}) %collective-permute-start.15) | collective-permute-done | bytes 262176 | tf_op jit(solution)/shard_map/ppermute | solution.py:115
  163.9 3.5 %collective-permute-done.13 = bf16[128,1024]{1,0:T(8,128)(2,1)} collective-permute-done((bf16[128,1024]{1,0:T(8,128)(2,1)}, bf16[128,1024]{1,0:T(8,128)(2,1)}, u32[]{:S(2)}, u32[]{:S(2)}) %collective-permute-start.13) | collective-permute-done | bytes 262176 | tf_op jit(solution)/shard_map/ppermute | solution.py:114
  172.1 4.0 %collective-permute-start.14 = (bf16[128,1024]{1,0:T(8,128)(2,1)S(1)}, bf16[128,1024]{1,0:T(8,128)(2,1)S(1)}, u32[]{:S(2)}, u32[]{:S(2)}) collective-permute-start(bf16[128,1024]{1,0:T(8,128)(2,1)S(1)} %get-tuple-element.20), channel_id=1, source_target_pairs={{1,0},{2,1},{3,2},{5,4},{6,5},{7,6},{9,8},{10,9},{11,10},{13,12},{... | collective-permute-start | bytes 786440 | tf_op jit(solution)/shard_map/ppermute | solution.py:114
  181.3 3.9 %collective-permute-start.20 = (bf16[128,1024]{1,0:T(8,128)(2,1)S(1)}, bf16[128,1024]{1,0:T(8,128)(2,1)S(1)}, u32[]{:S(2)}, u32[]{:S(2)}) collective-permute-start(bf16[128,1024]{1,0:T(8,128)(2,1)S(1)} %get-tuple-element.24), channel_id=1, source_target_pairs={{1,0},{2,1},{3,2},{5,4},{6,5},{7,6},{9,8},{10,9},{11,10},{13,12},{... | collective-permute-start | bytes 786440 | tf_op jit(solution)/shard_map/ppermute | solution.py:114
  187.0 2.4 %collective-permute-start.23 = (bf16[128,1024]{1,0:T(8,128)(2,1)S(1)}, bf16[128,1024]{1,0:T(8,128)(2,1)S(1)}, u32[]{:S(2)}, u32[]{:S(2)}) collective-permute-start(bf16[128,1024]{1,0:T(8,128)(2,1)S(1)} %add_convert_fusion.1), channel_id=1, source_target_pairs={{0,1},{1,2},{2,3},{4,5},{5,6},{6,7},{8,9},{9,10},{10,11},{12,13},{... | collective-permute-start | bytes 786440 | tf_op jit(solution)/shard_map/ppermute | solution.py:115
  189.5 2.6 %collective-permute-done.17 = bf16[128,1024]{1,0:T(8,128)(2,1)S(1)} collective-permute-done((bf16[128,1024]{1,0:T(8,128)(2,1)S(1)}, bf16[128,1024]{1,0:T(8,128)(2,1)S(1)}, u32[]{:S(2)}, u32[]{:S(2)}) %collective-permute-start.17) | collective-permute-done | bytes 262176 | tf_op jit(solution)/shard_map/ppermute | solution.py:115
  192.2 3.1 %collective-permute-done.23 = bf16[128,1024]{1,0:T(8,128)(2,1)S(1)} collective-permute-done((bf16[128,1024]{1,0:T(8,128)(2,1)S(1)}, bf16[128,1024]{1,0:T(8,128)(2,1)S(1)}, u32[]{:S(2)}, u32[]{:S(2)}) %collective-permute-start.23) | collective-permute-done | bytes 262176 | tf_op jit(solution)/shard_map/ppermute | solution.py:115
  (117 shorter events, 78.5 us)
Async XLA Ops:
  2.7 13.2 %collective-permute-start = (bf16[128,1024]{1,0:T(8,128)(2,1)S(1)}, bf16[128,1024]{1,0:T(8,128)(2,1)S(1)}, u32[]{:S(2)}, u32[]{:S(2)}) collective-permute-start(bf16[128,1024]{1,0:T(8,128)(2,1)S(1)} %pad_maximum_fusion.4), channel_id=1, source_target_pairs={{0,1},{1,2},{2,3},{4,5},{5,6},{6,7},{8,9},{9,10},{10,11},{12,13},{... | collective-permute-start | bytes 786440 | tf_op jit(solution)/shard_map/ppermute | solution.py:91
  6.1 13.9 %collective-permute-start.3 = (bf16[128,1024]{1,0:T(8,128)(2,1)S(1)}, bf16[128,1024]{1,0:T(8,128)(2,1)S(1)}, u32[]{:S(2)}, u32[]{:S(2)}) collective-permute-start(bf16[128,1024]{1,0:T(8,128)(2,1)S(1)} %pad_maximum_fusion.4), channel_id=1, source_target_pairs={{1,0},{2,1},{3,2},{5,4},{6,5},{7,6},{9,8},{10,9},{11,10},{13,12},{... | collective-permute-start | bytes 786440 | tf_op jit(solution)/shard_map/ppermute | solution.py:94
  8.6 13.4 %collective-permute-start.6 = (bf16[128,1024]{1,0:T(8,128)(2,1)S(1)}, bf16[128,1024]{1,0:T(8,128)(2,1)S(1)}, u32[]{:S(2)}, u32[]{:S(2)}) collective-permute-start(bf16[128,1024]{1,0:T(8,128)(2,1)S(1)} %pad_maximum_fusion.5), channel_id=1, source_target_pairs={{0,1},{1,2},{2,3},{4,5},{5,6},{6,7},{8,9},{9,10},{10,11},{12,13},{... | collective-permute-start | bytes 786440 | tf_op jit(solution)/shard_map/ppermute | solution.py:91
  12.0 13.9 %collective-permute-start.9 = (bf16[128,1024]{1,0:T(8,128)(2,1)S(1)}, bf16[128,1024]{1,0:T(8,128)(2,1)S(1)}, u32[]{:S(2)}, u32[]{:S(2)}) collective-permute-start(bf16[128,1024]{1,0:T(8,128)(2,1)S(1)} %pad_maximum_fusion.5), channel_id=1, source_target_pairs={{1,0},{2,1},{3,2},{5,4},{6,5},{7,6},{9,8},{10,9},{11,10},{13,12},{... | collective-permute-start | bytes 786440 | tf_op jit(solution)/shard_map/ppermute | solution.py:94
  15.8 12.1 %collective-permute-start.1 = (bf16[128,1024]{1,0:T(8,128)(2,1)S(1)}, bf16[128,1024]{1,0:T(8,128)(2,1)S(1)}, u32[]{:S(2)}, u32[]{:S(2)}) collective-permute-start(bf16[128,1024]{1,0:T(8,128)(2,1)S(1)} %collective-permute-done), channel_id=1, source_target_pairs={{1,2},{2,3},{5,6},{6,7},{9,10},{10,11},{13,14},{14,15},{17,18},{18... | collective-permute-start | bytes 786440 | tf_op jit(solution)/shard_map/ppermute | solution.py:91
  20.0 9.3 %collective-permute-start.4 = (bf16[128,1024]{1,0:T(8,128)(2,1)S(1)}, bf16[128,1024]{1,0:T(8,128)(2,1)S(1)}, u32[]{:S(2)}, u32[]{:S(2)}) collective-permute-start(bf16[128,1024]{1,0:T(8,128)(2,1)S(1)} %collective-permute-done.3), channel_id=1, source_target_pairs={{1,0},{2,1},{5,4},{6,5},{9,8},{10,9},{13,12},{14,13},{17,16},{18,1... | collective-permute-start | bytes 786440 | tf_op jit(solution)/shard_map/ppermute | solution.py:94
  27.9 11.8 %collective-permute-start.2 = (bf16[128,1024]{1,0:T(8,128)(2,1)S(1)}, bf16[128,1024]{1,0:T(8,128)(2,1)S(1)}, u32[]{:S(2)}, u32[]{:S(2)}) collective-permute-start(bf16[128,1024]{1,0:T(8,128)(2,1)S(1)} %collective-permute-done.1), channel_id=1, source_target_pairs={{2,3},{6,7},{10,11},{14,15},{18,19},{22,23},{26,27},{30,31}} | collective-permute-start | bytes 786440 | tf_op jit(solution)/shard_map/ppermute | solution.py:91
  29.3 12.6 %collective-permute-start.5 = (bf16[128,1024]{1,0:T(8,128)(2,1)S(1)}, bf16[128,1024]{1,0:T(8,128)(2,1)S(1)}, u32[]{:S(2)}, u32[]{:S(2)}) collective-permute-start(bf16[128,1024]{1,0:T(8,128)(2,1)S(1)} %collective-permute-done.4), channel_id=1, source_target_pairs={{1,0},{5,4},{9,8},{13,12},{17,16},{21,20},{25,24},{29,28}} | collective-permute-start | bytes 786440 | tf_op jit(solution)/shard_map/ppermute | solution.py:94
  31.0 19.9 %collective-permute-start.8 = (bf16[128,1024]{1,0:T(8,128)(2,1)S(1)}, bf16[128,1024]{1,0:T(8,128)(2,1)}, u32[]{:S(2)}, u32[]{:S(2)}) collective-permute-start(bf16[128,1024]{1,0:T(8,128)(2,1)S(1)} %collective-permute-done.7), channel_id=1, source_target_pairs={{2,3},{6,7},{10,11},{14,15},{18,19},{22,23},{26,27},{30,31}} | collective-permute-start | bytes 786440 | tf_op jit(solution)/shard_map/ppermute | solution.py:91
  34.6 19.4 %collective-permute-start.11 = (bf16[128,1024]{1,0:T(8,128)(2,1)S(1)}, bf16[128,1024]{1,0:T(8,128)(2,1)}, u32[]{:S(2)}, u32[]{:S(2)}) collective-permute-start(bf16[128,1024]{1,0:T(8,128)(2,1)S(1)} %collective-permute-done.10), channel_id=1, source_target_pairs={{1,0},{5,4},{9,8},{13,12},{17,16},{21,20},{25,24},{29,28}} | collective-permute-start | bytes 786440 | tf_op jit(solution)/shard_map/ppermute | solution.py:94
  46.6 18.2 %all-to-all-start = ((bf16[8,64,1024]{2,1,0:T(8,128)(2,1)}), bf16[8,64,1024]{2,1,0:T(8,128)(2,1)S(1)}, u32[]{:S(2)}, u32[]{:S(2)}) async-start(bf16[8,64,1024]{2,1,0:T(8,128)(2,1)} %broadcast_in_dim.4), calls=%async_computation | async-start | bytes 2097152 | tf_op jit(solution)/shard_map/all_to_all | solution.py:126
  65.8 33.0 %all-to-all-start.1 = ((bf16[8,64,1024]{2,1,0:T(8,128)(2,1)}), bf16[8,64,1024]{2,1,0:T(8,128)(2,1)}, u32[]{:S(2)}, u32[]{:S(2)}) async-start(bf16[8,64,1024]{2,1,0:T(8,128)(2,1)} %broadcast_in_dim.5), calls=%async_computation.1 | async-start | bytes 2097152 | tf_op jit(solution)/shard_map/all_to_all | solution.py:126
  98.9 30.0 %all-to-all-start.2 = ((bf16[8,64,1024]{2,1,0:T(8,128)(2,1)}), bf16[8,64,1024]{2,1,0:T(8,128)(2,1)S(1)}, u32[]{:S(2)}, u32[]{:S(2)}) async-start(bf16[8,64,1024]{2,1,0:T(8,128)(2,1)} %bitcast.23), calls=%async_computation.2 | async-start | bytes 2097152 | tf_op jit(solution)/shard_map/all_to_all | solution.py:135
  128.9 18.2 %all-to-all-start.3 = ((bf16[8,64,1024]{2,1,0:T(8,128)(2,1)}), bf16[8,64,1024]{2,1,0:T(8,128)(2,1)}, u32[]{:S(2)}, u32[]{:S(2)}) async-start(bf16[8,64,1024]{2,1,0:T(8,128)(2,1)} %bitcast.24), calls=%async_computation.3 | async-start | bytes 2097152 | tf_op jit(solution)/shard_map/all_to_all | solution.py:135
  142.9 11.3 %collective-permute-start.12 = (bf16[128,1024]{1,0:T(8,128)(2,1)}, bf16[128,1024]{1,0:T(8,128)(2,1)}, u32[]{:S(2)}, u32[]{:S(2)}) collective-permute-start(bf16[128,1024]{1,0:T(8,128)(2,1)} %get-tuple-element.22), channel_id=1, source_target_pairs={{3,2},{7,6},{11,10},{15,14},{19,18},{23,22},{27,26},{31,30}} | collective-permute-start | bytes 786440 | tf_op jit(solution)/shard_map/ppermute | solution.py:114
  152.8 11.1 %collective-permute-start.15 = (bf16[128,1024]{1,0:T(8,128)(2,1)}, bf16[128,1024]{1,0:T(8,128)(2,1)}, u32[]{:S(2)}, u32[]{:S(2)}) collective-permute-start(bf16[128,1024]{1,0:T(8,128)(2,1)} %get-tuple-element.23), channel_id=1, source_target_pairs={{0,1},{4,5},{8,9},{12,13},{16,17},{20,21},{24,25},{28,29}} | collective-permute-start | bytes 786440 | tf_op jit(solution)/shard_map/ppermute | solution.py:115
  156.1 11.4 %collective-permute-start.13 = (bf16[128,1024]{1,0:T(8,128)(2,1)}, bf16[128,1024]{1,0:T(8,128)(2,1)}, u32[]{:S(2)}, u32[]{:S(2)}) collective-permute-start(bf16[128,1024]{1,0:T(8,128)(2,1)} %add_convert_fusion.9), channel_id=1, source_target_pairs={{2,1},{3,2},{6,5},{7,6},{10,9},{11,10},{14,13},{15,14},{18,17},{19... | collective-permute-start | bytes 786440 | tf_op jit(solution)/shard_map/ppermute | solution.py:114
  157.4 18.6 %collective-permute-start.21 = (bf16[128,1024]{1,0:T(8,128)(2,1)S(1)}, bf16[128,1024]{1,0:T(8,128)(2,1)S(1)}, u32[]{:S(2)}, u32[]{:S(2)}) collective-permute-start(bf16[128,1024]{1,0:T(8,128)(2,1)S(1)} %get-tuple-element.27), channel_id=1, source_target_pairs={{0,1},{4,5},{8,9},{12,13},{16,17},{20,21},{24,25},{28,29}} | collective-permute-start | bytes 786440 | tf_op jit(solution)/shard_map/ppermute | solution.py:115
  159.7 16.3 %collective-permute-start.19 = (bf16[128,1024]{1,0:T(8,128)(2,1)S(1)}, bf16[128,1024]{1,0:T(8,128)(2,1)S(1)}, u32[]{:S(2)}, u32[]{:S(2)}) collective-permute-start(bf16[128,1024]{1,0:T(8,128)(2,1)S(1)} %add_convert_fusion.4), channel_id=1, source_target_pairs={{2,1},{3,2},{6,5},{7,6},{10,9},{11,10},{14,13},{15,14},{18,17},{19... | collective-permute-start | bytes 786440 | tf_op jit(solution)/shard_map/ppermute | solution.py:114
  169.0 9.3 %collective-permute-start.16 = (bf16[128,1024]{1,0:T(8,128)(2,1)S(1)}, bf16[128,1024]{1,0:T(8,128)(2,1)S(1)}, u32[]{:S(2)}, u32[]{:S(2)}) collective-permute-start(bf16[128,1024]{1,0:T(8,128)(2,1)S(1)} %get-tuple-element.21), channel_id=1, source_target_pairs={{0,1},{1,2},{4,5},{5,6},{8,9},{9,10},{12,13},{13,14},{16,17},{17,1... | collective-permute-start | bytes 786440 | tf_op jit(solution)/shard_map/ppermute | solution.py:115
  172.1 17.4 %collective-permute-start.14 = (bf16[128,1024]{1,0:T(8,128)(2,1)S(1)}, bf16[128,1024]{1,0:T(8,128)(2,1)S(1)}, u32[]{:S(2)}, u32[]{:S(2)}) collective-permute-start(bf16[128,1024]{1,0:T(8,128)(2,1)S(1)} %get-tuple-element.20), channel_id=1, source_target_pairs={{1,0},{2,1},{3,2},{5,4},{6,5},{7,6},{9,8},{10,9},{11,10},{13,12},{... | collective-permute-start | bytes 786440 | tf_op jit(solution)/shard_map/ppermute | solution.py:114
  176.2 10.7 %collective-permute-start.22 = (bf16[128,1024]{1,0:T(8,128)(2,1)S(1)}, bf16[128,1024]{1,0:T(8,128)(2,1)S(1)}, u32[]{:S(2)}, u32[]{:S(2)}) collective-permute-start(bf16[128,1024]{1,0:T(8,128)(2,1)S(1)} %get-tuple-element.25), channel_id=1, source_target_pairs={{0,1},{1,2},{4,5},{5,6},{8,9},{9,10},{12,13},{13,14},{16,17},{17,1... | collective-permute-start | bytes 786440 | tf_op jit(solution)/shard_map/ppermute | solution.py:115
  178.3 13.8 %collective-permute-start.17 = (bf16[128,1024]{1,0:T(8,128)(2,1)S(1)}, bf16[128,1024]{1,0:T(8,128)(2,1)S(1)}, u32[]{:S(2)}, u32[]{:S(2)}) collective-permute-start(bf16[128,1024]{1,0:T(8,128)(2,1)S(1)} %add_convert_fusion.6), channel_id=1, source_target_pairs={{0,1},{1,2},{2,3},{4,5},{5,6},{6,7},{8,9},{9,10},{10,11},{12,13},{... | collective-permute-start | bytes 786440 | tf_op jit(solution)/shard_map/ppermute | solution.py:115
  181.3 10.9 %collective-permute-start.20 = (bf16[128,1024]{1,0:T(8,128)(2,1)S(1)}, bf16[128,1024]{1,0:T(8,128)(2,1)S(1)}, u32[]{:S(2)}, u32[]{:S(2)}) collective-permute-start(bf16[128,1024]{1,0:T(8,128)(2,1)S(1)} %get-tuple-element.24), channel_id=1, source_target_pairs={{1,0},{2,1},{3,2},{5,4},{6,5},{7,6},{9,8},{10,9},{11,10},{13,12},{... | collective-permute-start | bytes 786440 | tf_op jit(solution)/shard_map/ppermute | solution.py:114
  (16 other events, 121.3 us)

commit v5 on v4

--- a/solution.py
+++ b/solution.py
@@ -176,5 +176,5 @@
         P(("ctx", "head"), None),
         P(("ctx", "head"), None),
     )
-    body = functools.partial(local, heads_axis=mesh.shape["head"], ctx_axis=mesh.shape["ctx"], parts=2)
+    body = functools.partial(local, heads_axis=mesh.shape["head"], ctx_axis=mesh.shape["ctx"], parts=4)
     return jax.shard_map(body, mesh=mesh, in_specs=in_specs, out_specs=out_specs, check_vma=False)

time: 199 us -> 302 us (1.52)
  starting transfers between devices: 74.3 us -> 147 us
  local copies, waits for them, and re-layouts: 39.6 us -> 52.6 us
  Pallas kernels: 34.8 us -> 40.4 us
  waiting for transfers between devices: 25.2 us -> 30.7 us
  other arithmetic: 21.8 us -> 26.5 us
    ppermute x6 -> x12, starting transfers between devices: 11.1 us -> 33.4 us  [head_reduce(): lax.ppermute(send_right, axis, [(j, j + 1) for j in range(0, min(step, co...]
    ppermute x6 -> x12, starting transfers between devices: 15.3 us -> 30.8 us  [head_gather(): lax.ppermute(from_right[-1], axis, [(j + 1, j) for j in range(count - ste...]
    ppermute x6 -> x12, starting transfers between devices: 16.4 us -> 30 us  [head_gather(): lax.ppermute(from_left[-1], axis, [(j, j + 1) for j in range(step - 1, co...]
    all_to_all x2 -> x4, starting transfers between devices: 8.42 us -> 18.3 us  [local_part(): lax.all_to_all(kv_grads[window:].astype(jnp.bfloat16).reshape(ctx_axis, p...]
    all_to_all x2 -> x4, starting transfers between devices: 9.88 us -> 16.8 us  [local_part(): lax.all_to_all(jnp.broadcast_to(own_beacon_rows[None], (ctx_axis,) + own_...]
    ppermute x6 -> x12, waiting for transfers between devices: 3.56 us -> 9.89 us  [head_reduce(): lax.ppermute(send_left, axis, [(j, j - 1) for j in range(max(1, count - s...]
    all_to_all x2 -> x4, waiting for transfers between devices: 6.27 us -> 0.01 us  [local_part(): lax.all_to_all(jnp.broadcast_to(own_beacon_rows[None], (ctx_axis,) + own_...]
    pallas_call x2 -> x4, Pallas kernels: 34.8 us -> 40.4 us  [attend_all(): pl.pallas_call(kernel, grid_spec=pltpu.PrefetchScalarGridSpec(num_scalar_...]
  transfers between devices with their start and end apart: 28 -> 56, of which waited for: 8 -> 10; matrix products, arithmetic and copies ran while one was open for 27% -> 23% of each run, Pallas kernels for 18% -> 14%
where the time goes in v5:
time: 302 us; the launch traced here: 299 us
  starting transfers between devices  147 us (49%)
  local copies, waits for them, and re-layouts  52.6 us (17%)
  Pallas kernels  40.4 us (13%)
  waiting for transfers between devices  30.7 us (10%)
  other arithmetic  26.5 us (9%)
    pallas_call x4, Pallas kernels, attend_all(): pl.pallas_call(kernel, grid_spec=pltpu.PrefetchScalarGridSpec(num_scalar_...  40.4 us
    ppermute x12, starting transfers between devices, head_reduce(): lax.ppermute(send_right, axis, [(j, j + 1) for j in range(0, min(step, co...  33.4 us
    ppermute x12, starting transfers between devices, head_gather(): lax.ppermute(from_right[-1], axis, [(j + 1, j) for j in range(count - ste...  30.8 us
    ppermute x12, starting transfers between devices, head_gather(): lax.ppermute(from_left[-1], axis, [(j, j + 1) for j in range(step - 1, co...  30 us
    unnamed x76, local copies, waits for them, and re-layouts  18.8 us
    all_to_all x4, starting transfers between devices, local_part(): lax.all_to_all(kv_grads[window:].astype(jnp.bfloat16).reshape(ctx_axis, p...  18.3 us
    ppermute x12, starting transfers between devices, head_reduce(): lax.ppermute(send_left, axis, [(j, j - 1) for j in range(max(1, count - s...  17.4 us
    all_to_all x4, starting transfers between devices, local_part(): lax.all_to_all(jnp.broadcast_to(own_beacon_rows[None], (ctx_axis,) + own_...  16.8 us
  transfers between devices with their start and end apart: 56, of which 10 were waited for; matrix products, arithmetic and copies ran while one was open for 23% of the time, Pallas kernels for 14%

profile of v5, /device:TPU:10, one launch (start us, length us, event | category | flops | bytes accessed | tf_op | source)
XLA Modules:
  0.0 298.8 jit_solution(9502003018968008834)
XLA Ops:
  22.7 3.6 %collective-permute-start.15 = (bf16[128,512]{1,0:T(8,128)(2,1)}, bf16[128,512]{1,0:T(8,128)(2,1)S(1)}, u32[]{:S(2)}, u32[]{:S(2)}) collective-permute-start(bf16[128,512]{1,0:T(8,128)(2,1)} %pad_maximum_fusion.10), channel_id=1, source_target_pairs={{1,0},{2,1},{3,2},{5,4},{6,5},{7,6},{9,8},{10,9},{11,10},{13,12},{... | collective-permute-start | bytes 393224 | tf_op jit(solution)/shard_map/ppermute | solution.py:94
  40.0 4.2 %collective-permute-start.7 = (bf16[128,512]{1,0:T(8,128)(2,1)}, bf16[128,512]{1,0:T(8,128)(2,1)S(1)}, u32[]{:S(2)}, u32[]{:S(2)}) collective-permute-start(bf16[128,512]{1,0:T(8,128)(2,1)} %collective-permute-done.6), channel_id=1, source_target_pairs={{1,2},{2,3},{5,6},{6,7},{9,10},{10,11},{13,14},{14,15},{17,18},{18... | collective-permute-start | bytes 393224 | tf_op jit(solution)/shard_map/ppermute | solution.py:91
  47.1 4.2 %collective-permute-start.13 = (bf16[128,512]{1,0:T(8,128)(2,1)S(1)}, bf16[128,512]{1,0:T(8,128)(2,1)S(1)}, u32[]{:S(2)}, u32[]{:S(2)}) collective-permute-start(bf16[128,512]{1,0:T(8,128)(2,1)S(1)} %collective-permute-done.12), channel_id=1, source_target_pairs={{1,2},{2,3},{5,6},{6,7},{9,10},{10,11},{13,14},{14,15},{17,18},{18... | collective-permute-start | bytes 393224 | tf_op jit(solution)/shard_map/ppermute | solution.py:91
  51.3 4.2 %collective-permute-start.19 = (bf16[128,512]{1,0:T(8,128)(2,1)S(1)}, bf16[128,512]{1,0:T(8,128)(2,1)S(1)}, u32[]{:S(2)}, u32[]{:S(2)}) collective-permute-start(bf16[128,512]{1,0:T(8,128)(2,1)S(1)} %collective-permute-done.18), channel_id=1, source_target_pairs={{1,2},{2,3},{5,6},{6,7},{9,10},{10,11},{13,14},{14,15},{17,18},{18... | collective-permute-start | bytes 393224 | tf_op jit(solution)/shard_map/ppermute | solution.py:91
  73.8 4.3 %all-to-all-start = ((bf16[8,64,512]{2,1,0:T(8,128)(2,1)}), bf16[8,64,512]{2,1,0:T(8,128)(2,1)S(1)}, u32[]{:S(2)}, u32[]{:S(2)}) async-start(bf16[8,64,512]{2,1,0:T(8,128)(2,1)} %broadcast_in_dim.8), calls=%async_computation | async-start | bytes 1048576 | tf_op jit(solution)/shard_map/all_to_all | solution.py:126
  79.4 4.3 %collective-permute-start.11 = (bf16[128,512]{1,0:T(8,128)(2,1)S(1)}, bf16[128,512]{1,0:T(8,128)(2,1)S(1)}, u32[]{:S(2)}, u32[]{:S(2)}) collective-permute-start(bf16[128,512]{1,0:T(8,128)(2,1)S(1)} %collective-permute-done.10), channel_id=1, source_target_pairs={{1,0},{5,4},{9,8},{13,12},{17,16},{21,20},{25,24},{29,28}} | collective-permute-start | bytes 393224 | tf_op jit(solution)/shard_map/ppermute | solution.py:94
  96.5 4.2 %all-to-all-start.1 = ((bf16[8,64,512]{2,1,0:T(8,128)(2,1)}), bf16[8,64,512]{2,1,0:T(8,128)(2,1)S(1)}, u32[]{:S(2)}, u32[]{:S(2)}) async-start(bf16[8,64,512]{2,1,0:T(8,128)(2,1)} %broadcast_in_dim.9), calls=%async_computation.1 | async-start | bytes 1048576 | tf_op jit(solution)/shard_map/all_to_all | solution.py:126
  110.7 4.2 %all-to-all-start.2 = ((bf16[8,64,512]{2,1,0:T(8,128)(2,1)}), bf16[8,64,512]{2,1,0:T(8,128)(2,1)S(1)}, u32[]{:S(2)}, u32[]{:S(2)}) async-start(bf16[8,64,512]{2,1,0:T(8,128)(2,1)} %broadcast_in_dim.10), calls=%async_computation.2 | async-start | bytes 1048576 | tf_op jit(solution)/shard_map/all_to_all | solution.py:126
  115.9 10.1 %shard_map.84 = (bf16[128,1024]{1,0:T(8,128)(2,1)}, bf16[128,1024]{1,0:T(8,128)(2,1)}, f32[1024,256]{1,0:T(8,128)}, f32[1024,256]{1,0:T(8,128)}) custom-call(s32[2]{0:T(128)} %pad_add_fusion.ids_ref, bf16[128,1024]{1,0:T(8,128)(2,1)} %get-tuple-element.83.q_ref, bf16[128,1024]{1,0:T(8,128)(2,1)} %get-tuple-element.52.g_ref, ...), custom_call_target="tpu_custom_call" | custom-call | tf_op jit(solution)/shard_map/pallas_call | solution.py:69
  126.0 10.2 %shard_map.85 = (bf16[128,1024]{1,0:T(8,128)(2,1)}, bf16[128,1024]{1,0:T(8,128)(2,1)}, f32[1024,256]{1,0:T(8,128)}, f32[1024,256]{1,0:T(8,128)}) custom-call(s32[2]{0:T(128)} %pad_add_fusion.ids_ref, bf16[128,1024]{1,0:T(8,128)(2,1)} %get-tuple-element.82.q_ref, bf16[128,1024]{1,0:T(8,128)(2,1)} %get-tuple-element.53.g_ref, ...), custom_call_target="tpu_custom_call" | custom-call | tf_op jit(solution)/shard_map/pallas_call | solution.py:69
  140.9 4.2 %all-to-all-start.3 = ((bf16[8,64,512]{2,1,0:T(8,128)(2,1)}), bf16[8,64,512]{2,1,0:T(8,128)(2,1)S(1)}, u32[]{:S(2)}, u32[]{:S(2)}) async-start(bf16[8,64,512]{2,1,0:T(8,128)(2,1)} %broadcast_in_dim.11), calls=%async_computation.3 | async-start | bytes 1048576 | tf_op jit(solution)/shard_map/all_to_all | solution.py:126
  151.4 10.0 %shard_map.86 = (bf16[128,1024]{1,0:T(8,128)(2,1)}, bf16[128,1024]{1,0:T(8,128)(2,1)}, f32[1024,256]{1,0:T(8,128)}, f32[1024,256]{1,0:T(8,128)}) custom-call(s32[2]{0:T(128)} %pad_add_fusion.ids_ref, bf16[128,1024]{1,0:T(8,128)(2,1)} %get-tuple-element.80.q_ref, bf16[128,1024]{1,0:T(8,128)(2,1)} %get-tuple-element.55.g_ref, ...), custom_call_target="tpu_custom_call" | custom-call | tf_op jit(solution)/shard_map/pallas_call | solution.py:69
  165.3 4.2 %all-to-all-start.4 = ((bf16[8,64,512]{2,1,0:T(8,128)(2,1)}), bf16[8,64,512]{2,1,0:T(8,128)(2,1)S(1)}, u32[]{:S(2)}, u32[]{:S(2)}) async-start(bf16[8,64,512]{2,1,0:T(8,128)(2,1)} %bitcast.41), calls=%async_computation.4 | async-start | bytes 1048576 | tf_op jit(solution)/shard_map/all_to_all | solution.py:135
  170.6 10.1 %shard_map.87 = (bf16[128,1024]{1,0:T(8,128)(2,1)}, bf16[128,1024]{1,0:T(8,128)(2,1)}, f32[1024,256]{1,0:T(8,128)}, f32[1024,256]{1,0:T(8,128)}) custom-call(s32[2]{0:T(128)} %pad_add_fusion.ids_ref, bf16[128,1024]{1,0:T(8,128)(2,1)} %get-tuple-element.81.q_ref, bf16[128,1024]{1,0:T(8,128)(2,1)} %get-tuple-element.54.g_ref, ...), custom_call_target="tpu_custom_call" | custom-call | tf_op jit(solution)/shard_map/pallas_call | solution.py:69
  182.8 4.3 %all-to-all-start.5 = ((bf16[8,64,512]{2,1,0:T(8,128)(2,1)}), bf16[8,64,512]{2,1,0:T(8,128)(2,1)S(1)}, u32[]{:S(2)}, u32[]{:S(2)}) async-start(bf16[8,64,512]{2,1,0:T(8,128)(2,1)} %bitcast.42), calls=%async_computation.5 | async-start | bytes 1048576 | tf_op jit(solution)/shard_map/all_to_all | solution.py:135
  188.2 7.2 %all-to-all-done.5 = bf16[8,64,512]{2,1,0:T(8,128)(2,1)S(1)} async-done(((bf16[8,64,512]{2,1,0:T(8,128)(2,1)}), bf16[8,64,512]{2,1,0:T(8,128)(2,1)S(1)}, u32[]{:S(2)}, u32[]{:S(2)}) %all-to-all-start.5) | async-done | bytes 524320 | tf_op jit(solution)/shard_map/all_to_all | solution.py:135
  195.4 5.5 %all-to-all-start.6 = ((bf16[8,64,512]{2,1,0:T(8,128)(2,1)}), bf16[8,64,512]{2,1,0:T(8,128)(2,1)}, u32[]{:S(2)}, u32[]{:S(2)}) async-start(bf16[8,64,512]{2,1,0:T(8,128)(2,1)} %bitcast.43), calls=%async_computation.6 | async-start | bytes 1048576 | tf_op jit(solution)/shard_map/all_to_all | solution.py:135
  213.7 4.2 %all-to-all-start.7 = ((bf16[8,64,512]{2,1,0:T(8,128)(2,1)}), bf16[8,64,512]{2,1,0:T(8,128)(2,1)}, u32[]{:S(2)}, u32[]{:S(2)}) async-start(bf16[8,64,512]{2,1,0:T(8,128)(2,1)} %bitcast.84), calls=%async_computation.7 | async-start | bytes 1048576 | tf_op jit(solution)/shard_map/all_to_all | solution.py:135
  239.9 9.9 %collective-permute-done.25 = bf16[128,512]{1,0:T(8,128)(2,1)S(1)} collective-permute-done((bf16[128,512]{1,0:T(8,128)(2,1)S(1)}, bf16[128,512]{1,0:T(8,128)(2,1)S(1)}, u32[]{:S(2)}, u32[]{:S(2)}) %collective-permute-start.25) | collective-permute-done | bytes 131104 | tf_op jit(solution)/shard_map/ppermute | solution.py:114
  252.5 5.2 %collective-permute-start.28 = (bf16[128,512]{1,0:T(8,128)(2,1)S(1)}, bf16[128,512]{1,0:T(8,128)(2,1)S(1)}, u32[]{:S(2)}, u32[]{:S(2)}) collective-permute-start(bf16[128,512]{1,0:T(8,128)(2,1)S(1)} %get-tuple-element.37), channel_id=1, source_target_pairs={{0,1},{1,2},{4,5},{5,6},{8,9},{9,10},{12,13},{13,14},{16,17},{17,1... | collective-permute-start | bytes 393224 | tf_op jit(solution)/shard_map/ppermute | solution.py:115
  259.7 3.9 %collective-permute-start.34 = (bf16[128,512]{1,0:T(8,128)(2,1)S(1)}, bf16[128,512]{1,0:T(8,128)(2,1)S(1)}, u32[]{:S(2)}, u32[]{:S(2)}) collective-permute-start(bf16[128,512]{1,0:T(8,128)(2,1)S(1)} %get-tuple-element.41), channel_id=1, source_target_pairs={{0,1},{1,2},{4,5},{5,6},{8,9},{9,10},{12,13},{13,14},{16,17},{17,1... | collective-permute-start | bytes 393224 | tf_op jit(solution)/shard_map/ppermute | solution.py:115
  265.7 3.9 %collective-permute-start.40 = (bf16[128,512]{1,0:T(8,128)(2,1)S(1)}, bf16[128,512]{1,0:T(8,128)(2,1)S(1)}, u32[]{:S(2)}, u32[]{:S(2)}) collective-permute-start(bf16[128,512]{1,0:T(8,128)(2,1)S(1)} %get-tuple-element.45), channel_id=1, source_target_pairs={{0,1},{1,2},{4,5},{5,6},{8,9},{9,10},{12,13},{13,14},{16,17},{17,1... | collective-permute-start | bytes 393224 | tf_op jit(solution)/shard_map/ppermute | solution.py:115
  271.7 3.9 %collective-permute-start.46 = (bf16[128,512]{1,0:T(8,128)(2,1)S(1)}, bf16[128,512]{1,0:T(8,128)(2,1)S(1)}, u32[]{:S(2)}, u32[]{:S(2)}) collective-permute-start(bf16[128,512]{1,0:T(8,128)(2,1)S(1)} %get-tuple-element.49), channel_id=1, source_target_pairs={{0,1},{1,2},{4,5},{5,6},{8,9},{9,10},{12,13},{13,14},{16,17},{17,1... | collective-permute-start | bytes 393224 | tf_op jit(solution)/shard_map/ppermute | solution.py:115
  278.6 3.8 %collective-permute-start.29 = (bf16[128,512]{1,0:T(8,128)(2,1)S(1)}, bf16[128,512]{1,0:T(8,128)(2,1)S(1)}, u32[]{:S(2)}, u32[]{:S(2)}) collective-permute-start(bf16[128,512]{1,0:T(8,128)(2,1)S(1)} %add_convert_fusion.16), channel_id=1, source_target_pairs={{0,1},{1,2},{2,3},{4,5},{5,6},{6,7},{8,9},{9,10},{10,11},{12,13},{... | collective-permute-start | bytes 393224 | tf_op jit(solution)/shard_map/ppermute | solution.py:115
  (250 shorter events, 163.0 us)
Async XLA Ops:
  3.4 19.3 %collective-permute-start = (bf16[128,512]{1,0:T(8,128)(2,1)}, bf16[128,512]{1,0:T(8,128)(2,1)}, u32[]{:S(2)}, u32[]{:S(2)}) collective-permute-start(bf16[128,512]{1,0:T(8,128)(2,1)} %pad_maximum_fusion.8), channel_id=1, source_target_pairs={{0,1},{1,2},{2,3},{4,5},{5,6},{6,7},{8,9},{9,10},{10,11},{12,13},{... | collective-permute-start | bytes 393224 | tf_op jit(solution)/shard_map/ppermute | solution.py:91
  6.9 44.4 %collective-permute-start.3 = (bf16[128,512]{1,0:T(8,128)(2,1)}, bf16[128,512]{1,0:T(8,128)(2,1)S(1)}, u32[]{:S(2)}, u32[]{:S(2)}) collective-permute-start(bf16[128,512]{1,0:T(8,128)(2,1)} %pad_maximum_fusion.8), channel_id=1, source_target_pairs={{1,0},{2,1},{3,2},{5,4},{6,5},{7,6},{9,8},{10,9},{11,10},{13,12},{... | collective-permute-start | bytes 393224 | tf_op jit(solution)/shard_map/ppermute | solution.py:94
  13.4 42.1 %collective-permute-start.9 = (bf16[128,512]{1,0:T(8,128)(2,1)}, bf16[128,512]{1,0:T(8,128)(2,1)}, u32[]{:S(2)}, u32[]{:S(2)}) collective-permute-start(bf16[128,512]{1,0:T(8,128)(2,1)} %pad_maximum_fusion.9), channel_id=1, source_target_pairs={{1,0},{2,1},{3,2},{5,4},{6,5},{7,6},{9,8},{10,9},{11,10},{13,12},{... | collective-permute-start | bytes 393224 | tf_op jit(solution)/shard_map/ppermute | solution.py:94
  22.7 34.7 %collective-permute-start.15 = (bf16[128,512]{1,0:T(8,128)(2,1)}, bf16[128,512]{1,0:T(8,128)(2,1)S(1)}, u32[]{:S(2)}, u32[]{:S(2)}) collective-permute-start(bf16[128,512]{1,0:T(8,128)(2,1)} %pad_maximum_fusion.10), channel_id=1, source_target_pairs={{1,0},{2,1},{3,2},{5,4},{6,5},{7,6},{9,8},{10,9},{11,10},{13,12},{... | collective-permute-start | bytes 393224 | tf_op jit(solution)/shard_map/ppermute | solution.py:94
  31.3 28.1 %collective-permute-start.21 = (bf16[128,512]{1,0:T(8,128)(2,1)S(1)}, bf16[128,512]{1,0:T(8,128)(2,1)S(1)}, u32[]{:S(2)}, u32[]{:S(2)}) collective-permute-start(bf16[128,512]{1,0:T(8,128)(2,1)S(1)} %pad_maximum_fusion.11), channel_id=1, source_target_pairs={{1,0},{2,1},{3,2},{5,4},{6,5},{7,6},{9,8},{10,9},{11,10},{13,12},{... | collective-permute-start | bytes 393224 | tf_op jit(solution)/shard_map/ppermute | solution.py:94
  57.5 20.6 %collective-permute-start.10 = (bf16[128,512]{1,0:T(8,128)(2,1)}, bf16[128,512]{1,0:T(8,128)(2,1)S(1)}, u32[]{:S(2)}, u32[]{:S(2)}) collective-permute-start(bf16[128,512]{1,0:T(8,128)(2,1)} %collective-permute-done.9), channel_id=1, source_target_pairs={{1,0},{2,1},{5,4},{6,5},{9,8},{10,9},{13,12},{14,13},{17,16},{18,1... | collective-permute-start | bytes 393224 | tf_op jit(solution)/shard_map/ppermute | solution.py:94
  59.4 20.0 %collective-permute-start.16 = (bf16[128,512]{1,0:T(8,128)(2,1)S(1)}, bf16[128,512]{1,0:T(8,128)(2,1)S(1)}, u32[]{:S(2)}, u32[]{:S(2)}) collective-permute-start(bf16[128,512]{1,0:T(8,128)(2,1)S(1)} %collective-permute-done.15), channel_id=1, source_target_pairs={{1,0},{2,1},{5,4},{6,5},{9,8},{10,9},{13,12},{14,13},{17,16},{18,1... | collective-permute-start | bytes 393224 | tf_op jit(solution)/shard_map/ppermute | solution.py:94
  61.3 22.4 %collective-permute-start.22 = (bf16[128,512]{1,0:T(8,128)(2,1)S(1)}, bf16[128,512]{1,0:T(8,128)(2,1)S(1)}, u32[]{:S(2)}, u32[]{:S(2)}) collective-permute-start(bf16[128,512]{1,0:T(8,128)(2,1)S(1)} %collective-permute-done.21), channel_id=1, source_target_pairs={{1,0},{2,1},{5,4},{6,5},{9,8},{10,9},{13,12},{14,13},{17,16},{18,1... | collective-permute-start | bytes 393224 | tf_op jit(solution)/shard_map/ppermute | solution.py:94
  64.0 21.7 %collective-permute-start.8 = (bf16[128,512]{1,0:T(8,128)(2,1)S(1)}, bf16[128,512]{1,0:T(8,128)(2,1)S(1)}, u32[]{:S(2)}, u32[]{:S(2)}) collective-permute-start(bf16[128,512]{1,0:T(8,128)(2,1)S(1)} %collective-permute-done.7), channel_id=1, source_target_pairs={{2,3},{6,7},{10,11},{14,15},{18,19},{22,23},{26,27},{30,31}} | collective-permute-start | bytes 393224 | tf_op jit(solution)/shard_map/ppermute | solution.py:91
  68.5 21.4 %collective-permute-start.14 = (bf16[128,512]{1,0:T(8,128)(2,1)S(1)}, bf16[128,512]{1,0:T(8,128)(2,1)}, u32[]{:S(2)}, u32[]{:S(2)}) collective-permute-start(bf16[128,512]{1,0:T(8,128)(2,1)S(1)} %collective-permute-done.13), channel_id=1, source_target_pairs={{2,3},{6,7},{10,11},{14,15},{18,19},{22,23},{26,27},{30,31}} | collective-permute-start | bytes 393224 | tf_op jit(solution)/shard_map/ppermute | solution.py:91
  73.8 21.9 %all-to-all-start = ((bf16[8,64,512]{2,1,0:T(8,128)(2,1)}), bf16[8,64,512]{2,1,0:T(8,128)(2,1)S(1)}, u32[]{:S(2)}, u32[]{:S(2)}) async-start(bf16[8,64,512]{2,1,0:T(8,128)(2,1)} %broadcast_in_dim.8), calls=%async_computation | async-start | bytes 1048576 | tf_op jit(solution)/shard_map/all_to_all | solution.py:126
  85.7 19.1 %collective-permute-start.23 = (bf16[128,512]{1,0:T(8,128)(2,1)S(1)}, bf16[128,512]{1,0:T(8,128)(2,1)}, u32[]{:S(2)}, u32[]{:S(2)}) collective-permute-start(bf16[128,512]{1,0:T(8,128)(2,1)S(1)} %collective-permute-done.22), channel_id=1, source_target_pairs={{1,0},{5,4},{9,8},{13,12},{17,16},{21,20},{25,24},{29,28}} | collective-permute-start | bytes 393224 | tf_op jit(solution)/shard_map/ppermute | solution.py:94
  110.7 29.4 %all-to-all-start.2 = ((bf16[8,64,512]{2,1,0:T(8,128)(2,1)}), bf16[8,64,512]{2,1,0:T(8,128)(2,1)S(1)}, u32[]{:S(2)}, u32[]{:S(2)}) async-start(bf16[8,64,512]{2,1,0:T(8,128)(2,1)} %broadcast_in_dim.10), calls=%async_computation.2 | async-start | bytes 1048576 | tf_op jit(solution)/shard_map/all_to_all | solution.py:126
  140.9 24.5 %all-to-all-start.3 = ((bf16[8,64,512]{2,1,0:T(8,128)(2,1)}), bf16[8,64,512]{2,1,0:T(8,128)(2,1)S(1)}, u32[]{:S(2)}, u32[]{:S(2)}) async-start(bf16[8,64,512]{2,1,0:T(8,128)(2,1)} %broadcast_in_dim.11), calls=%async_computation.3 | async-start | bytes 1048576 | tf_op jit(solution)/shard_map/all_to_all | solution.py:126
  195.4 18.2 %all-to-all-start.6 = ((bf16[8,64,512]{2,1,0:T(8,128)(2,1)}), bf16[8,64,512]{2,1,0:T(8,128)(2,1)}, u32[]{:S(2)}, u32[]{:S(2)}) async-start(bf16[8,64,512]{2,1,0:T(8,128)(2,1)} %bitcast.43), calls=%async_computation.6 | async-start | bytes 1048576 | tf_op jit(solution)/shard_map/all_to_all | solution.py:135
  211.1 19.8 %collective-permute-start.24 = (bf16[128,512]{1,0:T(8,128)(2,1)}, bf16[128,512]{1,0:T(8,128)(2,1)}, u32[]{:S(2)}, u32[]{:S(2)}) collective-permute-start(bf16[128,512]{1,0:T(8,128)(2,1)} %get-tuple-element.38), channel_id=1, source_target_pairs={{3,2},{7,6},{11,10},{15,14},{19,18},{23,22},{27,26},{31,30}} | collective-permute-start | bytes 393224 | tf_op jit(solution)/shard_map/ppermute | solution.py:114
  212.4 26.2 %collective-permute-start.27 = (bf16[128,512]{1,0:T(8,128)(2,1)}, bf16[128,512]{1,0:T(8,128)(2,1)S(1)}, u32[]{:S(2)}, u32[]{:S(2)}) collective-permute-start(bf16[128,512]{1,0:T(8,128)(2,1)} %get-tuple-element.39), channel_id=1, source_target_pairs={{0,1},{4,5},{8,9},{12,13},{16,17},{20,21},{24,25},{28,29}} | collective-permute-start | bytes 393224 | tf_op jit(solution)/shard_map/ppermute | solution.py:115
  222.4 28.7 %collective-permute-start.33 = (bf16[128,512]{1,0:T(8,128)(2,1)}, bf16[128,512]{1,0:T(8,128)(2,1)S(1)}, u32[]{:S(2)}, u32[]{:S(2)}) collective-permute-start(bf16[128,512]{1,0:T(8,128)(2,1)} %get-tuple-element.43), channel_id=1, source_target_pairs={{0,1},{4,5},{8,9},{12,13},{16,17},{20,21},{24,25},{28,29}} | collective-permute-start | bytes 393224 | tf_op jit(solution)/shard_map/ppermute | solution.py:115
  230.9 26.9 %collective-permute-start.39 = (bf16[128,512]{1,0:T(8,128)(2,1)}, bf16[128,512]{1,0:T(8,128)(2,1)S(1)}, u32[]{:S(2)}, u32[]{:S(2)}) collective-permute-start(bf16[128,512]{1,0:T(8,128)(2,1)} %get-tuple-element.47), channel_id=1, source_target_pairs={{0,1},{4,5},{8,9},{12,13},{16,17},{20,21},{24,25},{28,29}} | collective-permute-start | bytes 393224 | tf_op jit(solution)/shard_map/ppermute | solution.py:115
  235.0 28.7 %collective-permute-start.45 = (bf16[128,512]{1,0:T(8,128)(2,1)S(1)}, bf16[128,512]{1,0:T(8,128)(2,1)S(1)}, u32[]{:S(2)}, u32[]{:S(2)}) collective-permute-start(bf16[128,512]{1,0:T(8,128)(2,1)S(1)} %get-tuple-element.51), channel_id=1, source_target_pairs={{0,1},{4,5},{8,9},{12,13},{16,17},{20,21},{24,25},{28,29}} | collective-permute-start | bytes 393224 | tf_op jit(solution)/shard_map/ppermute | solution.py:115
  257.8 24.8 %collective-permute-start.26 = (bf16[128,512]{1,0:T(8,128)(2,1)S(1)}, bf16[128,512]{1,0:T(8,128)(2,1)S(1)}, u32[]{:S(2)}, u32[]{:S(2)}) collective-permute-start(bf16[128,512]{1,0:T(8,128)(2,1)S(1)} %get-tuple-element.36), channel_id=1, source_target_pairs={{1,0},{2,1},{3,2},{5,4},{6,5},{7,6},{9,8},{10,9},{11,10},{13,12},{... | collective-permute-start | bytes 393224 | tf_op jit(solution)/shard_map/ppermute | solution.py:114
  263.7 26.6 %collective-permute-start.32 = (bf16[128,512]{1,0:T(8,128)(2,1)S(1)}, bf16[128,512]{1,0:T(8,128)(2,1)S(1)}, u32[]{:S(2)}, u32[]{:S(2)}) collective-permute-start(bf16[128,512]{1,0:T(8,128)(2,1)S(1)} %get-tuple-element.40), channel_id=1, source_target_pairs={{1,0},{2,1},{3,2},{5,4},{6,5},{7,6},{9,8},{10,9},{11,10},{13,12},{... | collective-permute-start | bytes 393224 | tf_op jit(solution)/shard_map/ppermute | solution.py:114
  269.7 22.7 %collective-permute-start.38 = (bf16[128,512]{1,0:T(8,128)(2,1)S(1)}, bf16[128,512]{1,0:T(8,128)(2,1)S(1)}, u32[]{:S(2)}, u32[]{:S(2)}) collective-permute-start(bf16[128,512]{1,0:T(8,128)(2,1)S(1)} %get-tuple-element.44), channel_id=1, source_target_pairs={{1,0},{2,1},{3,2},{5,4},{6,5},{7,6},{9,8},{10,9},{11,10},{13,12},{... | collective-permute-start | bytes 393224 | tf_op jit(solution)/shard_map/ppermute | solution.py:114
  275.7 18.0 %collective-permute-start.44 = (bf16[128,512]{1,0:T(8,128)(2,1)S(1)}, bf16[128,512]{1,0:T(8,128)(2,1)S(1)}, u32[]{:S(2)}, u32[]{:S(2)}) collective-permute-start(bf16[128,512]{1,0:T(8,128)(2,1)S(1)} %get-tuple-element.48), channel_id=1, source_target_pairs={{1,0},{2,1},{3,2},{5,4},{6,5},{7,6},{9,8},{10,9},{11,10},{13,12},{... | collective-permute-start | bytes 393224 | tf_op jit(solution)/shard_map/ppermute | solution.py:114
  (58 other events, 563.6 us)

commit v6 on v4

--- a/solution.py
+++ b/solution.py
@@ -86,13 +86,9 @@
 def head_gather(block, axis, count):
     index = lax.axis_index(axis)
     from_left, from_right = [block], [block]
-    for step in range(1, count):
-        from_left.append(
-            lax.ppermute(from_left[-1], axis, [(j, j + 1) for j in range(step - 1, count - 1)])
-        )
-        from_right.append(
-            lax.ppermute(from_right[-1], axis, [(j + 1, j) for j in range(count - step)])
-        )
+    for shift in range(1, count):
+        from_left.append(lax.ppermute(block, axis, [(j, j + shift) for j in range(count - shift)]))
+        from_right.append(lax.ppermute(block, axis, [(j + shift, j) for j in range(count - shift)]))
     pieces = jnp.stack(from_left + from_right[1:])
     order = jnp.arange(count)
     pick = jnp.where(order <= index, index - order, count - 1 + order - index)
@@ -106,40 +102,43 @@
     def block_of(target):
         return lax.dynamic_slice_in_dim(partials, jnp.clip(target, 0, count - 1) * rows, rows, 0)
 
-    left = jnp.zeros((rows, partials.shape[1]), jnp.bfloat16)
-    right = jnp.zeros((rows, partials.shape[1]), jnp.bfloat16)
-    for step in range(1, count):
-        send_left = (block_of(index + step - count) + left.astype(jnp.float32)).astype(jnp.bfloat16)
-        send_right = (block_of(index - step + count) + right.astype(jnp.float32)).astype(jnp.bfloat16)
-        left = lax.ppermute(send_left, axis, [(j, j - 1) for j in range(max(1, count - step), count)])
-        right = lax.ppermute(send_right, axis, [(j, j + 1) for j in range(0, min(step, count - 1))])
-    return block_of(index) + left.astype(jnp.float32) + right.astype(jnp.float32)
+    total = block_of(index)
+    for shift in range(1, count):
+        to_left = block_of(index - shift).astype(jnp.bfloat16)
+        to_right = block_of(index + shift).astype(jnp.bfloat16)
+        total = total + lax.ppermute(to_left, axis, [(j + shift, j) for j in range(count - shift)]).astype(jnp.float32)
+        total = total + lax.ppermute(to_right, axis, [(j, j + shift) for j in range(count - shift)]).astype(jnp.float32)
+    return total
 
 
-def local_part(queries, keys, values, out_grad, positions, ids, heads_axis, ctx_axis):
+def gather_part(keys, values, positions, heads_axis, ctx_axis):
     kv_width = keys.shape[1]
     per_shard = positions.shape[0]
     kv_rows = jnp.concatenate([keys, values], axis=1)
     kv_window = head_gather(kv_rows, "head", heads_axis)
-    window = kv_window.shape[0]
     own_beacon_rows = kv_window[positions]
     kv_beacons = lax.all_to_all(
         jnp.broadcast_to(own_beacon_rows[None], (ctx_axis,) + own_beacon_rows.shape),
         "ctx", 0, 0, tiled=True,
     ).reshape(ctx_axis * per_shard, 2 * kv_width)
+    return kv_window, kv_beacons
+
+
+def grads_part(queries, out_grad, kv_window, kv_beacons, positions, ids, ctx_axis):
+    window = kv_window.shape[0]
+    per_shard = positions.shape[0]
     kv_all = jnp.concatenate([kv_window, kv_beacons], axis=0)
     attended_out, query_out, key_grad, value_grad = attend_all(
         ids, queries, out_grad, kv_all, window, per_shard
     )
     kv_grads = jnp.concatenate([key_grad, value_grad], axis=1)
     beacon_parts = lax.all_to_all(
-        kv_grads[window:].astype(jnp.bfloat16).reshape(ctx_axis, per_shard, 2 * kv_width),
+        kv_grads[window:].astype(jnp.bfloat16).reshape(ctx_axis, per_shard, kv_grads.shape[1]),
         "ctx", 0, 0, tiled=True,
     )
     own_beacons = jnp.sum(beacon_parts.astype(jnp.float32), axis=0)
     window_grads = kv_grads[:window].at[positions].add(own_beacons)
-    own_grads = head_reduce(window_grads, "head", heads_axis).astype(jnp.bfloat16)
-    return attended_out, query_out, own_grads[:, :kv_width], own_grads[:, kv_width:]
+    return attended_out, query_out, window_grads
 
 
 def local(queries, keys, values, out_grad, beacon_pos, *, heads_axis, ctx_axis, parts):
@@ -149,17 +148,36 @@
     positions = beacon_pos[0]
     q_cols = queries.shape[1] // parts
     kv_cols = keys.shape[1] // parts
-    results = []
+    gathered = []
+    ready = None
+    for part in range(parts):
+        ks = slice(part * kv_cols, (part + 1) * kv_cols)
+        part_keys, part_values = keys[:, ks], values[:, ks]
+        if ready is not None:
+            ready, part_keys, part_values = lax.optimization_barrier((ready, part_keys, part_values))
+        gathered.append(gather_part(part_keys, part_values, positions, heads_axis, ctx_axis))
+        ready = gathered[-1][0]
+    attended, query_grad, key_grad, value_grad = [], [], [], []
+    previous = None
     for part in range(parts):
         qs = slice(part * q_cols, (part + 1) * q_cols)
-        ks = slice(part * kv_cols, (part + 1) * kv_cols)
-        results.append(
-            local_part(
-                queries[:, qs], keys[:, ks], values[:, ks], out_grad[:, qs],
-                positions, ids, heads_axis, ctx_axis,
-            )
+        kv_window, kv_beacons = gathered[part]
+        if previous is not None:
+            previous, kv_window = lax.optimization_barrier((previous, kv_window))
+        attended_out, query_out, window_grads = grads_part(
+            queries[:, qs], out_grad[:, qs], kv_window, kv_beacons, positions, ids, ctx_axis
         )
-    return tuple(jnp.concatenate(outs, axis=1) for outs in zip(*results))
+        if previous is not None:
+            own = head_reduce(previous, "head", heads_axis).astype(jnp.bfloat16)
+            key_grad.append(own[:, :kv_cols])
+            value_grad.append(own[:, kv_cols:])
+        previous = window_grads
+        attended.append(attended_out)
+        query_grad.append(query_out)
+    own = head_reduce(previous, "head", heads_axis).astype(jnp.bfloat16)
+    key_grad.append(own[:, :kv_cols])
+    value_grad.append(own[:, kv_cols:])
+    return tuple(jnp.concatenate(outs, axis=1) for outs in (attended, query_grad, key_grad, value_grad))
 
 
 def solution(mesh):

time: 199 us -> 225 us (1.13)
  waiting for transfers between devices: 25.2 us -> 51.3 us
  starting transfers between devices: 74.3 us -> 82.1 us
  other arithmetic: 21.8 us -> 15.3 us
    ppermute x24, waiting for transfers between devices: 16.1 us -> 33.1 us  [the longest x6 18.7 us: head_gather(): lax.ppermute(block, axis, [(j, j + shift) for j in range(count - shift)])]
    all_to_all x4, waiting for transfers between devices: 9.11 us -> 18.2 us  [the longest x2 10.1 us: gather_part(): lax.all_to_all(jnp.broadcast_to(own_beacon_rows[None], (ctx_axis,) + own_...]
    ppermute x24, starting transfers between devices: 56 us -> 63 us  [the longest x6 19.5 us: head_reduce(): lax.ppermute(to_right, axis, [(j, j + shift) for j in range(count - shift)])]
    unnamed x36 -> x42, local copies, waits for them, and re-layouts: 15.3 us -> 18.7 us
    convert_element_type x8 -> x2, other arithmetic: 4.89 us -> 2.01 us  [local(): own = head_reduce(previous, 'head', heads_axis).astype(jnp.bfloat16)]
    scatter-add x2, other arithmetic: 6.03 us -> 3.76 us  [grads_part(): window_grads = kv_grads[:window].at[positions].add(own_beacons)]
    slice x8 -> x7, local copies, waits for them, and re-layouts: 7.83 us -> 7.2 us  [the longest x2 3.69 us: grads_part(): window_grads = kv_grads[:window].at[positions].add(own_beacons)]
    concatenate x8 -> x7, other arithmetic: 7.91 us -> 7.87 us  [the longest x2 4.3 us: grads_part(): kv_all = jnp.concatenate([kv_window, kv_beacons], axis=0)]
  transfers between devices with their start and end apart: 28 -> 28, of which waited for: 8 -> 7; matrix products, arithmetic and copies ran while one was open for 27% -> 16% of each run, Pallas kernels for 18% -> 8%
where the time goes in v6:
time: 225 us; the launch traced here: 222 us
  starting transfers between devices  82.1 us (36%)
  waiting for transfers between devices  51.3 us (23%)
  local copies, waits for them, and re-layouts  37.6 us (17%)
  Pallas kernels  34.7 us (15%)
  other arithmetic  15.3 us (7%)
    pallas_call x2, Pallas kernels, attend_all(): pl.pallas_call(kernel, grid_spec=pltpu.PrefetchScalarGridSpec(num_scalar_...  34.7 us
    ppermute x6, starting transfers between devices, head_reduce(): lax.ppermute(to_right, axis, [(j, j + shift) for j in range(count - shift)])  19.5 us
    unnamed x42, local copies, waits for them, and re-layouts  18.7 us
    ppermute x6, waiting for transfers between devices, head_gather(): lax.ppermute(block, axis, [(j, j + shift) for j in range(count - shift)])  18.7 us
    ppermute x6, starting transfers between devices, head_reduce(): lax.ppermute(to_left, axis, [(j + shift, j) for j in range(count - shift)])  15.4 us
    ppermute x6, starting transfers between devices, head_gather(): lax.ppermute(block, axis, [(j, j + shift) for j in range(count - shift)])  14.3 us
    ppermute x6, starting transfers between devices, head_gather(): lax.ppermute(block, axis, [(j + shift, j) for j in range(count - shift)])  13.7 us
    ppermute x6, waiting for transfers between devices, head_reduce(): lax.ppermute(to_right, axis, [(j, j + shift) for j in range(count - shift)])  12 us
  transfers between devices with their start and end apart: 28, of which 7 were waited for; matrix products, arithmetic and copies ran while one was open for 16% of the time, Pallas kernels for 8%

profile of v6, /device:TPU:10, one launch (start us, length us, event | category | flops | bytes accessed | tf_op | source)
XLA Modules:
  0.0 222.2 jit_solution(9475707261749222811)
XLA Ops:
  1.9 3.5 %collective-permute-start = (bf16[128,1024]{1,0:T(8,128)(2,1)S(1)}, bf16[128,1024]{1,0:T(8,128)(2,1)}, u32[]{:S(2)}, u32[]{:S(2)}) collective-permute-start(bf16[128,1024]{1,0:T(8,128)(2,1)S(1)} %pad_maximum_fusion.4), channel_id=1, source_target_pairs={{0,1},{1,2},{2,3},{4,5},{5,6},{6,7},{8,9},{9,10},{10,11},{12,13},{... | collective-permute-start | bytes 786440 | tf_op jit(solution)/shard_map/ppermute | solution.py:90
  5.4 3.0 %collective-permute-start.1 = (bf16[128,1024]{1,0:T(8,128)(2,1)S(1)}, bf16[128,1024]{1,0:T(8,128)(2,1)}, u32[]{:S(2)}, u32[]{:S(2)}) collective-permute-start(bf16[128,1024]{1,0:T(8,128)(2,1)S(1)} %pad_maximum_fusion.4), channel_id=1, source_target_pairs={{0,2},{1,3},{4,6},{5,7},{8,10},{9,11},{12,14},{13,15},{16,18},{17,... | collective-permute-start | bytes 786440 | tf_op jit(solution)/shard_map/ppermute | solution.py:90
  9.8 5.2 %collective-permute-start.3 = (bf16[128,1024]{1,0:T(8,128)(2,1)S(1)}, bf16[128,1024]{1,0:T(8,128)(2,1)}, u32[]{:S(2)}, u32[]{:S(2)}) collective-permute-start(bf16[128,1024]{1,0:T(8,128)(2,1)S(1)} %pad_maximum_fusion.4), channel_id=1, source_target_pairs={{1,0},{2,1},{3,2},{5,4},{6,5},{7,6},{9,8},{10,9},{11,10},{13,12},{... | collective-permute-start | bytes 786440 | tf_op jit(solution)/shard_map/ppermute | solution.py:91
  16.9 2.5 %fusion.2 = (bf16[128,2048]{1,0:T(8,128)(2,1)}, bf16[128,2048]{1,0:T(8,128)(2,1)}, bf16[128,2048]{1,0:T(8,128)(2,1)}, bf16[128,2048]{1,0:T(8,128)(2,1)}) fusion(bf16[128,4096]{1,0:T(8,128)(2,1)S(1)} %copy-done.8, bf16[128,4096]{1,0:T(8,128)(2,1)} %param.5), kind=kLoop, calls=%fused_computation.59 | loop fusion | bytes 4194304 | tf_op jit(solution)/shard_map/slice | solution.py:168
  19.5 3.8 %collective-permute-done = bf16[128,1024]{1,0:T(8,128)(2,1)} collective-permute-done((bf16[128,1024]{1,0:T(8,128)(2,1)S(1)}, bf16[128,1024]{1,0:T(8,128)(2,1)}, u32[]{:S(2)}, u32[]{:S(2)}) %collective-permute-start) | collective-permute-done | bytes 262176 | tf_op jit(solution)/shard_map/ppermute | solution.py:90
  25.0 2.8 %collective-permute-done.1 = bf16[128,1024]{1,0:T(8,128)(2,1)} collective-permute-done((bf16[128,1024]{1,0:T(8,128)(2,1)S(1)}, bf16[128,1024]{1,0:T(8,128)(2,1)}, u32[]{:S(2)}, u32[]{:S(2)}) %collective-permute-start.1) | collective-permute-done | bytes 262176 | tf_op jit(solution)/shard_map/ppermute | solution.py:90
  29.7 2.5 %collective-permute-done.3 = bf16[128,1024]{1,0:T(8,128)(2,1)} collective-permute-done((bf16[128,1024]{1,0:T(8,128)(2,1)S(1)}, bf16[128,1024]{1,0:T(8,128)(2,1)}, u32[]{:S(2)}, u32[]{:S(2)}) %collective-permute-start.3) | collective-permute-done | bytes 262176 | tf_op jit(solution)/shard_map/ppermute | solution.py:91
  36.6 4.3 %all-to-all-start = ((bf16[8,64,1024]{2,1,0:T(8,128)(2,1)}), bf16[8,64,1024]{2,1,0:T(8,128)(2,1)S(1)}, u32[]{:S(2)}, u32[]{:S(2)}) async-start(bf16[8,64,1024]{2,1,0:T(8,128)(2,1)} %broadcast_in_dim.4), calls=%async_computation | async-start | bytes 2097152 | tf_op jit(solution)/shard_map/all_to_all | solution.py:120
  40.9 4.5 %collective-permute-start.6 = (bf16[128,1024]{1,0:T(8,128)(2,1)S(1)}, bf16[128,1024]{1,0:T(8,128)(2,1)S(1)}, u32[]{:S(2)}, u32[]{:S(2)}) collective-permute-start(bf16[128,1024]{1,0:T(8,128)(2,1)S(1)} %constant_dynamic-update-slice_fusion.2), channel_id=1, source_target_pairs={{0,1},{1,2},{2,3},{4,5},{5,6},{6,7},{8,9},{9,10},{10,11},{12,13},{... | collective-permute-start | bytes 786440 | tf_op jit(solution)/shard_map/ppermute | solution.py:90
  48.8 4.6 %collective-permute-start.9 = (bf16[128,1024]{1,0:T(8,128)(2,1)S(1)}, bf16[128,1024]{1,0:T(8,128)(2,1)S(1)}, u32[]{:S(2)}, u32[]{:S(2)}) collective-permute-start(bf16[128,1024]{1,0:T(8,128)(2,1)S(1)} %constant_dynamic-update-slice_fusion.2), channel_id=1, source_target_pairs={{1,0},{2,1},{3,2},{5,4},{6,5},{7,6},{9,8},{10,9},{11,10},{13,12},{... | collective-permute-start | bytes 786440 | tf_op jit(solution)/shard_map/ppermute | solution.py:91
  56.1 12.0 %collective-permute-done.7 = bf16[128,1024]{1,0:T(8,128)(2,1)S(1)} collective-permute-done((bf16[128,1024]{1,0:T(8,128)(2,1)S(1)}, bf16[128,1024]{1,0:T(8,128)(2,1)S(1)}, u32[]{:S(2)}, u32[]{:S(2)}) %collective-permute-start.7) | collective-permute-done | bytes 262176 | tf_op jit(solution)/shard_map/ppermute | solution.py:90
  70.4 17.4 %shard_map.84 = (bf16[128,2048]{1,0:T(8,128)(2,1)}, bf16[128,2048]{1,0:T(8,128)(2,1)}, f32[1024,512]{1,0:T(8,128)}, f32[1024,512]{1,0:T(8,128)}) custom-call(s32[2]{0:T(128)} %pad_add_fusion.ids_ref, bf16[128,2048]{1,0:T(8,128)(2,1)} %get-tuple-element.55.q_ref, bf16[128,2048]{1,0:T(8,128)(2,1)} %get-tuple-element.40.g_ref, ...), custom_call_target="tpu_custom_call" | custom-call | tf_op jit(solution)/shard_map/pallas_call | solution.py:69
  93.4 4.2 %all-to-all-start.1 = ((bf16[8,64,1024]{2,1,0:T(8,128)(2,1)}), bf16[8,64,1024]{2,1,0:T(8,128)(2,1)S(1)}, u32[]{:S(2)}, u32[]{:S(2)}) async-start(bf16[8,64,1024]{2,1,0:T(8,128)(2,1)} %bitcast.14), calls=%async_computation.1 | async-start | bytes 2097152 | tf_op jit(solution)/shard_map/all_to_all | solution.py:135
  103.4 8.1 %all-to-all-done.1 = bf16[8,64,1024]{2,1,0:T(8,128)(2,1)S(1)} async-done(((bf16[8,64,1024]{2,1,0:T(8,128)(2,1)}), bf16[8,64,1024]{2,1,0:T(8,128)(2,1)S(1)}, u32[]{:S(2)}, u32[]{:S(2)}) %all-to-all-start.1) | async-done | bytes 1048608 | tf_op jit(solution)/shard_map/all_to_all | solution.py:135
  112.8 5.6 %all-to-all-start.2 = ((bf16[8,64,1024]{2,1,0:T(8,128)(2,1)}), bf16[8,64,1024]{2,1,0:T(8,128)(2,1)}, u32[]{:S(2)}, u32[]{:S(2)}) async-start(bf16[8,64,1024]{2,1,0:T(8,128)(2,1)} %broadcast_in_dim.5), calls=%async_computation.2 | async-start | bytes 2097152 | tf_op jit(solution)/shard_map/all_to_all | solution.py:120
  122.3 10.1 %all-to-all-done.2 = bf16[8,64,1024]{2,1,0:T(8,128)(2,1)} async-done(((bf16[8,64,1024]{2,1,0:T(8,128)(2,1)}), bf16[8,64,1024]{2,1,0:T(8,128)(2,1)}, u32[]{:S(2)}, u32[]{:S(2)}) %all-to-all-start.2) | async-done | bytes 1048608 | tf_op jit(solution)/shard_map/all_to_all | solution.py:120
  132.4 2.8 %pad_maximum_fusion.1.k_ref.v_ref = bf16[1024,1024]{1,0:T(8,128)(2,1)} fusion(bf16[512,1024]{1,0:T(8,128)(2,1)} %bitcast.23, bf16[512,1024]{1,0:T(8,128)(2,1)S(1)} %bitcast.45), kind=kLoop, calls=%fused_computation.9 | loop fusion | flops 4194304 | bytes 4194304 | tf_op jit(solution)/shard_map/concatenate | solution.py:130
  135.2 17.3 %shard_map.85 = (bf16[128,2048]{1,0:T(8,128)(2,1)}, bf16[128,2048]{1,0:T(8,128)(2,1)}, f32[1024,512]{1,0:T(8,128)}, f32[1024,512]{1,0:T(8,128)}) custom-call(s32[2]{0:T(128)} %pad_add_fusion.ids_ref, bf16[128,2048]{1,0:T(8,128)(2,1)} %get-tuple-element.54.q_ref, bf16[128,2048]{1,0:T(8,128)(2,1)} %get-tuple-element.41.g_ref, ...), custom_call_target="tpu_custom_call" | custom-call | tf_op jit(solution)/shard_map/pallas_call | solution.py:69
  158.1 5.0 %all-to-all-start.3 = ((bf16[8,64,1024]{2,1,0:T(8,128)(2,1)}), bf16[8,64,1024]{2,1,0:T(8,128)(2,1)S(1)}, u32[]{:S(2)}, u32[]{:S(2)}) async-start(bf16[8,64,1024]{2,1,0:T(8,128)(2,1)} %bitcast.24), calls=%async_computation.3 | async-start | bytes 2097152 | tf_op jit(solution)/shard_map/all_to_all | solution.py:135
  168.4 3.9 %collective-permute-start.13 = (bf16[128,1024]{1,0:T(8,128)(2,1)}, bf16[128,1024]{1,0:T(8,128)(2,1)}, u32[]{:S(2)}, u32[]{:S(2)}) collective-permute-start(bf16[128,1024]{1,0:T(8,128)(2,1)} %get-tuple-element.33), channel_id=1, source_target_pairs={{0,1},{1,2},{2,3},{4,5},{5,6},{6,7},{8,9},{9,10},{10,11},{12,13},{... | collective-permute-start | bytes 786440 | tf_op jit(solution)/shard_map/ppermute | solution.py:110
  173.6 6.9 %collective-permute-start.15 = (bf16[128,1024]{1,0:T(8,128)(2,1)}, bf16[128,1024]{1,0:T(8,128)(2,1)}, u32[]{:S(2)}, u32[]{:S(2)}) collective-permute-start(bf16[128,1024]{1,0:T(8,128)(2,1)} %get-tuple-element.31), channel_id=1, source_target_pairs={{0,2},{1,3},{4,6},{5,7},{8,10},{9,11},{12,14},{13,15},{16,18},{17,... | collective-permute-start | bytes 786440 | tf_op jit(solution)/shard_map/ppermute | solution.py:110
  186.6 8.9 %collective-permute-start.18 = (bf16[128,1024]{1,0:T(8,128)(2,1)S(1)}, bf16[128,1024]{1,0:T(8,128)(2,1)S(1)}, u32[]{:S(2)}, u32[]{:S(2)}) collective-permute-start(bf16[128,1024]{1,0:T(8,128)(2,1)S(1)} %get-tuple-element.34), channel_id=1, source_target_pairs={{1,0},{2,1},{3,2},{5,4},{6,5},{7,6},{9,8},{10,9},{11,10},{13,12},{... | collective-permute-start | bytes 786440 | tf_op jit(solution)/shard_map/ppermute | solution.py:109
  199.9 5.5 %collective-permute-start.21 = (bf16[128,1024]{1,0:T(8,128)(2,1)S(1)}, bf16[128,1024]{1,0:T(8,128)(2,1)S(1)}, u32[]{:S(2)}, u32[]{:S(2)}) collective-permute-start(bf16[128,1024]{1,0:T(8,128)(2,1)S(1)} %get-tuple-element.37), channel_id=1, source_target_pairs={{0,2},{1,3},{4,6},{5,7},{8,10},{9,11},{12,14},{13,15},{16,18},{17,... | collective-permute-start | bytes 786440 | tf_op jit(solution)/shard_map/ppermute | solution.py:110
  208.5 12.0 %collective-permute-done.21 = bf16[128,1024]{1,0:T(8,128)(2,1)S(1)} collective-permute-done((bf16[128,1024]{1,0:T(8,128)(2,1)S(1)}, bf16[128,1024]{1,0:T(8,128)(2,1)S(1)}, u32[]{:S(2)}, u32[]{:S(2)}) %collective-permute-start.21) | collective-permute-done | bytes 262176 | tf_op jit(solution)/shard_map/ppermute | solution.py:110
  (116 shorter events, 64.7 us)
Async XLA Ops:
  1.9 21.4 %collective-permute-start = (bf16[128,1024]{1,0:T(8,128)(2,1)S(1)}, bf16[128,1024]{1,0:T(8,128)(2,1)}, u32[]{:S(2)}, u32[]{:S(2)}) collective-permute-start(bf16[128,1024]{1,0:T(8,128)(2,1)S(1)} %pad_maximum_fusion.4), channel_id=1, source_target_pairs={{0,1},{1,2},{2,3},{4,5},{5,6},{6,7},{8,9},{9,10},{10,11},{12,13},{... | collective-permute-start | bytes 786440 | tf_op jit(solution)/shard_map/ppermute | solution.py:90
  5.4 22.4 %collective-permute-start.1 = (bf16[128,1024]{1,0:T(8,128)(2,1)S(1)}, bf16[128,1024]{1,0:T(8,128)(2,1)}, u32[]{:S(2)}, u32[]{:S(2)}) collective-permute-start(bf16[128,1024]{1,0:T(8,128)(2,1)S(1)} %pad_maximum_fusion.4), channel_id=1, source_target_pairs={{0,2},{1,3},{4,6},{5,7},{8,10},{9,11},{12,14},{13,15},{16,18},{17,... | collective-permute-start | bytes 786440 | tf_op jit(solution)/shard_map/ppermute | solution.py:90
  8.4 20.4 %collective-permute-start.2 = (bf16[128,1024]{1,0:T(8,128)(2,1)S(1)}, bf16[128,1024]{1,0:T(8,128)(2,1)}, u32[]{:S(2)}, u32[]{:S(2)}) collective-permute-start(bf16[128,1024]{1,0:T(8,128)(2,1)S(1)} %pad_maximum_fusion.4), channel_id=1, source_target_pairs={{0,3},{4,7},{8,11},{12,15},{16,19},{20,23},{24,27},{28,31}} | collective-permute-start | bytes 786440 | tf_op jit(solution)/shard_map/ppermute | solution.py:90
  9.8 22.5 %collective-permute-start.3 = (bf16[128,1024]{1,0:T(8,128)(2,1)S(1)}, bf16[128,1024]{1,0:T(8,128)(2,1)}, u32[]{:S(2)}, u32[]{:S(2)}) collective-permute-start(bf16[128,1024]{1,0:T(8,128)(2,1)S(1)} %pad_maximum_fusion.4), channel_id=1, source_target_pairs={{1,0},{2,1},{3,2},{5,4},{6,5},{7,6},{9,8},{10,9},{11,10},{13,12},{... | collective-permute-start | bytes 786440 | tf_op jit(solution)/shard_map/ppermute | solution.py:91
  14.9 18.2 %collective-permute-start.4 = (bf16[128,1024]{1,0:T(8,128)(2,1)S(1)}, bf16[128,1024]{1,0:T(8,128)(2,1)}, u32[]{:S(2)}, u32[]{:S(2)}) collective-permute-start(bf16[128,1024]{1,0:T(8,128)(2,1)S(1)} %pad_maximum_fusion.4), channel_id=1, source_target_pairs={{2,0},{3,1},{6,4},{7,5},{10,8},{11,9},{14,12},{15,13},{18,16},{19,... | collective-permute-start | bytes 786440 | tf_op jit(solution)/shard_map/ppermute | solution.py:91
  36.6 32.2 %all-to-all-start = ((bf16[8,64,1024]{2,1,0:T(8,128)(2,1)}), bf16[8,64,1024]{2,1,0:T(8,128)(2,1)S(1)}, u32[]{:S(2)}, u32[]{:S(2)}) async-start(bf16[8,64,1024]{2,1,0:T(8,128)(2,1)} %broadcast_in_dim.4), calls=%async_computation | async-start | bytes 2097152 | tf_op jit(solution)/shard_map/all_to_all | solution.py:120
  46.1 22.1 %collective-permute-start.7 = (bf16[128,1024]{1,0:T(8,128)(2,1)S(1)}, bf16[128,1024]{1,0:T(8,128)(2,1)S(1)}, u32[]{:S(2)}, u32[]{:S(2)}) collective-permute-start(bf16[128,1024]{1,0:T(8,128)(2,1)S(1)} %constant_dynamic-update-slice_fusion.2), channel_id=1, source_target_pairs={{0,2},{1,3},{4,6},{5,7},{8,10},{9,11},{12,14},{13,15},{16,18},{17,... | collective-permute-start | bytes 786440 | tf_op jit(solution)/shard_map/ppermute | solution.py:90
  48.1 49.5 %collective-permute-start.8 = (bf16[128,1024]{1,0:T(8,128)(2,1)S(1)}, bf16[128,1024]{1,0:T(8,128)(2,1)S(1)}, u32[]{:S(2)}, u32[]{:S(2)}) collective-permute-start(bf16[128,1024]{1,0:T(8,128)(2,1)S(1)} %constant_dynamic-update-slice_fusion.2), channel_id=1, source_target_pairs={{0,3},{4,7},{8,11},{12,15},{16,19},{20,23},{24,27},{28,31}} | collective-permute-start | bytes 786440 | tf_op jit(solution)/shard_map/ppermute | solution.py:90
  48.8 49.5 %collective-permute-start.9 = (bf16[128,1024]{1,0:T(8,128)(2,1)S(1)}, bf16[128,1024]{1,0:T(8,128)(2,1)S(1)}, u32[]{:S(2)}, u32[]{:S(2)}) collective-permute-start(bf16[128,1024]{1,0:T(8,128)(2,1)S(1)} %constant_dynamic-update-slice_fusion.2), channel_id=1, source_target_pairs={{1,0},{2,1},{3,2},{5,4},{6,5},{7,6},{9,8},{10,9},{11,10},{13,12},{... | collective-permute-start | bytes 786440 | tf_op jit(solution)/shard_map/ppermute | solution.py:91
  53.4 45.6 %collective-permute-start.10 = (bf16[128,1024]{1,0:T(8,128)(2,1)S(1)}, bf16[128,1024]{1,0:T(8,128)(2,1)S(1)}, u32[]{:S(2)}, u32[]{:S(2)}) collective-permute-start(bf16[128,1024]{1,0:T(8,128)(2,1)S(1)} %constant_dynamic-update-slice_fusion.2), channel_id=1, source_target_pairs={{2,0},{3,1},{6,4},{7,5},{10,8},{11,9},{14,12},{15,13},{18,16},{19,... | collective-permute-start | bytes 786440 | tf_op jit(solution)/shard_map/ppermute | solution.py:91
  54.7 45.1 %collective-permute-start.11 = (bf16[128,1024]{1,0:T(8,128)(2,1)S(1)}, bf16[128,1024]{1,0:T(8,128)(2,1)S(1)}, u32[]{:S(2)}, u32[]{:S(2)}) collective-permute-start(bf16[128,1024]{1,0:T(8,128)(2,1)S(1)} %constant_dynamic-update-slice_fusion.2), channel_id=1, source_target_pairs={{3,0},{7,4},{11,8},{15,12},{19,16},{23,20},{27,24},{31,28}} | collective-permute-start | bytes 786440 | tf_op jit(solution)/shard_map/ppermute | solution.py:91
  93.4 18.1 %all-to-all-start.1 = ((bf16[8,64,1024]{2,1,0:T(8,128)(2,1)}), bf16[8,64,1024]{2,1,0:T(8,128)(2,1)S(1)}, u32[]{:S(2)}, u32[]{:S(2)}) async-start(bf16[8,64,1024]{2,1,0:T(8,128)(2,1)} %bitcast.14), calls=%async_computation.1 | async-start | bytes 2097152 | tf_op jit(solution)/shard_map/all_to_all | solution.py:135
  112.8 19.6 %all-to-all-start.2 = ((bf16[8,64,1024]{2,1,0:T(8,128)(2,1)}), bf16[8,64,1024]{2,1,0:T(8,128)(2,1)}, u32[]{:S(2)}, u32[]{:S(2)}) async-start(bf16[8,64,1024]{2,1,0:T(8,128)(2,1)} %broadcast_in_dim.5), calls=%async_computation.2 | async-start | bytes 2097152 | tf_op jit(solution)/shard_map/all_to_all | solution.py:120
  158.1 24.8 %all-to-all-start.3 = ((bf16[8,64,1024]{2,1,0:T(8,128)(2,1)}), bf16[8,64,1024]{2,1,0:T(8,128)(2,1)S(1)}, u32[]{:S(2)}, u32[]{:S(2)}) async-start(bf16[8,64,1024]{2,1,0:T(8,128)(2,1)} %bitcast.24), calls=%async_computation.3 | async-start | bytes 2097152 | tf_op jit(solution)/shard_map/all_to_all | solution.py:135
  166.5 18.8 %collective-permute-start.12 = (bf16[128,1024]{1,0:T(8,128)(2,1)}, bf16[128,1024]{1,0:T(8,128)(2,1)}, u32[]{:S(2)}, u32[]{:S(2)}) collective-permute-start(bf16[128,1024]{1,0:T(8,128)(2,1)} %get-tuple-element.28), channel_id=1, source_target_pairs={{1,0},{2,1},{3,2},{5,4},{6,5},{7,6},{9,8},{10,9},{11,10},{13,12},{... | collective-permute-start | bytes 786440 | tf_op jit(solution)/shard_map/ppermute | solution.py:109
  168.4 18.2 %collective-permute-start.13 = (bf16[128,1024]{1,0:T(8,128)(2,1)}, bf16[128,1024]{1,0:T(8,128)(2,1)}, u32[]{:S(2)}, u32[]{:S(2)}) collective-permute-start(bf16[128,1024]{1,0:T(8,128)(2,1)} %get-tuple-element.33), channel_id=1, source_target_pairs={{0,1},{1,2},{2,3},{4,5},{5,6},{6,7},{8,9},{9,10},{10,11},{12,13},{... | collective-permute-start | bytes 786440 | tf_op jit(solution)/shard_map/ppermute | solution.py:110
  172.3 24.3 %collective-permute-start.14 = (bf16[128,1024]{1,0:T(8,128)(2,1)}, bf16[128,1024]{1,0:T(8,128)(2,1)}, u32[]{:S(2)}, u32[]{:S(2)}) collective-permute-start(bf16[128,1024]{1,0:T(8,128)(2,1)} %get-tuple-element.32), channel_id=1, source_target_pairs={{2,0},{3,1},{6,4},{7,5},{10,8},{11,9},{14,12},{15,13},{18,16},{19,... | collective-permute-start | bytes 786440 | tf_op jit(solution)/shard_map/ppermute | solution.py:109
  173.6 24.9 %collective-permute-start.15 = (bf16[128,1024]{1,0:T(8,128)(2,1)}, bf16[128,1024]{1,0:T(8,128)(2,1)}, u32[]{:S(2)}, u32[]{:S(2)}) collective-permute-start(bf16[128,1024]{1,0:T(8,128)(2,1)} %get-tuple-element.31), channel_id=1, source_target_pairs={{0,2},{1,3},{4,6},{5,7},{8,10},{9,11},{12,14},{13,15},{16,18},{17,... | collective-permute-start | bytes 786440 | tf_op jit(solution)/shard_map/ppermute | solution.py:110
  180.5 19.3 %collective-permute-start.16 = (bf16[128,1024]{1,0:T(8,128)(2,1)}, bf16[128,1024]{1,0:T(8,128)(2,1)}, u32[]{:S(2)}, u32[]{:S(2)}) collective-permute-start(bf16[128,1024]{1,0:T(8,128)(2,1)} %get-tuple-element.30), channel_id=1, source_target_pairs={{3,0},{7,4},{11,8},{15,12},{19,16},{23,20},{27,24},{31,28}} | collective-permute-start | bytes 786440 | tf_op jit(solution)/shard_map/ppermute | solution.py:109
  185.9 19.4 %collective-permute-start.17 = (bf16[128,1024]{1,0:T(8,128)(2,1)S(1)}, bf16[128,1024]{1,0:T(8,128)(2,1)S(1)}, u32[]{:S(2)}, u32[]{:S(2)}) collective-permute-start(bf16[128,1024]{1,0:T(8,128)(2,1)S(1)} %copy-done.13), channel_id=1, source_target_pairs={{0,3},{4,7},{8,11},{12,15},{16,19},{20,23},{24,27},{28,31}} | collective-permute-start | bytes 786440 | tf_op jit(solution)/shard_map/ppermute | solution.py:110
  186.6 19.4 %collective-permute-start.18 = (bf16[128,1024]{1,0:T(8,128)(2,1)S(1)}, bf16[128,1024]{1,0:T(8,128)(2,1)S(1)}, u32[]{:S(2)}, u32[]{:S(2)}) collective-permute-start(bf16[128,1024]{1,0:T(8,128)(2,1)S(1)} %get-tuple-element.34), channel_id=1, source_target_pairs={{1,0},{2,1},{3,2},{5,4},{6,5},{7,6},{9,8},{10,9},{11,10},{13,12},{... | collective-permute-start | bytes 786440 | tf_op jit(solution)/shard_map/ppermute | solution.py:109
  199.9 20.6 %collective-permute-start.21 = (bf16[128,1024]{1,0:T(8,128)(2,1)S(1)}, bf16[128,1024]{1,0:T(8,128)(2,1)S(1)}, u32[]{:S(2)}, u32[]{:S(2)}) collective-permute-start(bf16[128,1024]{1,0:T(8,128)(2,1)S(1)} %get-tuple-element.37), channel_id=1, source_target_pairs={{0,2},{1,3},{4,6},{5,7},{8,10},{9,11},{12,14},{13,15},{16,18},{17,... | collective-permute-start | bytes 786440 | tf_op jit(solution)/shard_map/ppermute | solution.py:110
  205.3 15.1 %collective-permute-start.22 = (bf16[128,1024]{1,0:T(8,128)(2,1)S(1)}, bf16[128,1024]{1,0:T(8,128)(2,1)S(1)}, u32[]{:S(2)}, u32[]{:S(2)}) collective-permute-start(bf16[128,1024]{1,0:T(8,128)(2,1)S(1)} %get-tuple-element.36), channel_id=1, source_target_pairs={{3,0},{7,4},{11,8},{15,12},{19,16},{23,20},{27,24},{31,28}} | collective-permute-start | bytes 786440 | tf_op jit(solution)/shard_map/ppermute | solution.py:109
  206.0 14.4 %collective-permute-start.23 = (bf16[128,1024]{1,0:T(8,128)(2,1)S(1)}, bf16[128,1024]{1,0:T(8,128)(2,1)S(1)}, u32[]{:S(2)}, u32[]{:S(2)}) collective-permute-start(bf16[128,1024]{1,0:T(8,128)(2,1)S(1)} %get-tuple-element.35), channel_id=1, source_target_pairs={{0,3},{4,7},{8,11},{12,15},{16,19},{20,23},{24,27},{28,31}} | collective-permute-start | bytes 786440 | tf_op jit(solution)/shard_map/ppermute | solution.py:110
  (18 other events, 144.6 us)

commit v7 on v4

--- a/solution.py
+++ b/solution.py
@@ -100,20 +100,11 @@
 
 
 def head_reduce(partials, axis, count):
-    index = lax.axis_index(axis)
     rows = partials.shape[0] // count
-
-    def block_of(target):
-        return lax.dynamic_slice_in_dim(partials, jnp.clip(target, 0, count - 1) * rows, rows, 0)
-
-    left = jnp.zeros((rows, partials.shape[1]), jnp.bfloat16)
-    right = jnp.zeros((rows, partials.shape[1]), jnp.bfloat16)
-    for step in range(1, count):
-        send_left = (block_of(index + step - count) + left.astype(jnp.float32)).astype(jnp.bfloat16)
-        send_right = (block_of(index - step + count) + right.astype(jnp.float32)).astype(jnp.bfloat16)
-        left = lax.ppermute(send_left, axis, [(j, j - 1) for j in range(max(1, count - step), count)])
-        right = lax.ppermute(send_right, axis, [(j, j + 1) for j in range(0, min(step, count - 1))])
-    return block_of(index) + left.astype(jnp.float32) + right.astype(jnp.float32)
+    received = lax.all_to_all(
+        partials.astype(jnp.bfloat16).reshape(count, rows, partials.shape[1]), axis, 0, 0, tiled=True
+    )
+    return jnp.sum(received.astype(jnp.float32), axis=0)
 
 
 def local_part(queries, keys, values, out_grad, positions, ids, heads_axis, ctx_axis):

time: 199 us -> 209 us (1.050); the launches traced: 197 us -> 205 us
  waiting for transfers between devices: 25.2 us -> 53.1 us
  starting transfers between devices: 74.3 us -> 61.2 us
  other arithmetic: 21.8 us -> 18.4 us
  local copies, waits for them, and re-layouts: 39.6 us -> 36.4 us
    all_to_all x0 -> x2, waiting for transfers between devices: none -> 35.4 us  [head_reduce(): lax.all_to_all(partials.astype(jnp.bfloat16).reshape(count, rows, partial...]
    ppermute x12 -> x0, starting transfers between devices: 24.3 us -> none  [the longest x6 13.2 us: head_reduce(): lax.ppermute(send_left, axis, [(j, j - 1) for j in range(max(1, count - s...]
    ppermute x12 -> x0, waiting for transfers between devices: 13.8 us -> none  [the longest x6 10.3 us: head_reduce(): lax.ppermute(send_right, axis, [(j, j + 1) for j in range(0, min(step, co...]
    all_to_all x0 -> x2, starting transfers between devices: none -> 11.1 us  [head_reduce(): lax.all_to_all(partials.astype(jnp.bfloat16).reshape(count, rows, partial...]
    all_to_all x2, waiting for transfers between devices: 2.85 us -> 9.08 us  [local_part(): lax.all_to_all(kv_grads[window:].astype(jnp.bfloat16).reshape(ctx_axis, p...]
    convert_element_type x2 -> x0, local copies, waits for them, and re-layouts: 2.85 us -> none  [head_reduce(): (block_of(index + step - count) + left.astype(jnp.float32)).astype(jnp.bf...]
    convert_element_type x8 -> x2, other arithmetic: 4.89 us -> 2.29 us  [head_reduce(): partials.astype(jnp.bfloat16).reshape(count, rows, partials.shape[1])]
    scatter-add x2, other arithmetic: 6.03 us -> 3.76 us  [local_part(): window_grads = kv_grads[:window].at[positions].add(own_beacons)]
  transfers between devices with their start and end apart: 28 -> 18, of which waited for: 8 -> 5; matrix products, arithmetic and copies ran while one was open for 27% -> 22% of each run, Pallas kernels for 18% -> 17%
where the time goes in v7:
time: 209 us; the launch traced here: 205 us
  starting transfers between devices  61.2 us (29%)
  waiting for transfers between devices  53.1 us (25%)
  local copies, waits for them, and re-layouts  36.4 us (17%)
  Pallas kernels  34.7 us (17%)
  other arithmetic  18.4 us (9%)
    all_to_all x2, waiting for transfers between devices, head_reduce(): lax.all_to_all(partials.astype(jnp.bfloat16).reshape(count, rows, partial...  35.4 us
    pallas_call x2, Pallas kernels, attend_all(): pl.pallas_call(kernel, grid_spec=pltpu.PrefetchScalarGridSpec(num_scalar_...  34.7 us
    ppermute x6, starting transfers between devices, head_gather(): lax.ppermute(from_left[-1], axis, [(j, j + 1) for j in range(step - 1, co...  16.4 us
    ppermute x6, starting transfers between devices, head_gather(): lax.ppermute(from_right[-1], axis, [(j + 1, j) for j in range(count - ste...  15.3 us
    unnamed x30, local copies, waits for them, and re-layouts  15.2 us
    all_to_all x2, starting transfers between devices, head_reduce(): lax.all_to_all(partials.astype(jnp.bfloat16).reshape(count, rows, partial...  11.1 us
    all_to_all x2, starting transfers between devices, local_part(): lax.all_to_all(jnp.broadcast_to(own_beacon_rows[None], (ctx_axis,) + own_...  9.89 us
    all_to_all x2, waiting for transfers between devices, local_part(): lax.all_to_all(kv_grads[window:].astype(jnp.bfloat16).reshape(ctx_axis, p...  9.08 us
  transfers between devices with their start and end apart: 18, of which 5 were waited for; matrix products, arithmetic and copies ran while one was open for 22% of the time, Pallas kernels for 17%

profile of v7, /device:TPU:10, one launch (start us, length us, event | category | flops | bytes accessed | tf_op | source)
XLA Modules:
  0.0 204.8 jit_solution(15950944359584828610)
XLA Ops:
  2.7 3.5 %collective-permute-start = (bf16[128,1024]{1,0:T(8,128)(2,1)S(1)}, bf16[128,1024]{1,0:T(8,128)(2,1)S(1)}, u32[]{:S(2)}, u32[]{:S(2)}) collective-permute-start(bf16[128,1024]{1,0:T(8,128)(2,1)S(1)} %pad_maximum_fusion.4), channel_id=1, source_target_pairs={{0,1},{1,2},{2,3},{4,5},{5,6},{6,7},{8,9},{9,10},{10,11},{12,13},{... | collective-permute-start | bytes 786440 | tf_op jit(solution)/shard_map/ppermute | solution.py:91
  6.1 2.4 %collective-permute-start.3 = (bf16[128,1024]{1,0:T(8,128)(2,1)S(1)}, bf16[128,1024]{1,0:T(8,128)(2,1)S(1)}, u32[]{:S(2)}, u32[]{:S(2)}) collective-permute-start(bf16[128,1024]{1,0:T(8,128)(2,1)S(1)} %pad_maximum_fusion.4), channel_id=1, source_target_pairs={{1,0},{2,1},{3,2},{5,4},{6,5},{7,6},{9,8},{10,9},{11,10},{13,12},{... | collective-permute-start | bytes 786440 | tf_op jit(solution)/shard_map/ppermute | solution.py:94
  8.6 3.5 %collective-permute-start.6 = (bf16[128,1024]{1,0:T(8,128)(2,1)S(1)}, bf16[128,1024]{1,0:T(8,128)(2,1)S(1)}, u32[]{:S(2)}, u32[]{:S(2)}) collective-permute-start(bf16[128,1024]{1,0:T(8,128)(2,1)S(1)} %pad_maximum_fusion.5), channel_id=1, source_target_pairs={{0,1},{1,2},{2,3},{4,5},{5,6},{6,7},{8,9},{9,10},{10,11},{12,13},{... | collective-permute-start | bytes 786440 | tf_op jit(solution)/shard_map/ppermute | solution.py:91
  12.0 2.4 %collective-permute-start.9 = (bf16[128,1024]{1,0:T(8,128)(2,1)S(1)}, bf16[128,1024]{1,0:T(8,128)(2,1)S(1)}, u32[]{:S(2)}, u32[]{:S(2)}) collective-permute-start(bf16[128,1024]{1,0:T(8,128)(2,1)S(1)} %pad_maximum_fusion.5), channel_id=1, source_target_pairs={{1,0},{2,1},{3,2},{5,4},{6,5},{7,6},{9,8},{10,9},{11,10},{13,12},{... | collective-permute-start | bytes 786440 | tf_op jit(solution)/shard_map/ppermute | solution.py:94
  15.9 3.5 %collective-permute-start.1 = (bf16[128,1024]{1,0:T(8,128)(2,1)S(1)}, bf16[128,1024]{1,0:T(8,128)(2,1)S(1)}, u32[]{:S(2)}, u32[]{:S(2)}) collective-permute-start(bf16[128,1024]{1,0:T(8,128)(2,1)S(1)} %collective-permute-done), channel_id=1, source_target_pairs={{1,2},{2,3},{5,6},{6,7},{9,10},{10,11},{13,14},{14,15},{17,18},{18... | collective-permute-start | bytes 786440 | tf_op jit(solution)/shard_map/ppermute | solution.py:91
  22.0 3.9 %collective-permute-start.7 = (bf16[128,1024]{1,0:T(8,128)(2,1)S(1)}, bf16[128,1024]{1,0:T(8,128)(2,1)S(1)}, u32[]{:S(2)}, u32[]{:S(2)}) collective-permute-start(bf16[128,1024]{1,0:T(8,128)(2,1)S(1)} %collective-permute-done.6), channel_id=1, source_target_pairs={{1,2},{2,3},{5,6},{6,7},{9,10},{10,11},{13,14},{14,15},{17,18},{18... | collective-permute-start | bytes 786440 | tf_op jit(solution)/shard_map/ppermute | solution.py:91
  32.4 2.2 %collective-permute-done.10 = bf16[128,1024]{1,0:T(8,128)(2,1)S(1)} collective-permute-done((bf16[128,1024]{1,0:T(8,128)(2,1)S(1)}, bf16[128,1024]{1,0:T(8,128)(2,1)S(1)}, u32[]{:S(2)}, u32[]{:S(2)}) %collective-permute-start.10) | collective-permute-done | bytes 262176 | tf_op jit(solution)/shard_map/ppermute | solution.py:94
  34.6 5.1 %collective-permute-start.11 = (bf16[128,1024]{1,0:T(8,128)(2,1)S(1)}, bf16[128,1024]{1,0:T(8,128)(2,1)}, u32[]{:S(2)}, u32[]{:S(2)}) collective-permute-start(bf16[128,1024]{1,0:T(8,128)(2,1)S(1)} %collective-permute-done.10), channel_id=1, source_target_pairs={{1,0},{5,4},{9,8},{13,12},{17,16},{21,20},{25,24},{29,28}} | collective-permute-start | bytes 786440 | tf_op jit(solution)/shard_map/ppermute | solution.py:94
  42.7 2.1 %gather_fusion = bf16[4,128,1024]{2,1,0:T(8,128)(2,1)S(1)} fusion(bf16[7,128,1024]{2,1,0:T(8,128)(2,1)} %bitcast_dynamic-update-slice_fusion.7, s32[1024]{0:T(1024)S(1)} %pad_clamp_fusion.1), kind=kCustom, calls=%fused_computation | custom fusion | bytes 2097168 | tf_op jit(solution)/shard_map/gather | solution.py:99
  46.6 4.3 %all-to-all-start = ((bf16[8,64,1024]{2,1,0:T(8,128)(2,1)}), bf16[8,64,1024]{2,1,0:T(8,128)(2,1)S(1)}, u32[]{:S(2)}, u32[]{:S(2)}) async-start(bf16[8,64,1024]{2,1,0:T(8,128)(2,1)} %broadcast_in_dim.4), calls=%async_computation | async-start | bytes 2097152 | tf_op jit(solution)/shard_map/all_to_all | solution.py:117
  58.5 6.3 %all-to-all-done = bf16[8,64,1024]{2,1,0:T(8,128)(2,1)S(1)} async-done(((bf16[8,64,1024]{2,1,0:T(8,128)(2,1)}), bf16[8,64,1024]{2,1,0:T(8,128)(2,1)S(1)}, u32[]{:S(2)}, u32[]{:S(2)}) %all-to-all-start) | async-done | bytes 1048608 | tf_op jit(solution)/shard_map/all_to_all | solution.py:117
  65.9 5.6 %all-to-all-start.1 = ((bf16[8,64,1024]{2,1,0:T(8,128)(2,1)}), bf16[8,64,1024]{2,1,0:T(8,128)(2,1)}, u32[]{:S(2)}, u32[]{:S(2)}) async-start(bf16[8,64,1024]{2,1,0:T(8,128)(2,1)} %broadcast_in_dim.5), calls=%async_computation.1 | async-start | bytes 2097152 | tf_op jit(solution)/shard_map/all_to_all | solution.py:117
  71.5 2.9 %fusion.2 = (bf16[128,2048]{1,0:T(8,128)(2,1)}, bf16[128,2048]{1,0:T(8,128)(2,1)}, bf16[128,2048]{1,0:T(8,128)(2,1)}, bf16[128,2048]{1,0:T(8,128)(2,1)}) fusion(bf16[128,4096]{1,0:T(8,128)(2,1)} %param.8, bf16[128,4096]{1,0:T(8,128)(2,1)} %param.5), kind=kLoop, calls=%fused_computation.44 | loop fusion | bytes 4194304 | tf_op jit(solution)/shard_map/slice | solution.py:149
  75.9 17.4 %shard_map.84 = (bf16[128,2048]{1,0:T(8,128)(2,1)}, bf16[128,2048]{1,0:T(8,128)(2,1)}, f32[1024,512]{1,0:T(8,128)}, f32[1024,512]{1,0:T(8,128)}) custom-call(s32[2]{0:T(128)} %pad_add_fusion.ids_ref, bf16[128,2048]{1,0:T(8,128)(2,1)} %get-tuple-element.35.q_ref, bf16[128,2048]{1,0:T(8,128)(2,1)} %get-tuple-element.20.g_ref, ...), custom_call_target="tpu_custom_call" | custom-call | tf_op jit(solution)/shard_map/pallas_call | solution.py:69
  98.8 4.2 %all-to-all-start.2 = ((bf16[8,64,1024]{2,1,0:T(8,128)(2,1)}), bf16[8,64,1024]{2,1,0:T(8,128)(2,1)S(1)}, u32[]{:S(2)}, u32[]{:S(2)}) async-start(bf16[8,64,1024]{2,1,0:T(8,128)(2,1)} %bitcast.23), calls=%async_computation.2 | async-start | bytes 2097152 | tf_op jit(solution)/shard_map/all_to_all | solution.py:126
  103.0 2.7 %pad_maximum_fusion.1.k_ref.v_ref = bf16[1024,1024]{1,0:T(8,128)(2,1)} fusion(bf16[512,1024]{1,0:T(8,128)(2,1)} %bitcast.22, bf16[512,1024]{1,0:T(8,128)(2,1)S(1)} %bitcast.47), kind=kLoop, calls=%fused_computation.9 | loop fusion | flops 4194304 | bytes 4194304 | tf_op jit(solution)/shard_map/concatenate | solution.py:121
  105.7 17.4 %shard_map.85 = (bf16[128,2048]{1,0:T(8,128)(2,1)}, bf16[128,2048]{1,0:T(8,128)(2,1)}, f32[1024,512]{1,0:T(8,128)}, f32[1024,512]{1,0:T(8,128)}) custom-call(s32[2]{0:T(128)} %pad_add_fusion.ids_ref, bf16[128,2048]{1,0:T(8,128)(2,1)} %get-tuple-element.34.q_ref, bf16[128,2048]{1,0:T(8,128)(2,1)} %get-tuple-element.21.g_ref, ...), custom_call_target="tpu_custom_call" | custom-call | tf_op jit(solution)/shard_map/pallas_call | solution.py:69
  128.7 4.2 %all-to-all-start.4 = ((bf16[8,64,1024]{2,1,0:T(8,128)(2,1)}), bf16[8,64,1024]{2,1,0:T(8,128)(2,1)}, u32[]{:S(2)}, u32[]{:S(2)}) async-start(bf16[8,64,1024]{2,1,0:T(8,128)(2,1)} %bitcast.25), calls=%async_computation.4 | async-start | bytes 2097152 | tf_op jit(solution)/shard_map/all_to_all | solution.py:126
  137.8 9.1 %all-to-all-done.4 = bf16[8,64,1024]{2,1,0:T(8,128)(2,1)} async-done(((bf16[8,64,1024]{2,1,0:T(8,128)(2,1)}), bf16[8,64,1024]{2,1,0:T(8,128)(2,1)}, u32[]{:S(2)}, u32[]{:S(2)}) %all-to-all-start.4) | async-done | bytes 1048608 | tf_op jit(solution)/shard_map/all_to_all | solution.py:126
  146.9 4.2 %all-to-all-start.3 = ((bf16[4,128,1024]{2,1,0:T(8,128)(2,1)}), bf16[4,128,1024]{2,1,0:T(8,128)(2,1)S(1)}, u32[]{:S(2)}, u32[]{:S(2)}) async-start(bf16[4,128,1024]{2,1,0:T(8,128)(2,1)} %bitcast.24), calls=%async_computation.3 | async-start | bytes 2097152 | tf_op jit(solution)/shard_map/all_to_all | solution.py:104
  157.4 16.8 %all-to-all-done.3 = bf16[4,128,1024]{2,1,0:T(8,128)(2,1)S(1)} async-done(((bf16[4,128,1024]{2,1,0:T(8,128)(2,1)}), bf16[4,128,1024]{2,1,0:T(8,128)(2,1)S(1)}, u32[]{:S(2)}, u32[]{:S(2)}) %all-to-all-start.3) | async-done | bytes 1048608 | tf_op jit(solution)/shard_map/all_to_all | solution.py:104
  174.1 6.9 %all-to-all-start.5 = ((bf16[4,128,1024]{2,1,0:T(8,128)(2,1)}), bf16[4,128,1024]{2,1,0:T(8,128)(2,1)S(1)}, u32[]{:S(2)}, u32[]{:S(2)}) async-start(bf16[4,128,1024]{2,1,0:T(8,128)(2,1)} %bitcast.26), calls=%async_computation.5 | async-start | bytes 2097152 | tf_op jit(solution)/shard_map/all_to_all | solution.py:104
  181.0 2.1 %pad_maximum_fusion.3 = bf16[128,4096]{1,0:T(8,128)(2,1)} fusion(bf16[128,2048]{1,0:T(8,128)(2,1)} %get-tuple-element.15, bf16[128,2048]{1,0:T(8,128)(2,1)S(1)} %copy-done.6), kind=kLoop, calls=%fused_computation.13 | loop fusion | flops 2097152 | bytes 2097152 | tf_op jit(solution)/shard_map/concatenate | solution.py:153
  184.5 18.7 %all-to-all-done.5 = bf16[4,128,1024]{2,1,0:T(8,128)(2,1)S(1)} async-done(((bf16[4,128,1024]{2,1,0:T(8,128)(2,1)}), bf16[4,128,1024]{2,1,0:T(8,128)(2,1)S(1)}, u32[]{:S(2)}, u32[]{:S(2)}) %all-to-all-start.5) | async-done | bytes 1048608 | tf_op jit(solution)/shard_map/all_to_all | solution.py:104
  (85 shorter events, 52.5 us)
Async XLA Ops:
  0.6 13.8 %copy-start.8 = (s32[1,64]{1,0:T(1,128)S(1)}, s32[1,64]{1,0:T(1,128)}, u32[]{:S(2)}) copy-start(s32[1,64]{1,0:T(1,128)} %param.9) | copy-start | bytes 772
  2.7 13.2 %collective-permute-start = (bf16[128,1024]{1,0:T(8,128)(2,1)S(1)}, bf16[128,1024]{1,0:T(8,128)(2,1)S(1)}, u32[]{:S(2)}, u32[]{:S(2)}) collective-permute-start(bf16[128,1024]{1,0:T(8,128)(2,1)S(1)} %pad_maximum_fusion.4), channel_id=1, source_target_pairs={{0,1},{1,2},{2,3},{4,5},{5,6},{6,7},{8,9},{9,10},{10,11},{12,13},{... | collective-permute-start | bytes 786440 | tf_op jit(solution)/shard_map/ppermute | solution.py:91
  6.1 13.9 %collective-permute-start.3 = (bf16[128,1024]{1,0:T(8,128)(2,1)S(1)}, bf16[128,1024]{1,0:T(8,128)(2,1)S(1)}, u32[]{:S(2)}, u32[]{:S(2)}) collective-permute-start(bf16[128,1024]{1,0:T(8,128)(2,1)S(1)} %pad_maximum_fusion.4), channel_id=1, source_target_pairs={{1,0},{2,1},{3,2},{5,4},{6,5},{7,6},{9,8},{10,9},{11,10},{13,12},{... | collective-permute-start | bytes 786440 | tf_op jit(solution)/shard_map/ppermute | solution.py:94
  8.6 13.4 %collective-permute-start.6 = (bf16[128,1024]{1,0:T(8,128)(2,1)S(1)}, bf16[128,1024]{1,0:T(8,128)(2,1)S(1)}, u32[]{:S(2)}, u32[]{:S(2)}) collective-permute-start(bf16[128,1024]{1,0:T(8,128)(2,1)S(1)} %pad_maximum_fusion.5), channel_id=1, source_target_pairs={{0,1},{1,2},{2,3},{4,5},{5,6},{6,7},{8,9},{9,10},{10,11},{12,13},{... | collective-permute-start | bytes 786440 | tf_op jit(solution)/shard_map/ppermute | solution.py:91
  12.0 13.9 %collective-permute-start.9 = (bf16[128,1024]{1,0:T(8,128)(2,1)S(1)}, bf16[128,1024]{1,0:T(8,128)(2,1)S(1)}, u32[]{:S(2)}, u32[]{:S(2)}) collective-permute-start(bf16[128,1024]{1,0:T(8,128)(2,1)S(1)} %pad_maximum_fusion.5), channel_id=1, source_target_pairs={{1,0},{2,1},{3,2},{5,4},{6,5},{7,6},{9,8},{10,9},{11,10},{13,12},{... | collective-permute-start | bytes 786440 | tf_op jit(solution)/shard_map/ppermute | solution.py:94
  15.9 12.0 %collective-permute-start.1 = (bf16[128,1024]{1,0:T(8,128)(2,1)S(1)}, bf16[128,1024]{1,0:T(8,128)(2,1)S(1)}, u32[]{:S(2)}, u32[]{:S(2)}) collective-permute-start(bf16[128,1024]{1,0:T(8,128)(2,1)S(1)} %collective-permute-done), channel_id=1, source_target_pairs={{1,2},{2,3},{5,6},{6,7},{9,10},{10,11},{13,14},{14,15},{17,18},{18... | collective-permute-start | bytes 786440 | tf_op jit(solution)/shard_map/ppermute | solution.py:91
  20.1 9.3 %collective-permute-start.4 = (bf16[128,1024]{1,0:T(8,128)(2,1)S(1)}, bf16[128,1024]{1,0:T(8,128)(2,1)S(1)}, u32[]{:S(2)}, u32[]{:S(2)}) collective-permute-start(bf16[128,1024]{1,0:T(8,128)(2,1)S(1)} %collective-permute-done.3), channel_id=1, source_target_pairs={{1,0},{2,1},{5,4},{6,5},{9,8},{10,9},{13,12},{14,13},{17,16},{18,1... | collective-permute-start | bytes 786440 | tf_op jit(solution)/shard_map/ppermute | solution.py:94
  22.0 9.0 %collective-permute-start.7 = (bf16[128,1024]{1,0:T(8,128)(2,1)S(1)}, bf16[128,1024]{1,0:T(8,128)(2,1)S(1)}, u32[]{:S(2)}, u32[]{:S(2)}) collective-permute-start(bf16[128,1024]{1,0:T(8,128)(2,1)S(1)} %collective-permute-done.6), channel_id=1, source_target_pairs={{1,2},{2,3},{5,6},{6,7},{9,10},{10,11},{13,14},{14,15},{17,18},{18... | collective-permute-start | bytes 786440 | tf_op jit(solution)/shard_map/ppermute | solution.py:91
  26.0 8.7 %collective-permute-start.10 = (bf16[128,1024]{1,0:T(8,128)(2,1)S(1)}, bf16[128,1024]{1,0:T(8,128)(2,1)S(1)}, u32[]{:S(2)}, u32[]{:S(2)}) collective-permute-start(bf16[128,1024]{1,0:T(8,128)(2,1)S(1)} %collective-permute-done.9), channel_id=1, source_target_pairs={{1,0},{2,1},{5,4},{6,5},{9,8},{10,9},{13,12},{14,13},{17,16},{18,1... | collective-permute-start | bytes 786440 | tf_op jit(solution)/shard_map/ppermute | solution.py:94
  27.9 11.8 %collective-permute-start.2 = (bf16[128,1024]{1,0:T(8,128)(2,1)S(1)}, bf16[128,1024]{1,0:T(8,128)(2,1)S(1)}, u32[]{:S(2)}, u32[]{:S(2)}) collective-permute-start(bf16[128,1024]{1,0:T(8,128)(2,1)S(1)} %collective-permute-done.1), channel_id=1, source_target_pairs={{2,3},{6,7},{10,11},{14,15},{18,19},{22,23},{26,27},{30,31}} | collective-permute-start | bytes 786440 | tf_op jit(solution)/shard_map/ppermute | solution.py:91
  29.3 12.6 %collective-permute-start.5 = (bf16[128,1024]{1,0:T(8,128)(2,1)S(1)}, bf16[128,1024]{1,0:T(8,128)(2,1)S(1)}, u32[]{:S(2)}, u32[]{:S(2)}) collective-permute-start(bf16[128,1024]{1,0:T(8,128)(2,1)S(1)} %collective-permute-done.4), channel_id=1, source_target_pairs={{1,0},{5,4},{9,8},{13,12},{17,16},{21,20},{25,24},{29,28}} | collective-permute-start | bytes 786440 | tf_op jit(solution)/shard_map/ppermute | solution.py:94
  31.0 19.8 %collective-permute-start.8 = (bf16[128,1024]{1,0:T(8,128)(2,1)S(1)}, bf16[128,1024]{1,0:T(8,128)(2,1)}, u32[]{:S(2)}, u32[]{:S(2)}) collective-permute-start(bf16[128,1024]{1,0:T(8,128)(2,1)S(1)} %collective-permute-done.7), channel_id=1, source_target_pairs={{2,3},{6,7},{10,11},{14,15},{18,19},{22,23},{26,27},{30,31}} | collective-permute-start | bytes 786440 | tf_op jit(solution)/shard_map/ppermute | solution.py:91
  34.6 19.3 %collective-permute-start.11 = (bf16[128,1024]{1,0:T(8,128)(2,1)S(1)}, bf16[128,1024]{1,0:T(8,128)(2,1)}, u32[]{:S(2)}, u32[]{:S(2)}) collective-permute-start(bf16[128,1024]{1,0:T(8,128)(2,1)S(1)} %collective-permute-done.10), channel_id=1, source_target_pairs={{1,0},{5,4},{9,8},{13,12},{17,16},{21,20},{25,24},{29,28}} | collective-permute-start | bytes 786440 | tf_op jit(solution)/shard_map/ppermute | solution.py:94
  39.7 2.3 %copy-start.4 = (bf16[7,128,1024]{2,1,0:T(8,128)(2,1)}, bf16[7,128,1024]{2,1,0:T(8,128)(2,1)S(1)}, u32[]{:S(2)}) copy-start(bf16[7,128,1024]{2,1,0:T(8,128)(2,1)S(1)} %bitcast_dynamic-update-slice_fusion.4) | copy-start | bytes 5505028
  46.6 18.2 %all-to-all-start = ((bf16[8,64,1024]{2,1,0:T(8,128)(2,1)}), bf16[8,64,1024]{2,1,0:T(8,128)(2,1)S(1)}, u32[]{:S(2)}, u32[]{:S(2)}) async-start(bf16[8,64,1024]{2,1,0:T(8,128)(2,1)} %broadcast_in_dim.4), calls=%async_computation | async-start | bytes 2097152 | tf_op jit(solution)/shard_map/all_to_all | solution.py:117
  65.9 32.9 %all-to-all-start.1 = ((bf16[8,64,1024]{2,1,0:T(8,128)(2,1)}), bf16[8,64,1024]{2,1,0:T(8,128)(2,1)}, u32[]{:S(2)}, u32[]{:S(2)}) async-start(bf16[8,64,1024]{2,1,0:T(8,128)(2,1)} %broadcast_in_dim.5), calls=%async_computation.1 | async-start | bytes 2097152 | tf_op jit(solution)/shard_map/all_to_all | solution.py:117
  93.2 2.2 %copy-start.3 = (f32[1024,512]{1,0:T(8,128)S(1)}, f32[1024,512]{1,0:T(8,128)}, u32[]{:S(2)}) copy-start(f32[1024,512]{1,0:T(8,128)} %get-tuple-element.17) | copy-start | bytes 6291460
  98.8 29.9 %all-to-all-start.2 = ((bf16[8,64,1024]{2,1,0:T(8,128)(2,1)}), bf16[8,64,1024]{2,1,0:T(8,128)(2,1)S(1)}, u32[]{:S(2)}, u32[]{:S(2)}) async-start(bf16[8,64,1024]{2,1,0:T(8,128)(2,1)} %bitcast.23), calls=%async_computation.2 | async-start | bytes 2097152 | tf_op jit(solution)/shard_map/all_to_all | solution.py:126
  123.1 2.2 %copy-start.2 = (f32[1024,512]{1,0:T(8,128)S(1)}, f32[1024,512]{1,0:T(8,128)}, u32[]{:S(2)}) copy-start(f32[1024,512]{1,0:T(8,128)} %get-tuple-element.19) | copy-start | bytes 6291460
  128.7 18.2 %all-to-all-start.4 = ((bf16[8,64,1024]{2,1,0:T(8,128)(2,1)}), bf16[8,64,1024]{2,1,0:T(8,128)(2,1)}, u32[]{:S(2)}, u32[]{:S(2)}) async-start(bf16[8,64,1024]{2,1,0:T(8,128)(2,1)} %bitcast.25), calls=%async_computation.4 | async-start | bytes 2097152 | tf_op jit(solution)/shard_map/all_to_all | solution.py:126
  146.9 27.2 %all-to-all-start.3 = ((bf16[4,128,1024]{2,1,0:T(8,128)(2,1)}), bf16[4,128,1024]{2,1,0:T(8,128)(2,1)S(1)}, u32[]{:S(2)}, u32[]{:S(2)}) async-start(bf16[4,128,1024]{2,1,0:T(8,128)(2,1)} %bitcast.24), calls=%async_computation.3 | async-start | bytes 2097152 | tf_op jit(solution)/shard_map/all_to_all | solution.py:104
  157.4 23.7 %copy-start.6 = (bf16[128,2048]{1,0:T(8,128)(2,1)S(1)}, bf16[128,2048]{1,0:T(8,128)(2,1)}, u32[]{:S(2)}) copy-start(bf16[128,2048]{1,0:T(8,128)(2,1)} %get-tuple-element.14) | copy-start | bytes 1572868
  174.1 9.1 %copy-start.5 = (bf16[128,2048]{1,0:T(8,128)(2,1)S(1)}, bf16[128,2048]{1,0:T(8,128)(2,1)}, u32[]{:S(2)}) copy-start(bf16[128,2048]{1,0:T(8,128)(2,1)} %get-tuple-element.12) | copy-start | bytes 1572868
  174.1 29.0 %all-to-all-start.5 = ((bf16[4,128,1024]{2,1,0:T(8,128)(2,1)}), bf16[4,128,1024]{2,1,0:T(8,128)(2,1)S(1)}, u32[]{:S(2)}, u32[]{:S(2)}) async-start(bf16[4,128,1024]{2,1,0:T(8,128)(2,1)} %bitcast.26), calls=%async_computation.5 | async-start | bytes 2097152 | tf_op jit(solution)/shard_map/all_to_all | solution.py:104
  (3 other events, 6.1 us)

commit v8 on v4

--- a/solution.py
+++ b/solution.py
@@ -13,14 +13,15 @@
 
 
 def attention_kernel(
-    ids_ref, q_ref, g_ref, k_ref, v_ref, att_ref, dq_ref, dk_ref, dv_ref, *, rows, window, per_shard, group_size
+    ids_ref, q_ref, g_ref, kw_ref, vw_ref, kb_ref, vb_ref, wgrad_ref, bgrad_ref,
+    att_ref, dq_ref, *, rows, window, per_shard, group_size
 ):
     scaling = HD ** (-0.5)
     head_id = ids_ref[0]
     shard_id = ids_ref[1]
-    key_count = k_ref.shape[0]
-    k = k_ref[...]
-    v = v_ref[...]
+    k = jnp.concatenate([kw_ref[...], kb_ref[...]], axis=0)
+    v = jnp.concatenate([vw_ref[...], vb_ref[...]], axis=0)
+    key_count = k.shape[0]
     row = lax.broadcasted_iota(jnp.int32, (rows, key_count), 0) + head_id * rows
     col = lax.broadcasted_iota(jnp.int32, (rows, key_count), 1)
     in_window = col < window
@@ -39,7 +40,7 @@
         scores = jnp.where(visible, scores, NEG_FILL)
         row_max = jnp.max(scores, axis=1, keepdims=True)
         weights = jnp.exp(scores - row_max)
-        probs = weights / jnp.sum(weights, axis=1, keepdims=True)
+        probs = weights * (1.0 / jnp.sum(weights, axis=1, keepdims=True))
         probs_low = probs.astype(jnp.bfloat16)
         attended = jnp.dot(probs_low, v, preferred_element_type=jnp.float32).astype(jnp.bfloat16)
         att_ref[:, cols] = attended
@@ -51,36 +52,44 @@
         ).astype(jnp.bfloat16)
         dk_acc = dk_acc + lax.dot_general(grad_scores, q, tn, preferred_element_type=jnp.float32)
         dv_acc = dv_acc + lax.dot_general(probs_low, do, tn, preferred_element_type=jnp.float32)
-    dk_ref[...] = dk_acc * scaling
-    dv_ref[...] = dv_acc
+    dk_acc = dk_acc * scaling
+    wgrad_ref[:, :HD] = dk_acc[:window]
+    wgrad_ref[:, HD:] = dv_acc[:window]
+    bgrad_ref[:, :HD] = dk_acc[window:].astype(jnp.bfloat16)
+    bgrad_ref[:, HD:] = dv_acc[window:].astype(jnp.bfloat16)
 
 
-def attend_all(ids, queries, out_grad, kv_all, window, per_shard):
+def attend_all(ids, queries, out_grad, kv_window, kv_beacons, per_shard):
     rows, q_width = queries.shape
-    key_count, kv_double = kv_all.shape
+    window, kv_double = kv_window.shape
+    beacon_total = kv_beacons.shape[0]
     kv_heads = kv_double // 2 // HD
     group_size = q_width // HD // kv_heads
     kernel = functools.partial(
         attention_kernel, rows=rows, window=window, per_shard=per_shard, group_size=group_size
     )
     qblock = pl.BlockSpec((rows, group_size * HD), lambda h, ids: (0, h))
-    kblock = pl.BlockSpec((key_count, HD), lambda h, ids: (0, h))
-    vblock = pl.BlockSpec((key_count, HD), lambda h, ids: (0, h + kv_heads))
+    kwblock = pl.BlockSpec((window, HD), lambda h, ids: (0, h))
+    vwblock = pl.BlockSpec((window, HD), lambda h, ids: (0, h + kv_heads))
+    kbblock = pl.BlockSpec((beacon_total, HD), lambda h, ids: (0, h))
+    vbblock = pl.BlockSpec((beacon_total, HD), lambda h, ids: (0, h + kv_heads))
+    wgblock = pl.BlockSpec((window, 2 * HD), lambda h, ids: (0, h))
+    bgblock = pl.BlockSpec((beacon_total, 2 * HD), lambda h, ids: (0, h))
     return pl.pallas_call(
         kernel,
         grid_spec=pltpu.PrefetchScalarGridSpec(
             num_scalar_prefetch=1,
             grid=(kv_heads,),
-            in_specs=[qblock, qblock, kblock, vblock],
-            out_specs=[qblock, qblock, kblock, kblock],
+            in_specs=[qblock, qblock, kwblock, vwblock, kbblock, vbblock],
+            out_specs=[wgblock, bgblock, qblock, qblock],
         ),
         out_shape=[
+            jax.ShapeDtypeStruct((window, kv_double), jnp.float32),
+            jax.ShapeDtypeStruct((beacon_total, kv_double), jnp.bfloat16),
             jax.ShapeDtypeStruct((rows, q_width), jnp.bfloat16),
             jax.ShapeDtypeStruct((rows, q_width), jnp.bfloat16),
-            jax.ShapeDtypeStruct((key_count, kv_heads * HD), jnp.float32),
-            jax.ShapeDtypeStruct((key_count, kv_heads * HD), jnp.float32),
         ],
-    )(ids, queries, out_grad, kv_all, kv_all)
+    )(ids, queries, out_grad, kv_window, kv_window, kv_beacons, kv_beacons)
 
 
 def head_gather(block, axis, count):
@@ -127,19 +136,21 @@
         jnp.broadcast_to(own_beacon_rows[None], (ctx_axis,) + own_beacon_rows.shape),
         "ctx", 0, 0, tiled=True,
     ).reshape(ctx_axis * per_shard, 2 * kv_width)
-    kv_all = jnp.concatenate([kv_window, kv_beacons], axis=0)
-    attended_out, query_out, key_grad, value_grad = attend_all(
-        ids, queries, out_grad, kv_all, window, per_shard
+    window_grads, beacon_grads, attended_out, query_out = attend_all(
+        ids, queries, out_grad, kv_window, kv_beacons, per_shard
     )
-    kv_grads = jnp.concatenate([key_grad, value_grad], axis=1)
     beacon_parts = lax.all_to_all(
-        kv_grads[window:].astype(jnp.bfloat16).reshape(ctx_axis, per_shard, 2 * kv_width),
-        "ctx", 0, 0, tiled=True,
+        beacon_grads.reshape(ctx_axis, per_shard, 2 * kv_width), "ctx", 0, 0, tiled=True
     )
     own_beacons = jnp.sum(beacon_parts.astype(jnp.float32), axis=0)
-    window_grads = kv_grads[:window].at[positions].add(own_beacons)
+    window_grads = window_grads.at[positions].add(own_beacons)
     own_grads = head_reduce(window_grads, "head", heads_axis).astype(jnp.bfloat16)
-    return attended_out, query_out, own_grads[:, :kv_width], own_grads[:, kv_width:]
+    own_grads = own_grads.reshape(own_grads.shape[0], kv_width // HD, 2, HD)
+    rows = own_grads.shape[0]
+    return (
+        attended_out, query_out,
+        own_grads[:, :, 0].reshape(rows, kv_width), own_grads[:, :, 1].reshape(rows, kv_width),
+    )
 
 
 def local(queries, keys, values, out_grad, beacon_pos, *, heads_axis, ctx_axis, parts):

time: 199 us -> 187 us (0.940)
  local copies, waits for them, and re-layouts: 39.6 us -> 26.5 us
  waiting for transfers between devices: 25.2 us -> 32.5 us
  other arithmetic: 21.8 us -> 17.3 us
    unnamed x36 -> x40, local copies, waits for them, and re-layouts: 15.3 us -> 8.33 us
    all_to_all x2, waiting for transfers between devices: 2.85 us -> 8.33 us  [local_part(): lax.all_to_all(beacon_grads.reshape(ctx_axis, per_shard, 2 * kv_width), '...]
    slice x6 -> x2, local copies, waits for them, and re-layouts: 5.85 us -> 0.73 us  [local_part(): own_grads[:, :, 1].reshape(rows, kv_width)]
    concatenate x2 -> x0, other arithmetic: 4.3 us -> none  [local_part(): kv_all = jnp.concatenate([kv_window, kv_beacons], axis=0)]
  transfers between devices with their start and end apart: 28 -> 28, of which waited for: 8 -> 8; matrix products, arithmetic and copies ran while one was open for 27% -> 20% of each run, Pallas kernels for 18% -> 19%
where the time goes in v8:
time: 187 us; the launch traced here: 185 us
  starting transfers between devices  72.5 us (39%)
  Pallas kernels  34.9 us (19%)
  waiting for transfers between devices  32.5 us (17%)
  local copies, waits for them, and re-layouts  26.5 us (14%)
  other arithmetic  17.3 us (9%)
    pallas_call x2, Pallas kernels, attend_all(): pl.pallas_call(kernel, grid_spec=pltpu.PrefetchScalarGridSpec(num_scalar_...  34.9 us
    ppermute x6, starting transfers between devices, head_gather(): lax.ppermute(from_left[-1], axis, [(j, j + 1) for j in range(step - 1, co...  15.7 us
    ppermute x6, starting transfers between devices, head_gather(): lax.ppermute(from_right[-1], axis, [(j + 1, j) for j in range(count - ste...  14.6 us
    ppermute x6, starting transfers between devices, head_reduce(): lax.ppermute(send_left, axis, [(j, j - 1) for j in range(max(1, count - s...  13.5 us
    ppermute x6, starting transfers between devices, head_reduce(): lax.ppermute(send_right, axis, [(j, j + 1) for j in range(0, min(step, co...  10.8 us
    ppermute x6, waiting for transfers between devices, head_reduce(): lax.ppermute(send_right, axis, [(j, j + 1) for j in range(0, min(step, co...  9.57 us
    all_to_all x2, starting transfers between devices, local_part(): lax.all_to_all(jnp.broadcast_to(own_beacon_rows[None], (ctx_axis,) + own_...  9.23 us
    all_to_all x2, starting transfers between devices, local_part(): lax.all_to_all(beacon_grads.reshape(ctx_axis, per_shard, 2 * kv_width), '...  8.6 us
  transfers between devices with their start and end apart: 28, of which 8 were waited for; matrix products, arithmetic and copies ran while one was open for 20% of the time, Pallas kernels for 19%

profile of v8, /device:TPU:10, one launch (start us, length us, event | category | flops | bytes accessed | tf_op | source)
XLA Modules:
  0.0 184.9 jit_solution(15113877306108065673)
XLA Ops:
  2.7 3.5 %collective-permute-start = (bf16[128,1024]{1,0:T(8,128)(2,1)S(1)}, bf16[128,1024]{1,0:T(8,128)(2,1)S(1)}, u32[]{:S(2)}, u32[]{:S(2)}) collective-permute-start(bf16[128,1024]{1,0:T(8,128)(2,1)S(1)} %pad_maximum_fusion.2), channel_id=1, source_target_pairs={{0,1},{1,2},{2,3},{4,5},{5,6},{6,7},{8,9},{9,10},{10,11},{12,13},{... | collective-permute-start | bytes 786440 | tf_op jit(solution)/shard_map/ppermute | solution.py:100
  6.1 2.4 %collective-permute-start.3 = (bf16[128,1024]{1,0:T(8,128)(2,1)S(1)}, bf16[128,1024]{1,0:T(8,128)(2,1)S(1)}, u32[]{:S(2)}, u32[]{:S(2)}) collective-permute-start(bf16[128,1024]{1,0:T(8,128)(2,1)S(1)} %pad_maximum_fusion.2), channel_id=1, source_target_pairs={{1,0},{2,1},{3,2},{5,4},{6,5},{7,6},{9,8},{10,9},{11,10},{13,12},{... | collective-permute-start | bytes 786440 | tf_op jit(solution)/shard_map/ppermute | solution.py:103
  8.6 3.5 %collective-permute-start.6 = (bf16[128,1024]{1,0:T(8,128)(2,1)S(1)}, bf16[128,1024]{1,0:T(8,128)(2,1)S(1)}, u32[]{:S(2)}, u32[]{:S(2)}) collective-permute-start(bf16[128,1024]{1,0:T(8,128)(2,1)S(1)} %pad_maximum_fusion.3), channel_id=1, source_target_pairs={{0,1},{1,2},{2,3},{4,5},{5,6},{6,7},{8,9},{9,10},{10,11},{12,13},{... | collective-permute-start | bytes 786440 | tf_op jit(solution)/shard_map/ppermute | solution.py:100
  12.0 2.4 %collective-permute-start.9 = (bf16[128,1024]{1,0:T(8,128)(2,1)S(1)}, bf16[128,1024]{1,0:T(8,128)(2,1)S(1)}, u32[]{:S(2)}, u32[]{:S(2)}) collective-permute-start(bf16[128,1024]{1,0:T(8,128)(2,1)S(1)} %pad_maximum_fusion.3), channel_id=1, source_target_pairs={{1,0},{2,1},{3,2},{5,4},{6,5},{7,6},{9,8},{10,9},{11,10},{13,12},{... | collective-permute-start | bytes 786440 | tf_op jit(solution)/shard_map/ppermute | solution.py:103
  15.2 3.5 %collective-permute-start.1 = (bf16[128,1024]{1,0:T(8,128)(2,1)S(1)}, bf16[128,1024]{1,0:T(8,128)(2,1)S(1)}, u32[]{:S(2)}, u32[]{:S(2)}) collective-permute-start(bf16[128,1024]{1,0:T(8,128)(2,1)S(1)} %collective-permute-done), channel_id=1, source_target_pairs={{1,2},{2,3},{5,6},{6,7},{9,10},{10,11},{13,14},{14,15},{17,18},{18... | collective-permute-start | bytes 786440 | tf_op jit(solution)/shard_map/ppermute | solution.py:100
  21.4 3.9 %collective-permute-start.7 = (bf16[128,1024]{1,0:T(8,128)(2,1)S(1)}, bf16[128,1024]{1,0:T(8,128)(2,1)S(1)}, u32[]{:S(2)}, u32[]{:S(2)}) collective-permute-start(bf16[128,1024]{1,0:T(8,128)(2,1)S(1)} %collective-permute-done.6), channel_id=1, source_target_pairs={{1,2},{2,3},{5,6},{6,7},{9,10},{10,11},{13,14},{14,15},{17,18},{18... | collective-permute-start | bytes 786440 | tf_op jit(solution)/shard_map/ppermute | solution.py:100
  31.1 2.9 %collective-permute-done.10 = bf16[128,1024]{1,0:T(8,128)(2,1)S(1)} collective-permute-done((bf16[128,1024]{1,0:T(8,128)(2,1)S(1)}, bf16[128,1024]{1,0:T(8,128)(2,1)S(1)}, u32[]{:S(2)}, u32[]{:S(2)}) %collective-permute-start.10) | collective-permute-done | bytes 262176 | tf_op jit(solution)/shard_map/ppermute | solution.py:103
  34.0 4.4 %collective-permute-start.11 = (bf16[128,1024]{1,0:T(8,128)(2,1)S(1)}, bf16[128,1024]{1,0:T(8,128)(2,1)S(1)}, u32[]{:S(2)}, u32[]{:S(2)}) collective-permute-start(bf16[128,1024]{1,0:T(8,128)(2,1)S(1)} %collective-permute-done.10), channel_id=1, source_target_pairs={{1,0},{5,4},{9,8},{13,12},{17,16},{21,20},{25,24},{29,28}} | collective-permute-start | bytes 786440 | tf_op jit(solution)/shard_map/ppermute | solution.py:103
  45.3 4.3 %all-to-all-start = ((bf16[8,64,1024]{2,1,0:T(8,128)(2,1)}), bf16[8,64,1024]{2,1,0:T(8,128)(2,1)S(1)}, u32[]{:S(2)}, u32[]{:S(2)}) async-start(bf16[8,64,1024]{2,1,0:T(8,128)(2,1)} %broadcast_in_dim.4), calls=%async_computation | async-start | bytes 2097152 | tf_op jit(solution)/shard_map/all_to_all | solution.py:135
  55.3 8.1 %all-to-all-done = bf16[8,64,1024]{2,1,0:T(8,128)(2,1)S(1)} async-done(((bf16[8,64,1024]{2,1,0:T(8,128)(2,1)}), bf16[8,64,1024]{2,1,0:T(8,128)(2,1)S(1)}, u32[]{:S(2)}, u32[]{:S(2)}) %all-to-all-start) | async-done | bytes 1048608 | tf_op jit(solution)/shard_map/all_to_all | solution.py:135
  64.7 5.0 %all-to-all-start.1 = ((bf16[8,64,1024]{2,1,0:T(8,128)(2,1)}), bf16[8,64,1024]{2,1,0:T(8,128)(2,1)S(1)}, u32[]{:S(2)}, u32[]{:S(2)}) async-start(bf16[8,64,1024]{2,1,0:T(8,128)(2,1)} %broadcast_in_dim.5), calls=%async_computation.1 | async-start | bytes 2097152 | tf_op jit(solution)/shard_map/all_to_all | solution.py:135
  70.3 2.9 %fusion.2 = (bf16[128,2048]{1,0:T(8,128)(2,1)}, bf16[128,2048]{1,0:T(8,128)(2,1)}, bf16[128,2048]{1,0:T(8,128)(2,1)}, bf16[128,2048]{1,0:T(8,128)(2,1)}) fusion(bf16[128,4096]{1,0:T(8,128)(2,1)} %param.8, bf16[128,4096]{1,0:T(8,128)(2,1)} %param.5), kind=kLoop, calls=%fused_computation.50 | loop fusion | bytes 4194304 | tf_op jit(solution)/shard_map/slice | solution.py:169
  73.2 17.4 %shard_map.84 = (f32[512,1024]{1,0:T(8,128)}, bf16[512,1024]{1,0:T(8,128)(2,1)}, bf16[128,2048]{1,0:T(8,128)(2,1)}, bf16[128,2048]{1,0:T(8,128)(2,1)}) custom-call(s32[2]{0:T(128)} %pad_add_fusion.ids_ref, bf16[128,2048]{1,0:T(8,128)(2,1)} %get-tuple-element.47.q_ref, bf16[128,2048]{1,0:T(8,128)(2,1)} %get-tuple-element.32.g_ref, ...), custom_call_target="tpu_custom_call" | custom-call | tf_op jit(solution)/shard_map/pallas_call | solution.py:78
  90.7 4.2 %all-to-all-start.2 = ((bf16[8,64,1024]{2,1,0:T(8,128)(2,1)}), bf16[8,64,1024]{2,1,0:T(8,128)(2,1)}, u32[]{:S(2)}, u32[]{:S(2)}) async-start(bf16[8,64,1024]{2,1,0:T(8,128)(2,1)} %bitcast.57), calls=%async_computation.2 | async-start | bytes 2097152 | tf_op jit(solution)/shard_map/all_to_all | solution.py:142
  94.9 17.4 %shard_map.85 = (f32[512,1024]{1,0:T(8,128)}, bf16[512,1024]{1,0:T(8,128)(2,1)}, bf16[128,2048]{1,0:T(8,128)(2,1)}, bf16[128,2048]{1,0:T(8,128)(2,1)}) custom-call(s32[2]{0:T(128)} %pad_add_fusion.ids_ref, bf16[128,2048]{1,0:T(8,128)(2,1)} %get-tuple-element.46.q_ref, bf16[128,2048]{1,0:T(8,128)(2,1)} %get-tuple-element.33.g_ref, ...), custom_call_target="tpu_custom_call" | custom-call | tf_op jit(solution)/shard_map/pallas_call | solution.py:78
  112.4 4.4 %all-to-all-start.3 = ((bf16[8,64,1024]{2,1,0:T(8,128)(2,1)}), bf16[8,64,1024]{2,1,0:T(8,128)(2,1)S(1)}, u32[]{:S(2)}, u32[]{:S(2)}) async-start(bf16[8,64,1024]{2,1,0:T(8,128)(2,1)} %bitcast.56), calls=%async_computation.3 | async-start | bytes 2097152 | tf_op jit(solution)/shard_map/all_to_all | solution.py:142
  122.3 8.3 %all-to-all-done.3 = bf16[8,64,1024]{2,1,0:T(8,128)(2,1)S(1)} async-done(((bf16[8,64,1024]{2,1,0:T(8,128)(2,1)}), bf16[8,64,1024]{2,1,0:T(8,128)(2,1)S(1)}, u32[]{:S(2)}, u32[]{:S(2)}) %all-to-all-start.3) | async-done | bytes 1048608 | tf_op jit(solution)/shard_map/all_to_all | solution.py:142
  130.8 4.0 %scatter_fusion.1 = f32[512,1024]{1,0:T(8,128)} fusion(f32[512,1024]{1,0:T(8,128)} %get-tuple-element.18, s32[64]{0:T(128)S(1)} %fusion, f32[64,1024]{1,0:T(8,128)S(1)} %convert_reduce_fusion), kind=kCustom, calls=%fused_computation.5 | custom fusion | flops 65536 | bytes 786688 | tf_op jit(solution)/shard_map/scatter-add | solution.py:146
  146.5 2.6 %collective-permute-done.15 = bf16[128,1024]{1,0:T(8,128)(2,1)} collective-permute-done((bf16[128,1024]{1,0:T(8,128)(2,1)}, bf16[128,1024]{1,0:T(8,128)(2,1)}, u32[]{:S(2)}, u32[]{:S(2)}) %collective-permute-start.15) | collective-permute-done | bytes 262176 | tf_op jit(solution)/shard_map/ppermute | solution.py:124
  149.1 3.5 %collective-permute-done.13 = bf16[128,1024]{1,0:T(8,128)(2,1)} collective-permute-done((bf16[128,1024]{1,0:T(8,128)(2,1)}, bf16[128,1024]{1,0:T(8,128)(2,1)}, u32[]{:S(2)}, u32[]{:S(2)}) %collective-permute-start.13) | collective-permute-done | bytes 262176 | tf_op jit(solution)/shard_map/ppermute | solution.py:123
  156.8 4.1 %collective-permute-start.14 = (bf16[128,1024]{1,0:T(8,128)(2,1)S(1)}, bf16[128,1024]{1,0:T(8,128)(2,1)S(1)}, u32[]{:S(2)}, u32[]{:S(2)}) collective-permute-start(bf16[128,1024]{1,0:T(8,128)(2,1)S(1)} %get-tuple-element.24), channel_id=1, source_target_pairs={{1,0},{2,1},{3,2},{5,4},{6,5},{7,6},{9,8},{10,9},{11,10},{13,12},{... | collective-permute-start | bytes 786440 | tf_op jit(solution)/shard_map/ppermute | solution.py:123
  166.9 3.9 %collective-permute-start.20 = (bf16[128,1024]{1,0:T(8,128)(2,1)}, bf16[128,1024]{1,0:T(8,128)(2,1)S(1)}, u32[]{:S(2)}, u32[]{:S(2)}) collective-permute-start(bf16[128,1024]{1,0:T(8,128)(2,1)} %get-tuple-element.28), channel_id=1, source_target_pairs={{1,0},{2,1},{3,2},{5,4},{6,5},{7,6},{9,8},{10,9},{11,10},{13,12},{... | collective-permute-start | bytes 786440 | tf_op jit(solution)/shard_map/ppermute | solution.py:123
  174.9 2.4 %collective-permute-done.17 = bf16[128,1024]{1,0:T(8,128)(2,1)S(1)} collective-permute-done((bf16[128,1024]{1,0:T(8,128)(2,1)S(1)}, bf16[128,1024]{1,0:T(8,128)(2,1)S(1)}, u32[]{:S(2)}, u32[]{:S(2)}) %collective-permute-start.17) | collective-permute-done | bytes 262176 | tf_op jit(solution)/shard_map/ppermute | solution.py:124
  178.1 2.9 %collective-permute-done.23 = bf16[128,1024]{1,0:T(8,128)(2,1)S(1)} collective-permute-done((bf16[128,1024]{1,0:T(8,128)(2,1)S(1)}, bf16[128,1024]{1,0:T(8,128)(2,1)S(1)}, u32[]{:S(2)}, u32[]{:S(2)}) %collective-permute-start.23) | collective-permute-done | bytes 262176 | tf_op jit(solution)/shard_map/ppermute | solution.py:124
  (115 shorter events, 61.8 us)
Async XLA Ops:
  2.7 12.6 %collective-permute-start = (bf16[128,1024]{1,0:T(8,128)(2,1)S(1)}, bf16[128,1024]{1,0:T(8,128)(2,1)S(1)}, u32[]{:S(2)}, u32[]{:S(2)}) collective-permute-start(bf16[128,1024]{1,0:T(8,128)(2,1)S(1)} %pad_maximum_fusion.2), channel_id=1, source_target_pairs={{0,1},{1,2},{2,3},{4,5},{5,6},{6,7},{8,9},{9,10},{10,11},{12,13},{... | collective-permute-start | bytes 786440 | tf_op jit(solution)/shard_map/ppermute | solution.py:100
  6.1 13.3 %collective-permute-start.3 = (bf16[128,1024]{1,0:T(8,128)(2,1)S(1)}, bf16[128,1024]{1,0:T(8,128)(2,1)S(1)}, u32[]{:S(2)}, u32[]{:S(2)}) collective-permute-start(bf16[128,1024]{1,0:T(8,128)(2,1)S(1)} %pad_maximum_fusion.2), channel_id=1, source_target_pairs={{1,0},{2,1},{3,2},{5,4},{6,5},{7,6},{9,8},{10,9},{11,10},{13,12},{... | collective-permute-start | bytes 786440 | tf_op jit(solution)/shard_map/ppermute | solution.py:103
  8.6 12.8 %collective-permute-start.6 = (bf16[128,1024]{1,0:T(8,128)(2,1)S(1)}, bf16[128,1024]{1,0:T(8,128)(2,1)S(1)}, u32[]{:S(2)}, u32[]{:S(2)}) collective-permute-start(bf16[128,1024]{1,0:T(8,128)(2,1)S(1)} %pad_maximum_fusion.3), channel_id=1, source_target_pairs={{0,1},{1,2},{2,3},{4,5},{5,6},{6,7},{8,9},{9,10},{10,11},{12,13},{... | collective-permute-start | bytes 786440 | tf_op jit(solution)/shard_map/ppermute | solution.py:100
  12.0 13.3 %collective-permute-start.9 = (bf16[128,1024]{1,0:T(8,128)(2,1)S(1)}, bf16[128,1024]{1,0:T(8,128)(2,1)S(1)}, u32[]{:S(2)}, u32[]{:S(2)}) collective-permute-start(bf16[128,1024]{1,0:T(8,128)(2,1)S(1)} %pad_maximum_fusion.3), channel_id=1, source_target_pairs={{1,0},{2,1},{3,2},{5,4},{6,5},{7,6},{9,8},{10,9},{11,10},{13,12},{... | collective-permute-start | bytes 786440 | tf_op jit(solution)/shard_map/ppermute | solution.py:103
  15.2 12.1 %collective-permute-start.1 = (bf16[128,1024]{1,0:T(8,128)(2,1)S(1)}, bf16[128,1024]{1,0:T(8,128)(2,1)S(1)}, u32[]{:S(2)}, u32[]{:S(2)}) collective-permute-start(bf16[128,1024]{1,0:T(8,128)(2,1)S(1)} %collective-permute-done), channel_id=1, source_target_pairs={{1,2},{2,3},{5,6},{6,7},{9,10},{10,11},{13,14},{14,15},{17,18},{18... | collective-permute-start | bytes 786440 | tf_op jit(solution)/shard_map/ppermute | solution.py:100
  19.4 9.3 %collective-permute-start.4 = (bf16[128,1024]{1,0:T(8,128)(2,1)S(1)}, bf16[128,1024]{1,0:T(8,128)(2,1)S(1)}, u32[]{:S(2)}, u32[]{:S(2)}) collective-permute-start(bf16[128,1024]{1,0:T(8,128)(2,1)S(1)} %collective-permute-done.3), channel_id=1, source_target_pairs={{1,0},{2,1},{5,4},{6,5},{9,8},{10,9},{13,12},{14,13},{17,16},{18,1... | collective-permute-start | bytes 786440 | tf_op jit(solution)/shard_map/ppermute | solution.py:103
  27.3 11.1 %collective-permute-start.2 = (bf16[128,1024]{1,0:T(8,128)(2,1)S(1)}, bf16[128,1024]{1,0:T(8,128)(2,1)S(1)}, u32[]{:S(2)}, u32[]{:S(2)}) collective-permute-start(bf16[128,1024]{1,0:T(8,128)(2,1)S(1)} %collective-permute-done.1), channel_id=1, source_target_pairs={{2,3},{6,7},{10,11},{14,15},{18,19},{22,23},{26,27},{30,31}} | collective-permute-start | bytes 786440 | tf_op jit(solution)/shard_map/ppermute | solution.py:100
  28.7 11.9 %collective-permute-start.5 = (bf16[128,1024]{1,0:T(8,128)(2,1)S(1)}, bf16[128,1024]{1,0:T(8,128)(2,1)S(1)}, u32[]{:S(2)}, u32[]{:S(2)}) collective-permute-start(bf16[128,1024]{1,0:T(8,128)(2,1)S(1)} %collective-permute-done.4), channel_id=1, source_target_pairs={{1,0},{5,4},{9,8},{13,12},{17,16},{21,20},{25,24},{29,28}} | collective-permute-start | bytes 786440 | tf_op jit(solution)/shard_map/ppermute | solution.py:103
  30.4 19.2 %collective-permute-start.8 = (bf16[128,1024]{1,0:T(8,128)(2,1)S(1)}, bf16[128,1024]{1,0:T(8,128)(2,1)S(1)}, u32[]{:S(2)}, u32[]{:S(2)}) collective-permute-start(bf16[128,1024]{1,0:T(8,128)(2,1)S(1)} %collective-permute-done.7), channel_id=1, source_target_pairs={{2,3},{6,7},{10,11},{14,15},{18,19},{22,23},{26,27},{30,31}} | collective-permute-start | bytes 786440 | tf_op jit(solution)/shard_map/ppermute | solution.py:100
  34.0 17.8 %collective-permute-start.11 = (bf16[128,1024]{1,0:T(8,128)(2,1)S(1)}, bf16[128,1024]{1,0:T(8,128)(2,1)S(1)}, u32[]{:S(2)}, u32[]{:S(2)}) collective-permute-start(bf16[128,1024]{1,0:T(8,128)(2,1)S(1)} %collective-permute-done.10), channel_id=1, source_target_pairs={{1,0},{5,4},{9,8},{13,12},{17,16},{21,20},{25,24},{29,28}} | collective-permute-start | bytes 786440 | tf_op jit(solution)/shard_map/ppermute | solution.py:103
  45.3 18.2 %all-to-all-start = ((bf16[8,64,1024]{2,1,0:T(8,128)(2,1)}), bf16[8,64,1024]{2,1,0:T(8,128)(2,1)S(1)}, u32[]{:S(2)}, u32[]{:S(2)}) async-start(bf16[8,64,1024]{2,1,0:T(8,128)(2,1)} %broadcast_in_dim.4), calls=%async_computation | async-start | bytes 2097152 | tf_op jit(solution)/shard_map/all_to_all | solution.py:135
  64.7 25.9 %all-to-all-start.1 = ((bf16[8,64,1024]{2,1,0:T(8,128)(2,1)}), bf16[8,64,1024]{2,1,0:T(8,128)(2,1)S(1)}, u32[]{:S(2)}, u32[]{:S(2)}) async-start(bf16[8,64,1024]{2,1,0:T(8,128)(2,1)} %broadcast_in_dim.5), calls=%async_computation.1 | async-start | bytes 2097152 | tf_op jit(solution)/shard_map/all_to_all | solution.py:135
  90.7 21.7 %all-to-all-start.2 = ((bf16[8,64,1024]{2,1,0:T(8,128)(2,1)}), bf16[8,64,1024]{2,1,0:T(8,128)(2,1)}, u32[]{:S(2)}, u32[]{:S(2)}) async-start(bf16[8,64,1024]{2,1,0:T(8,128)(2,1)} %bitcast.57), calls=%async_computation.2 | async-start | bytes 2097152 | tf_op jit(solution)/shard_map/all_to_all | solution.py:142
  112.4 18.3 %all-to-all-start.3 = ((bf16[8,64,1024]{2,1,0:T(8,128)(2,1)}), bf16[8,64,1024]{2,1,0:T(8,128)(2,1)S(1)}, u32[]{:S(2)}, u32[]{:S(2)}) async-start(bf16[8,64,1024]{2,1,0:T(8,128)(2,1)} %bitcast.56), calls=%async_computation.3 | async-start | bytes 2097152 | tf_op jit(solution)/shard_map/all_to_all | solution.py:142
  120.9 18.5 %collective-permute-start.12 = (bf16[128,1024]{1,0:T(8,128)(2,1)}, bf16[128,1024]{1,0:T(8,128)(2,1)}, u32[]{:S(2)}, u32[]{:S(2)}) collective-permute-start(bf16[128,1024]{1,0:T(8,128)(2,1)} %get-tuple-element.26), channel_id=1, source_target_pairs={{3,2},{7,6},{11,10},{15,14},{19,18},{23,22},{27,26},{31,30}} | collective-permute-start | bytes 786440 | tf_op jit(solution)/shard_map/ppermute | solution.py:123
  138.1 11.0 %collective-permute-start.15 = (bf16[128,1024]{1,0:T(8,128)(2,1)}, bf16[128,1024]{1,0:T(8,128)(2,1)}, u32[]{:S(2)}, u32[]{:S(2)}) collective-permute-start(bf16[128,1024]{1,0:T(8,128)(2,1)} %get-tuple-element.27), channel_id=1, source_target_pairs={{0,1},{4,5},{8,9},{12,13},{16,17},{20,21},{24,25},{28,29}} | collective-permute-start | bytes 786440 | tf_op jit(solution)/shard_map/ppermute | solution.py:124
  141.1 11.5 %collective-permute-start.13 = (bf16[128,1024]{1,0:T(8,128)(2,1)}, bf16[128,1024]{1,0:T(8,128)(2,1)}, u32[]{:S(2)}, u32[]{:S(2)}) collective-permute-start(bf16[128,1024]{1,0:T(8,128)(2,1)} %add_convert_fusion.9), channel_id=1, source_target_pairs={{2,1},{3,2},{6,5},{7,6},{10,9},{11,10},{14,13},{15,14},{18,17},{19... | collective-permute-start | bytes 786440 | tf_op jit(solution)/shard_map/ppermute | solution.py:123
  142.5 18.3 %collective-permute-start.21 = (bf16[128,1024]{1,0:T(8,128)(2,1)S(1)}, bf16[128,1024]{1,0:T(8,128)(2,1)S(1)}, u32[]{:S(2)}, u32[]{:S(2)}) collective-permute-start(bf16[128,1024]{1,0:T(8,128)(2,1)S(1)} %get-tuple-element.31), channel_id=1, source_target_pairs={{0,1},{4,5},{8,9},{12,13},{16,17},{20,21},{24,25},{28,29}} | collective-permute-start | bytes 786440 | tf_op jit(solution)/shard_map/ppermute | solution.py:124
  145.0 15.8 %collective-permute-start.19 = (bf16[128,1024]{1,0:T(8,128)(2,1)S(1)}, bf16[128,1024]{1,0:T(8,128)(2,1)S(1)}, u32[]{:S(2)}, u32[]{:S(2)}) collective-permute-start(bf16[128,1024]{1,0:T(8,128)(2,1)S(1)} %add_convert_fusion.4), channel_id=1, source_target_pairs={{2,1},{3,2},{6,5},{7,6},{10,9},{11,10},{14,13},{15,14},{18,17},{19... | collective-permute-start | bytes 786440 | tf_op jit(solution)/shard_map/ppermute | solution.py:123
  153.8 10.1 %collective-permute-start.16 = (bf16[128,1024]{1,0:T(8,128)(2,1)S(1)}, bf16[128,1024]{1,0:T(8,128)(2,1)S(1)}, u32[]{:S(2)}, u32[]{:S(2)}) collective-permute-start(bf16[128,1024]{1,0:T(8,128)(2,1)S(1)} %get-tuple-element.25), channel_id=1, source_target_pairs={{0,1},{1,2},{4,5},{5,6},{8,9},{9,10},{12,13},{13,14},{16,17},{17,1... | collective-permute-start | bytes 786440 | tf_op jit(solution)/shard_map/ppermute | solution.py:124
  156.8 18.1 %collective-permute-start.14 = (bf16[128,1024]{1,0:T(8,128)(2,1)S(1)}, bf16[128,1024]{1,0:T(8,128)(2,1)S(1)}, u32[]{:S(2)}, u32[]{:S(2)}) collective-permute-start(bf16[128,1024]{1,0:T(8,128)(2,1)S(1)} %get-tuple-element.24), channel_id=1, source_target_pairs={{1,0},{2,1},{3,2},{5,4},{6,5},{7,6},{9,8},{10,9},{11,10},{13,12},{... | collective-permute-start | bytes 786440 | tf_op jit(solution)/shard_map/ppermute | solution.py:123
  161.7 10.8 %collective-permute-start.22 = (bf16[128,1024]{1,0:T(8,128)(2,1)S(1)}, bf16[128,1024]{1,0:T(8,128)(2,1)S(1)}, u32[]{:S(2)}, u32[]{:S(2)}) collective-permute-start(bf16[128,1024]{1,0:T(8,128)(2,1)S(1)} %get-tuple-element.29), channel_id=1, source_target_pairs={{0,1},{1,2},{4,5},{5,6},{8,9},{9,10},{12,13},{13,14},{16,17},{17,1... | collective-permute-start | bytes 786440 | tf_op jit(solution)/shard_map/ppermute | solution.py:124
  163.9 13.3 %collective-permute-start.17 = (bf16[128,1024]{1,0:T(8,128)(2,1)S(1)}, bf16[128,1024]{1,0:T(8,128)(2,1)S(1)}, u32[]{:S(2)}, u32[]{:S(2)}) collective-permute-start(bf16[128,1024]{1,0:T(8,128)(2,1)S(1)} %add_convert_fusion.6), channel_id=1, source_target_pairs={{0,1},{1,2},{2,3},{4,5},{5,6},{6,7},{8,9},{9,10},{10,11},{12,13},{... | collective-permute-start | bytes 786440 | tf_op jit(solution)/shard_map/ppermute | solution.py:124
  166.9 11.1 %collective-permute-start.20 = (bf16[128,1024]{1,0:T(8,128)(2,1)}, bf16[128,1024]{1,0:T(8,128)(2,1)S(1)}, u32[]{:S(2)}, u32[]{:S(2)}) collective-permute-start(bf16[128,1024]{1,0:T(8,128)(2,1)} %get-tuple-element.28), channel_id=1, source_target_pairs={{1,0},{2,1},{3,2},{5,4},{6,5},{7,6},{9,8},{10,9},{11,10},{13,12},{... | collective-permute-start | bytes 786440 | tf_op jit(solution)/shard_map/ppermute | solution.py:123
  (16 other events, 144.1 us)

commit v9 on v8

--- a/solution.py
+++ b/solution.py
@@ -22,41 +22,39 @@
     k = jnp.concatenate([kw_ref[...], kb_ref[...]], axis=0)
     v = jnp.concatenate([vw_ref[...], vb_ref[...]], axis=0)
     key_count = k.shape[0]
-    row = lax.broadcasted_iota(jnp.int32, (rows, key_count), 0) + head_id * rows
-    col = lax.broadcasted_iota(jnp.int32, (rows, key_count), 1)
+    stacked = rows * group_size
+    row = lax.rem(lax.broadcasted_iota(jnp.int32, (stacked, key_count), 0), rows) + head_id * rows
+    col = lax.broadcasted_iota(jnp.int32, (stacked, key_count), 1)
     in_window = col < window
     visible = (in_window & (row >= col)) | (
         jnp.logical_not(in_window) & (col < window + shard_id * per_shard)
     )
     nt = (((1,), (1,)), ((), ()))
     tn = (((0,), (0,)), ((), ()))
-    dk_acc = jnp.zeros((key_count, HD), jnp.float32)
-    dv_acc = jnp.zeros((key_count, HD), jnp.float32)
+    q = jnp.concatenate([q_ref[:, g * HD:(g + 1) * HD] for g in range(group_size)], axis=0)
+    do = jnp.concatenate([g_ref[:, g * HD:(g + 1) * HD] for g in range(group_size)], axis=0)
+    scores = lax.dot_general(q, k, nt, preferred_element_type=jnp.float32) * scaling
+    scores = jnp.where(visible, scores, NEG_FILL)
+    row_max = jnp.max(scores, axis=1, keepdims=True)
+    weights = jnp.exp(scores - row_max)
+    probs = weights / jnp.sum(weights, axis=1, keepdims=True)
+    probs_low = probs.astype(jnp.bfloat16)
+    attended = jnp.dot(probs_low, v, preferred_element_type=jnp.float32).astype(jnp.bfloat16)
+    row_dot = jnp.sum(do.astype(jnp.float32) * attended.astype(jnp.float32), axis=1, keepdims=True)
+    dprob = lax.dot_general(do, v, nt, preferred_element_type=jnp.float32)
+    grad_scores = (probs * (dprob - row_dot)).astype(jnp.bfloat16)
+    query_grad = (
+        jnp.dot(grad_scores, k, preferred_element_type=jnp.float32) * scaling
+    ).astype(jnp.bfloat16)
     for g in range(group_size):
-        cols = slice(g * HD, (g + 1) * HD)
-        q = q_ref[:, cols]
-        do = g_ref[:, cols]
-        scores = lax.dot_general(q, k, nt, preferred_element_type=jnp.float32) * scaling
-        scores = jnp.where(visible, scores, NEG_FILL)
-        row_max = jnp.max(scores, axis=1, keepdims=True)
-        weights = jnp.exp(scores - row_max)
-        probs = weights * (1.0 / jnp.sum(weights, axis=1, keepdims=True))
-        probs_low = probs.astype(jnp.bfloat16)
-        attended = jnp.dot(probs_low, v, preferred_element_type=jnp.float32).astype(jnp.bfloat16)
-        att_ref[:, cols] = attended
-        row_dot = jnp.sum(do.astype(jnp.float32) * attended.astype(jnp.float32), axis=1, keepdims=True)
-        dprob = lax.dot_general(do, v, nt, preferred_element_type=jnp.float32)
-        grad_scores = (probs * (dprob - row_dot)).astype(jnp.bfloat16)
-        dq_ref[:, cols] = (
-            jnp.dot(grad_scores, k, preferred_element_type=jnp.float32) * scaling
-        ).astype(jnp.bfloat16)
-        dk_acc = dk_acc + lax.dot_general(grad_scores, q, tn, preferred_element_type=jnp.float32)
-        dv_acc = dv_acc + lax.dot_general(probs_low, do, tn, preferred_element_type=jnp.float32)
-    dk_acc = dk_acc * scaling
-    wgrad_ref[:, :HD] = dk_acc[:window]
-    wgrad_ref[:, HD:] = dv_acc[:window]
-    bgrad_ref[:, :HD] = dk_acc[window:].astype(jnp.bfloat16)
-    bgrad_ref[:, HD:] = dv_acc[window:].astype(jnp.bfloat16)
+        att_ref[:, g * HD:(g + 1) * HD] = attended[g * rows:(g + 1) * rows]
+        dq_ref[:, g * HD:(g + 1) * HD] = query_grad[g * rows:(g + 1) * rows]
+    key_grad = (lax.dot_general(q, grad_scores, tn, preferred_element_type=jnp.float32) * scaling).T
+    value_grad = lax.dot_general(do, probs_low, tn, preferred_element_type=jnp.float32).T
+    wgrad_ref[:, :HD] = key_grad[:window]
+    wgrad_ref[:, HD:] = value_grad[:window]
+    bgrad_ref[:, :HD] = key_grad[window:].astype(jnp.bfloat16)
+    bgrad_ref[:, HD:] = value_grad[window:].astype(jnp.bfloat16)
 
 
 def attend_all(ids, queries, out_grad, kv_window, kv_beacons, per_shard):

time: 187 us -> 178 us (0.952)
  Pallas kernels: 34.9 us -> 24.3 us
    pallas_call x2, Pallas kernels: 34.9 us -> 24.3 us  [attend_all(): pl.pallas_call(kernel, grid_spec=pltpu.PrefetchScalarGridSpec(num_scalar_...]
  transfers between devices with their start and end apart: 28 -> 28, of which waited for: 8 -> 9; matrix products, arithmetic and copies ran while one was open for 20% -> 21% of each run, Pallas kernels for 19% -> 14%
where the time goes in v9:
time: 178 us; the launch traced here: 177 us
  starting transfers between devices  73 us (41%)
  waiting for transfers between devices  34.3 us (19%)
  local copies, waits for them, and re-layouts  26.5 us (15%)
  Pallas kernels  24.3 us (14%)
  other arithmetic  17.3 us (10%)
    pallas_call x2, Pallas kernels, attend_all(): pl.pallas_call(kernel, grid_spec=pltpu.PrefetchScalarGridSpec(num_scalar_...  24.3 us
    ppermute x6, starting transfers between devices, head_gather(): lax.ppermute(from_left[-1], axis, [(j, j + 1) for j in range(step - 1, co...  15.7 us
    ppermute x6, starting transfers between devices, head_gather(): lax.ppermute(from_right[-1], axis, [(j + 1, j) for j in range(count - ste...  14.6 us
    ppermute x6, starting transfers between devices, head_reduce(): lax.ppermute(send_left, axis, [(j, j - 1) for j in range(max(1, count - s...  13.5 us
    ppermute x6, starting transfers between devices, head_reduce(): lax.ppermute(send_right, axis, [(j, j + 1) for j in range(0, min(step, co...  10.7 us
    all_to_all x2, waiting for transfers between devices, local_part(): lax.all_to_all(beacon_grads.reshape(ctx_axis, per_shard, 2 * kv_width), '...  10.2 us
    ppermute x6, waiting for transfers between devices, head_reduce(): lax.ppermute(send_right, axis, [(j, j + 1) for j in range(0, min(step, co...  9.52 us
    all_to_all x2, starting transfers between devices, local_part(): lax.all_to_all(jnp.broadcast_to(own_beacon_rows[None], (ctx_axis,) + own_...  9.23 us
  transfers between devices with their start and end apart: 28, of which 9 were waited for; matrix products, arithmetic and copies ran while one was open for 21% of the time, Pallas kernels for 14%

profile of v9, /device:TPU:10, one launch (start us, length us, event | category | flops | bytes accessed | tf_op | source)
XLA Modules:
  0.0 176.7 jit_solution(4457012189721816129)
XLA Ops:
  2.7 3.5 %collective-permute-start = (bf16[128,1024]{1,0:T(8,128)(2,1)S(1)}, bf16[128,1024]{1,0:T(8,128)(2,1)S(1)}, u32[]{:S(2)}, u32[]{:S(2)}) collective-permute-start(bf16[128,1024]{1,0:T(8,128)(2,1)S(1)} %pad_maximum_fusion.2), channel_id=1, source_target_pairs={{0,1},{1,2},{2,3},{4,5},{5,6},{6,7},{8,9},{9,10},{10,11},{12,13},{... | collective-permute-start | bytes 786440 | tf_op jit(solution)/shard_map/ppermute | solution.py:98
  6.1 2.4 %collective-permute-start.3 = (bf16[128,1024]{1,0:T(8,128)(2,1)S(1)}, bf16[128,1024]{1,0:T(8,128)(2,1)S(1)}, u32[]{:S(2)}, u32[]{:S(2)}) collective-permute-start(bf16[128,1024]{1,0:T(8,128)(2,1)S(1)} %pad_maximum_fusion.2), channel_id=1, source_target_pairs={{1,0},{2,1},{3,2},{5,4},{6,5},{7,6},{9,8},{10,9},{11,10},{13,12},{... | collective-permute-start | bytes 786440 | tf_op jit(solution)/shard_map/ppermute | solution.py:101
  8.6 3.5 %collective-permute-start.6 = (bf16[128,1024]{1,0:T(8,128)(2,1)S(1)}, bf16[128,1024]{1,0:T(8,128)(2,1)S(1)}, u32[]{:S(2)}, u32[]{:S(2)}) collective-permute-start(bf16[128,1024]{1,0:T(8,128)(2,1)S(1)} %pad_maximum_fusion.3), channel_id=1, source_target_pairs={{0,1},{1,2},{2,3},{4,5},{5,6},{6,7},{8,9},{9,10},{10,11},{12,13},{... | collective-permute-start | bytes 786440 | tf_op jit(solution)/shard_map/ppermute | solution.py:98
  12.0 2.4 %collective-permute-start.9 = (bf16[128,1024]{1,0:T(8,128)(2,1)S(1)}, bf16[128,1024]{1,0:T(8,128)(2,1)S(1)}, u32[]{:S(2)}, u32[]{:S(2)}) collective-permute-start(bf16[128,1024]{1,0:T(8,128)(2,1)S(1)} %pad_maximum_fusion.3), channel_id=1, source_target_pairs={{1,0},{2,1},{3,2},{5,4},{6,5},{7,6},{9,8},{10,9},{11,10},{13,12},{... | collective-permute-start | bytes 786440 | tf_op jit(solution)/shard_map/ppermute | solution.py:101
  15.2 3.5 %collective-permute-start.1 = (bf16[128,1024]{1,0:T(8,128)(2,1)S(1)}, bf16[128,1024]{1,0:T(8,128)(2,1)S(1)}, u32[]{:S(2)}, u32[]{:S(2)}) collective-permute-start(bf16[128,1024]{1,0:T(8,128)(2,1)S(1)} %collective-permute-done), channel_id=1, source_target_pairs={{1,2},{2,3},{5,6},{6,7},{9,10},{10,11},{13,14},{14,15},{17,18},{18... | collective-permute-start | bytes 786440 | tf_op jit(solution)/shard_map/ppermute | solution.py:98
  21.4 3.9 %collective-permute-start.7 = (bf16[128,1024]{1,0:T(8,128)(2,1)S(1)}, bf16[128,1024]{1,0:T(8,128)(2,1)S(1)}, u32[]{:S(2)}, u32[]{:S(2)}) collective-permute-start(bf16[128,1024]{1,0:T(8,128)(2,1)S(1)} %collective-permute-done.6), channel_id=1, source_target_pairs={{1,2},{2,3},{5,6},{6,7},{9,10},{10,11},{13,14},{14,15},{17,18},{18... | collective-permute-start | bytes 786440 | tf_op jit(solution)/shard_map/ppermute | solution.py:98
  31.1 2.9 %collective-permute-done.10 = bf16[128,1024]{1,0:T(8,128)(2,1)S(1)} collective-permute-done((bf16[128,1024]{1,0:T(8,128)(2,1)S(1)}, bf16[128,1024]{1,0:T(8,128)(2,1)S(1)}, u32[]{:S(2)}, u32[]{:S(2)}) %collective-permute-start.10) | collective-permute-done | bytes 262176 | tf_op jit(solution)/shard_map/ppermute | solution.py:101
  34.0 4.4 %collective-permute-start.11 = (bf16[128,1024]{1,0:T(8,128)(2,1)S(1)}, bf16[128,1024]{1,0:T(8,128)(2,1)S(1)}, u32[]{:S(2)}, u32[]{:S(2)}) collective-permute-start(bf16[128,1024]{1,0:T(8,128)(2,1)S(1)} %collective-permute-done.10), channel_id=1, source_target_pairs={{1,0},{5,4},{9,8},{13,12},{17,16},{21,20},{25,24},{29,28}} | collective-permute-start | bytes 786440 | tf_op jit(solution)/shard_map/ppermute | solution.py:101
  45.3 4.3 %all-to-all-start = ((bf16[8,64,1024]{2,1,0:T(8,128)(2,1)}), bf16[8,64,1024]{2,1,0:T(8,128)(2,1)S(1)}, u32[]{:S(2)}, u32[]{:S(2)}) async-start(bf16[8,64,1024]{2,1,0:T(8,128)(2,1)} %broadcast_in_dim.4), calls=%async_computation | async-start | bytes 2097152 | tf_op jit(solution)/shard_map/all_to_all | solution.py:133
  55.3 8.1 %all-to-all-done = bf16[8,64,1024]{2,1,0:T(8,128)(2,1)S(1)} async-done(((bf16[8,64,1024]{2,1,0:T(8,128)(2,1)}), bf16[8,64,1024]{2,1,0:T(8,128)(2,1)S(1)}, u32[]{:S(2)}, u32[]{:S(2)}) %all-to-all-start) | async-done | bytes 1048608 | tf_op jit(solution)/shard_map/all_to_all | solution.py:133
  64.7 5.0 %all-to-all-start.1 = ((bf16[8,64,1024]{2,1,0:T(8,128)(2,1)}), bf16[8,64,1024]{2,1,0:T(8,128)(2,1)S(1)}, u32[]{:S(2)}, u32[]{:S(2)}) async-start(bf16[8,64,1024]{2,1,0:T(8,128)(2,1)} %broadcast_in_dim.5), calls=%async_computation.1 | async-start | bytes 2097152 | tf_op jit(solution)/shard_map/all_to_all | solution.py:133
  70.3 2.9 %fusion.2 = (bf16[128,2048]{1,0:T(8,128)(2,1)}, bf16[128,2048]{1,0:T(8,128)(2,1)}, bf16[128,2048]{1,0:T(8,128)(2,1)}, bf16[128,2048]{1,0:T(8,128)(2,1)}) fusion(bf16[128,4096]{1,0:T(8,128)(2,1)} %param.8, bf16[128,4096]{1,0:T(8,128)(2,1)} %param.5), kind=kLoop, calls=%fused_computation.50 | loop fusion | bytes 4194304 | tf_op jit(solution)/shard_map/slice | solution.py:167
  73.2 12.2 %shard_map.84 = (f32[512,1024]{1,0:T(8,128)}, bf16[512,1024]{1,0:T(8,128)(2,1)}, bf16[128,2048]{1,0:T(8,128)(2,1)}, bf16[128,2048]{1,0:T(8,128)(2,1)}) custom-call(s32[2]{0:T(128)} %pad_add_fusion.ids_ref, bf16[128,2048]{1,0:T(8,128)(2,1)} %get-tuple-element.47.q_ref, bf16[128,2048]{1,0:T(8,128)(2,1)} %get-tuple-element.32.g_ref, ...), custom_call_target="tpu_custom_call" | custom-call | tf_op jit(solution)/shard_map/pallas_call | solution.py:76
  85.4 4.2 %all-to-all-start.2 = ((bf16[8,64,1024]{2,1,0:T(8,128)(2,1)}), bf16[8,64,1024]{2,1,0:T(8,128)(2,1)}, u32[]{:S(2)}, u32[]{:S(2)}) async-start(bf16[8,64,1024]{2,1,0:T(8,128)(2,1)} %bitcast.57), calls=%async_computation.2 | async-start | bytes 2097152 | tf_op jit(solution)/shard_map/all_to_all | solution.py:140
  89.6 12.2 %shard_map.85 = (f32[512,1024]{1,0:T(8,128)}, bf16[512,1024]{1,0:T(8,128)(2,1)}, bf16[128,2048]{1,0:T(8,128)(2,1)}, bf16[128,2048]{1,0:T(8,128)(2,1)}) custom-call(s32[2]{0:T(128)} %pad_add_fusion.ids_ref, bf16[128,2048]{1,0:T(8,128)(2,1)} %get-tuple-element.46.q_ref, bf16[128,2048]{1,0:T(8,128)(2,1)} %get-tuple-element.33.g_ref, ...), custom_call_target="tpu_custom_call" | custom-call | tf_op jit(solution)/shard_map/pallas_call | solution.py:76
  103.7 5.0 %all-to-all-start.3 = ((bf16[8,64,1024]{2,1,0:T(8,128)(2,1)}), bf16[8,64,1024]{2,1,0:T(8,128)(2,1)S(1)}, u32[]{:S(2)}, u32[]{:S(2)}) async-start(bf16[8,64,1024]{2,1,0:T(8,128)(2,1)} %bitcast.56), calls=%async_computation.3 | async-start | bytes 2097152 | tf_op jit(solution)/shard_map/all_to_all | solution.py:140
  114.2 8.3 %all-to-all-done.3 = bf16[8,64,1024]{2,1,0:T(8,128)(2,1)S(1)} async-done(((bf16[8,64,1024]{2,1,0:T(8,128)(2,1)}), bf16[8,64,1024]{2,1,0:T(8,128)(2,1)S(1)}, u32[]{:S(2)}, u32[]{:S(2)}) %all-to-all-start.3) | async-done | bytes 1048608 | tf_op jit(solution)/shard_map/all_to_all | solution.py:140
  122.7 4.0 %scatter_fusion.1 = f32[512,1024]{1,0:T(8,128)} fusion(f32[512,1024]{1,0:T(8,128)} %get-tuple-element.18, s32[64]{0:T(128)S(1)} %fusion, f32[64,1024]{1,0:T(8,128)S(1)} %convert_reduce_fusion), kind=kCustom, calls=%fused_computation.5 | custom fusion | flops 65536 | bytes 786688 | tf_op jit(solution)/shard_map/scatter-add | solution.py:144
  138.4 2.6 %collective-permute-done.15 = bf16[128,1024]{1,0:T(8,128)(2,1)} collective-permute-done((bf16[128,1024]{1,0:T(8,128)(2,1)}, bf16[128,1024]{1,0:T(8,128)(2,1)}, u32[]{:S(2)}, u32[]{:S(2)}) %collective-permute-start.15) | collective-permute-done | bytes 262176 | tf_op jit(solution)/shard_map/ppermute | solution.py:122
  141.0 3.5 %collective-permute-done.13 = bf16[128,1024]{1,0:T(8,128)(2,1)} collective-permute-done((bf16[128,1024]{1,0:T(8,128)(2,1)}, bf16[128,1024]{1,0:T(8,128)(2,1)}, u32[]{:S(2)}, u32[]{:S(2)}) %collective-permute-start.13) | collective-permute-done | bytes 262176 | tf_op jit(solution)/shard_map/ppermute | solution.py:121
  148.7 4.1 %collective-permute-start.14 = (bf16[128,1024]{1,0:T(8,128)(2,1)S(1)}, bf16[128,1024]{1,0:T(8,128)(2,1)S(1)}, u32[]{:S(2)}, u32[]{:S(2)}) collective-permute-start(bf16[128,1024]{1,0:T(8,128)(2,1)S(1)} %get-tuple-element.24), channel_id=1, source_target_pairs={{1,0},{2,1},{3,2},{5,4},{6,5},{7,6},{9,8},{10,9},{11,10},{13,12},{... | collective-permute-start | bytes 786440 | tf_op jit(solution)/shard_map/ppermute | solution.py:121
  158.7 3.9 %collective-permute-start.20 = (bf16[128,1024]{1,0:T(8,128)(2,1)}, bf16[128,1024]{1,0:T(8,128)(2,1)S(1)}, u32[]{:S(2)}, u32[]{:S(2)}) collective-permute-start(bf16[128,1024]{1,0:T(8,128)(2,1)} %get-tuple-element.28), channel_id=1, source_target_pairs={{1,0},{2,1},{3,2},{5,4},{6,5},{7,6},{9,8},{10,9},{11,10},{13,12},{... | collective-permute-start | bytes 786440 | tf_op jit(solution)/shard_map/ppermute | solution.py:121
  164.4 2.4 %collective-permute-start.23 = (bf16[128,1024]{1,0:T(8,128)(2,1)S(1)}, bf16[128,1024]{1,0:T(8,128)(2,1)S(1)}, u32[]{:S(2)}, u32[]{:S(2)}) collective-permute-start(bf16[128,1024]{1,0:T(8,128)(2,1)S(1)} %add_convert_fusion.1), channel_id=1, source_target_pairs={{0,1},{1,2},{2,3},{4,5},{5,6},{6,7},{8,9},{9,10},{10,11},{12,13},{... | collective-permute-start | bytes 786440 | tf_op jit(solution)/shard_map/ppermute | solution.py:122
  169.9 2.8 %collective-permute-done.23 = bf16[128,1024]{1,0:T(8,128)(2,1)S(1)} collective-permute-done((bf16[128,1024]{1,0:T(8,128)(2,1)S(1)}, bf16[128,1024]{1,0:T(8,128)(2,1)S(1)}, u32[]{:S(2)}, u32[]{:S(2)}) %collective-permute-start.23) | collective-permute-done | bytes 262176 | tf_op jit(solution)/shard_map/ppermute | solution.py:122
  (115 shorter events, 63.6 us)
Async XLA Ops:
  2.7 12.6 %collective-permute-start = (bf16[128,1024]{1,0:T(8,128)(2,1)S(1)}, bf16[128,1024]{1,0:T(8,128)(2,1)S(1)}, u32[]{:S(2)}, u32[]{:S(2)}) collective-permute-start(bf16[128,1024]{1,0:T(8,128)(2,1)S(1)} %pad_maximum_fusion.2), channel_id=1, source_target_pairs={{0,1},{1,2},{2,3},{4,5},{5,6},{6,7},{8,9},{9,10},{10,11},{12,13},{... | collective-permute-start | bytes 786440 | tf_op jit(solution)/shard_map/ppermute | solution.py:98
  6.1 13.3 %collective-permute-start.3 = (bf16[128,1024]{1,0:T(8,128)(2,1)S(1)}, bf16[128,1024]{1,0:T(8,128)(2,1)S(1)}, u32[]{:S(2)}, u32[]{:S(2)}) collective-permute-start(bf16[128,1024]{1,0:T(8,128)(2,1)S(1)} %pad_maximum_fusion.2), channel_id=1, source_target_pairs={{1,0},{2,1},{3,2},{5,4},{6,5},{7,6},{9,8},{10,9},{11,10},{13,12},{... | collective-permute-start | bytes 786440 | tf_op jit(solution)/shard_map/ppermute | solution.py:101
  8.6 12.8 %collective-permute-start.6 = (bf16[128,1024]{1,0:T(8,128)(2,1)S(1)}, bf16[128,1024]{1,0:T(8,128)(2,1)S(1)}, u32[]{:S(2)}, u32[]{:S(2)}) collective-permute-start(bf16[128,1024]{1,0:T(8,128)(2,1)S(1)} %pad_maximum_fusion.3), channel_id=1, source_target_pairs={{0,1},{1,2},{2,3},{4,5},{5,6},{6,7},{8,9},{9,10},{10,11},{12,13},{... | collective-permute-start | bytes 786440 | tf_op jit(solution)/shard_map/ppermute | solution.py:98
  12.0 13.3 %collective-permute-start.9 = (bf16[128,1024]{1,0:T(8,128)(2,1)S(1)}, bf16[128,1024]{1,0:T(8,128)(2,1)S(1)}, u32[]{:S(2)}, u32[]{:S(2)}) collective-permute-start(bf16[128,1024]{1,0:T(8,128)(2,1)S(1)} %pad_maximum_fusion.3), channel_id=1, source_target_pairs={{1,0},{2,1},{3,2},{5,4},{6,5},{7,6},{9,8},{10,9},{11,10},{13,12},{... | collective-permute-start | bytes 786440 | tf_op jit(solution)/shard_map/ppermute | solution.py:101
  15.2 12.1 %collective-permute-start.1 = (bf16[128,1024]{1,0:T(8,128)(2,1)S(1)}, bf16[128,1024]{1,0:T(8,128)(2,1)S(1)}, u32[]{:S(2)}, u32[]{:S(2)}) collective-permute-start(bf16[128,1024]{1,0:T(8,128)(2,1)S(1)} %collective-permute-done), channel_id=1, source_target_pairs={{1,2},{2,3},{5,6},{6,7},{9,10},{10,11},{13,14},{14,15},{17,18},{18... | collective-permute-start | bytes 786440 | tf_op jit(solution)/shard_map/ppermute | solution.py:98
  19.4 9.3 %collective-permute-start.4 = (bf16[128,1024]{1,0:T(8,128)(2,1)S(1)}, bf16[128,1024]{1,0:T(8,128)(2,1)S(1)}, u32[]{:S(2)}, u32[]{:S(2)}) collective-permute-start(bf16[128,1024]{1,0:T(8,128)(2,1)S(1)} %collective-permute-done.3), channel_id=1, source_target_pairs={{1,0},{2,1},{5,4},{6,5},{9,8},{10,9},{13,12},{14,13},{17,16},{18,1... | collective-permute-start | bytes 786440 | tf_op jit(solution)/shard_map/ppermute | solution.py:101
  27.3 11.1 %collective-permute-start.2 = (bf16[128,1024]{1,0:T(8,128)(2,1)S(1)}, bf16[128,1024]{1,0:T(8,128)(2,1)S(1)}, u32[]{:S(2)}, u32[]{:S(2)}) collective-permute-start(bf16[128,1024]{1,0:T(8,128)(2,1)S(1)} %collective-permute-done.1), channel_id=1, source_target_pairs={{2,3},{6,7},{10,11},{14,15},{18,19},{22,23},{26,27},{30,31}} | collective-permute-start | bytes 786440 | tf_op jit(solution)/shard_map/ppermute | solution.py:98
  28.7 11.9 %collective-permute-start.5 = (bf16[128,1024]{1,0:T(8,128)(2,1)S(1)}, bf16[128,1024]{1,0:T(8,128)(2,1)S(1)}, u32[]{:S(2)}, u32[]{:S(2)}) collective-permute-start(bf16[128,1024]{1,0:T(8,128)(2,1)S(1)} %collective-permute-done.4), channel_id=1, source_target_pairs={{1,0},{5,4},{9,8},{13,12},{17,16},{21,20},{25,24},{29,28}} | collective-permute-start | bytes 786440 | tf_op jit(solution)/shard_map/ppermute | solution.py:101
  30.4 19.2 %collective-permute-start.8 = (bf16[128,1024]{1,0:T(8,128)(2,1)S(1)}, bf16[128,1024]{1,0:T(8,128)(2,1)S(1)}, u32[]{:S(2)}, u32[]{:S(2)}) collective-permute-start(bf16[128,1024]{1,0:T(8,128)(2,1)S(1)} %collective-permute-done.7), channel_id=1, source_target_pairs={{2,3},{6,7},{10,11},{14,15},{18,19},{22,23},{26,27},{30,31}} | collective-permute-start | bytes 786440 | tf_op jit(solution)/shard_map/ppermute | solution.py:98
  34.0 17.8 %collective-permute-start.11 = (bf16[128,1024]{1,0:T(8,128)(2,1)S(1)}, bf16[128,1024]{1,0:T(8,128)(2,1)S(1)}, u32[]{:S(2)}, u32[]{:S(2)}) collective-permute-start(bf16[128,1024]{1,0:T(8,128)(2,1)S(1)} %collective-permute-done.10), channel_id=1, source_target_pairs={{1,0},{5,4},{9,8},{13,12},{17,16},{21,20},{25,24},{29,28}} | collective-permute-start | bytes 786440 | tf_op jit(solution)/shard_map/ppermute | solution.py:101
  45.3 18.2 %all-to-all-start = ((bf16[8,64,1024]{2,1,0:T(8,128)(2,1)}), bf16[8,64,1024]{2,1,0:T(8,128)(2,1)S(1)}, u32[]{:S(2)}, u32[]{:S(2)}) async-start(bf16[8,64,1024]{2,1,0:T(8,128)(2,1)} %broadcast_in_dim.4), calls=%async_computation | async-start | bytes 2097152 | tf_op jit(solution)/shard_map/all_to_all | solution.py:133
  64.7 20.6 %all-to-all-start.1 = ((bf16[8,64,1024]{2,1,0:T(8,128)(2,1)}), bf16[8,64,1024]{2,1,0:T(8,128)(2,1)S(1)}, u32[]{:S(2)}, u32[]{:S(2)}) async-start(bf16[8,64,1024]{2,1,0:T(8,128)(2,1)} %broadcast_in_dim.5), calls=%async_computation.1 | async-start | bytes 2097152 | tf_op jit(solution)/shard_map/all_to_all | solution.py:133
  85.4 18.3 %all-to-all-start.2 = ((bf16[8,64,1024]{2,1,0:T(8,128)(2,1)}), bf16[8,64,1024]{2,1,0:T(8,128)(2,1)}, u32[]{:S(2)}, u32[]{:S(2)}) async-start(bf16[8,64,1024]{2,1,0:T(8,128)(2,1)} %bitcast.57), calls=%async_computation.2 | async-start | bytes 2097152 | tf_op jit(solution)/shard_map/all_to_all | solution.py:140
  103.7 18.9 %all-to-all-start.3 = ((bf16[8,64,1024]{2,1,0:T(8,128)(2,1)}), bf16[8,64,1024]{2,1,0:T(8,128)(2,1)S(1)}, u32[]{:S(2)}, u32[]{:S(2)}) async-start(bf16[8,64,1024]{2,1,0:T(8,128)(2,1)} %bitcast.56), calls=%async_computation.3 | async-start | bytes 2097152 | tf_op jit(solution)/shard_map/all_to_all | solution.py:140
  112.8 18.5 %collective-permute-start.12 = (bf16[128,1024]{1,0:T(8,128)(2,1)}, bf16[128,1024]{1,0:T(8,128)(2,1)}, u32[]{:S(2)}, u32[]{:S(2)}) collective-permute-start(bf16[128,1024]{1,0:T(8,128)(2,1)} %get-tuple-element.26), channel_id=1, source_target_pairs={{3,2},{7,6},{11,10},{15,14},{19,18},{23,22},{27,26},{31,30}} | collective-permute-start | bytes 786440 | tf_op jit(solution)/shard_map/ppermute | solution.py:121
  130.0 11.0 %collective-permute-start.15 = (bf16[128,1024]{1,0:T(8,128)(2,1)}, bf16[128,1024]{1,0:T(8,128)(2,1)}, u32[]{:S(2)}, u32[]{:S(2)}) collective-permute-start(bf16[128,1024]{1,0:T(8,128)(2,1)} %get-tuple-element.27), channel_id=1, source_target_pairs={{0,1},{4,5},{8,9},{12,13},{16,17},{20,21},{24,25},{28,29}} | collective-permute-start | bytes 786440 | tf_op jit(solution)/shard_map/ppermute | solution.py:122
  133.0 11.5 %collective-permute-start.13 = (bf16[128,1024]{1,0:T(8,128)(2,1)}, bf16[128,1024]{1,0:T(8,128)(2,1)}, u32[]{:S(2)}, u32[]{:S(2)}) collective-permute-start(bf16[128,1024]{1,0:T(8,128)(2,1)} %add_convert_fusion.9), channel_id=1, source_target_pairs={{2,1},{3,2},{6,5},{7,6},{10,9},{11,10},{14,13},{15,14},{18,17},{19... | collective-permute-start | bytes 786440 | tf_op jit(solution)/shard_map/ppermute | solution.py:121
  134.5 18.3 %collective-permute-start.21 = (bf16[128,1024]{1,0:T(8,128)(2,1)S(1)}, bf16[128,1024]{1,0:T(8,128)(2,1)S(1)}, u32[]{:S(2)}, u32[]{:S(2)}) collective-permute-start(bf16[128,1024]{1,0:T(8,128)(2,1)S(1)} %get-tuple-element.31), channel_id=1, source_target_pairs={{0,1},{4,5},{8,9},{12,13},{16,17},{20,21},{24,25},{28,29}} | collective-permute-start | bytes 786440 | tf_op jit(solution)/shard_map/ppermute | solution.py:122
  137.0 15.8 %collective-permute-start.19 = (bf16[128,1024]{1,0:T(8,128)(2,1)S(1)}, bf16[128,1024]{1,0:T(8,128)(2,1)S(1)}, u32[]{:S(2)}, u32[]{:S(2)}) collective-permute-start(bf16[128,1024]{1,0:T(8,128)(2,1)S(1)} %add_convert_fusion.4), channel_id=1, source_target_pairs={{2,1},{3,2},{6,5},{7,6},{10,9},{11,10},{14,13},{15,14},{18,17},{19... | collective-permute-start | bytes 786440 | tf_op jit(solution)/shard_map/ppermute | solution.py:121
  145.7 9.9 %collective-permute-start.16 = (bf16[128,1024]{1,0:T(8,128)(2,1)S(1)}, bf16[128,1024]{1,0:T(8,128)(2,1)S(1)}, u32[]{:S(2)}, u32[]{:S(2)}) collective-permute-start(bf16[128,1024]{1,0:T(8,128)(2,1)S(1)} %get-tuple-element.25), channel_id=1, source_target_pairs={{0,1},{1,2},{4,5},{5,6},{8,9},{9,10},{12,13},{13,14},{16,17},{17,1... | collective-permute-start | bytes 786440 | tf_op jit(solution)/shard_map/ppermute | solution.py:122
  148.7 18.1 %collective-permute-start.14 = (bf16[128,1024]{1,0:T(8,128)(2,1)S(1)}, bf16[128,1024]{1,0:T(8,128)(2,1)S(1)}, u32[]{:S(2)}, u32[]{:S(2)}) collective-permute-start(bf16[128,1024]{1,0:T(8,128)(2,1)S(1)} %get-tuple-element.24), channel_id=1, source_target_pairs={{1,0},{2,1},{3,2},{5,4},{6,5},{7,6},{9,8},{10,9},{11,10},{13,12},{... | collective-permute-start | bytes 786440 | tf_op jit(solution)/shard_map/ppermute | solution.py:121
  153.7 10.7 %collective-permute-start.22 = (bf16[128,1024]{1,0:T(8,128)(2,1)S(1)}, bf16[128,1024]{1,0:T(8,128)(2,1)S(1)}, u32[]{:S(2)}, u32[]{:S(2)}) collective-permute-start(bf16[128,1024]{1,0:T(8,128)(2,1)S(1)} %get-tuple-element.29), channel_id=1, source_target_pairs={{0,1},{1,2},{4,5},{5,6},{8,9},{9,10},{12,13},{13,14},{16,17},{17,1... | collective-permute-start | bytes 786440 | tf_op jit(solution)/shard_map/ppermute | solution.py:122
  155.7 13.4 %collective-permute-start.17 = (bf16[128,1024]{1,0:T(8,128)(2,1)S(1)}, bf16[128,1024]{1,0:T(8,128)(2,1)S(1)}, u32[]{:S(2)}, u32[]{:S(2)}) collective-permute-start(bf16[128,1024]{1,0:T(8,128)(2,1)S(1)} %add_convert_fusion.6), channel_id=1, source_target_pairs={{0,1},{1,2},{2,3},{4,5},{5,6},{6,7},{8,9},{9,10},{10,11},{12,13},{... | collective-permute-start | bytes 786440 | tf_op jit(solution)/shard_map/ppermute | solution.py:122
  158.7 11.2 %collective-permute-start.20 = (bf16[128,1024]{1,0:T(8,128)(2,1)}, bf16[128,1024]{1,0:T(8,128)(2,1)S(1)}, u32[]{:S(2)}, u32[]{:S(2)}) collective-permute-start(bf16[128,1024]{1,0:T(8,128)(2,1)} %get-tuple-element.28), channel_id=1, source_target_pairs={{1,0},{2,1},{3,2},{5,4},{6,5},{7,6},{9,8},{10,9},{11,10},{13,12},{... | collective-permute-start | bytes 786440 | tf_op jit(solution)/shard_map/ppermute | solution.py:121
  (16 other events, 146.2 us)

commit v10 on v9

--- a/solution.py
+++ b/solution.py
@@ -148,6 +148,7 @@
     return (
         attended_out, query_out,
         own_grads[:, :, 0].reshape(rows, kv_width), own_grads[:, :, 1].reshape(rows, kv_width),
+        kv_window,
     )
 
 
@@ -159,16 +160,21 @@
     q_cols = queries.shape[1] // parts
     kv_cols = keys.shape[1] // parts
     results = []
+    ready = None
     for part in range(parts):
         qs = slice(part * q_cols, (part + 1) * q_cols)
         ks = slice(part * kv_cols, (part + 1) * kv_cols)
+        part_keys, part_values = keys[:, ks], values[:, ks]
+        if ready is not None:
+            ready, part_keys, part_values = lax.optimization_barrier((ready, part_keys, part_values))
         results.append(
             local_part(
-                queries[:, qs], keys[:, ks], values[:, ks], out_grad[:, qs],
+                queries[:, qs], part_keys, part_values, out_grad[:, qs],
                 positions, ids, heads_axis, ctx_axis,
             )
         )
-    return tuple(jnp.concatenate(outs, axis=1) for outs in zip(*results))
+        ready = results[-1][4]
+    return tuple(jnp.concatenate(outs, axis=1) for outs in list(zip(*results))[:4])
 
 
 def solution(mesh):

time: 178 us -> 185 us (1.039)
  waiting for transfers between devices: 34.3 us -> 37.8 us
    ppermute x6, waiting for transfers between devices: 0.02 us -> 8.42 us  [head_gather(): lax.ppermute(from_left[-1], axis, [(j, j + 1) for j in range(step - 1, co...]
    ppermute x6, waiting for transfers between devices: 3.51 us -> 10.5 us  [head_reduce(): lax.ppermute(send_left, axis, [(j, j - 1) for j in range(max(1, count - s...]
    all_to_all x2, waiting for transfers between devices: 10.2 us -> 3.52 us  [local_part(): lax.all_to_all(beacon_grads.reshape(ctx_axis, per_shard, 2 * kv_width), '...]
    all_to_all x2, waiting for transfers between devices: 8.15 us -> 1.52 us  [local_part(): lax.all_to_all(jnp.broadcast_to(own_beacon_rows[None], (ctx_axis,) + own_...]
    ppermute x6, waiting for transfers between devices: 2.93 us -> 8.12 us  [head_gather(): lax.ppermute(from_right[-1], axis, [(j + 1, j) for j in range(count - ste...]
    ppermute x6, starting transfers between devices: 10.7 us -> 15.5 us  [head_reduce(): lax.ppermute(send_right, axis, [(j, j + 1) for j in range(0, min(step, co...]
    ppermute x6, waiting for transfers between devices: 9.52 us -> 5.73 us  [head_reduce(): lax.ppermute(send_right, axis, [(j, j + 1) for j in range(0, min(step, co...]
    unnamed x40 -> x38, local copies, waits for them, and re-layouts: 8.33 us -> 10.3 us
  transfers between devices with their start and end apart: 28 -> 28, of which waited for: 9 -> 14; matrix products, arithmetic and copies ran while one was open for 21% -> 21% of each run, Pallas kernels for 14% -> 13%
where the time goes in v10:
time: 185 us; the launch traced here: 183 us
  starting transfers between devices  73.4 us (40%)
  waiting for transfers between devices  37.8 us (20%)
  local copies, waits for them, and re-layouts  27.8 us (15%)
  Pallas kernels  24.3 us (13%)
  other arithmetic  18.1 us (10%)
    pallas_call x2, Pallas kernels, attend_all(): pl.pallas_call(kernel, grid_spec=pltpu.PrefetchScalarGridSpec(num_scalar_...  24.3 us
    ppermute x6, starting transfers between devices, head_reduce(): lax.ppermute(send_right, axis, [(j, j + 1) for j in range(0, min(step, co...  15.5 us
    ppermute x6, starting transfers between devices, head_gather(): lax.ppermute(from_left[-1], axis, [(j, j + 1) for j in range(step - 1, co...  14.2 us
    ppermute x6, starting transfers between devices, head_gather(): lax.ppermute(from_right[-1], axis, [(j + 1, j) for j in range(count - ste...  13.1 us
    ppermute x6, starting transfers between devices, head_reduce(): lax.ppermute(send_left, axis, [(j, j - 1) for j in range(max(1, count - s...  12.1 us
    ppermute x6, waiting for transfers between devices, head_reduce(): lax.ppermute(send_left, axis, [(j, j - 1) for j in range(max(1, count - s...  10.5 us
    unnamed x38, local copies, waits for them, and re-layouts  10.3 us
    all_to_all x2, starting transfers between devices, local_part(): lax.all_to_all(jnp.broadcast_to(own_beacon_rows[None], (ctx_axis,) + own_...  9.23 us
  transfers between devices with their start and end apart: 28, of which 14 were waited for; matrix products, arithmetic and copies ran while one was open for 21% of the time, Pallas kernels for 13%

profile of v10, /device:TPU:10, one launch (start us, length us, event | category | flops | bytes accessed | tf_op | source)
XLA Modules:
  0.0 182.5 jit_solution(6701282243362945459)
XLA Ops:
  1.8 3.5 %collective-permute-start = (bf16[128,1024]{1,0:T(8,128)(2,1)S(1)}, bf16[128,1024]{1,0:T(8,128)(2,1)S(1)}, u32[]{:S(2)}, u32[]{:S(2)}) collective-permute-start(bf16[128,1024]{1,0:T(8,128)(2,1)S(1)} %pad_maximum_fusion.2), channel_id=1, source_target_pairs={{0,1},{1,2},{2,3},{4,5},{5,6},{6,7},{8,9},{9,10},{10,11},{12,13},{... | collective-permute-start | bytes 786440 | tf_op jit(solution)/shard_map/ppermute | solution.py:98
  7.7 4.1 %collective-permute-done = bf16[128,1024]{1,0:T(8,128)(2,1)S(1)} collective-permute-done((bf16[128,1024]{1,0:T(8,128)(2,1)S(1)}, bf16[128,1024]{1,0:T(8,128)(2,1)S(1)}, u32[]{:S(2)}, u32[]{:S(2)}) %collective-permute-start) | collective-permute-done | bytes 262176 | tf_op jit(solution)/shard_map/ppermute | solution.py:98
  11.7 3.5 %collective-permute-start.1 = (bf16[128,1024]{1,0:T(8,128)(2,1)S(1)}, bf16[128,1024]{1,0:T(8,128)(2,1)S(1)}, u32[]{:S(2)}, u32[]{:S(2)}) collective-permute-start(bf16[128,1024]{1,0:T(8,128)(2,1)S(1)} %collective-permute-done), channel_id=1, source_target_pairs={{1,2},{2,3},{5,6},{6,7},{9,10},{10,11},{13,14},{14,15},{17,18},{18... | collective-permute-start | bytes 786440 | tf_op jit(solution)/shard_map/ppermute | solution.py:98
  21.3 3.5 %collective-permute-done.4 = bf16[128,1024]{1,0:T(8,128)(2,1)S(1)} collective-permute-done((bf16[128,1024]{1,0:T(8,128)(2,1)S(1)}, bf16[128,1024]{1,0:T(8,128)(2,1)S(1)}, u32[]{:S(2)}, u32[]{:S(2)}) %collective-permute-start.4) | collective-permute-done | bytes 262176 | tf_op jit(solution)/shard_map/ppermute | solution.py:101
  33.7 3.0 %collective-permute-start.6 = (bf16[128,1024]{1,0:T(8,128)(2,1)S(1)}, bf16[128,1024]{1,0:T(8,128)(2,1)S(1)}, u32[]{:S(2)}, u32[]{:S(2)}) collective-permute-start(bf16[128,1024]{1,0:T(8,128)(2,1)S(1)} %constant_dynamic-update-slice_fusion), channel_id=1, source_target_pairs={{0,1},{1,2},{2,3},{4,5},{5,6},{6,7},{8,9},{9,10},{10,11},{12,13},{... | collective-permute-start | bytes 786440 | tf_op jit(solution)/shard_map/ppermute | solution.py:98
  36.7 2.9 %collective-permute-start.9 = (bf16[128,1024]{1,0:T(8,128)(2,1)S(1)}, bf16[128,1024]{1,0:T(8,128)(2,1)S(1)}, u32[]{:S(2)}, u32[]{:S(2)}) collective-permute-start(bf16[128,1024]{1,0:T(8,128)(2,1)S(1)} %constant_dynamic-update-slice_fusion), channel_id=1, source_target_pairs={{1,0},{2,1},{3,2},{5,4},{6,5},{7,6},{9,8},{10,9},{11,10},{13,12},{... | collective-permute-start | bytes 786440 | tf_op jit(solution)/shard_map/ppermute | solution.py:101
  42.0 3.0 %collective-permute-start.7 = (bf16[128,1024]{1,0:T(8,128)(2,1)S(1)}, bf16[128,1024]{1,0:T(8,128)(2,1)S(1)}, u32[]{:S(2)}, u32[]{:S(2)}) collective-permute-start(bf16[128,1024]{1,0:T(8,128)(2,1)S(1)} %collective-permute-done.6), channel_id=1, source_target_pairs={{1,2},{2,3},{5,6},{6,7},{9,10},{10,11},{13,14},{14,15},{17,18},{18... | collective-permute-start | bytes 786440 | tf_op jit(solution)/shard_map/ppermute | solution.py:98
  50.4 4.3 %all-to-all-start = ((bf16[8,64,1024]{2,1,0:T(8,128)(2,1)}), bf16[8,64,1024]{2,1,0:T(8,128)(2,1)S(1)}, u32[]{:S(2)}, u32[]{:S(2)}) async-start(bf16[8,64,1024]{2,1,0:T(8,128)(2,1)} %broadcast_in_dim.4), calls=%async_computation | async-start | bytes 2097152 | tf_op jit(solution)/shard_map/all_to_all | solution.py:133
  60.2 3.2 %collective-permute-done.11 = bf16[128,1024]{1,0:T(8,128)(2,1)S(1)} collective-permute-done((bf16[128,1024]{1,0:T(8,128)(2,1)S(1)}, bf16[128,1024]{1,0:T(8,128)(2,1)S(1)}, u32[]{:S(2)}, u32[]{:S(2)}) %collective-permute-start.11) | collective-permute-done | bytes 262176 | tf_op jit(solution)/shard_map/ppermute | solution.py:101
  69.7 5.0 %all-to-all-start.1 = ((bf16[8,64,1024]{2,1,0:T(8,128)(2,1)}), bf16[8,64,1024]{2,1,0:T(8,128)(2,1)S(1)}, u32[]{:S(2)}, u32[]{:S(2)}) async-start(bf16[8,64,1024]{2,1,0:T(8,128)(2,1)} %broadcast_in_dim.5), calls=%async_computation.1 | async-start | bytes 2097152 | tf_op jit(solution)/shard_map/all_to_all | solution.py:133
  75.3 2.9 %fusion.2 = (bf16[128,2048]{1,0:T(8,128)(2,1)}, bf16[128,2048]{1,0:T(8,128)(2,1)}, bf16[128,2048]{1,0:T(8,128)(2,1)}, bf16[128,2048]{1,0:T(8,128)(2,1)}) fusion(bf16[128,4096]{1,0:T(8,128)(2,1)} %param.8, bf16[128,4096]{1,0:T(8,128)(2,1)} %param.5), kind=kLoop, calls=%fused_computation.51 | loop fusion | bytes 4194304 | tf_op jit(solution)/shard_map/slice | solution.py:172
  78.2 12.1 %shard_map.84 = (f32[512,1024]{1,0:T(8,128)}, bf16[512,1024]{1,0:T(8,128)(2,1)}, bf16[128,2048]{1,0:T(8,128)(2,1)}, bf16[128,2048]{1,0:T(8,128)(2,1)}) custom-call(s32[2]{0:T(128)} %pad_add_fusion.ids_ref, bf16[128,2048]{1,0:T(8,128)(2,1)} %get-tuple-element.51.q_ref, bf16[128,2048]{1,0:T(8,128)(2,1)} %get-tuple-element.36.g_ref, ...), custom_call_target="tpu_custom_call" | custom-call | tf_op jit(solution)/shard_map/pallas_call | solution.py:76
  90.4 4.2 %all-to-all-start.2 = ((bf16[8,64,1024]{2,1,0:T(8,128)(2,1)}), bf16[8,64,1024]{2,1,0:T(8,128)(2,1)S(1)}, u32[]{:S(2)}, u32[]{:S(2)}) async-start(bf16[8,64,1024]{2,1,0:T(8,128)(2,1)} %bitcast.57), calls=%async_computation.2 | async-start | bytes 2097152 | tf_op jit(solution)/shard_map/all_to_all | solution.py:140
  94.6 12.2 %shard_map.85 = (f32[512,1024]{1,0:T(8,128)}, bf16[512,1024]{1,0:T(8,128)(2,1)}, bf16[128,2048]{1,0:T(8,128)(2,1)}, bf16[128,2048]{1,0:T(8,128)(2,1)}) custom-call(s32[2]{0:T(128)} %pad_add_fusion.ids_ref, bf16[128,2048]{1,0:T(8,128)(2,1)} %get-tuple-element.50.q_ref, bf16[128,2048]{1,0:T(8,128)(2,1)} %get-tuple-element.37.g_ref, ...), custom_call_target="tpu_custom_call" | custom-call | tf_op jit(solution)/shard_map/pallas_call | solution.py:76
  108.5 5.0 %all-to-all-start.3 = ((bf16[8,64,1024]{2,1,0:T(8,128)(2,1)}), bf16[8,64,1024]{2,1,0:T(8,128)(2,1)S(1)}, u32[]{:S(2)}, u32[]{:S(2)}) async-start(bf16[8,64,1024]{2,1,0:T(8,128)(2,1)} %bitcast.56), calls=%async_computation.3 | async-start | bytes 2097152 | tf_op jit(solution)/shard_map/all_to_all | solution.py:140
  113.7 4.0 %scatter_fusion = f32[512,1024]{1,0:T(8,128)} fusion(f32[512,1024]{1,0:T(8,128)} %get-tuple-element.20, s32[64]{0:T(128)S(1)} %fusion, f32[64,1024]{1,0:T(8,128)S(1)} %convert_reduce_fusion.1), kind=kCustom, calls=%fused_computation.4 | custom fusion | flops 65536 | bytes 786688 | tf_op jit(solution)/shard_map/scatter-add | solution.py:144
  131.8 9.8 %collective-permute-done.13 = bf16[128,1024]{1,0:T(8,128)(2,1)} collective-permute-done((bf16[128,1024]{1,0:T(8,128)(2,1)}, bf16[128,1024]{1,0:T(8,128)(2,1)}, u32[]{:S(2)}, u32[]{:S(2)}) %collective-permute-start.13) | collective-permute-done | bytes 262176 | tf_op jit(solution)/shard_map/ppermute | solution.py:121
  143.1 4.2 %collective-permute-start.16 = (bf16[128,1024]{1,0:T(8,128)(2,1)S(1)}, bf16[128,1024]{1,0:T(8,128)(2,1)S(1)}, u32[]{:S(2)}, u32[]{:S(2)}) collective-permute-start(bf16[128,1024]{1,0:T(8,128)(2,1)S(1)} %get-tuple-element.29), channel_id=1, source_target_pairs={{0,1},{1,2},{4,5},{5,6},{8,9},{9,10},{12,13},{13,14},{16,17},{17,1... | collective-permute-start | bytes 786440 | tf_op jit(solution)/shard_map/ppermute | solution.py:122
  152.0 4.1 %collective-permute-start.14 = (bf16[128,1024]{1,0:T(8,128)(2,1)S(1)}, bf16[128,1024]{1,0:T(8,128)(2,1)S(1)}, u32[]{:S(2)}, u32[]{:S(2)}) collective-permute-start(bf16[128,1024]{1,0:T(8,128)(2,1)S(1)} %get-tuple-element.28), channel_id=1, source_target_pairs={{1,0},{2,1},{3,2},{5,4},{6,5},{7,6},{9,8},{10,9},{11,10},{13,12},{... | collective-permute-start | bytes 786440 | tf_op jit(solution)/shard_map/ppermute | solution.py:121
  157.2 2.5 %collective-permute-start.17 = (bf16[128,1024]{1,0:T(8,128)(2,1)S(1)}, bf16[128,1024]{1,0:T(8,128)(2,1)S(1)}, u32[]{:S(2)}, u32[]{:S(2)}) collective-permute-start(bf16[128,1024]{1,0:T(8,128)(2,1)S(1)} %add_convert_fusion.6), channel_id=1, source_target_pairs={{0,1},{1,2},{2,3},{4,5},{5,6},{6,7},{8,9},{9,10},{10,11},{12,13},{... | collective-permute-start | bytes 786440 | tf_op jit(solution)/shard_map/ppermute | solution.py:122
  161.3 3.2 %collective-permute-start.22 = (bf16[128,1024]{1,0:T(8,128)(2,1)S(1)}, bf16[128,1024]{1,0:T(8,128)(2,1)S(1)}, u32[]{:S(2)}, u32[]{:S(2)}) collective-permute-start(bf16[128,1024]{1,0:T(8,128)(2,1)S(1)} %get-tuple-element.33), channel_id=1, source_target_pairs={{0,1},{1,2},{4,5},{5,6},{8,9},{9,10},{12,13},{13,14},{16,17},{17,1... | collective-permute-start | bytes 786440 | tf_op jit(solution)/shard_map/ppermute | solution.py:122
  165.6 2.6 %collective-permute-start.20 = (bf16[128,1024]{1,0:T(8,128)(2,1)}, bf16[128,1024]{1,0:T(8,128)(2,1)S(1)}, u32[]{:S(2)}, u32[]{:S(2)}) collective-permute-start(bf16[128,1024]{1,0:T(8,128)(2,1)} %get-tuple-element.32), channel_id=1, source_target_pairs={{1,0},{2,1},{3,2},{5,4},{6,5},{7,6},{9,8},{10,9},{11,10},{13,12},{... | collective-permute-start | bytes 786440 | tf_op jit(solution)/shard_map/ppermute | solution.py:121
  171.3 3.0 %collective-permute-start.23 = (bf16[128,1024]{1,0:T(8,128)(2,1)}, bf16[128,1024]{1,0:T(8,128)(2,1)S(1)}, u32[]{:S(2)}, u32[]{:S(2)}) collective-permute-start(bf16[128,1024]{1,0:T(8,128)(2,1)} %add_convert_fusion.1), channel_id=1, source_target_pairs={{0,1},{1,2},{2,3},{4,5},{5,6},{6,7},{8,9},{9,10},{10,11},{12,13},{... | collective-permute-start | bytes 786440 | tf_op jit(solution)/shard_map/ppermute | solution.py:122
  176.4 3.4 %collective-permute-done.23 = bf16[128,1024]{1,0:T(8,128)(2,1)S(1)} collective-permute-done((bf16[128,1024]{1,0:T(8,128)(2,1)}, bf16[128,1024]{1,0:T(8,128)(2,1)S(1)}, u32[]{:S(2)}, u32[]{:S(2)}) %collective-permute-start.23) | collective-permute-done | bytes 262176 | tf_op jit(solution)/shard_map/ppermute | solution.py:122
  (112 shorter events, 72.4 us)
Async XLA Ops:
  1.8 9.9 %collective-permute-start = (bf16[128,1024]{1,0:T(8,128)(2,1)S(1)}, bf16[128,1024]{1,0:T(8,128)(2,1)S(1)}, u32[]{:S(2)}, u32[]{:S(2)}) collective-permute-start(bf16[128,1024]{1,0:T(8,128)(2,1)S(1)} %pad_maximum_fusion.2), channel_id=1, source_target_pairs={{0,1},{1,2},{2,3},{4,5},{5,6},{6,7},{8,9},{9,10},{10,11},{12,13},{... | collective-permute-start | bytes 786440 | tf_op jit(solution)/shard_map/ppermute | solution.py:98
  5.3 10.7 %collective-permute-start.3 = (bf16[128,1024]{1,0:T(8,128)(2,1)S(1)}, bf16[128,1024]{1,0:T(8,128)(2,1)S(1)}, u32[]{:S(2)}, u32[]{:S(2)}) collective-permute-start(bf16[128,1024]{1,0:T(8,128)(2,1)S(1)} %pad_maximum_fusion.2), channel_id=1, source_target_pairs={{1,0},{2,1},{3,2},{5,4},{6,5},{7,6},{9,8},{10,9},{11,10},{13,12},{... | collective-permute-start | bytes 786440 | tf_op jit(solution)/shard_map/ppermute | solution.py:101
  11.7 8.2 %collective-permute-start.1 = (bf16[128,1024]{1,0:T(8,128)(2,1)S(1)}, bf16[128,1024]{1,0:T(8,128)(2,1)S(1)}, u32[]{:S(2)}, u32[]{:S(2)}) collective-permute-start(bf16[128,1024]{1,0:T(8,128)(2,1)S(1)} %collective-permute-done), channel_id=1, source_target_pairs={{1,2},{2,3},{5,6},{6,7},{9,10},{10,11},{13,14},{14,15},{17,18},{18... | collective-permute-start | bytes 786440 | tf_op jit(solution)/shard_map/ppermute | solution.py:98
  16.0 8.8 %collective-permute-start.4 = (bf16[128,1024]{1,0:T(8,128)(2,1)S(1)}, bf16[128,1024]{1,0:T(8,128)(2,1)S(1)}, u32[]{:S(2)}, u32[]{:S(2)}) collective-permute-start(bf16[128,1024]{1,0:T(8,128)(2,1)S(1)} %collective-permute-done.3), channel_id=1, source_target_pairs={{1,0},{2,1},{5,4},{6,5},{9,8},{10,9},{13,12},{14,13},{17,16},{18,1... | collective-permute-start | bytes 786440 | tf_op jit(solution)/shard_map/ppermute | solution.py:101
  19.9 7.8 %collective-permute-start.2 = (bf16[128,1024]{1,0:T(8,128)(2,1)S(1)}, bf16[128,1024]{1,0:T(8,128)(2,1)S(1)}, u32[]{:S(2)}, u32[]{:S(2)}) collective-permute-start(bf16[128,1024]{1,0:T(8,128)(2,1)S(1)} %collective-permute-done.1), channel_id=1, source_target_pairs={{2,3},{6,7},{10,11},{14,15},{18,19},{22,23},{26,27},{30,31}} | collective-permute-start | bytes 786440 | tf_op jit(solution)/shard_map/ppermute | solution.py:98
  33.7 8.3 %collective-permute-start.6 = (bf16[128,1024]{1,0:T(8,128)(2,1)S(1)}, bf16[128,1024]{1,0:T(8,128)(2,1)S(1)}, u32[]{:S(2)}, u32[]{:S(2)}) collective-permute-start(bf16[128,1024]{1,0:T(8,128)(2,1)S(1)} %constant_dynamic-update-slice_fusion), channel_id=1, source_target_pairs={{0,1},{1,2},{2,3},{4,5},{5,6},{6,7},{8,9},{9,10},{10,11},{12,13},{... | collective-permute-start | bytes 786440 | tf_op jit(solution)/shard_map/ppermute | solution.py:98
  36.7 8.7 %collective-permute-start.9 = (bf16[128,1024]{1,0:T(8,128)(2,1)S(1)}, bf16[128,1024]{1,0:T(8,128)(2,1)S(1)}, u32[]{:S(2)}, u32[]{:S(2)}) collective-permute-start(bf16[128,1024]{1,0:T(8,128)(2,1)S(1)} %constant_dynamic-update-slice_fusion), channel_id=1, source_target_pairs={{1,0},{2,1},{3,2},{5,4},{6,5},{7,6},{9,8},{10,9},{11,10},{13,12},{... | collective-permute-start | bytes 786440 | tf_op jit(solution)/shard_map/ppermute | solution.py:101
  42.0 12.7 %collective-permute-start.7 = (bf16[128,1024]{1,0:T(8,128)(2,1)S(1)}, bf16[128,1024]{1,0:T(8,128)(2,1)S(1)}, u32[]{:S(2)}, u32[]{:S(2)}) collective-permute-start(bf16[128,1024]{1,0:T(8,128)(2,1)S(1)} %collective-permute-done.6), channel_id=1, source_target_pairs={{1,2},{2,3},{5,6},{6,7},{9,10},{10,11},{13,14},{14,15},{17,18},{18... | collective-permute-start | bytes 786440 | tf_op jit(solution)/shard_map/ppermute | solution.py:98
  45.4 10.6 %collective-permute-start.10 = (bf16[128,1024]{1,0:T(8,128)(2,1)S(1)}, bf16[128,1024]{1,0:T(8,128)(2,1)S(1)}, u32[]{:S(2)}, u32[]{:S(2)}) collective-permute-start(bf16[128,1024]{1,0:T(8,128)(2,1)S(1)} %collective-permute-done.9), channel_id=1, source_target_pairs={{1,0},{2,1},{5,4},{6,5},{9,8},{10,9},{13,12},{14,13},{17,16},{18,1... | collective-permute-start | bytes 786440 | tf_op jit(solution)/shard_map/ppermute | solution.py:101
  50.4 18.2 %all-to-all-start = ((bf16[8,64,1024]{2,1,0:T(8,128)(2,1)}), bf16[8,64,1024]{2,1,0:T(8,128)(2,1)S(1)}, u32[]{:S(2)}, u32[]{:S(2)}) async-start(bf16[8,64,1024]{2,1,0:T(8,128)(2,1)} %broadcast_in_dim.4), calls=%async_computation | async-start | bytes 2097152 | tf_op jit(solution)/shard_map/all_to_all | solution.py:133
  69.7 20.6 %all-to-all-start.1 = ((bf16[8,64,1024]{2,1,0:T(8,128)(2,1)}), bf16[8,64,1024]{2,1,0:T(8,128)(2,1)S(1)}, u32[]{:S(2)}, u32[]{:S(2)}) async-start(bf16[8,64,1024]{2,1,0:T(8,128)(2,1)} %broadcast_in_dim.5), calls=%async_computation.1 | async-start | bytes 2097152 | tf_op jit(solution)/shard_map/all_to_all | solution.py:133
  90.4 18.1 %all-to-all-start.2 = ((bf16[8,64,1024]{2,1,0:T(8,128)(2,1)}), bf16[8,64,1024]{2,1,0:T(8,128)(2,1)S(1)}, u32[]{:S(2)}, u32[]{:S(2)}) async-start(bf16[8,64,1024]{2,1,0:T(8,128)(2,1)} %bitcast.57), calls=%async_computation.2 | async-start | bytes 2097152 | tf_op jit(solution)/shard_map/all_to_all | solution.py:140
  108.5 18.9 %all-to-all-start.3 = ((bf16[8,64,1024]{2,1,0:T(8,128)(2,1)}), bf16[8,64,1024]{2,1,0:T(8,128)(2,1)S(1)}, u32[]{:S(2)}, u32[]{:S(2)}) async-start(bf16[8,64,1024]{2,1,0:T(8,128)(2,1)} %bitcast.56), calls=%async_computation.3 | async-start | bytes 2097152 | tf_op jit(solution)/shard_map/all_to_all | solution.py:140
  121.2 10.6 %collective-permute-start.15 = (bf16[128,1024]{1,0:T(8,128)(2,1)}, bf16[128,1024]{1,0:T(8,128)(2,1)}, u32[]{:S(2)}, u32[]{:S(2)}) collective-permute-start(bf16[128,1024]{1,0:T(8,128)(2,1)} %get-tuple-element.31), channel_id=1, source_target_pairs={{0,1},{4,5},{8,9},{12,13},{16,17},{20,21},{24,25},{28,29}} | collective-permute-start | bytes 786440 | tf_op jit(solution)/shard_map/ppermute | solution.py:122
  124.4 17.2 %collective-permute-start.13 = (bf16[128,1024]{1,0:T(8,128)(2,1)}, bf16[128,1024]{1,0:T(8,128)(2,1)}, u32[]{:S(2)}, u32[]{:S(2)}) collective-permute-start(bf16[128,1024]{1,0:T(8,128)(2,1)} %add_convert_fusion.9), channel_id=1, source_target_pairs={{2,1},{3,2},{6,5},{7,6},{10,9},{11,10},{14,13},{15,14},{18,17},{19... | collective-permute-start | bytes 786440 | tf_op jit(solution)/shard_map/ppermute | solution.py:121
  130.3 18.3 %collective-permute-start.18 = (bf16[128,1024]{1,0:T(8,128)(2,1)}, bf16[128,1024]{1,0:T(8,128)(2,1)}, u32[]{:S(2)}, u32[]{:S(2)}) collective-permute-start(bf16[128,1024]{1,0:T(8,128)(2,1)} %get-tuple-element.34), channel_id=1, source_target_pairs={{3,2},{7,6},{11,10},{15,14},{19,18},{23,22},{27,26},{31,30}} | collective-permute-start | bytes 786440 | tf_op jit(solution)/shard_map/ppermute | solution.py:121
  143.1 13.0 %collective-permute-start.16 = (bf16[128,1024]{1,0:T(8,128)(2,1)S(1)}, bf16[128,1024]{1,0:T(8,128)(2,1)S(1)}, u32[]{:S(2)}, u32[]{:S(2)}) collective-permute-start(bf16[128,1024]{1,0:T(8,128)(2,1)S(1)} %get-tuple-element.29), channel_id=1, source_target_pairs={{0,1},{1,2},{4,5},{5,6},{8,9},{9,10},{12,13},{13,14},{16,17},{17,1... | collective-permute-start | bytes 786440 | tf_op jit(solution)/shard_map/ppermute | solution.py:122
  147.3 12.4 %collective-permute-start.21 = (bf16[128,1024]{1,0:T(8,128)(2,1)S(1)}, bf16[128,1024]{1,0:T(8,128)(2,1)S(1)}, u32[]{:S(2)}, u32[]{:S(2)}) collective-permute-start(bf16[128,1024]{1,0:T(8,128)(2,1)S(1)} %get-tuple-element.35), channel_id=1, source_target_pairs={{0,1},{4,5},{8,9},{12,13},{16,17},{20,21},{24,25},{28,29}} | collective-permute-start | bytes 786440 | tf_op jit(solution)/shard_map/ppermute | solution.py:122
  149.6 10.8 %collective-permute-start.19 = (bf16[128,1024]{1,0:T(8,128)(2,1)S(1)}, bf16[128,1024]{1,0:T(8,128)(2,1)S(1)}, u32[]{:S(2)}, u32[]{:S(2)}) collective-permute-start(bf16[128,1024]{1,0:T(8,128)(2,1)S(1)} %add_convert_fusion.4), channel_id=1, source_target_pairs={{2,1},{3,2},{6,5},{7,6},{10,9},{11,10},{14,13},{15,14},{18,17},{19... | collective-permute-start | bytes 786440 | tf_op jit(solution)/shard_map/ppermute | solution.py:121
  152.0 22.4 %collective-permute-start.14 = (bf16[128,1024]{1,0:T(8,128)(2,1)S(1)}, bf16[128,1024]{1,0:T(8,128)(2,1)S(1)}, u32[]{:S(2)}, u32[]{:S(2)}) collective-permute-start(bf16[128,1024]{1,0:T(8,128)(2,1)S(1)} %get-tuple-element.28), channel_id=1, source_target_pairs={{1,0},{2,1},{3,2},{5,4},{6,5},{7,6},{9,8},{10,9},{11,10},{13,12},{... | collective-permute-start | bytes 786440 | tf_op jit(solution)/shard_map/ppermute | solution.py:121
  157.2 17.2 %collective-permute-start.17 = (bf16[128,1024]{1,0:T(8,128)(2,1)S(1)}, bf16[128,1024]{1,0:T(8,128)(2,1)S(1)}, u32[]{:S(2)}, u32[]{:S(2)}) collective-permute-start(bf16[128,1024]{1,0:T(8,128)(2,1)S(1)} %add_convert_fusion.6), channel_id=1, source_target_pairs={{0,1},{1,2},{2,3},{4,5},{5,6},{6,7},{8,9},{9,10},{10,11},{12,13},{... | collective-permute-start | bytes 786440 | tf_op jit(solution)/shard_map/ppermute | solution.py:122
  161.3 9.3 %collective-permute-start.22 = (bf16[128,1024]{1,0:T(8,128)(2,1)S(1)}, bf16[128,1024]{1,0:T(8,128)(2,1)S(1)}, u32[]{:S(2)}, u32[]{:S(2)}) collective-permute-start(bf16[128,1024]{1,0:T(8,128)(2,1)S(1)} %get-tuple-element.33), channel_id=1, source_target_pairs={{0,1},{1,2},{4,5},{5,6},{8,9},{9,10},{12,13},{13,14},{16,17},{17,1... | collective-permute-start | bytes 786440 | tf_op jit(solution)/shard_map/ppermute | solution.py:122
  165.6 10.8 %collective-permute-start.20 = (bf16[128,1024]{1,0:T(8,128)(2,1)}, bf16[128,1024]{1,0:T(8,128)(2,1)S(1)}, u32[]{:S(2)}, u32[]{:S(2)}) collective-permute-start(bf16[128,1024]{1,0:T(8,128)(2,1)} %get-tuple-element.32), channel_id=1, source_target_pairs={{1,0},{2,1},{3,2},{5,4},{6,5},{7,6},{9,8},{10,9},{11,10},{13,12},{... | collective-permute-start | bytes 786440 | tf_op jit(solution)/shard_map/ppermute | solution.py:121
  171.3 8.5 %collective-permute-start.23 = (bf16[128,1024]{1,0:T(8,128)(2,1)}, bf16[128,1024]{1,0:T(8,128)(2,1)S(1)}, u32[]{:S(2)}, u32[]{:S(2)}) collective-permute-start(bf16[128,1024]{1,0:T(8,128)(2,1)} %add_convert_fusion.1), channel_id=1, source_target_pairs={{0,1},{1,2},{2,3},{4,5},{5,6},{6,7},{8,9},{9,10},{10,11},{12,13},{... | collective-permute-start | bytes 786440 | tf_op jit(solution)/shard_map/ppermute | solution.py:122
  (14 other events, 140.5 us)

commit v11 on v9

--- a/solution.py
+++ b/solution.py
@@ -123,7 +123,7 @@
     return block_of(index) + left.astype(jnp.float32) + right.astype(jnp.float32)
 
 
-def local_part(queries, keys, values, out_grad, positions, ids, heads_axis, ctx_axis):
+def local_part(queries, keys, values, out_grad, positions, ids, heads_axis, ctx_axis, offload):
     kv_width = keys.shape[1]
     per_shard = positions.shape[0]
     kv_rows = jnp.concatenate([keys, values], axis=1)
@@ -142,7 +142,12 @@
     )
     own_beacons = jnp.sum(beacon_parts.astype(jnp.float32), axis=0)
     window_grads = window_grads.at[positions].add(own_beacons)
-    own_grads = head_reduce(window_grads, "head", heads_axis).astype(jnp.bfloat16)
+    if offload:
+        own_grads = lax.psum_scatter(
+            window_grads.astype(jnp.bfloat16), "head", scatter_dimension=0, tiled=True
+        )
+    else:
+        own_grads = head_reduce(window_grads, "head", heads_axis).astype(jnp.bfloat16)
     own_grads = own_grads.reshape(own_grads.shape[0], kv_width // HD, 2, HD)
     rows = own_grads.shape[0]
     return (
@@ -165,7 +170,7 @@
         results.append(
             local_part(
                 queries[:, qs], keys[:, ks], values[:, ks], out_grad[:, qs],
-                positions, ids, heads_axis, ctx_axis,
+                positions, ids, heads_axis, ctx_axis, part + 1 < parts,
             )
         )
     return tuple(jnp.concatenate(outs, axis=1) for outs in zip(*results))

time: 178 us -> 190 us (1.067)
  between operations: 1.24 us -> 14.5 us
  starting transfers between devices: 73 us -> 63.8 us
  waiting for transfers between devices: 34.3 us -> 41.3 us
    ppermute x6 -> x3, starting transfers between devices: 13.5 us -> 4.85 us  [head_reduce(): lax.ppermute(send_left, axis, [(j, j - 1) for j in range(max(1, count - s...]
    ppermute x6 -> x3, waiting for transfers between devices: 3.51 us -> 9.04 us  [head_reduce(): lax.ppermute(send_left, axis, [(j, j - 1) for j in range(max(1, count - s...]
    all_to_all x2, waiting for transfers between devices: 10.2 us -> 5.95 us  [local_part(): lax.all_to_all(beacon_grads.reshape(ctx_axis, per_shard, 2 * kv_width), '...]
    ppermute x6, waiting for transfers between devices: 2.93 us -> 6.45 us  [head_gather(): lax.ppermute(from_right[-1], axis, [(j + 1, j) for j in range(count - ste...]
    convert_element_type x0 -> x1, other arithmetic: none -> 2.73 us  [local_part(): window_grads.astype(jnp.bfloat16)]
    convert_element_type x2 -> x1, local copies, waits for them, and re-layouts: 2.86 us -> 0.79 us  [head_reduce(): (block_of(index + step - count) + left.astype(jnp.float32)).astype(jnp.bf...]
    convert_element_type x4 -> x2, other arithmetic: 4.94 us -> 2.89 us  [head_reduce(): (block_of(index + step - count) + left.astype(jnp.float32)).astype(jnp.bf...]
    ppermute x6 -> x3, starting transfers between devices: 10.7 us -> 10.3 us  [head_reduce(): lax.ppermute(send_right, axis, [(j, j + 1) for j in range(0, min(step, co...]
  transfers between devices with their start and end apart: 28 -> 23, of which waited for: 9 -> 12; matrix products, arithmetic and copies ran while one was open for 21% -> 19% of each run, Pallas kernels for 14% -> 13%
where the time goes in v11:
time: 190 us; the launch traced here: 187 us
  starting transfers between devices  63.8 us (34%)
  waiting for transfers between devices  41.3 us (22%)
  local copies, waits for them, and re-layouts  26.3 us (14%)
  Pallas kernels  24.3 us (13%)
  other arithmetic  16.7 us (9%)
  between operations  14.5 us (8%)
    pallas_call x2, Pallas kernels, attend_all(): pl.pallas_call(kernel, grid_spec=pltpu.PrefetchScalarGridSpec(num_scalar_...  24.3 us
    ppermute x6, starting transfers between devices, head_gather(): lax.ppermute(from_left[-1], axis, [(j, j + 1) for j in range(step - 1, co...  15.3 us
    ppermute x6, starting transfers between devices, head_gather(): lax.ppermute(from_right[-1], axis, [(j + 1, j) for j in range(count - ste...  15 us
    ppermute x3, starting transfers between devices, head_reduce(): lax.ppermute(send_right, axis, [(j, j + 1) for j in range(0, min(step, co...  10.3 us
    ppermute x3, waiting for transfers between devices, head_reduce(): lax.ppermute(send_right, axis, [(j, j + 1) for j in range(0, min(step, co...  9.52 us
    all_to_all x2, starting transfers between devices, local_part(): lax.all_to_all(jnp.broadcast_to(own_beacon_rows[None], (ctx_axis,) + own_...  9.23 us
    all_to_all x2, starting transfers between devices, local_part(): lax.all_to_all(beacon_grads.reshape(ctx_axis, per_shard, 2 * kv_width), '...  9.21 us
    unnamed x40, local copies, waits for them, and re-layouts  9.16 us
  transfers between devices with their start and end apart: 23, of which 12 were waited for; matrix products, arithmetic and copies ran while one was open for 19% of the time, Pallas kernels for 13%

profile of v11, /device:TPU:10, one launch (start us, length us, event | category | flops | bytes accessed | tf_op | source)
XLA Modules:
  0.0 187.0 jit_solution(17903362544948659418)
XLA Ops:
  9.2 3.5 %collective-permute-start = (bf16[128,1024]{1,0:T(8,128)(2,1)S(1)}, bf16[128,1024]{1,0:T(8,128)(2,1)S(1)}, u32[]{:S(2)}, u32[]{:S(2)}) collective-permute-start(bf16[128,1024]{1,0:T(8,128)(2,1)S(1)} %pad_maximum_fusion.2), channel_id=1, source_target_pairs={{0,1},{1,2},{2,3},{4,5},{5,6},{6,7},{8,9},{9,10},{10,11},{12,13},{... | collective-permute-start | bytes 786440 | tf_op jit(solution)/shard_map/ppermute | solution.py:98
  12.7 2.4 %collective-permute-start.3 = (bf16[128,1024]{1,0:T(8,128)(2,1)S(1)}, bf16[128,1024]{1,0:T(8,128)(2,1)S(1)}, u32[]{:S(2)}, u32[]{:S(2)}) collective-permute-start(bf16[128,1024]{1,0:T(8,128)(2,1)S(1)} %pad_maximum_fusion.2), channel_id=1, source_target_pairs={{1,0},{2,1},{3,2},{5,4},{6,5},{7,6},{9,8},{10,9},{11,10},{13,12},{... | collective-permute-start | bytes 786440 | tf_op jit(solution)/shard_map/ppermute | solution.py:101
  15.1 3.5 %collective-permute-start.6 = (bf16[128,1024]{1,0:T(8,128)(2,1)S(1)}, bf16[128,1024]{1,0:T(8,128)(2,1)S(1)}, u32[]{:S(2)}, u32[]{:S(2)}) collective-permute-start(bf16[128,1024]{1,0:T(8,128)(2,1)S(1)} %pad_maximum_fusion.3), channel_id=1, source_target_pairs={{0,1},{1,2},{2,3},{4,5},{5,6},{6,7},{8,9},{9,10},{10,11},{12,13},{... | collective-permute-start | bytes 786440 | tf_op jit(solution)/shard_map/ppermute | solution.py:98
  18.6 2.4 %collective-permute-start.9 = (bf16[128,1024]{1,0:T(8,128)(2,1)S(1)}, bf16[128,1024]{1,0:T(8,128)(2,1)S(1)}, u32[]{:S(2)}, u32[]{:S(2)}) collective-permute-start(bf16[128,1024]{1,0:T(8,128)(2,1)S(1)} %pad_maximum_fusion.3), channel_id=1, source_target_pairs={{1,0},{2,1},{3,2},{5,4},{6,5},{7,6},{9,8},{10,9},{11,10},{13,12},{... | collective-permute-start | bytes 786440 | tf_op jit(solution)/shard_map/ppermute | solution.py:101
  21.8 3.5 %collective-permute-start.1 = (bf16[128,1024]{1,0:T(8,128)(2,1)S(1)}, bf16[128,1024]{1,0:T(8,128)(2,1)S(1)}, u32[]{:S(2)}, u32[]{:S(2)}) collective-permute-start(bf16[128,1024]{1,0:T(8,128)(2,1)S(1)} %collective-permute-done), channel_id=1, source_target_pairs={{1,2},{2,3},{5,6},{6,7},{9,10},{10,11},{13,14},{14,15},{17,18},{18... | collective-permute-start | bytes 786440 | tf_op jit(solution)/shard_map/ppermute | solution.py:98
  25.2 3.5 %collective-permute-start.7 = (bf16[128,1024]{1,0:T(8,128)(2,1)S(1)}, bf16[128,1024]{1,0:T(8,128)(2,1)S(1)}, u32[]{:S(2)}, u32[]{:S(2)}) collective-permute-start(bf16[128,1024]{1,0:T(8,128)(2,1)S(1)} %collective-permute-done.6), channel_id=1, source_target_pairs={{1,2},{2,3},{5,6},{6,7},{9,10},{10,11},{13,14},{14,15},{17,18},{18... | collective-permute-start | bytes 786440 | tf_op jit(solution)/shard_map/ppermute | solution.py:98
  36.0 3.9 %collective-permute-done.4 = bf16[128,1024]{1,0:T(8,128)(2,1)S(1)} collective-permute-done((bf16[128,1024]{1,0:T(8,128)(2,1)S(1)}, bf16[128,1024]{1,0:T(8,128)(2,1)S(1)}, u32[]{:S(2)}, u32[]{:S(2)}) %collective-permute-start.4) | collective-permute-done | bytes 262176 | tf_op jit(solution)/shard_map/ppermute | solution.py:101
  43.1 4.4 %collective-permute-start.11 = (bf16[128,1024]{1,0:T(8,128)(2,1)S(1)}, bf16[128,1024]{1,0:T(8,128)(2,1)S(1)}, u32[]{:S(2)}, u32[]{:S(2)}) collective-permute-start(bf16[128,1024]{1,0:T(8,128)(2,1)S(1)} %collective-permute-done.10), channel_id=1, source_target_pairs={{1,0},{5,4},{9,8},{13,12},{17,16},{21,20},{25,24},{29,28}} | collective-permute-start | bytes 786440 | tf_op jit(solution)/shard_map/ppermute | solution.py:101
  56.4 4.3 %all-to-all-start.1 = ((bf16[8,64,1024]{2,1,0:T(8,128)(2,1)}), bf16[8,64,1024]{2,1,0:T(8,128)(2,1)S(1)}, u32[]{:S(2)}, u32[]{:S(2)}) async-start(bf16[8,64,1024]{2,1,0:T(8,128)(2,1)} %broadcast_in_dim.5), calls=%async_computation.1 | async-start | bytes 2097152 | tf_op jit(solution)/shard_map/all_to_all | solution.py:133
  66.4 8.2 %all-to-all-done.1 = bf16[8,64,1024]{2,1,0:T(8,128)(2,1)S(1)} async-done(((bf16[8,64,1024]{2,1,0:T(8,128)(2,1)}), bf16[8,64,1024]{2,1,0:T(8,128)(2,1)S(1)}, u32[]{:S(2)}, u32[]{:S(2)}) %all-to-all-start.1) | async-done | bytes 1048608 | tf_op jit(solution)/shard_map/all_to_all | solution.py:133
  75.8 5.0 %all-to-all-start = ((bf16[8,64,1024]{2,1,0:T(8,128)(2,1)}), bf16[8,64,1024]{2,1,0:T(8,128)(2,1)S(1)}, u32[]{:S(2)}, u32[]{:S(2)}) async-start(bf16[8,64,1024]{2,1,0:T(8,128)(2,1)} %broadcast_in_dim.4), calls=%async_computation | async-start | bytes 2097152 | tf_op jit(solution)/shard_map/all_to_all | solution.py:133
  81.3 2.9 %fusion.2 = (bf16[128,2048]{1,0:T(8,128)(2,1)}, bf16[128,2048]{1,0:T(8,128)(2,1)}, bf16[128,2048]{1,0:T(8,128)(2,1)}, bf16[128,2048]{1,0:T(8,128)(2,1)}) fusion(bf16[128,4096]{1,0:T(8,128)(2,1)} %param.8, bf16[128,4096]{1,0:T(8,128)(2,1)} %param.5), kind=kLoop, calls=%fused_computation.43 | loop fusion | bytes 4194304 | tf_op jit(solution)/shard_map/slice | solution.py:172
  84.3 12.2 %shard_map.85 = (f32[512,1024]{1,0:T(8,128)}, bf16[512,1024]{1,0:T(8,128)(2,1)}, bf16[128,2048]{1,0:T(8,128)(2,1)}, bf16[128,2048]{1,0:T(8,128)(2,1)}) custom-call(s32[2]{0:T(128)} %pad_add_fusion.ids_ref, bf16[128,2048]{1,0:T(8,128)(2,1)} %get-tuple-element.42.q_ref, bf16[128,2048]{1,0:T(8,128)(2,1)} %get-tuple-element.29.g_ref, ...), custom_call_target="tpu_custom_call" | custom-call | tf_op jit(solution)/shard_map/pallas_call | solution.py:76
  96.5 4.2 %all-to-all-start.3 = ((bf16[8,64,1024]{2,1,0:T(8,128)(2,1)}), bf16[8,64,1024]{2,1,0:T(8,128)(2,1)S(1)}, u32[]{:S(2)}, u32[]{:S(2)}) async-start(bf16[8,64,1024]{2,1,0:T(8,128)(2,1)} %bitcast.57), calls=%async_computation.4 | async-start | bytes 2097152 | tf_op jit(solution)/shard_map/all_to_all | solution.py:140
  100.7 12.1 %shard_map.84 = (f32[512,1024]{1,0:T(8,128)}, bf16[512,1024]{1,0:T(8,128)(2,1)}, bf16[128,2048]{1,0:T(8,128)(2,1)}, bf16[128,2048]{1,0:T(8,128)(2,1)}) custom-call(s32[2]{0:T(128)} %pad_add_fusion.ids_ref, bf16[128,2048]{1,0:T(8,128)(2,1)} %get-tuple-element.43.q_ref, bf16[128,2048]{1,0:T(8,128)(2,1)} %get-tuple-element.28.g_ref, ...), custom_call_target="tpu_custom_call" | custom-call | tf_op jit(solution)/shard_map/pallas_call | solution.py:76
  115.6 5.0 %all-to-all-start.2 = ((bf16[8,64,1024]{2,1,0:T(8,128)(2,1)}), bf16[8,64,1024]{2,1,0:T(8,128)(2,1)S(1)}, u32[]{:S(2)}, u32[]{:S(2)}) async-start(bf16[8,64,1024]{2,1,0:T(8,128)(2,1)} %bitcast.56), calls=%async_computation.2 | async-start | bytes 2097152 | tf_op jit(solution)/shard_map/all_to_all | solution.py:140
  130.4 4.1 %all-to-all-done.2 = bf16[8,64,1024]{2,1,0:T(8,128)(2,1)S(1)} async-done(((bf16[8,64,1024]{2,1,0:T(8,128)(2,1)}), bf16[8,64,1024]{2,1,0:T(8,128)(2,1)S(1)}, u32[]{:S(2)}, u32[]{:S(2)}) %all-to-all-start.2) | async-done | bytes 1048608 | tf_op jit(solution)/shard_map/all_to_all | solution.py:140
  134.7 4.0 %scatter_fusion = f32[512,1024]{1,0:T(8,128)} fusion(f32[512,1024]{1,0:T(8,128)} %get-tuple-element.16, s32[64]{0:T(128)S(1)} %fusion, f32[64,1024]{1,0:T(8,128)S(1)} %convert_reduce_fusion.1), kind=kCustom, calls=%fused_computation.4 | custom fusion | flops 65536 | bytes 786688 | tf_op jit(solution)/shard_map/scatter-add | solution.py:144
  138.6 2.7 %convert_element_type.52 = bf16[512,1024]{1,0:T(8,128)(2,1)} convert(f32[512,1024]{1,0:T(8,128)} %scatter_fusion) | non-fusion elementwise | flops 524288 | bytes 3145728 | tf_op jit(solution)/shard_map/convert_element_type | solution.py:147
  144.7 3.8 %collective-permute-start.16 = (bf16[128,1024]{1,0:T(8,128)(2,1)S(1)}, bf16[128,1024]{1,0:T(8,128)(2,1)S(1)}, u32[]{:S(2)}, u32[]{:S(2)}) collective-permute-start(bf16[128,1024]{1,0:T(8,128)(2,1)S(1)} %get-tuple-element.25), channel_id=1, source_target_pairs={{0,1},{1,2},{4,5},{5,6},{8,9},{9,10},{12,13},{13,14},{16,17},{17,1... | collective-permute-start | bytes 786440 | tf_op jit(solution)/shard_map/ppermute | solution.py:122
  151.8 7.2 %collective-permute-done.16 = bf16[128,1024]{1,0:T(8,128)(2,1)S(1)} collective-permute-done((bf16[128,1024]{1,0:T(8,128)(2,1)S(1)}, bf16[128,1024]{1,0:T(8,128)(2,1)S(1)}, u32[]{:S(2)}, u32[]{:S(2)}) %collective-permute-start.16) | collective-permute-done | bytes 262176 | tf_op jit(solution)/shard_map/ppermute | solution.py:122
  159.1 5.2 %collective-permute-start.17 = (bf16[128,1024]{1,0:T(8,128)(2,1)S(1)}, bf16[128,1024]{1,0:T(8,128)(2,1)S(1)}, u32[]{:S(2)}, u32[]{:S(2)}) collective-permute-start(bf16[128,1024]{1,0:T(8,128)(2,1)S(1)} %add_convert_fusion.1), channel_id=1, source_target_pairs={{0,1},{1,2},{2,3},{4,5},{5,6},{6,7},{8,9},{9,10},{10,11},{12,13},{... | collective-permute-start | bytes 786440 | tf_op jit(solution)/shard_map/ppermute | solution.py:122
  165.4 6.9 %collective-permute-done.14 = bf16[128,1024]{1,0:T(8,128)(2,1)S(1)} collective-permute-done((bf16[128,1024]{1,0:T(8,128)(2,1)S(1)}, bf16[128,1024]{1,0:T(8,128)(2,1)S(1)}, u32[]{:S(2)}, u32[]{:S(2)}) %collective-permute-start.14) | collective-permute-done | bytes 262176 | tf_op jit(solution)/shard_map/ppermute | solution.py:121
  172.3 2.3 %collective-permute-done.17 = bf16[128,1024]{1,0:T(8,128)(2,1)S(1)} collective-permute-done((bf16[128,1024]{1,0:T(8,128)(2,1)S(1)}, bf16[128,1024]{1,0:T(8,128)(2,1)S(1)}, u32[]{:S(2)}, u32[]{:S(2)}) %collective-permute-start.17) | collective-permute-done | bytes 262176 | tf_op jit(solution)/shard_map/ppermute | solution.py:122
  (102 shorter events, 55.4 us)
Async XLA Ops:
  9.2 12.6 %collective-permute-start = (bf16[128,1024]{1,0:T(8,128)(2,1)S(1)}, bf16[128,1024]{1,0:T(8,128)(2,1)S(1)}, u32[]{:S(2)}, u32[]{:S(2)}) collective-permute-start(bf16[128,1024]{1,0:T(8,128)(2,1)S(1)} %pad_maximum_fusion.2), channel_id=1, source_target_pairs={{0,1},{1,2},{2,3},{4,5},{5,6},{6,7},{8,9},{9,10},{10,11},{12,13},{... | collective-permute-start | bytes 786440 | tf_op jit(solution)/shard_map/ppermute | solution.py:98
  12.7 16.1 %collective-permute-start.3 = (bf16[128,1024]{1,0:T(8,128)(2,1)S(1)}, bf16[128,1024]{1,0:T(8,128)(2,1)S(1)}, u32[]{:S(2)}, u32[]{:S(2)}) collective-permute-start(bf16[128,1024]{1,0:T(8,128)(2,1)S(1)} %pad_maximum_fusion.2), channel_id=1, source_target_pairs={{1,0},{2,1},{3,2},{5,4},{6,5},{7,6},{9,8},{10,9},{11,10},{13,12},{... | collective-permute-start | bytes 786440 | tf_op jit(solution)/shard_map/ppermute | solution.py:101
  15.1 10.2 %collective-permute-start.6 = (bf16[128,1024]{1,0:T(8,128)(2,1)S(1)}, bf16[128,1024]{1,0:T(8,128)(2,1)S(1)}, u32[]{:S(2)}, u32[]{:S(2)}) collective-permute-start(bf16[128,1024]{1,0:T(8,128)(2,1)S(1)} %pad_maximum_fusion.3), channel_id=1, source_target_pairs={{0,1},{1,2},{2,3},{4,5},{5,6},{6,7},{8,9},{9,10},{10,11},{12,13},{... | collective-permute-start | bytes 786440 | tf_op jit(solution)/shard_map/ppermute | solution.py:98
  18.6 12.2 %collective-permute-start.9 = (bf16[128,1024]{1,0:T(8,128)(2,1)S(1)}, bf16[128,1024]{1,0:T(8,128)(2,1)S(1)}, u32[]{:S(2)}, u32[]{:S(2)}) collective-permute-start(bf16[128,1024]{1,0:T(8,128)(2,1)S(1)} %pad_maximum_fusion.3), channel_id=1, source_target_pairs={{1,0},{2,1},{3,2},{5,4},{6,5},{7,6},{9,8},{10,9},{11,10},{13,12},{... | collective-permute-start | bytes 786440 | tf_op jit(solution)/shard_map/ppermute | solution.py:101
  21.8 11.6 %collective-permute-start.1 = (bf16[128,1024]{1,0:T(8,128)(2,1)S(1)}, bf16[128,1024]{1,0:T(8,128)(2,1)S(1)}, u32[]{:S(2)}, u32[]{:S(2)}) collective-permute-start(bf16[128,1024]{1,0:T(8,128)(2,1)S(1)} %collective-permute-done), channel_id=1, source_target_pairs={{1,2},{2,3},{5,6},{6,7},{9,10},{10,11},{13,14},{14,15},{17,18},{18... | collective-permute-start | bytes 786440 | tf_op jit(solution)/shard_map/ppermute | solution.py:98
  25.2 10.0 %collective-permute-start.7 = (bf16[128,1024]{1,0:T(8,128)(2,1)S(1)}, bf16[128,1024]{1,0:T(8,128)(2,1)S(1)}, u32[]{:S(2)}, u32[]{:S(2)}) collective-permute-start(bf16[128,1024]{1,0:T(8,128)(2,1)S(1)} %collective-permute-done.6), channel_id=1, source_target_pairs={{1,2},{2,3},{5,6},{6,7},{9,10},{10,11},{13,14},{14,15},{17,18},{18... | collective-permute-start | bytes 786440 | tf_op jit(solution)/shard_map/ppermute | solution.py:98
  28.8 11.1 %collective-permute-start.4 = (bf16[128,1024]{1,0:T(8,128)(2,1)S(1)}, bf16[128,1024]{1,0:T(8,128)(2,1)S(1)}, u32[]{:S(2)}, u32[]{:S(2)}) collective-permute-start(bf16[128,1024]{1,0:T(8,128)(2,1)S(1)} %collective-permute-done.3), channel_id=1, source_target_pairs={{1,0},{2,1},{5,4},{6,5},{9,8},{10,9},{13,12},{14,13},{17,16},{18,1... | collective-permute-start | bytes 786440 | tf_op jit(solution)/shard_map/ppermute | solution.py:101
  30.7 12.3 %collective-permute-start.10 = (bf16[128,1024]{1,0:T(8,128)(2,1)S(1)}, bf16[128,1024]{1,0:T(8,128)(2,1)S(1)}, u32[]{:S(2)}, u32[]{:S(2)}) collective-permute-start(bf16[128,1024]{1,0:T(8,128)(2,1)S(1)} %collective-permute-done.9), channel_id=1, source_target_pairs={{1,0},{2,1},{5,4},{6,5},{9,8},{10,9},{13,12},{14,13},{17,16},{18,1... | collective-permute-start | bytes 786440 | tf_op jit(solution)/shard_map/ppermute | solution.py:101
  33.4 27.3 %collective-permute-start.2 = (bf16[128,1024]{1,0:T(8,128)(2,1)S(1)}, bf16[128,1024]{1,0:T(8,128)(2,1)S(1)}, u32[]{:S(2)}, u32[]{:S(2)}) collective-permute-start(bf16[128,1024]{1,0:T(8,128)(2,1)S(1)} %collective-permute-done.1), channel_id=1, source_target_pairs={{2,3},{6,7},{10,11},{14,15},{18,19},{22,23},{26,27},{30,31}} | collective-permute-start | bytes 786440 | tf_op jit(solution)/shard_map/ppermute | solution.py:98
  35.3 13.0 %collective-permute-start.8 = (bf16[128,1024]{1,0:T(8,128)(2,1)S(1)}, bf16[128,1024]{1,0:T(8,128)(2,1)S(1)}, u32[]{:S(2)}, u32[]{:S(2)}) collective-permute-start(bf16[128,1024]{1,0:T(8,128)(2,1)S(1)} %collective-permute-done.7), channel_id=1, source_target_pairs={{2,3},{6,7},{10,11},{14,15},{18,19},{22,23},{26,27},{30,31}} | collective-permute-start | bytes 786440 | tf_op jit(solution)/shard_map/ppermute | solution.py:98
  39.9 23.0 %collective-permute-start.5 = (bf16[128,1024]{1,0:T(8,128)(2,1)S(1)}, bf16[128,1024]{1,0:T(8,128)(2,1)S(1)}, u32[]{:S(2)}, u32[]{:S(2)}) collective-permute-start(bf16[128,1024]{1,0:T(8,128)(2,1)S(1)} %collective-permute-done.4), channel_id=1, source_target_pairs={{1,0},{5,4},{9,8},{13,12},{17,16},{21,20},{25,24},{29,28}} | collective-permute-start | bytes 786440 | tf_op jit(solution)/shard_map/ppermute | solution.py:101
  43.1 8.6 %collective-permute-start.11 = (bf16[128,1024]{1,0:T(8,128)(2,1)S(1)}, bf16[128,1024]{1,0:T(8,128)(2,1)S(1)}, u32[]{:S(2)}, u32[]{:S(2)}) collective-permute-start(bf16[128,1024]{1,0:T(8,128)(2,1)S(1)} %collective-permute-done.10), channel_id=1, source_target_pairs={{1,0},{5,4},{9,8},{13,12},{17,16},{21,20},{25,24},{29,28}} | collective-permute-start | bytes 786440 | tf_op jit(solution)/shard_map/ppermute | solution.py:101
  56.4 18.2 %all-to-all-start.1 = ((bf16[8,64,1024]{2,1,0:T(8,128)(2,1)}), bf16[8,64,1024]{2,1,0:T(8,128)(2,1)S(1)}, u32[]{:S(2)}, u32[]{:S(2)}) async-start(bf16[8,64,1024]{2,1,0:T(8,128)(2,1)} %broadcast_in_dim.5), calls=%async_computation.1 | async-start | bytes 2097152 | tf_op jit(solution)/shard_map/all_to_all | solution.py:133
  75.8 20.7 %all-to-all-start = ((bf16[8,64,1024]{2,1,0:T(8,128)(2,1)}), bf16[8,64,1024]{2,1,0:T(8,128)(2,1)S(1)}, u32[]{:S(2)}, u32[]{:S(2)}) async-start(bf16[8,64,1024]{2,1,0:T(8,128)(2,1)} %broadcast_in_dim.4), calls=%async_computation | async-start | bytes 2097152 | tf_op jit(solution)/shard_map/all_to_all | solution.py:133
  96.5 18.1 %all-to-all-start.3 = ((bf16[8,64,1024]{2,1,0:T(8,128)(2,1)}), bf16[8,64,1024]{2,1,0:T(8,128)(2,1)S(1)}, u32[]{:S(2)}, u32[]{:S(2)}) async-start(bf16[8,64,1024]{2,1,0:T(8,128)(2,1)} %bitcast.57), calls=%async_computation.4 | async-start | bytes 2097152 | tf_op jit(solution)/shard_map/all_to_all | solution.py:140
  115.6 18.9 %all-to-all-start.2 = ((bf16[8,64,1024]{2,1,0:T(8,128)(2,1)}), bf16[8,64,1024]{2,1,0:T(8,128)(2,1)S(1)}, u32[]{:S(2)}, u32[]{:S(2)}) async-start(bf16[8,64,1024]{2,1,0:T(8,128)(2,1)} %bitcast.56), calls=%async_computation.2 | async-start | bytes 2097152 | tf_op jit(solution)/shard_map/all_to_all | solution.py:140
  120.6 56.0 %reduce-scatter.2.cloned.1.call-start = ((), (), s32[]{:S(2)}) async-start(), calls=%async_computation.5 | async-start | bytes 1310720 | tf_op jit(solution)/shard_map/reduce_scatter | solution.py:146
  124.7 2.7 %collective-permute-start.12 = (bf16[128,1024]{1,0:T(8,128)(2,1)S(1)}, bf16[128,1024]{1,0:T(8,128)(2,1)}, u32[]{:S(2)}, u32[]{:S(2)}) collective-permute-start(bf16[128,1024]{1,0:T(8,128)(2,1)S(1)} %get-tuple-element.26), channel_id=1, source_target_pairs={{3,2},{7,6},{11,10},{15,14},{19,18},{23,22},{27,26},{31,30}} | collective-permute-start | bytes 786440 | tf_op jit(solution)/shard_map/ppermute | solution.py:121
  126.1 15.3 %collective-permute-start.15 = (bf16[128,1024]{1,0:T(8,128)(2,1)}, bf16[128,1024]{1,0:T(8,128)(2,1)}, u32[]{:S(2)}, u32[]{:S(2)}) collective-permute-start(bf16[128,1024]{1,0:T(8,128)(2,1)} %get-tuple-element.27), channel_id=1, source_target_pairs={{0,1},{4,5},{8,9},{12,13},{16,17},{20,21},{24,25},{28,29}} | collective-permute-start | bytes 786440 | tf_op jit(solution)/shard_map/ppermute | solution.py:122
  129.1 14.5 %collective-permute-start.13 = (bf16[128,1024]{1,0:T(8,128)(2,1)}, bf16[128,1024]{1,0:T(8,128)(2,1)}, u32[]{:S(2)}, u32[]{:S(2)}) collective-permute-start(bf16[128,1024]{1,0:T(8,128)(2,1)} %add_convert_fusion.4), channel_id=1, source_target_pairs={{2,1},{3,2},{6,5},{7,6},{10,9},{11,10},{14,13},{15,14},{18,17},{19... | collective-permute-start | bytes 786440 | tf_op jit(solution)/shard_map/ppermute | solution.py:121
  144.7 19.6 %copy-start.7 = (bf16[128,2048]{1,0:T(8,128)(2,1)S(1)}, bf16[128,2048]{1,0:T(8,128)(2,1)}, u32[]{:S(2)}) copy-start(bf16[128,2048]{1,0:T(8,128)(2,1)} %get-tuple-element.13) | copy-start | bytes 1572868
  144.7 14.3 %collective-permute-start.16 = (bf16[128,1024]{1,0:T(8,128)(2,1)S(1)}, bf16[128,1024]{1,0:T(8,128)(2,1)S(1)}, u32[]{:S(2)}, u32[]{:S(2)}) collective-permute-start(bf16[128,1024]{1,0:T(8,128)(2,1)S(1)} %get-tuple-element.25), channel_id=1, source_target_pairs={{0,1},{1,2},{4,5},{5,6},{8,9},{9,10},{12,13},{13,14},{16,17},{17,1... | collective-permute-start | bytes 786440 | tf_op jit(solution)/shard_map/ppermute | solution.py:122
  149.6 22.7 %collective-permute-start.14 = (bf16[128,1024]{1,0:T(8,128)(2,1)S(1)}, bf16[128,1024]{1,0:T(8,128)(2,1)S(1)}, u32[]{:S(2)}, u32[]{:S(2)}) collective-permute-start(bf16[128,1024]{1,0:T(8,128)(2,1)S(1)} %get-tuple-element.24), channel_id=1, source_target_pairs={{1,0},{2,1},{3,2},{5,4},{6,5},{7,6},{9,8},{10,9},{11,10},{13,12},{... | collective-permute-start | bytes 786440 | tf_op jit(solution)/shard_map/ppermute | solution.py:121
  159.1 15.5 %collective-permute-start.17 = (bf16[128,1024]{1,0:T(8,128)(2,1)S(1)}, bf16[128,1024]{1,0:T(8,128)(2,1)S(1)}, u32[]{:S(2)}, u32[]{:S(2)}) collective-permute-start(bf16[128,1024]{1,0:T(8,128)(2,1)S(1)} %add_convert_fusion.1), channel_id=1, source_target_pairs={{0,1},{1,2},{2,3},{4,5},{5,6},{6,7},{8,9},{9,10},{10,11},{12,13},{... | collective-permute-start | bytes 786440 | tf_op jit(solution)/shard_map/ppermute | solution.py:122
  (11 other events, 99.6 us)
Sparse Core Ops, SparseCore 0:
  141.5 35.0 reduce-scatter.1

commit v12 on v9

--- a/solution.py
+++ b/solution.py
@@ -57,8 +57,9 @@
     bgrad_ref[:, HD:] = value_grad[window:].astype(jnp.bfloat16)
 
 
-def attend_all(ids, queries, out_grad, kv_window, kv_beacons, per_shard):
+def attend_all(ids, queries, out_grad, kv_window, kv_beacons, per_shard, part, parts):
     rows, q_width = queries.shape
+    q_width = q_width // parts
     window, kv_double = kv_window.shape
     beacon_total = kv_beacons.shape[0]
     kv_heads = kv_double // 2 // HD
@@ -66,6 +67,7 @@
     kernel = functools.partial(
         attention_kernel, rows=rows, window=window, per_shard=per_shard, group_size=group_size
     )
+    qinblock = pl.BlockSpec((rows, group_size * HD), lambda h, ids: (0, h + part * kv_heads))
     qblock = pl.BlockSpec((rows, group_size * HD), lambda h, ids: (0, h))
     kwblock = pl.BlockSpec((window, HD), lambda h, ids: (0, h))
     vwblock = pl.BlockSpec((window, HD), lambda h, ids: (0, h + kv_heads))
@@ -78,7 +80,7 @@
         grid_spec=pltpu.PrefetchScalarGridSpec(
             num_scalar_prefetch=1,
             grid=(kv_heads,),
-            in_specs=[qblock, qblock, kwblock, vwblock, kbblock, vbblock],
+            in_specs=[qinblock, qinblock, kwblock, vwblock, kbblock, vbblock],
             out_specs=[wgblock, bgblock, qblock, qblock],
         ),
         out_shape=[
@@ -123,7 +125,7 @@
     return block_of(index) + left.astype(jnp.float32) + right.astype(jnp.float32)
 
 
-def local_part(queries, keys, values, out_grad, positions, ids, heads_axis, ctx_axis):
+def local_part(queries, keys, values, out_grad, positions, ids, heads_axis, ctx_axis, part, parts):
     kv_width = keys.shape[1]
     per_shard = positions.shape[0]
     kv_rows = jnp.concatenate([keys, values], axis=1)
@@ -135,7 +137,7 @@
         "ctx", 0, 0, tiled=True,
     ).reshape(ctx_axis * per_shard, 2 * kv_width)
     window_grads, beacon_grads, attended_out, query_out = attend_all(
-        ids, queries, out_grad, kv_window, kv_beacons, per_shard
+        ids, queries, out_grad, kv_window, kv_beacons, per_shard, part, parts
     )
     beacon_parts = lax.all_to_all(
         beacon_grads.reshape(ctx_axis, per_shard, 2 * kv_width), "ctx", 0, 0, tiled=True
@@ -164,8 +166,8 @@
         ks = slice(part * kv_cols, (part + 1) * kv_cols)
         results.append(
             local_part(
-                queries[:, qs], keys[:, ks], values[:, ks], out_grad[:, qs],
-                positions, ids, heads_axis, ctx_axis,
+                queries, keys[:, ks], values[:, ks], out_grad,
+                positions, ids, heads_axis, ctx_axis, part, parts,
             )
         )
     return tuple(jnp.concatenate(outs, axis=1) for outs in zip(*results))

time: 178 us -> 175 us (0.983)
  local copies, waits for them, and re-layouts: 26.5 us -> 23.7 us
  waiting for transfers between devices: 34.3 us -> 31.9 us
    slice x1 -> x0, local copies, waits for them, and re-layouts: 2.91 us -> none  [local(): out_grad[:, qs]]
    all_to_all x2, waiting for transfers between devices: 10.2 us -> 7.96 us  [local_part(): lax.all_to_all(beacon_grads.reshape(ctx_axis, per_shard, 2 * kv_width), '...]
    unnamed x40 -> x38, local copies, waits for them, and re-layouts: 8.33 us -> 8.25 us
  transfers between devices with their start and end apart: 28 -> 28, of which waited for: 9 -> 10; matrix products, arithmetic and copies ran while one was open for 21% -> 21% of each run, Pallas kernels for 14% -> 14%
where the time goes in v12:
time: 175 us; the launch traced here: 173 us
  starting transfers between devices  73.5 us (42%)
  waiting for transfers between devices  31.9 us (18%)
  Pallas kernels  24.2 us (14%)
  local copies, waits for them, and re-layouts  23.7 us (14%)
  other arithmetic  18.1 us (10%)
    pallas_call x2, Pallas kernels, attend_all(): pl.pallas_call(kernel, grid_spec=pltpu.PrefetchScalarGridSpec(num_scalar_...  24.2 us
    ppermute x6, starting transfers between devices, head_gather(): lax.ppermute(from_left[-1], axis, [(j, j + 1) for j in range(step - 1, co...  15.7 us
    ppermute x6, starting transfers between devices, head_gather(): lax.ppermute(from_right[-1], axis, [(j + 1, j) for j in range(count - ste...  14.6 us
    ppermute x6, starting transfers between devices, head_reduce(): lax.ppermute(send_left, axis, [(j, j - 1) for j in range(max(1, count - s...  13.4 us
    ppermute x6, starting transfers between devices, head_reduce(): lax.ppermute(send_right, axis, [(j, j + 1) for j in range(0, min(step, co...  10.5 us
    all_to_all x2, starting transfers between devices, local_part(): lax.all_to_all(beacon_grads.reshape(ctx_axis, per_shard, 2 * kv_width), '...  9.97 us
    all_to_all x2, waiting for transfers between devices, local_part(): lax.all_to_all(jnp.broadcast_to(own_beacon_rows[None], (ctx_axis,) + own_...  9.35 us
    all_to_all x2, starting transfers between devices, local_part(): lax.all_to_all(jnp.broadcast_to(own_beacon_rows[None], (ctx_axis,) + own_...  9.23 us
  transfers between devices with their start and end apart: 28, of which 10 were waited for; matrix products, arithmetic and copies ran while one was open for 21% of the time, Pallas kernels for 14%

profile of v12, /device:TPU:10, one launch (start us, length us, event | category | flops | bytes accessed | tf_op | source)
XLA Modules:
  0.0 172.7 jit_solution(8698202720399505881)
XLA Ops:
  2.7 3.5 %collective-permute-start = (bf16[128,1024]{1,0:T(8,128)(2,1)S(1)}, bf16[128,1024]{1,0:T(8,128)(2,1)S(1)}, u32[]{:S(2)}, u32[]{:S(2)}) collective-permute-start(bf16[128,1024]{1,0:T(8,128)(2,1)S(1)} %pad_maximum_fusion.2), channel_id=1, source_target_pairs={{0,1},{1,2},{2,3},{4,5},{5,6},{6,7},{8,9},{9,10},{10,11},{12,13},{... | collective-permute-start | bytes 786440 | tf_op jit(solution)/shard_map/ppermute | solution.py:100
  6.1 2.4 %collective-permute-start.3 = (bf16[128,1024]{1,0:T(8,128)(2,1)S(1)}, bf16[128,1024]{1,0:T(8,128)(2,1)S(1)}, u32[]{:S(2)}, u32[]{:S(2)}) collective-permute-start(bf16[128,1024]{1,0:T(8,128)(2,1)S(1)} %pad_maximum_fusion.2), channel_id=1, source_target_pairs={{1,0},{2,1},{3,2},{5,4},{6,5},{7,6},{9,8},{10,9},{11,10},{13,12},{... | collective-permute-start | bytes 786440 | tf_op jit(solution)/shard_map/ppermute | solution.py:103
  8.6 3.5 %collective-permute-start.6 = (bf16[128,1024]{1,0:T(8,128)(2,1)S(1)}, bf16[128,1024]{1,0:T(8,128)(2,1)S(1)}, u32[]{:S(2)}, u32[]{:S(2)}) collective-permute-start(bf16[128,1024]{1,0:T(8,128)(2,1)S(1)} %pad_maximum_fusion.3), channel_id=1, source_target_pairs={{0,1},{1,2},{2,3},{4,5},{5,6},{6,7},{8,9},{9,10},{10,11},{12,13},{... | collective-permute-start | bytes 786440 | tf_op jit(solution)/shard_map/ppermute | solution.py:100
  12.0 2.4 %collective-permute-start.9 = (bf16[128,1024]{1,0:T(8,128)(2,1)S(1)}, bf16[128,1024]{1,0:T(8,128)(2,1)S(1)}, u32[]{:S(2)}, u32[]{:S(2)}) collective-permute-start(bf16[128,1024]{1,0:T(8,128)(2,1)S(1)} %pad_maximum_fusion.3), channel_id=1, source_target_pairs={{1,0},{2,1},{3,2},{5,4},{6,5},{7,6},{9,8},{10,9},{11,10},{13,12},{... | collective-permute-start | bytes 786440 | tf_op jit(solution)/shard_map/ppermute | solution.py:103
  15.2 3.5 %collective-permute-start.1 = (bf16[128,1024]{1,0:T(8,128)(2,1)S(1)}, bf16[128,1024]{1,0:T(8,128)(2,1)S(1)}, u32[]{:S(2)}, u32[]{:S(2)}) collective-permute-start(bf16[128,1024]{1,0:T(8,128)(2,1)S(1)} %collective-permute-done), channel_id=1, source_target_pairs={{1,2},{2,3},{5,6},{6,7},{9,10},{10,11},{13,14},{14,15},{17,18},{18... | collective-permute-start | bytes 786440 | tf_op jit(solution)/shard_map/ppermute | solution.py:100
  21.4 3.9 %collective-permute-start.7 = (bf16[128,1024]{1,0:T(8,128)(2,1)S(1)}, bf16[128,1024]{1,0:T(8,128)(2,1)S(1)}, u32[]{:S(2)}, u32[]{:S(2)}) collective-permute-start(bf16[128,1024]{1,0:T(8,128)(2,1)S(1)} %collective-permute-done.6), channel_id=1, source_target_pairs={{1,2},{2,3},{5,6},{6,7},{9,10},{10,11},{13,14},{14,15},{17,18},{18... | collective-permute-start | bytes 786440 | tf_op jit(solution)/shard_map/ppermute | solution.py:100
  31.1 2.9 %collective-permute-done.10 = bf16[128,1024]{1,0:T(8,128)(2,1)S(1)} collective-permute-done((bf16[128,1024]{1,0:T(8,128)(2,1)S(1)}, bf16[128,1024]{1,0:T(8,128)(2,1)S(1)}, u32[]{:S(2)}, u32[]{:S(2)}) %collective-permute-start.10) | collective-permute-done | bytes 262176 | tf_op jit(solution)/shard_map/ppermute | solution.py:103
  34.0 4.4 %collective-permute-start.11 = (bf16[128,1024]{1,0:T(8,128)(2,1)S(1)}, bf16[128,1024]{1,0:T(8,128)(2,1)S(1)}, u32[]{:S(2)}, u32[]{:S(2)}) collective-permute-start(bf16[128,1024]{1,0:T(8,128)(2,1)S(1)} %collective-permute-done.10), channel_id=1, source_target_pairs={{1,0},{5,4},{9,8},{13,12},{17,16},{21,20},{25,24},{29,28}} | collective-permute-start | bytes 786440 | tf_op jit(solution)/shard_map/ppermute | solution.py:103
  45.3 4.3 %all-to-all-start = ((bf16[8,64,1024]{2,1,0:T(8,128)(2,1)}), bf16[8,64,1024]{2,1,0:T(8,128)(2,1)S(1)}, u32[]{:S(2)}, u32[]{:S(2)}) async-start(bf16[8,64,1024]{2,1,0:T(8,128)(2,1)} %broadcast_in_dim.4), calls=%async_computation | async-start | bytes 2097152 | tf_op jit(solution)/shard_map/all_to_all | solution.py:135
  55.3 8.1 %all-to-all-done = bf16[8,64,1024]{2,1,0:T(8,128)(2,1)S(1)} async-done(((bf16[8,64,1024]{2,1,0:T(8,128)(2,1)}), bf16[8,64,1024]{2,1,0:T(8,128)(2,1)S(1)}, u32[]{:S(2)}, u32[]{:S(2)}) %all-to-all-start) | async-done | bytes 1048608 | tf_op jit(solution)/shard_map/all_to_all | solution.py:135
  64.7 5.0 %all-to-all-start.1 = ((bf16[8,64,1024]{2,1,0:T(8,128)(2,1)}), bf16[8,64,1024]{2,1,0:T(8,128)(2,1)S(1)}, u32[]{:S(2)}, u32[]{:S(2)}) async-start(bf16[8,64,1024]{2,1,0:T(8,128)(2,1)} %broadcast_in_dim.5), calls=%async_computation.1 | async-start | bytes 2097152 | tf_op jit(solution)/shard_map/all_to_all | solution.py:135
  70.2 12.1 %shard_map.84 = (f32[512,1024]{1,0:T(8,128)}, bf16[512,1024]{1,0:T(8,128)(2,1)}, bf16[128,2048]{1,0:T(8,128)(2,1)}, bf16[128,2048]{1,0:T(8,128)(2,1)}) custom-call(s32[2]{0:T(128)} %pad_add_fusion.ids_ref, bf16[128,4096]{1,0:T(8,128)(2,1)} %q_ref.3, bf16[128,4096]{1,0:T(8,128)(2,1)} %g_ref.3, bf16[512,1024]{1,0:T(8,128)(2,1)} %bitcast.47, ...), custom_call_target="tpu_custom_call" | custom-call | tf_op jit(solution)/shard_map/pallas_call | solution.py:78
  83.6 5.0 %all-to-all-start.2 = ((bf16[8,64,1024]{2,1,0:T(8,128)(2,1)}), bf16[8,64,1024]{2,1,0:T(8,128)(2,1)S(1)}, u32[]{:S(2)}, u32[]{:S(2)}) async-start(bf16[8,64,1024]{2,1,0:T(8,128)(2,1)} %bitcast.57), calls=%async_computation.2 | async-start | bytes 2097152 | tf_op jit(solution)/shard_map/all_to_all | solution.py:142
  88.6 12.1 %shard_map.85 = (f32[512,1024]{1,0:T(8,128)}, bf16[512,1024]{1,0:T(8,128)(2,1)}, bf16[128,2048]{1,0:T(8,128)(2,1)}, bf16[128,2048]{1,0:T(8,128)(2,1)}) custom-call(s32[2]{0:T(128)} %pad_add_fusion.ids_ref, bf16[128,4096]{1,0:T(8,128)(2,1)} %q_ref.3, bf16[128,4096]{1,0:T(8,128)(2,1)} %g_ref.3, bf16[512,1024]{1,0:T(8,128)(2,1)} %bitcast.50, ...), custom_call_target="tpu_custom_call" | custom-call | tf_op jit(solution)/shard_map/pallas_call | solution.py:78
  102.5 5.0 %all-to-all-start.3 = ((bf16[8,64,1024]{2,1,0:T(8,128)(2,1)}), bf16[8,64,1024]{2,1,0:T(8,128)(2,1)S(1)}, u32[]{:S(2)}, u32[]{:S(2)}) async-start(bf16[8,64,1024]{2,1,0:T(8,128)(2,1)} %bitcast.56), calls=%async_computation.3 | async-start | bytes 2097152 | tf_op jit(solution)/shard_map/all_to_all | solution.py:142
  107.6 4.0 %scatter_fusion = f32[512,1024]{1,0:T(8,128)} fusion(f32[512,1024]{1,0:T(8,128)} %get-tuple-element.16, s32[64]{0:T(128)S(1)} %fusion, f32[64,1024]{1,0:T(8,128)S(1)} %convert_reduce_fusion.1), kind=kCustom, calls=%fused_computation.4 | custom fusion | flops 65536 | bytes 786688 | tf_op jit(solution)/shard_map/scatter-add | solution.py:146
  111.6 2.2 %dynamic-slice_convert_fusion.3 = (bf16[128,1024]{1,0:T(8,128)(2,1)}, bf16[128,1024]{1,0:T(8,128)(2,1)}) fusion(f32[512,1024]{1,0:T(8,128)} %scatter_fusion, s32[]{:T(128)S(6)} %select_n.70, s32[]{:T(128)S(6)} %select_n.73), kind=kLoop, calls=%fused_computation.23 | loop fusion | bytes 1048584 | tf_op jit(solution)/shard_map/convert_element_type | solution.py:121
  115.2 6.2 %all-to-all-done.3 = bf16[8,64,1024]{2,1,0:T(8,128)(2,1)S(1)} async-done(((bf16[8,64,1024]{2,1,0:T(8,128)(2,1)}), bf16[8,64,1024]{2,1,0:T(8,128)(2,1)S(1)}, u32[]{:S(2)}, u32[]{:S(2)}) %all-to-all-start.3) | async-done | bytes 1048608 | tf_op jit(solution)/shard_map/all_to_all | solution.py:142
  133.8 2.6 %collective-permute-done.15 = bf16[128,1024]{1,0:T(8,128)(2,1)} collective-permute-done((bf16[128,1024]{1,0:T(8,128)(2,1)}, bf16[128,1024]{1,0:T(8,128)(2,1)}, u32[]{:S(2)}, u32[]{:S(2)}) %collective-permute-start.15) | collective-permute-done | bytes 262176 | tf_op jit(solution)/shard_map/ppermute | solution.py:124
  136.5 3.8 %collective-permute-done.13 = bf16[128,1024]{1,0:T(8,128)(2,1)} collective-permute-done((bf16[128,1024]{1,0:T(8,128)(2,1)}, bf16[128,1024]{1,0:T(8,128)(2,1)}, u32[]{:S(2)}, u32[]{:S(2)}) %collective-permute-start.13) | collective-permute-done | bytes 262176 | tf_op jit(solution)/shard_map/ppermute | solution.py:123
  144.8 4.1 %collective-permute-start.14 = (bf16[128,1024]{1,0:T(8,128)(2,1)S(1)}, bf16[128,1024]{1,0:T(8,128)(2,1)S(1)}, u32[]{:S(2)}, u32[]{:S(2)}) collective-permute-start(bf16[128,1024]{1,0:T(8,128)(2,1)S(1)} %get-tuple-element.24), channel_id=1, source_target_pairs={{1,0},{2,1},{3,2},{5,4},{6,5},{7,6},{9,8},{10,9},{11,10},{13,12},{... | collective-permute-start | bytes 786440 | tf_op jit(solution)/shard_map/ppermute | solution.py:123
  155.8 3.9 %collective-permute-start.20 = (bf16[128,1024]{1,0:T(8,128)(2,1)}, bf16[128,1024]{1,0:T(8,128)(2,1)S(1)}, u32[]{:S(2)}, u32[]{:S(2)}) collective-permute-start(bf16[128,1024]{1,0:T(8,128)(2,1)} %get-tuple-element.28), channel_id=1, source_target_pairs={{1,0},{2,1},{3,2},{5,4},{6,5},{7,6},{9,8},{10,9},{11,10},{13,12},{... | collective-permute-start | bytes 786440 | tf_op jit(solution)/shard_map/ppermute | solution.py:123
  161.3 2.2 %collective-permute-start.23 = (bf16[128,1024]{1,0:T(8,128)(2,1)}, bf16[128,1024]{1,0:T(8,128)(2,1)S(1)}, u32[]{:S(2)}, u32[]{:S(2)}) collective-permute-start(bf16[128,1024]{1,0:T(8,128)(2,1)} %add_convert_fusion.1), channel_id=1, source_target_pairs={{0,1},{1,2},{2,3},{4,5},{5,6},{6,7},{8,9},{9,10},{10,11},{12,13},{... | collective-permute-start | bytes 786440 | tf_op jit(solution)/shard_map/ppermute | solution.py:124
  166.2 3.6 %collective-permute-done.23 = bf16[128,1024]{1,0:T(8,128)(2,1)S(1)} collective-permute-done((bf16[128,1024]{1,0:T(8,128)(2,1)}, bf16[128,1024]{1,0:T(8,128)(2,1)S(1)}, u32[]{:S(2)}, u32[]{:S(2)}) %collective-permute-start.23) | collective-permute-done | bytes 262176 | tf_op jit(solution)/shard_map/ppermute | solution.py:124
  (112 shorter events, 60.9 us)
Async XLA Ops:
  2.7 12.6 %collective-permute-start = (bf16[128,1024]{1,0:T(8,128)(2,1)S(1)}, bf16[128,1024]{1,0:T(8,128)(2,1)S(1)}, u32[]{:S(2)}, u32[]{:S(2)}) collective-permute-start(bf16[128,1024]{1,0:T(8,128)(2,1)S(1)} %pad_maximum_fusion.2), channel_id=1, source_target_pairs={{0,1},{1,2},{2,3},{4,5},{5,6},{6,7},{8,9},{9,10},{10,11},{12,13},{... | collective-permute-start | bytes 786440 | tf_op jit(solution)/shard_map/ppermute | solution.py:100
  6.1 13.3 %collective-permute-start.3 = (bf16[128,1024]{1,0:T(8,128)(2,1)S(1)}, bf16[128,1024]{1,0:T(8,128)(2,1)S(1)}, u32[]{:S(2)}, u32[]{:S(2)}) collective-permute-start(bf16[128,1024]{1,0:T(8,128)(2,1)S(1)} %pad_maximum_fusion.2), channel_id=1, source_target_pairs={{1,0},{2,1},{3,2},{5,4},{6,5},{7,6},{9,8},{10,9},{11,10},{13,12},{... | collective-permute-start | bytes 786440 | tf_op jit(solution)/shard_map/ppermute | solution.py:103
  8.6 12.8 %collective-permute-start.6 = (bf16[128,1024]{1,0:T(8,128)(2,1)S(1)}, bf16[128,1024]{1,0:T(8,128)(2,1)S(1)}, u32[]{:S(2)}, u32[]{:S(2)}) collective-permute-start(bf16[128,1024]{1,0:T(8,128)(2,1)S(1)} %pad_maximum_fusion.3), channel_id=1, source_target_pairs={{0,1},{1,2},{2,3},{4,5},{5,6},{6,7},{8,9},{9,10},{10,11},{12,13},{... | collective-permute-start | bytes 786440 | tf_op jit(solution)/shard_map/ppermute | solution.py:100
  12.0 13.3 %collective-permute-start.9 = (bf16[128,1024]{1,0:T(8,128)(2,1)S(1)}, bf16[128,1024]{1,0:T(8,128)(2,1)S(1)}, u32[]{:S(2)}, u32[]{:S(2)}) collective-permute-start(bf16[128,1024]{1,0:T(8,128)(2,1)S(1)} %pad_maximum_fusion.3), channel_id=1, source_target_pairs={{1,0},{2,1},{3,2},{5,4},{6,5},{7,6},{9,8},{10,9},{11,10},{13,12},{... | collective-permute-start | bytes 786440 | tf_op jit(solution)/shard_map/ppermute | solution.py:103
  15.2 12.1 %collective-permute-start.1 = (bf16[128,1024]{1,0:T(8,128)(2,1)S(1)}, bf16[128,1024]{1,0:T(8,128)(2,1)S(1)}, u32[]{:S(2)}, u32[]{:S(2)}) collective-permute-start(bf16[128,1024]{1,0:T(8,128)(2,1)S(1)} %collective-permute-done), channel_id=1, source_target_pairs={{1,2},{2,3},{5,6},{6,7},{9,10},{10,11},{13,14},{14,15},{17,18},{18... | collective-permute-start | bytes 786440 | tf_op jit(solution)/shard_map/ppermute | solution.py:100
  19.4 9.3 %collective-permute-start.4 = (bf16[128,1024]{1,0:T(8,128)(2,1)S(1)}, bf16[128,1024]{1,0:T(8,128)(2,1)S(1)}, u32[]{:S(2)}, u32[]{:S(2)}) collective-permute-start(bf16[128,1024]{1,0:T(8,128)(2,1)S(1)} %collective-permute-done.3), channel_id=1, source_target_pairs={{1,0},{2,1},{5,4},{6,5},{9,8},{10,9},{13,12},{14,13},{17,16},{18,1... | collective-permute-start | bytes 786440 | tf_op jit(solution)/shard_map/ppermute | solution.py:103
  27.3 11.1 %collective-permute-start.2 = (bf16[128,1024]{1,0:T(8,128)(2,1)S(1)}, bf16[128,1024]{1,0:T(8,128)(2,1)S(1)}, u32[]{:S(2)}, u32[]{:S(2)}) collective-permute-start(bf16[128,1024]{1,0:T(8,128)(2,1)S(1)} %collective-permute-done.1), channel_id=1, source_target_pairs={{2,3},{6,7},{10,11},{14,15},{18,19},{22,23},{26,27},{30,31}} | collective-permute-start | bytes 786440 | tf_op jit(solution)/shard_map/ppermute | solution.py:100
  28.7 12.0 %collective-permute-start.5 = (bf16[128,1024]{1,0:T(8,128)(2,1)S(1)}, bf16[128,1024]{1,0:T(8,128)(2,1)S(1)}, u32[]{:S(2)}, u32[]{:S(2)}) collective-permute-start(bf16[128,1024]{1,0:T(8,128)(2,1)S(1)} %collective-permute-done.4), channel_id=1, source_target_pairs={{1,0},{5,4},{9,8},{13,12},{17,16},{21,20},{25,24},{29,28}} | collective-permute-start | bytes 786440 | tf_op jit(solution)/shard_map/ppermute | solution.py:103
  30.4 19.2 %collective-permute-start.8 = (bf16[128,1024]{1,0:T(8,128)(2,1)S(1)}, bf16[128,1024]{1,0:T(8,128)(2,1)S(1)}, u32[]{:S(2)}, u32[]{:S(2)}) collective-permute-start(bf16[128,1024]{1,0:T(8,128)(2,1)S(1)} %collective-permute-done.7), channel_id=1, source_target_pairs={{2,3},{6,7},{10,11},{14,15},{18,19},{22,23},{26,27},{30,31}} | collective-permute-start | bytes 786440 | tf_op jit(solution)/shard_map/ppermute | solution.py:100
  34.0 17.8 %collective-permute-start.11 = (bf16[128,1024]{1,0:T(8,128)(2,1)S(1)}, bf16[128,1024]{1,0:T(8,128)(2,1)S(1)}, u32[]{:S(2)}, u32[]{:S(2)}) collective-permute-start(bf16[128,1024]{1,0:T(8,128)(2,1)S(1)} %collective-permute-done.10), channel_id=1, source_target_pairs={{1,0},{5,4},{9,8},{13,12},{17,16},{21,20},{25,24},{29,28}} | collective-permute-start | bytes 786440 | tf_op jit(solution)/shard_map/ppermute | solution.py:103
  45.3 18.2 %all-to-all-start = ((bf16[8,64,1024]{2,1,0:T(8,128)(2,1)}), bf16[8,64,1024]{2,1,0:T(8,128)(2,1)S(1)}, u32[]{:S(2)}, u32[]{:S(2)}) async-start(bf16[8,64,1024]{2,1,0:T(8,128)(2,1)} %broadcast_in_dim.4), calls=%async_computation | async-start | bytes 2097152 | tf_op jit(solution)/shard_map/all_to_all | solution.py:135
  64.7 18.9 %all-to-all-start.1 = ((bf16[8,64,1024]{2,1,0:T(8,128)(2,1)}), bf16[8,64,1024]{2,1,0:T(8,128)(2,1)S(1)}, u32[]{:S(2)}, u32[]{:S(2)}) async-start(bf16[8,64,1024]{2,1,0:T(8,128)(2,1)} %broadcast_in_dim.5), calls=%async_computation.1 | async-start | bytes 2097152 | tf_op jit(solution)/shard_map/all_to_all | solution.py:135
  83.6 18.9 %all-to-all-start.2 = ((bf16[8,64,1024]{2,1,0:T(8,128)(2,1)}), bf16[8,64,1024]{2,1,0:T(8,128)(2,1)S(1)}, u32[]{:S(2)}, u32[]{:S(2)}) async-start(bf16[8,64,1024]{2,1,0:T(8,128)(2,1)} %bitcast.57), calls=%async_computation.2 | async-start | bytes 2097152 | tf_op jit(solution)/shard_map/all_to_all | solution.py:142
  102.5 18.9 %all-to-all-start.3 = ((bf16[8,64,1024]{2,1,0:T(8,128)(2,1)}), bf16[8,64,1024]{2,1,0:T(8,128)(2,1)S(1)}, u32[]{:S(2)}, u32[]{:S(2)}) async-start(bf16[8,64,1024]{2,1,0:T(8,128)(2,1)} %bitcast.56), calls=%async_computation.3 | async-start | bytes 2097152 | tf_op jit(solution)/shard_map/all_to_all | solution.py:142
  113.9 13.0 %collective-permute-start.12 = (bf16[128,1024]{1,0:T(8,128)(2,1)}, bf16[128,1024]{1,0:T(8,128)(2,1)}, u32[]{:S(2)}, u32[]{:S(2)}) collective-permute-start(bf16[128,1024]{1,0:T(8,128)(2,1)} %get-tuple-element.26), channel_id=1, source_target_pairs={{3,2},{7,6},{11,10},{15,14},{19,18},{23,22},{27,26},{31,30}} | collective-permute-start | bytes 786440 | tf_op jit(solution)/shard_map/ppermute | solution.py:123
  125.6 10.9 %collective-permute-start.15 = (bf16[128,1024]{1,0:T(8,128)(2,1)}, bf16[128,1024]{1,0:T(8,128)(2,1)}, u32[]{:S(2)}, u32[]{:S(2)}) collective-permute-start(bf16[128,1024]{1,0:T(8,128)(2,1)} %get-tuple-element.27), channel_id=1, source_target_pairs={{0,1},{4,5},{8,9},{12,13},{16,17},{20,21},{24,25},{28,29}} | collective-permute-start | bytes 786440 | tf_op jit(solution)/shard_map/ppermute | solution.py:124
  128.8 11.5 %collective-permute-start.13 = (bf16[128,1024]{1,0:T(8,128)(2,1)}, bf16[128,1024]{1,0:T(8,128)(2,1)}, u32[]{:S(2)}, u32[]{:S(2)}) collective-permute-start(bf16[128,1024]{1,0:T(8,128)(2,1)} %add_convert_fusion.9), channel_id=1, source_target_pairs={{2,1},{3,2},{6,5},{7,6},{10,9},{11,10},{14,13},{15,14},{18,17},{19... | collective-permute-start | bytes 786440 | tf_op jit(solution)/shard_map/ppermute | solution.py:123
  130.2 18.6 %collective-permute-start.21 = (bf16[128,1024]{1,0:T(8,128)(2,1)S(1)}, bf16[128,1024]{1,0:T(8,128)(2,1)S(1)}, u32[]{:S(2)}, u32[]{:S(2)}) collective-permute-start(bf16[128,1024]{1,0:T(8,128)(2,1)S(1)} %get-tuple-element.31), channel_id=1, source_target_pairs={{0,1},{4,5},{8,9},{12,13},{16,17},{20,21},{24,25},{28,29}} | collective-permute-start | bytes 786440 | tf_op jit(solution)/shard_map/ppermute | solution.py:124
  132.5 16.3 %collective-permute-start.19 = (bf16[128,1024]{1,0:T(8,128)(2,1)S(1)}, bf16[128,1024]{1,0:T(8,128)(2,1)S(1)}, u32[]{:S(2)}, u32[]{:S(2)}) collective-permute-start(bf16[128,1024]{1,0:T(8,128)(2,1)S(1)} %add_convert_fusion.4), channel_id=1, source_target_pairs={{2,1},{3,2},{6,5},{7,6},{10,9},{11,10},{14,13},{15,14},{18,17},{19... | collective-permute-start | bytes 786440 | tf_op jit(solution)/shard_map/ppermute | solution.py:123
  141.8 9.9 %collective-permute-start.16 = (bf16[128,1024]{1,0:T(8,128)(2,1)S(1)}, bf16[128,1024]{1,0:T(8,128)(2,1)S(1)}, u32[]{:S(2)}, u32[]{:S(2)}) collective-permute-start(bf16[128,1024]{1,0:T(8,128)(2,1)S(1)} %get-tuple-element.25), channel_id=1, source_target_pairs={{0,1},{1,2},{4,5},{5,6},{8,9},{9,10},{12,13},{13,14},{16,17},{17,1... | collective-permute-start | bytes 786440 | tf_op jit(solution)/shard_map/ppermute | solution.py:124
  144.8 18.7 %collective-permute-start.14 = (bf16[128,1024]{1,0:T(8,128)(2,1)S(1)}, bf16[128,1024]{1,0:T(8,128)(2,1)S(1)}, u32[]{:S(2)}, u32[]{:S(2)}) collective-permute-start(bf16[128,1024]{1,0:T(8,128)(2,1)S(1)} %get-tuple-element.24), channel_id=1, source_target_pairs={{1,0},{2,1},{3,2},{5,4},{6,5},{7,6},{9,8},{10,9},{11,10},{13,12},{... | collective-permute-start | bytes 786440 | tf_op jit(solution)/shard_map/ppermute | solution.py:123
  149.7 10.8 %collective-permute-start.22 = (bf16[128,1024]{1,0:T(8,128)(2,1)S(1)}, bf16[128,1024]{1,0:T(8,128)(2,1)S(1)}, u32[]{:S(2)}, u32[]{:S(2)}) collective-permute-start(bf16[128,1024]{1,0:T(8,128)(2,1)S(1)} %get-tuple-element.29), channel_id=1, source_target_pairs={{0,1},{1,2},{4,5},{5,6},{8,9},{9,10},{12,13},{13,14},{16,17},{17,1... | collective-permute-start | bytes 786440 | tf_op jit(solution)/shard_map/ppermute | solution.py:124
  152.8 11.6 %collective-permute-start.17 = (bf16[128,1024]{1,0:T(8,128)(2,1)S(1)}, bf16[128,1024]{1,0:T(8,128)(2,1)S(1)}, u32[]{:S(2)}, u32[]{:S(2)}) collective-permute-start(bf16[128,1024]{1,0:T(8,128)(2,1)S(1)} %add_convert_fusion.6), channel_id=1, source_target_pairs={{0,1},{1,2},{2,3},{4,5},{5,6},{6,7},{8,9},{9,10},{10,11},{12,13},{... | collective-permute-start | bytes 786440 | tf_op jit(solution)/shard_map/ppermute | solution.py:124
  155.8 10.4 %collective-permute-start.20 = (bf16[128,1024]{1,0:T(8,128)(2,1)}, bf16[128,1024]{1,0:T(8,128)(2,1)S(1)}, u32[]{:S(2)}, u32[]{:S(2)}) collective-permute-start(bf16[128,1024]{1,0:T(8,128)(2,1)} %get-tuple-element.28), channel_id=1, source_target_pairs={{1,0},{2,1},{3,2},{5,4},{6,5},{7,6},{9,8},{10,9},{11,10},{13,12},{... | collective-permute-start | bytes 786440 | tf_op jit(solution)/shard_map/ppermute | solution.py:123
  (15 other events, 132.8 us)

commit v13 on v12

--- a/solution.py
+++ b/solution.py
@@ -103,9 +103,11 @@
             lax.ppermute(from_right[-1], axis, [(j + 1, j) for j in range(count - step)])
         )
     pieces = jnp.stack(from_left + from_right[1:])
-    order = jnp.arange(count)
-    pick = jnp.where(order <= index, index - order, count - 1 + order - index)
-    return pieces[pick].reshape((count * block.shape[0],) + block.shape[1:])
+    window = []
+    for order in range(count):
+        pick = jnp.where(order <= index, index - order, count - 1 + order - index)
+        window.append(lax.dynamic_index_in_dim(pieces, pick, 0, keepdims=False))
+    return jnp.concatenate(window, axis=0)
 
 
 def head_reduce(partials, axis, count):

time: 175 us -> 174 us (level)
    gather x2 -> x0, local copies, waits for them, and re-layouts: 4.22 us -> none  [head_gather(): return pieces[pick].reshape((count * block.shape[0],) + block.shape[1:])]
    squeeze x0 -> x2, local copies, waits for them, and re-layouts: none -> 2.54 us  [head_gather(): window.append(lax.dynamic_index_in_dim(pieces, pick, 0, keepdims=False))]
  transfers between devices with their start and end apart: 28 -> 28, of which waited for: 10 -> 10; matrix products, arithmetic and copies ran while one was open for 21% -> 20% of each run, Pallas kernels for 14% -> 14%
where the time goes in v13:
time: 174 us; the launch traced here: 172 us
  starting transfers between devices  73.4 us (42%)
  waiting for transfers between devices  32.9 us (19%)
  Pallas kernels  24.2 us (14%)
  local copies, waits for them, and re-layouts  22 us (13%)
  other arithmetic  18.3 us (11%)
    pallas_call x2, Pallas kernels, attend_all(): pl.pallas_call(kernel, grid_spec=pltpu.PrefetchScalarGridSpec(num_scalar_...  24.2 us
    ppermute x6, starting transfers between devices, head_gather(): lax.ppermute(from_left[-1], axis, [(j, j + 1) for j in range(step - 1, co...  15.7 us
    ppermute x6, starting transfers between devices, head_gather(): lax.ppermute(from_right[-1], axis, [(j + 1, j) for j in range(count - ste...  14.6 us
    ppermute x6, starting transfers between devices, head_reduce(): lax.ppermute(send_left, axis, [(j, j - 1) for j in range(max(1, count - s...  13.4 us
    ppermute x6, starting transfers between devices, head_reduce(): lax.ppermute(send_right, axis, [(j, j + 1) for j in range(0, min(step, co...  10.4 us
    all_to_all x2, waiting for transfers between devices, local_part(): lax.all_to_all(jnp.broadcast_to(own_beacon_rows[None], (ctx_axis,) + own_...  10.1 us
    all_to_all x2, starting transfers between devices, local_part(): lax.all_to_all(beacon_grads.reshape(ctx_axis, per_shard, 2 * kv_width), '...  9.97 us
    all_to_all x2, starting transfers between devices, local_part(): lax.all_to_all(jnp.broadcast_to(own_beacon_rows[None], (ctx_axis,) + own_...  9.23 us
  transfers between devices with their start and end apart: 28, of which 10 were waited for; matrix products, arithmetic and copies ran while one was open for 20% of the time, Pallas kernels for 14%

profile of v13, /device:TPU:10, one launch (start us, length us, event | category | flops | bytes accessed | tf_op | source)
XLA Modules:
  0.0 172.0 jit_solution(8459576184700992905)
XLA Ops:
  2.7 3.5 %collective-permute-start = (bf16[128,1024]{1,0:T(8,128)(2,1)S(1)}, bf16[128,1024]{1,0:T(8,128)(2,1)S(1)}, u32[]{:S(2)}, u32[]{:S(2)}) collective-permute-start(bf16[128,1024]{1,0:T(8,128)(2,1)S(1)} %pad_maximum_fusion.4), channel_id=1, source_target_pairs={{0,1},{1,2},{2,3},{4,5},{5,6},{6,7},{8,9},{9,10},{10,11},{12,13},{... | collective-permute-start | bytes 786440 | tf_op jit(solution)/shard_map/ppermute | solution.py:100
  6.1 2.4 %collective-permute-start.3 = (bf16[128,1024]{1,0:T(8,128)(2,1)S(1)}, bf16[128,1024]{1,0:T(8,128)(2,1)S(1)}, u32[]{:S(2)}, u32[]{:S(2)}) collective-permute-start(bf16[128,1024]{1,0:T(8,128)(2,1)S(1)} %pad_maximum_fusion.4), channel_id=1, source_target_pairs={{1,0},{2,1},{3,2},{5,4},{6,5},{7,6},{9,8},{10,9},{11,10},{13,12},{... | collective-permute-start | bytes 786440 | tf_op jit(solution)/shard_map/ppermute | solution.py:103
  8.6 3.5 %collective-permute-start.6 = (bf16[128,1024]{1,0:T(8,128)(2,1)S(1)}, bf16[128,1024]{1,0:T(8,128)(2,1)S(1)}, u32[]{:S(2)}, u32[]{:S(2)}) collective-permute-start(bf16[128,1024]{1,0:T(8,128)(2,1)S(1)} %pad_maximum_fusion.5), channel_id=1, source_target_pairs={{0,1},{1,2},{2,3},{4,5},{5,6},{6,7},{8,9},{9,10},{10,11},{12,13},{... | collective-permute-start | bytes 786440 | tf_op jit(solution)/shard_map/ppermute | solution.py:100
  12.0 2.4 %collective-permute-start.9 = (bf16[128,1024]{1,0:T(8,128)(2,1)S(1)}, bf16[128,1024]{1,0:T(8,128)(2,1)S(1)}, u32[]{:S(2)}, u32[]{:S(2)}) collective-permute-start(bf16[128,1024]{1,0:T(8,128)(2,1)S(1)} %pad_maximum_fusion.5), channel_id=1, source_target_pairs={{1,0},{2,1},{3,2},{5,4},{6,5},{7,6},{9,8},{10,9},{11,10},{13,12},{... | collective-permute-start | bytes 786440 | tf_op jit(solution)/shard_map/ppermute | solution.py:103
  15.2 3.5 %collective-permute-start.1 = (bf16[128,1024]{1,0:T(8,128)(2,1)S(1)}, bf16[128,1024]{1,0:T(8,128)(2,1)S(1)}, u32[]{:S(2)}, u32[]{:S(2)}) collective-permute-start(bf16[128,1024]{1,0:T(8,128)(2,1)S(1)} %collective-permute-done), channel_id=1, source_target_pairs={{1,2},{2,3},{5,6},{6,7},{9,10},{10,11},{13,14},{14,15},{17,18},{18... | collective-permute-start | bytes 786440 | tf_op jit(solution)/shard_map/ppermute | solution.py:100
  21.4 3.9 %collective-permute-start.7 = (bf16[128,1024]{1,0:T(8,128)(2,1)S(1)}, bf16[128,1024]{1,0:T(8,128)(2,1)S(1)}, u32[]{:S(2)}, u32[]{:S(2)}) collective-permute-start(bf16[128,1024]{1,0:T(8,128)(2,1)S(1)} %collective-permute-done.6), channel_id=1, source_target_pairs={{1,2},{2,3},{5,6},{6,7},{9,10},{10,11},{13,14},{14,15},{17,18},{18... | collective-permute-start | bytes 786440 | tf_op jit(solution)/shard_map/ppermute | solution.py:100
  31.1 2.9 %collective-permute-done.10 = bf16[128,1024]{1,0:T(8,128)(2,1)S(1)} collective-permute-done((bf16[128,1024]{1,0:T(8,128)(2,1)S(1)}, bf16[128,1024]{1,0:T(8,128)(2,1)S(1)}, u32[]{:S(2)}, u32[]{:S(2)}) %collective-permute-start.10) | collective-permute-done | bytes 262176 | tf_op jit(solution)/shard_map/ppermute | solution.py:103
  34.0 4.4 %collective-permute-start.11 = (bf16[128,1024]{1,0:T(8,128)(2,1)S(1)}, bf16[128,1024]{1,0:T(8,128)(2,1)S(1)}, u32[]{:S(2)}, u32[]{:S(2)}) collective-permute-start(bf16[128,1024]{1,0:T(8,128)(2,1)S(1)} %collective-permute-done.10), channel_id=1, source_target_pairs={{1,0},{5,4},{9,8},{13,12},{17,16},{21,20},{25,24},{29,28}} | collective-permute-start | bytes 786440 | tf_op jit(solution)/shard_map/ppermute | solution.py:103
  44.6 4.3 %all-to-all-start = ((bf16[8,64,1024]{2,1,0:T(8,128)(2,1)}), bf16[8,64,1024]{2,1,0:T(8,128)(2,1)S(1)}, u32[]{:S(2)}, u32[]{:S(2)}) async-start(bf16[8,64,1024]{2,1,0:T(8,128)(2,1)} %broadcast_in_dim.4), calls=%async_computation | async-start | bytes 2097152 | tf_op jit(solution)/shard_map/all_to_all | solution.py:137
  53.8 8.9 %all-to-all-done = bf16[8,64,1024]{2,1,0:T(8,128)(2,1)S(1)} async-done(((bf16[8,64,1024]{2,1,0:T(8,128)(2,1)}), bf16[8,64,1024]{2,1,0:T(8,128)(2,1)S(1)}, u32[]{:S(2)}, u32[]{:S(2)}) %all-to-all-start) | async-done | bytes 1048608 | tf_op jit(solution)/shard_map/all_to_all | solution.py:137
  63.9 5.0 %all-to-all-start.1 = ((bf16[8,64,1024]{2,1,0:T(8,128)(2,1)}), bf16[8,64,1024]{2,1,0:T(8,128)(2,1)S(1)}, u32[]{:S(2)}, u32[]{:S(2)}) async-start(bf16[8,64,1024]{2,1,0:T(8,128)(2,1)} %broadcast_in_dim.5), calls=%async_computation.1 | async-start | bytes 2097152 | tf_op jit(solution)/shard_map/all_to_all | solution.py:137
  69.5 12.1 %shard_map.84 = (f32[512,1024]{1,0:T(8,128)}, bf16[512,1024]{1,0:T(8,128)(2,1)}, bf16[128,2048]{1,0:T(8,128)(2,1)}, bf16[128,2048]{1,0:T(8,128)(2,1)}) custom-call(s32[2]{0:T(128)} %pad_add_fusion.ids_ref, bf16[128,4096]{1,0:T(8,128)(2,1)} %q_ref.3, bf16[128,4096]{1,0:T(8,128)(2,1)} %g_ref.3, bf16[512,1024]{1,0:T(8,128)(2,1)} %copy-done, ...), custom_call_target="tpu_custom_call" | custom-call | tf_op jit(solution)/shard_map/pallas_call | solution.py:78
  82.8 5.0 %all-to-all-start.2 = ((bf16[8,64,1024]{2,1,0:T(8,128)(2,1)}), bf16[8,64,1024]{2,1,0:T(8,128)(2,1)S(1)}, u32[]{:S(2)}, u32[]{:S(2)}) async-start(bf16[8,64,1024]{2,1,0:T(8,128)(2,1)} %bitcast.63), calls=%async_computation.2 | async-start | bytes 2097152 | tf_op jit(solution)/shard_map/all_to_all | solution.py:144
  87.8 12.1 %shard_map.85 = (f32[512,1024]{1,0:T(8,128)}, bf16[512,1024]{1,0:T(8,128)(2,1)}, bf16[128,2048]{1,0:T(8,128)(2,1)}, bf16[128,2048]{1,0:T(8,128)(2,1)}) custom-call(s32[2]{0:T(128)} %pad_add_fusion.ids_ref, bf16[128,4096]{1,0:T(8,128)(2,1)} %q_ref.3, bf16[128,4096]{1,0:T(8,128)(2,1)} %g_ref.3, bf16[512,1024]{1,0:T(8,128)(2,1)} %copy-done.1, ...), custom_call_target="tpu_custom_call" | custom-call | tf_op jit(solution)/shard_map/pallas_call | solution.py:78
  101.7 5.0 %all-to-all-start.3 = ((bf16[8,64,1024]{2,1,0:T(8,128)(2,1)}), bf16[8,64,1024]{2,1,0:T(8,128)(2,1)S(1)}, u32[]{:S(2)}, u32[]{:S(2)}) async-start(bf16[8,64,1024]{2,1,0:T(8,128)(2,1)} %bitcast.62), calls=%async_computation.3 | async-start | bytes 2097152 | tf_op jit(solution)/shard_map/all_to_all | solution.py:144
  106.9 4.0 %scatter_fusion = f32[512,1024]{1,0:T(8,128)} fusion(f32[512,1024]{1,0:T(8,128)} %get-tuple-element.16, s32[64]{0:T(128)S(1)} %fusion, f32[64,1024]{1,0:T(8,128)S(1)} %convert_reduce_fusion.1), kind=kCustom, calls=%fused_computation.2 | custom fusion | flops 65536 | bytes 786688 | tf_op jit(solution)/shard_map/scatter-add | solution.py:148
  110.9 2.2 %dynamic-slice_convert_fusion.3 = (bf16[128,1024]{1,0:T(8,128)(2,1)}, bf16[128,1024]{1,0:T(8,128)(2,1)}) fusion(f32[512,1024]{1,0:T(8,128)} %scatter_fusion, s32[]{:T(128)S(6)} %select_n.87, s32[]{:T(128)S(6)} %select_n.90), kind=kLoop, calls=%fused_computation.23 | loop fusion | bytes 1048584 | tf_op jit(solution)/shard_map/convert_element_type | solution.py:123
  114.5 6.2 %all-to-all-done.3 = bf16[8,64,1024]{2,1,0:T(8,128)(2,1)S(1)} async-done(((bf16[8,64,1024]{2,1,0:T(8,128)(2,1)}), bf16[8,64,1024]{2,1,0:T(8,128)(2,1)S(1)}, u32[]{:S(2)}, u32[]{:S(2)}) %all-to-all-start.3) | async-done | bytes 1048608 | tf_op jit(solution)/shard_map/all_to_all | solution.py:144
  133.1 2.6 %collective-permute-done.15 = bf16[128,1024]{1,0:T(8,128)(2,1)} collective-permute-done((bf16[128,1024]{1,0:T(8,128)(2,1)}, bf16[128,1024]{1,0:T(8,128)(2,1)}, u32[]{:S(2)}, u32[]{:S(2)}) %collective-permute-start.15) | collective-permute-done | bytes 262176 | tf_op jit(solution)/shard_map/ppermute | solution.py:126
  135.7 3.9 %collective-permute-done.13 = bf16[128,1024]{1,0:T(8,128)(2,1)} collective-permute-done((bf16[128,1024]{1,0:T(8,128)(2,1)}, bf16[128,1024]{1,0:T(8,128)(2,1)}, u32[]{:S(2)}, u32[]{:S(2)}) %collective-permute-start.13) | collective-permute-done | bytes 262176 | tf_op jit(solution)/shard_map/ppermute | solution.py:125
  144.1 4.1 %collective-permute-start.14 = (bf16[128,1024]{1,0:T(8,128)(2,1)S(1)}, bf16[128,1024]{1,0:T(8,128)(2,1)S(1)}, u32[]{:S(2)}, u32[]{:S(2)}) collective-permute-start(bf16[128,1024]{1,0:T(8,128)(2,1)S(1)} %get-tuple-element.24), channel_id=1, source_target_pairs={{1,0},{2,1},{3,2},{5,4},{6,5},{7,6},{9,8},{10,9},{11,10},{13,12},{... | collective-permute-start | bytes 786440 | tf_op jit(solution)/shard_map/ppermute | solution.py:125
  155.1 3.9 %collective-permute-start.20 = (bf16[128,1024]{1,0:T(8,128)(2,1)}, bf16[128,1024]{1,0:T(8,128)(2,1)S(1)}, u32[]{:S(2)}, u32[]{:S(2)}) collective-permute-start(bf16[128,1024]{1,0:T(8,128)(2,1)} %get-tuple-element.28), channel_id=1, source_target_pairs={{1,0},{2,1},{3,2},{5,4},{6,5},{7,6},{9,8},{10,9},{11,10},{13,12},{... | collective-permute-start | bytes 786440 | tf_op jit(solution)/shard_map/ppermute | solution.py:125
  160.6 2.1 %collective-permute-start.23 = (bf16[128,1024]{1,0:T(8,128)(2,1)}, bf16[128,1024]{1,0:T(8,128)(2,1)S(1)}, u32[]{:S(2)}, u32[]{:S(2)}) collective-permute-start(bf16[128,1024]{1,0:T(8,128)(2,1)} %add_convert_fusion.1), channel_id=1, source_target_pairs={{0,1},{1,2},{2,3},{4,5},{5,6},{6,7},{8,9},{9,10},{10,11},{12,13},{... | collective-permute-start | bytes 786440 | tf_op jit(solution)/shard_map/ppermute | solution.py:126
  165.5 3.6 %collective-permute-done.23 = bf16[128,1024]{1,0:T(8,128)(2,1)S(1)} collective-permute-done((bf16[128,1024]{1,0:T(8,128)(2,1)}, bf16[128,1024]{1,0:T(8,128)(2,1)S(1)}, u32[]{:S(2)}, u32[]{:S(2)}) %collective-permute-start.23) | collective-permute-done | bytes 262176 | tf_op jit(solution)/shard_map/ppermute | solution.py:126
  (112 shorter events, 59.6 us)
Async XLA Ops:
  2.7 12.6 %collective-permute-start = (bf16[128,1024]{1,0:T(8,128)(2,1)S(1)}, bf16[128,1024]{1,0:T(8,128)(2,1)S(1)}, u32[]{:S(2)}, u32[]{:S(2)}) collective-permute-start(bf16[128,1024]{1,0:T(8,128)(2,1)S(1)} %pad_maximum_fusion.4), channel_id=1, source_target_pairs={{0,1},{1,2},{2,3},{4,5},{5,6},{6,7},{8,9},{9,10},{10,11},{12,13},{... | collective-permute-start | bytes 786440 | tf_op jit(solution)/shard_map/ppermute | solution.py:100
  6.1 13.3 %collective-permute-start.3 = (bf16[128,1024]{1,0:T(8,128)(2,1)S(1)}, bf16[128,1024]{1,0:T(8,128)(2,1)S(1)}, u32[]{:S(2)}, u32[]{:S(2)}) collective-permute-start(bf16[128,1024]{1,0:T(8,128)(2,1)S(1)} %pad_maximum_fusion.4), channel_id=1, source_target_pairs={{1,0},{2,1},{3,2},{5,4},{6,5},{7,6},{9,8},{10,9},{11,10},{13,12},{... | collective-permute-start | bytes 786440 | tf_op jit(solution)/shard_map/ppermute | solution.py:103
  8.6 12.8 %collective-permute-start.6 = (bf16[128,1024]{1,0:T(8,128)(2,1)S(1)}, bf16[128,1024]{1,0:T(8,128)(2,1)S(1)}, u32[]{:S(2)}, u32[]{:S(2)}) collective-permute-start(bf16[128,1024]{1,0:T(8,128)(2,1)S(1)} %pad_maximum_fusion.5), channel_id=1, source_target_pairs={{0,1},{1,2},{2,3},{4,5},{5,6},{6,7},{8,9},{9,10},{10,11},{12,13},{... | collective-permute-start | bytes 786440 | tf_op jit(solution)/shard_map/ppermute | solution.py:100
  12.0 13.3 %collective-permute-start.9 = (bf16[128,1024]{1,0:T(8,128)(2,1)S(1)}, bf16[128,1024]{1,0:T(8,128)(2,1)S(1)}, u32[]{:S(2)}, u32[]{:S(2)}) collective-permute-start(bf16[128,1024]{1,0:T(8,128)(2,1)S(1)} %pad_maximum_fusion.5), channel_id=1, source_target_pairs={{1,0},{2,1},{3,2},{5,4},{6,5},{7,6},{9,8},{10,9},{11,10},{13,12},{... | collective-permute-start | bytes 786440 | tf_op jit(solution)/shard_map/ppermute | solution.py:103
  15.2 12.1 %collective-permute-start.1 = (bf16[128,1024]{1,0:T(8,128)(2,1)S(1)}, bf16[128,1024]{1,0:T(8,128)(2,1)S(1)}, u32[]{:S(2)}, u32[]{:S(2)}) collective-permute-start(bf16[128,1024]{1,0:T(8,128)(2,1)S(1)} %collective-permute-done), channel_id=1, source_target_pairs={{1,2},{2,3},{5,6},{6,7},{9,10},{10,11},{13,14},{14,15},{17,18},{18... | collective-permute-start | bytes 786440 | tf_op jit(solution)/shard_map/ppermute | solution.py:100
  19.4 9.3 %collective-permute-start.4 = (bf16[128,1024]{1,0:T(8,128)(2,1)S(1)}, bf16[128,1024]{1,0:T(8,128)(2,1)S(1)}, u32[]{:S(2)}, u32[]{:S(2)}) collective-permute-start(bf16[128,1024]{1,0:T(8,128)(2,1)S(1)} %collective-permute-done.3), channel_id=1, source_target_pairs={{1,0},{2,1},{5,4},{6,5},{9,8},{10,9},{13,12},{14,13},{17,16},{18,1... | collective-permute-start | bytes 786440 | tf_op jit(solution)/shard_map/ppermute | solution.py:103
  27.3 11.1 %collective-permute-start.2 = (bf16[128,1024]{1,0:T(8,128)(2,1)S(1)}, bf16[128,1024]{1,0:T(8,128)(2,1)S(1)}, u32[]{:S(2)}, u32[]{:S(2)}) collective-permute-start(bf16[128,1024]{1,0:T(8,128)(2,1)S(1)} %collective-permute-done.1), channel_id=1, source_target_pairs={{2,3},{6,7},{10,11},{14,15},{18,19},{22,23},{26,27},{30,31}} | collective-permute-start | bytes 786440 | tf_op jit(solution)/shard_map/ppermute | solution.py:100
  28.7 11.9 %collective-permute-start.5 = (bf16[128,1024]{1,0:T(8,128)(2,1)S(1)}, bf16[128,1024]{1,0:T(8,128)(2,1)S(1)}, u32[]{:S(2)}, u32[]{:S(2)}) collective-permute-start(bf16[128,1024]{1,0:T(8,128)(2,1)S(1)} %collective-permute-done.4), channel_id=1, source_target_pairs={{1,0},{5,4},{9,8},{13,12},{17,16},{21,20},{25,24},{29,28}} | collective-permute-start | bytes 786440 | tf_op jit(solution)/shard_map/ppermute | solution.py:103
  30.4 18.5 %collective-permute-start.8 = (bf16[128,1024]{1,0:T(8,128)(2,1)S(1)}, bf16[128,1024]{1,0:T(8,128)(2,1)S(1)}, u32[]{:S(2)}, u32[]{:S(2)}) collective-permute-start(bf16[128,1024]{1,0:T(8,128)(2,1)S(1)} %collective-permute-done.7), channel_id=1, source_target_pairs={{2,3},{6,7},{10,11},{14,15},{18,19},{22,23},{26,27},{30,31}} | collective-permute-start | bytes 786440 | tf_op jit(solution)/shard_map/ppermute | solution.py:100
  34.0 17.1 %collective-permute-start.11 = (bf16[128,1024]{1,0:T(8,128)(2,1)S(1)}, bf16[128,1024]{1,0:T(8,128)(2,1)S(1)}, u32[]{:S(2)}, u32[]{:S(2)}) collective-permute-start(bf16[128,1024]{1,0:T(8,128)(2,1)S(1)} %collective-permute-done.10), channel_id=1, source_target_pairs={{1,0},{5,4},{9,8},{13,12},{17,16},{21,20},{25,24},{29,28}} | collective-permute-start | bytes 786440 | tf_op jit(solution)/shard_map/ppermute | solution.py:103
  44.6 18.2 %all-to-all-start = ((bf16[8,64,1024]{2,1,0:T(8,128)(2,1)}), bf16[8,64,1024]{2,1,0:T(8,128)(2,1)S(1)}, u32[]{:S(2)}, u32[]{:S(2)}) async-start(bf16[8,64,1024]{2,1,0:T(8,128)(2,1)} %broadcast_in_dim.4), calls=%async_computation | async-start | bytes 2097152 | tf_op jit(solution)/shard_map/all_to_all | solution.py:137
  63.9 18.9 %all-to-all-start.1 = ((bf16[8,64,1024]{2,1,0:T(8,128)(2,1)}), bf16[8,64,1024]{2,1,0:T(8,128)(2,1)S(1)}, u32[]{:S(2)}, u32[]{:S(2)}) async-start(bf16[8,64,1024]{2,1,0:T(8,128)(2,1)} %broadcast_in_dim.5), calls=%async_computation.1 | async-start | bytes 2097152 | tf_op jit(solution)/shard_map/all_to_all | solution.py:137
  82.8 18.9 %all-to-all-start.2 = ((bf16[8,64,1024]{2,1,0:T(8,128)(2,1)}), bf16[8,64,1024]{2,1,0:T(8,128)(2,1)S(1)}, u32[]{:S(2)}, u32[]{:S(2)}) async-start(bf16[8,64,1024]{2,1,0:T(8,128)(2,1)} %bitcast.63), calls=%async_computation.2 | async-start | bytes 2097152 | tf_op jit(solution)/shard_map/all_to_all | solution.py:144
  101.7 18.9 %all-to-all-start.3 = ((bf16[8,64,1024]{2,1,0:T(8,128)(2,1)}), bf16[8,64,1024]{2,1,0:T(8,128)(2,1)S(1)}, u32[]{:S(2)}, u32[]{:S(2)}) async-start(bf16[8,64,1024]{2,1,0:T(8,128)(2,1)} %bitcast.62), calls=%async_computation.3 | async-start | bytes 2097152 | tf_op jit(solution)/shard_map/all_to_all | solution.py:144
  113.1 13.1 %collective-permute-start.12 = (bf16[128,1024]{1,0:T(8,128)(2,1)}, bf16[128,1024]{1,0:T(8,128)(2,1)}, u32[]{:S(2)}, u32[]{:S(2)}) collective-permute-start(bf16[128,1024]{1,0:T(8,128)(2,1)} %get-tuple-element.26), channel_id=1, source_target_pairs={{3,2},{7,6},{11,10},{15,14},{19,18},{23,22},{27,26},{31,30}} | collective-permute-start | bytes 786440 | tf_op jit(solution)/shard_map/ppermute | solution.py:125
  124.9 10.8 %collective-permute-start.15 = (bf16[128,1024]{1,0:T(8,128)(2,1)}, bf16[128,1024]{1,0:T(8,128)(2,1)}, u32[]{:S(2)}, u32[]{:S(2)}) collective-permute-start(bf16[128,1024]{1,0:T(8,128)(2,1)} %get-tuple-element.27), channel_id=1, source_target_pairs={{0,1},{4,5},{8,9},{12,13},{16,17},{20,21},{24,25},{28,29}} | collective-permute-start | bytes 786440 | tf_op jit(solution)/shard_map/ppermute | solution.py:126
  128.1 11.5 %collective-permute-start.13 = (bf16[128,1024]{1,0:T(8,128)(2,1)}, bf16[128,1024]{1,0:T(8,128)(2,1)}, u32[]{:S(2)}, u32[]{:S(2)}) collective-permute-start(bf16[128,1024]{1,0:T(8,128)(2,1)} %add_convert_fusion.9), channel_id=1, source_target_pairs={{2,1},{3,2},{6,5},{7,6},{10,9},{11,10},{14,13},{15,14},{18,17},{19... | collective-permute-start | bytes 786440 | tf_op jit(solution)/shard_map/ppermute | solution.py:125
  129.5 18.6 %collective-permute-start.21 = (bf16[128,1024]{1,0:T(8,128)(2,1)S(1)}, bf16[128,1024]{1,0:T(8,128)(2,1)S(1)}, u32[]{:S(2)}, u32[]{:S(2)}) collective-permute-start(bf16[128,1024]{1,0:T(8,128)(2,1)S(1)} %get-tuple-element.31), channel_id=1, source_target_pairs={{0,1},{4,5},{8,9},{12,13},{16,17},{20,21},{24,25},{28,29}} | collective-permute-start | bytes 786440 | tf_op jit(solution)/shard_map/ppermute | solution.py:126
  131.8 16.3 %collective-permute-start.19 = (bf16[128,1024]{1,0:T(8,128)(2,1)S(1)}, bf16[128,1024]{1,0:T(8,128)(2,1)S(1)}, u32[]{:S(2)}, u32[]{:S(2)}) collective-permute-start(bf16[128,1024]{1,0:T(8,128)(2,1)S(1)} %add_convert_fusion.4), channel_id=1, source_target_pairs={{2,1},{3,2},{6,5},{7,6},{10,9},{11,10},{14,13},{15,14},{18,17},{19... | collective-permute-start | bytes 786440 | tf_op jit(solution)/shard_map/ppermute | solution.py:125
  141.1 9.9 %collective-permute-start.16 = (bf16[128,1024]{1,0:T(8,128)(2,1)S(1)}, bf16[128,1024]{1,0:T(8,128)(2,1)S(1)}, u32[]{:S(2)}, u32[]{:S(2)}) collective-permute-start(bf16[128,1024]{1,0:T(8,128)(2,1)S(1)} %get-tuple-element.25), channel_id=1, source_target_pairs={{0,1},{1,2},{4,5},{5,6},{8,9},{9,10},{12,13},{13,14},{16,17},{17,1... | collective-permute-start | bytes 786440 | tf_op jit(solution)/shard_map/ppermute | solution.py:126
  144.1 18.7 %collective-permute-start.14 = (bf16[128,1024]{1,0:T(8,128)(2,1)S(1)}, bf16[128,1024]{1,0:T(8,128)(2,1)S(1)}, u32[]{:S(2)}, u32[]{:S(2)}) collective-permute-start(bf16[128,1024]{1,0:T(8,128)(2,1)S(1)} %get-tuple-element.24), channel_id=1, source_target_pairs={{1,0},{2,1},{3,2},{5,4},{6,5},{7,6},{9,8},{10,9},{11,10},{13,12},{... | collective-permute-start | bytes 786440 | tf_op jit(solution)/shard_map/ppermute | solution.py:125
  149.0 10.9 %collective-permute-start.22 = (bf16[128,1024]{1,0:T(8,128)(2,1)S(1)}, bf16[128,1024]{1,0:T(8,128)(2,1)S(1)}, u32[]{:S(2)}, u32[]{:S(2)}) collective-permute-start(bf16[128,1024]{1,0:T(8,128)(2,1)S(1)} %get-tuple-element.29), channel_id=1, source_target_pairs={{0,1},{1,2},{4,5},{5,6},{8,9},{9,10},{12,13},{13,14},{16,17},{17,1... | collective-permute-start | bytes 786440 | tf_op jit(solution)/shard_map/ppermute | solution.py:126
  152.1 11.6 %collective-permute-start.17 = (bf16[128,1024]{1,0:T(8,128)(2,1)S(1)}, bf16[128,1024]{1,0:T(8,128)(2,1)S(1)}, u32[]{:S(2)}, u32[]{:S(2)}) collective-permute-start(bf16[128,1024]{1,0:T(8,128)(2,1)S(1)} %add_convert_fusion.6), channel_id=1, source_target_pairs={{0,1},{1,2},{2,3},{4,5},{5,6},{6,7},{8,9},{9,10},{10,11},{12,13},{... | collective-permute-start | bytes 786440 | tf_op jit(solution)/shard_map/ppermute | solution.py:126
  155.1 10.5 %collective-permute-start.20 = (bf16[128,1024]{1,0:T(8,128)(2,1)}, bf16[128,1024]{1,0:T(8,128)(2,1)S(1)}, u32[]{:S(2)}, u32[]{:S(2)}) collective-permute-start(bf16[128,1024]{1,0:T(8,128)(2,1)} %get-tuple-element.28), channel_id=1, source_target_pairs={{1,0},{2,1},{3,2},{5,4},{6,5},{7,6},{9,8},{10,9},{11,10},{13,12},{... | collective-permute-start | bytes 786440 | tf_op jit(solution)/shard_map/ppermute | solution.py:125
  (15 other events, 135.6 us)

commit v14 on v13

--- a/solution.py
+++ b/solution.py
@@ -13,9 +13,9 @@
 
 
 def attention_kernel(
-    ids_ref, q_ref, g_ref, kw_ref, vw_ref, kb_ref, vb_ref, wgrad_ref, bgrad_ref,
-    att_ref, dq_ref, *, rows, window, per_shard, group_size
+    ids_ref, q_ref, g_ref, kw_ref, vw_ref, kb_ref, vb_ref, *refs, rows, window, per_shard, group_size
 ):
+    wgrad_ref, bgrad_ref, att_ref, dq_ref = refs[-4:]
     scaling = HD ** (-0.5)
     head_id = ids_ref[0]
     shard_id = ids_ref[1]
@@ -57,7 +57,7 @@
     bgrad_ref[:, HD:] = value_grad[window:].astype(jnp.bfloat16)
 
 
-def attend_all(ids, queries, out_grad, kv_window, kv_beacons, per_shard, part, parts):
+def attend_all(ids, queries, out_grad, kv_window, kv_beacons, per_shard, part, parts, earlier):
     rows, q_width = queries.shape
     q_width = q_width // parts
     window, kv_double = kv_window.shape
@@ -68,7 +68,7 @@
         attention_kernel, rows=rows, window=window, per_shard=per_shard, group_size=group_size
     )
     qinblock = pl.BlockSpec((rows, group_size * HD), lambda h, ids: (0, h + part * kv_heads))
-    qblock = pl.BlockSpec((rows, group_size * HD), lambda h, ids: (0, h))
+    qblock = pl.BlockSpec((rows, group_size * HD), lambda h, ids: (0, h + part * kv_heads))
     kwblock = pl.BlockSpec((window, HD), lambda h, ids: (0, h))
     vwblock = pl.BlockSpec((window, HD), lambda h, ids: (0, h + kv_heads))
     kbblock = pl.BlockSpec((beacon_total, HD), lambda h, ids: (0, h))
@@ -80,16 +80,18 @@
         grid_spec=pltpu.PrefetchScalarGridSpec(
             num_scalar_prefetch=1,
             grid=(kv_heads,),
-            in_specs=[qinblock, qinblock, kwblock, vwblock, kbblock, vbblock],
+            in_specs=[qinblock, qinblock, kwblock, vwblock, kbblock, vbblock]
+            + [pl.BlockSpec(memory_space=pl.ANY) for _ in earlier],
             out_specs=[wgblock, bgblock, qblock, qblock],
         ),
         out_shape=[
             jax.ShapeDtypeStruct((window, kv_double), jnp.float32),
             jax.ShapeDtypeStruct((beacon_total, kv_double), jnp.bfloat16),
-            jax.ShapeDtypeStruct((rows, q_width), jnp.bfloat16),
-            jax.ShapeDtypeStruct((rows, q_width), jnp.bfloat16),
+            jax.ShapeDtypeStruct((rows, q_width * parts), jnp.bfloat16),
+            jax.ShapeDtypeStruct((rows, q_width * parts), jnp.bfloat16),
         ],
-    )(ids, queries, out_grad, kv_window, kv_window, kv_beacons, kv_beacons)
+        input_output_aliases={7 + i: 2 + i for i in range(len(earlier))},
+    )(ids, queries, out_grad, kv_window, kv_window, kv_beacons, kv_beacons, *earlier)
 
 
 def head_gather(block, axis, count):
@@ -127,7 +129,7 @@
     return block_of(index) + left.astype(jnp.float32) + right.astype(jnp.float32)
 
 
-def local_part(queries, keys, values, out_grad, positions, ids, heads_axis, ctx_axis, part, parts):
+def local_part(queries, keys, values, out_grad, positions, ids, heads_axis, ctx_axis, part, parts, earlier):
     kv_width = keys.shape[1]
     per_shard = positions.shape[0]
     kv_rows = jnp.concatenate([keys, values], axis=1)
@@ -139,7 +141,7 @@
         "ctx", 0, 0, tiled=True,
     ).reshape(ctx_axis * per_shard, 2 * kv_width)
     window_grads, beacon_grads, attended_out, query_out = attend_all(
-        ids, queries, out_grad, kv_window, kv_beacons, per_shard, part, parts
+        ids, queries, out_grad, kv_window, kv_beacons, per_shard, part, parts, earlier
     )
     beacon_parts = lax.all_to_all(
         beacon_grads.reshape(ctx_axis, per_shard, 2 * kv_width), "ctx", 0, 0, tiled=True
@@ -170,9 +172,11 @@
             local_part(
                 queries, keys[:, ks], values[:, ks], out_grad,
                 positions, ids, heads_axis, ctx_axis, part, parts,
+                results[-1][:2] if results else (),
             )
         )
-    return tuple(jnp.concatenate(outs, axis=1) for outs in zip(*results))
+    key_grad, value_grad = (jnp.concatenate(outs, axis=1) for outs in list(zip(*results))[2:])
+    return results[-1][0], results[-1][1], key_grad, value_grad
 
 
 def solution(mesh):

time: 174 us -> 173 us (level)
  local copies, waits for them, and re-layouts: 22 us -> 15.8 us
  waiting for transfers between devices: 32.9 us -> 37 us
  starting transfers between devices: 73.4 us -> 75.6 us
  other arithmetic: 18.3 us -> 16.3 us
    ppermute x6, waiting for transfers between devices: 2.93 us -> 7.48 us  [head_gather(): lax.ppermute(from_right[-1], axis, [(j + 1, j) for j in range(count - ste...]
    unnamed x38 -> x32, local copies, waits for them, and re-layouts: 8.33 us -> 4.64 us
    ppermute x6, starting transfers between devices: 10.4 us -> 13.7 us  [head_reduce(): lax.ppermute(send_right, axis, [(j, j + 1) for j in range(0, min(step, co...]
    concatenate x4 -> x2, other arithmetic: 2.15 us -> 0.04 us  [local(): jnp.concatenate(outs, axis=1)]
    ppermute x6, starting transfers between devices: 13.4 us -> 11.5 us  [head_reduce(): lax.ppermute(send_left, axis, [(j, j - 1) for j in range(max(1, count - s...]
  transfers between devices with their start and end apart: 28 -> 28, of which waited for: 10 -> 11; matrix products, arithmetic and copies ran while one was open for 20% -> 15% of each run, Pallas kernels for 14% -> 14%
where the time goes in v14:
time: 173 us; the launch traced here: 170 us
  starting transfers between devices  75.6 us (44%)
  waiting for transfers between devices  37 us (21%)
  Pallas kernels  24.1 us (14%)
  other arithmetic  16.3 us (9%)
  local copies, waits for them, and re-layouts  15.8 us (9%)
    pallas_call x2, Pallas kernels, attend_all(): pl.pallas_call(kernel, grid_spec=pltpu.PrefetchScalarGridSpec(num_scalar_...  24.1 us
    ppermute x6, starting transfers between devices, head_gather(): lax.ppermute(from_left[-1], axis, [(j, j + 1) for j in range(step - 1, co...  15.7 us
    ppermute x6, starting transfers between devices, head_gather(): lax.ppermute(from_right[-1], axis, [(j + 1, j) for j in range(count - ste...  15.5 us
    ppermute x6, starting transfers between devices, head_reduce(): lax.ppermute(send_right, axis, [(j, j + 1) for j in range(0, min(step, co...  13.7 us
    ppermute x6, starting transfers between devices, head_reduce(): lax.ppermute(send_left, axis, [(j, j - 1) for j in range(max(1, count - s...  11.5 us
    all_to_all x2, waiting for transfers between devices, local_part(): lax.all_to_all(jnp.broadcast_to(own_beacon_rows[None], (ctx_axis,) + own_...  10.2 us
    all_to_all x2, starting transfers between devices, local_part(): lax.all_to_all(beacon_grads.reshape(ctx_axis, per_shard, 2 * kv_width), '...  9.97 us
    all_to_all x2, starting transfers between devices, local_part(): lax.all_to_all(jnp.broadcast_to(own_beacon_rows[None], (ctx_axis,) + own_...  9.23 us
  transfers between devices with their start and end apart: 28, of which 11 were waited for; matrix products, arithmetic and copies ran while one was open for 15% of the time, Pallas kernels for 14%

profile of v14, /device:TPU:10, one launch (start us, length us, event | category | flops | bytes accessed | tf_op | source)
XLA Modules:
  0.0 170.1 jit_solution(2352129830792636971)
XLA Ops:
  2.7 3.5 %collective-permute-start = (bf16[128,1024]{1,0:T(8,128)(2,1)S(1)}, bf16[128,1024]{1,0:T(8,128)(2,1)S(1)}, u32[]{:S(2)}, u32[]{:S(2)}) collective-permute-start(bf16[128,1024]{1,0:T(8,128)(2,1)S(1)} %pad_maximum_fusion.2), channel_id=1, source_target_pairs={{0,1},{1,2},{2,3},{4,5},{5,6},{6,7},{8,9},{9,10},{10,11},{12,13},{... | collective-permute-start | bytes 786440 | tf_op jit(solution)/shard_map/ppermute | solution.py:102
  8.6 3.5 %collective-permute-start.6 = (bf16[128,1024]{1,0:T(8,128)(2,1)S(1)}, bf16[128,1024]{1,0:T(8,128)(2,1)S(1)}, u32[]{:S(2)}, u32[]{:S(2)}) collective-permute-start(bf16[128,1024]{1,0:T(8,128)(2,1)S(1)} %pad_maximum_fusion.3), channel_id=1, source_target_pairs={{0,1},{1,2},{2,3},{4,5},{5,6},{6,7},{8,9},{9,10},{10,11},{12,13},{... | collective-permute-start | bytes 786440 | tf_op jit(solution)/shard_map/ppermute | solution.py:102
  14.6 3.5 %collective-permute-start.1 = (bf16[128,1024]{1,0:T(8,128)(2,1)S(1)}, bf16[128,1024]{1,0:T(8,128)(2,1)S(1)}, u32[]{:S(2)}, u32[]{:S(2)}) collective-permute-start(bf16[128,1024]{1,0:T(8,128)(2,1)S(1)} %collective-permute-done), channel_id=1, source_target_pairs={{1,2},{2,3},{5,6},{6,7},{9,10},{10,11},{13,14},{14,15},{17,18},{18... | collective-permute-start | bytes 786440 | tf_op jit(solution)/shard_map/ppermute | solution.py:102
  20.0 3.9 %collective-permute-start.7 = (bf16[128,1024]{1,0:T(8,128)(2,1)S(1)}, bf16[128,1024]{1,0:T(8,128)(2,1)S(1)}, u32[]{:S(2)}, u32[]{:S(2)}) collective-permute-start(bf16[128,1024]{1,0:T(8,128)(2,1)S(1)} %collective-permute-done.6), channel_id=1, source_target_pairs={{1,2},{2,3},{5,6},{6,7},{9,10},{10,11},{13,14},{14,15},{17,18},{18... | collective-permute-start | bytes 786440 | tf_op jit(solution)/shard_map/ppermute | solution.py:102
  27.7 2.5 %collective-permute-start.5 = (bf16[128,1024]{1,0:T(8,128)(2,1)S(1)}, bf16[128,1024]{1,0:T(8,128)(2,1)S(1)}, u32[]{:S(2)}, u32[]{:S(2)}) collective-permute-start(bf16[128,1024]{1,0:T(8,128)(2,1)S(1)} %collective-permute-done.4), channel_id=1, source_target_pairs={{1,0},{5,4},{9,8},{13,12},{17,16},{21,20},{25,24},{29,28}} | collective-permute-start | bytes 786440 | tf_op jit(solution)/shard_map/ppermute | solution.py:105
  32.7 4.4 %collective-permute-start.11 = (bf16[128,1024]{1,0:T(8,128)(2,1)S(1)}, bf16[128,1024]{1,0:T(8,128)(2,1)S(1)}, u32[]{:S(2)}, u32[]{:S(2)}) collective-permute-start(bf16[128,1024]{1,0:T(8,128)(2,1)S(1)} %collective-permute-done.10), channel_id=1, source_target_pairs={{1,0},{5,4},{9,8},{13,12},{17,16},{21,20},{25,24},{29,28}} | collective-permute-start | bytes 786440 | tf_op jit(solution)/shard_map/ppermute | solution.py:105
  37.2 4.7 %collective-permute-done.11 = bf16[128,1024]{1,0:T(8,128)(2,1)S(1)} collective-permute-done((bf16[128,1024]{1,0:T(8,128)(2,1)S(1)}, bf16[128,1024]{1,0:T(8,128)(2,1)S(1)}, u32[]{:S(2)}, u32[]{:S(2)}) %collective-permute-start.11) | collective-permute-done | bytes 262176 | tf_op jit(solution)/shard_map/ppermute | solution.py:105
  43.9 4.3 %all-to-all-start.1 = ((bf16[8,64,1024]{2,1,0:T(8,128)(2,1)}), bf16[8,64,1024]{2,1,0:T(8,128)(2,1)S(1)}, u32[]{:S(2)}, u32[]{:S(2)}) async-start(bf16[8,64,1024]{2,1,0:T(8,128)(2,1)} %broadcast_in_dim.5), calls=%async_computation.1 | async-start | bytes 2097152 | tf_op jit(solution)/shard_map/all_to_all | solution.py:139
  53.1 9.0 %all-to-all-done.1 = bf16[8,64,1024]{2,1,0:T(8,128)(2,1)S(1)} async-done(((bf16[8,64,1024]{2,1,0:T(8,128)(2,1)}), bf16[8,64,1024]{2,1,0:T(8,128)(2,1)S(1)}, u32[]{:S(2)}, u32[]{:S(2)}) %all-to-all-start.1) | async-done | bytes 1048608 | tf_op jit(solution)/shard_map/all_to_all | solution.py:139
  63.3 5.0 %all-to-all-start = ((bf16[8,64,1024]{2,1,0:T(8,128)(2,1)}), bf16[8,64,1024]{2,1,0:T(8,128)(2,1)S(1)}, u32[]{:S(2)}, u32[]{:S(2)}) async-start(bf16[8,64,1024]{2,1,0:T(8,128)(2,1)} %broadcast_in_dim.4), calls=%async_computation | async-start | bytes 2097152 | tf_op jit(solution)/shard_map/all_to_all | solution.py:139
  68.9 12.1 %shard_map.84 = (f32[512,1024]{1,0:T(8,128)}, bf16[512,1024]{1,0:T(8,128)(2,1)}, bf16[128,4096]{1,0:T(8,128)(2,1)}, bf16[128,4096]{1,0:T(8,128)(2,1)}) custom-call(s32[2]{0:T(128)} %pad_add_fusion.ids_ref, bf16[128,4096]{1,0:T(8,128)(2,1)} %q_ref.3, bf16[128,4096]{1,0:T(8,128)(2,1)} %g_ref.3, bf16[512,1024]{1,0:T(8,128)(2,1)} %copy-done, ...), custom_call_target="tpu_custom_call" | custom-call | tf_op jit(solution)/shard_map/pallas_call | solution.py:78
  82.2 5.0 %all-to-all-start.2 = ((bf16[8,64,1024]{2,1,0:T(8,128)(2,1)}), bf16[8,64,1024]{2,1,0:T(8,128)(2,1)S(1)}, u32[]{:S(2)}, u32[]{:S(2)}) async-start(bf16[8,64,1024]{2,1,0:T(8,128)(2,1)} %bitcast.63), calls=%async_computation.2 | async-start | bytes 2097152 | tf_op jit(solution)/shard_map/all_to_all | solution.py:146
  87.2 12.0 %shard_map.85 = (f32[512,1024]{1,0:T(8,128)}, bf16[512,1024]{1,0:T(8,128)(2,1)}, bf16[128,4096]{1,0:T(8,128)(2,1)}, bf16[128,4096]{1,0:T(8,128)(2,1)}) custom-call(s32[2]{0:T(128)} %pad_add_fusion.ids_ref, bf16[128,4096]{1,0:T(8,128)(2,1)} %q_ref.3, bf16[128,4096]{1,0:T(8,128)(2,1)} %g_ref.3, ...), custom_call_target="tpu_custom_call", output_to_operand_aliasing={{2}: (7, {}), {3}: (8, {})} | custom-call | tf_op jit(solution)/shard_map/pallas_call | solution.py:78
  101.1 5.0 %all-to-all-start.3 = ((bf16[8,64,1024]{2,1,0:T(8,128)(2,1)}), bf16[8,64,1024]{2,1,0:T(8,128)(2,1)S(1)}, u32[]{:S(2)}, u32[]{:S(2)}) async-start(bf16[8,64,1024]{2,1,0:T(8,128)(2,1)} %bitcast.62), calls=%async_computation.3 | async-start | bytes 2097152 | tf_op jit(solution)/shard_map/all_to_all | solution.py:146
  106.3 4.0 %scatter_fusion = f32[512,1024]{1,0:T(8,128)} fusion(f32[512,1024]{1,0:T(8,128)} %get-tuple-element.16, s32[64]{0:T(128)S(1)} %fusion, f32[64,1024]{1,0:T(8,128)S(1)} %convert_reduce_fusion.1), kind=kCustom, calls=%fused_computation.2 | custom fusion | flops 65536 | bytes 786688 | tf_op jit(solution)/shard_map/scatter-add | solution.py:150
  113.8 6.2 %all-to-all-done.3 = bf16[8,64,1024]{2,1,0:T(8,128)(2,1)S(1)} async-done(((bf16[8,64,1024]{2,1,0:T(8,128)(2,1)}), bf16[8,64,1024]{2,1,0:T(8,128)(2,1)S(1)}, u32[]{:S(2)}, u32[]{:S(2)}) %all-to-all-start.3) | async-done | bytes 1048608 | tf_op jit(solution)/shard_map/all_to_all | solution.py:146
  129.4 4.6 %collective-permute-done.15 = bf16[128,1024]{1,0:T(8,128)(2,1)} collective-permute-done((bf16[128,1024]{1,0:T(8,128)(2,1)S(1)}, bf16[128,1024]{1,0:T(8,128)(2,1)}, u32[]{:S(2)}, u32[]{:S(2)}) %collective-permute-start.15) | collective-permute-done | bytes 262176 | tf_op jit(solution)/shard_map/ppermute | solution.py:128
  134.0 2.5 %collective-permute-done.13 = bf16[128,1024]{1,0:T(8,128)(2,1)} collective-permute-done((bf16[128,1024]{1,0:T(8,128)(2,1)S(1)}, bf16[128,1024]{1,0:T(8,128)(2,1)}, u32[]{:S(2)}, u32[]{:S(2)}) %collective-permute-start.13) | collective-permute-done | bytes 262176 | tf_op jit(solution)/shard_map/ppermute | solution.py:127
  138.8 3.9 %collective-permute-start.16 = (bf16[128,1024]{1,0:T(8,128)(2,1)}, bf16[128,1024]{1,0:T(8,128)(2,1)S(1)}, u32[]{:S(2)}, u32[]{:S(2)}) collective-permute-start(bf16[128,1024]{1,0:T(8,128)(2,1)} %get-tuple-element.25), channel_id=1, source_target_pairs={{0,1},{1,2},{4,5},{5,6},{8,9},{9,10},{12,13},{13,14},{16,17},{17,1... | collective-permute-start | bytes 786440 | tf_op jit(solution)/shard_map/ppermute | solution.py:128
  144.6 2.4 %collective-permute-start.22 = (bf16[128,1024]{1,0:T(8,128)(2,1)}, bf16[128,1024]{1,0:T(8,128)(2,1)S(1)}, u32[]{:S(2)}, u32[]{:S(2)}) collective-permute-start(bf16[128,1024]{1,0:T(8,128)(2,1)} %get-tuple-element.29), channel_id=1, source_target_pairs={{0,1},{1,2},{4,5},{5,6},{8,9},{9,10},{12,13},{13,14},{16,17},{17,1... | collective-permute-start | bytes 786440 | tf_op jit(solution)/shard_map/ppermute | solution.py:128
  147.1 3.4 %collective-permute-start.14 = (bf16[128,1024]{1,0:T(8,128)(2,1)}, bf16[128,1024]{1,0:T(8,128)(2,1)S(1)}, u32[]{:S(2)}, u32[]{:S(2)}) collective-permute-start(bf16[128,1024]{1,0:T(8,128)(2,1)} %get-tuple-element.24), channel_id=1, source_target_pairs={{1,0},{2,1},{3,2},{5,4},{6,5},{7,6},{9,8},{10,9},{11,10},{13,12},{... | collective-permute-start | bytes 786440 | tf_op jit(solution)/shard_map/ppermute | solution.py:127
  152.3 2.4 %collective-permute-start.17 = (bf16[128,1024]{1,0:T(8,128)(2,1)}, bf16[128,1024]{1,0:T(8,128)(2,1)S(1)}, u32[]{:S(2)}, u32[]{:S(2)}) collective-permute-start(bf16[128,1024]{1,0:T(8,128)(2,1)} %add_convert_fusion.6), channel_id=1, source_target_pairs={{0,1},{1,2},{2,3},{4,5},{5,6},{6,7},{8,9},{9,10},{10,11},{12,13},{... | collective-permute-start | bytes 786440 | tf_op jit(solution)/shard_map/ppermute | solution.py:128
  154.7 3.4 %collective-permute-start.20 = (bf16[128,1024]{1,0:T(8,128)(2,1)}, bf16[128,1024]{1,0:T(8,128)(2,1)S(1)}, u32[]{:S(2)}, u32[]{:S(2)}) collective-permute-start(bf16[128,1024]{1,0:T(8,128)(2,1)} %get-tuple-element.28), channel_id=1, source_target_pairs={{1,0},{2,1},{3,2},{5,4},{6,5},{7,6},{9,8},{10,9},{11,10},{13,12},{... | collective-permute-start | bytes 786440 | tf_op jit(solution)/shard_map/ppermute | solution.py:127
  163.6 3.8 %collective-permute-done.23 = bf16[128,1024]{1,0:T(8,128)(2,1)S(1)} collective-permute-done((bf16[128,1024]{1,0:T(8,128)(2,1)}, bf16[128,1024]{1,0:T(8,128)(2,1)S(1)}, u32[]{:S(2)}, u32[]{:S(2)}) %collective-permute-start.23) | collective-permute-done | bytes 262176 | tf_op jit(solution)/shard_map/ppermute | solution.py:128
  (104 shorter events, 53.8 us)
Async XLA Ops:
  2.7 11.9 %collective-permute-start = (bf16[128,1024]{1,0:T(8,128)(2,1)S(1)}, bf16[128,1024]{1,0:T(8,128)(2,1)S(1)}, u32[]{:S(2)}, u32[]{:S(2)}) collective-permute-start(bf16[128,1024]{1,0:T(8,128)(2,1)S(1)} %pad_maximum_fusion.2), channel_id=1, source_target_pairs={{0,1},{1,2},{2,3},{4,5},{5,6},{6,7},{8,9},{9,10},{10,11},{12,13},{... | collective-permute-start | bytes 786440 | tf_op jit(solution)/shard_map/ppermute | solution.py:102
  6.1 11.9 %collective-permute-start.3 = (bf16[128,1024]{1,0:T(8,128)(2,1)S(1)}, bf16[128,1024]{1,0:T(8,128)(2,1)S(1)}, u32[]{:S(2)}, u32[]{:S(2)}) collective-permute-start(bf16[128,1024]{1,0:T(8,128)(2,1)S(1)} %pad_maximum_fusion.2), channel_id=1, source_target_pairs={{1,0},{2,1},{3,2},{5,4},{6,5},{7,6},{9,8},{10,9},{11,10},{13,12},{... | collective-permute-start | bytes 786440 | tf_op jit(solution)/shard_map/ppermute | solution.py:105
  8.6 11.4 %collective-permute-start.6 = (bf16[128,1024]{1,0:T(8,128)(2,1)S(1)}, bf16[128,1024]{1,0:T(8,128)(2,1)S(1)}, u32[]{:S(2)}, u32[]{:S(2)}) collective-permute-start(bf16[128,1024]{1,0:T(8,128)(2,1)S(1)} %pad_maximum_fusion.3), channel_id=1, source_target_pairs={{0,1},{1,2},{2,3},{4,5},{5,6},{6,7},{8,9},{9,10},{10,11},{12,13},{... | collective-permute-start | bytes 786440 | tf_op jit(solution)/shard_map/ppermute | solution.py:102
  12.0 11.9 %collective-permute-start.9 = (bf16[128,1024]{1,0:T(8,128)(2,1)S(1)}, bf16[128,1024]{1,0:T(8,128)(2,1)S(1)}, u32[]{:S(2)}, u32[]{:S(2)}) collective-permute-start(bf16[128,1024]{1,0:T(8,128)(2,1)S(1)} %pad_maximum_fusion.3), channel_id=1, source_target_pairs={{1,0},{2,1},{3,2},{5,4},{6,5},{7,6},{9,8},{10,9},{11,10},{13,12},{... | collective-permute-start | bytes 786440 | tf_op jit(solution)/shard_map/ppermute | solution.py:105
  14.6 11.4 %collective-permute-start.1 = (bf16[128,1024]{1,0:T(8,128)(2,1)S(1)}, bf16[128,1024]{1,0:T(8,128)(2,1)S(1)}, u32[]{:S(2)}, u32[]{:S(2)}) collective-permute-start(bf16[128,1024]{1,0:T(8,128)(2,1)S(1)} %collective-permute-done), channel_id=1, source_target_pairs={{1,2},{2,3},{5,6},{6,7},{9,10},{10,11},{13,14},{14,15},{17,18},{18... | collective-permute-start | bytes 786440 | tf_op jit(solution)/shard_map/ppermute | solution.py:102
  18.1 9.6 %collective-permute-start.4 = (bf16[128,1024]{1,0:T(8,128)(2,1)S(1)}, bf16[128,1024]{1,0:T(8,128)(2,1)S(1)}, u32[]{:S(2)}, u32[]{:S(2)}) collective-permute-start(bf16[128,1024]{1,0:T(8,128)(2,1)S(1)} %collective-permute-done.3), channel_id=1, source_target_pairs={{1,0},{2,1},{5,4},{6,5},{9,8},{10,9},{13,12},{14,13},{17,16},{18,1... | collective-permute-start | bytes 786440 | tf_op jit(solution)/shard_map/ppermute | solution.py:105
  20.0 10.3 %collective-permute-start.7 = (bf16[128,1024]{1,0:T(8,128)(2,1)S(1)}, bf16[128,1024]{1,0:T(8,128)(2,1)S(1)}, u32[]{:S(2)}, u32[]{:S(2)}) collective-permute-start(bf16[128,1024]{1,0:T(8,128)(2,1)S(1)} %collective-permute-done.6), channel_id=1, source_target_pairs={{1,2},{2,3},{5,6},{6,7},{9,10},{10,11},{13,14},{14,15},{17,18},{18... | collective-permute-start | bytes 786440 | tf_op jit(solution)/shard_map/ppermute | solution.py:102
  26.0 22.2 %collective-permute-start.2 = (bf16[128,1024]{1,0:T(8,128)(2,1)S(1)}, bf16[128,1024]{1,0:T(8,128)(2,1)S(1)}, u32[]{:S(2)}, u32[]{:S(2)}) collective-permute-start(bf16[128,1024]{1,0:T(8,128)(2,1)S(1)} %collective-permute-done.1), channel_id=1, source_target_pairs={{2,3},{6,7},{10,11},{14,15},{18,19},{22,23},{26,27},{30,31}} | collective-permute-start | bytes 786440 | tf_op jit(solution)/shard_map/ppermute | solution.py:102
  27.7 22.6 %collective-permute-start.5 = (bf16[128,1024]{1,0:T(8,128)(2,1)S(1)}, bf16[128,1024]{1,0:T(8,128)(2,1)S(1)}, u32[]{:S(2)}, u32[]{:S(2)}) collective-permute-start(bf16[128,1024]{1,0:T(8,128)(2,1)S(1)} %collective-permute-done.4), channel_id=1, source_target_pairs={{1,0},{5,4},{9,8},{13,12},{17,16},{21,20},{25,24},{29,28}} | collective-permute-start | bytes 786440 | tf_op jit(solution)/shard_map/ppermute | solution.py:105
  32.7 9.2 %collective-permute-start.11 = (bf16[128,1024]{1,0:T(8,128)(2,1)S(1)}, bf16[128,1024]{1,0:T(8,128)(2,1)S(1)}, u32[]{:S(2)}, u32[]{:S(2)}) collective-permute-start(bf16[128,1024]{1,0:T(8,128)(2,1)S(1)} %collective-permute-done.10), channel_id=1, source_target_pairs={{1,0},{5,4},{9,8},{13,12},{17,16},{21,20},{25,24},{29,28}} | collective-permute-start | bytes 786440 | tf_op jit(solution)/shard_map/ppermute | solution.py:105
  43.9 18.2 %all-to-all-start.1 = ((bf16[8,64,1024]{2,1,0:T(8,128)(2,1)}), bf16[8,64,1024]{2,1,0:T(8,128)(2,1)S(1)}, u32[]{:S(2)}, u32[]{:S(2)}) async-start(bf16[8,64,1024]{2,1,0:T(8,128)(2,1)} %broadcast_in_dim.5), calls=%async_computation.1 | async-start | bytes 2097152 | tf_op jit(solution)/shard_map/all_to_all | solution.py:139
  63.3 18.9 %all-to-all-start = ((bf16[8,64,1024]{2,1,0:T(8,128)(2,1)}), bf16[8,64,1024]{2,1,0:T(8,128)(2,1)S(1)}, u32[]{:S(2)}, u32[]{:S(2)}) async-start(bf16[8,64,1024]{2,1,0:T(8,128)(2,1)} %broadcast_in_dim.4), calls=%async_computation | async-start | bytes 2097152 | tf_op jit(solution)/shard_map/all_to_all | solution.py:139
  82.2 18.9 %all-to-all-start.2 = ((bf16[8,64,1024]{2,1,0:T(8,128)(2,1)}), bf16[8,64,1024]{2,1,0:T(8,128)(2,1)S(1)}, u32[]{:S(2)}, u32[]{:S(2)}) async-start(bf16[8,64,1024]{2,1,0:T(8,128)(2,1)} %bitcast.63), calls=%async_computation.2 | async-start | bytes 2097152 | tf_op jit(solution)/shard_map/all_to_all | solution.py:146
  101.1 18.9 %all-to-all-start.3 = ((bf16[8,64,1024]{2,1,0:T(8,128)(2,1)}), bf16[8,64,1024]{2,1,0:T(8,128)(2,1)S(1)}, u32[]{:S(2)}, u32[]{:S(2)}) async-start(bf16[8,64,1024]{2,1,0:T(8,128)(2,1)} %bitcast.62), calls=%async_computation.3 | async-start | bytes 2097152 | tf_op jit(solution)/shard_map/all_to_all | solution.py:146
  112.5 11.7 %collective-permute-start.12 = (bf16[128,1024]{1,0:T(8,128)(2,1)}, bf16[128,1024]{1,0:T(8,128)(2,1)}, u32[]{:S(2)}, u32[]{:S(2)}) collective-permute-start(bf16[128,1024]{1,0:T(8,128)(2,1)} %get-tuple-element.26), channel_id=1, source_target_pairs={{3,2},{7,6},{11,10},{15,14},{19,18},{23,22},{27,26},{31,30}} | collective-permute-start | bytes 786440 | tf_op jit(solution)/shard_map/ppermute | solution.py:127
  122.9 11.1 %collective-permute-start.15 = (bf16[128,1024]{1,0:T(8,128)(2,1)S(1)}, bf16[128,1024]{1,0:T(8,128)(2,1)}, u32[]{:S(2)}, u32[]{:S(2)}) collective-permute-start(bf16[128,1024]{1,0:T(8,128)(2,1)S(1)} %copy-done.6), channel_id=1, source_target_pairs={{0,1},{4,5},{8,9},{12,13},{16,17},{20,21},{24,25},{28,29}} | collective-permute-start | bytes 786440 | tf_op jit(solution)/shard_map/ppermute | solution.py:128
  125.4 11.2 %collective-permute-start.13 = (bf16[128,1024]{1,0:T(8,128)(2,1)S(1)}, bf16[128,1024]{1,0:T(8,128)(2,1)}, u32[]{:S(2)}, u32[]{:S(2)}) collective-permute-start(bf16[128,1024]{1,0:T(8,128)(2,1)S(1)} %add_convert_fusion.9), channel_id=1, source_target_pairs={{2,1},{3,2},{6,5},{7,6},{10,9},{11,10},{14,13},{15,14},{18,17},{19... | collective-permute-start | bytes 786440 | tf_op jit(solution)/shard_map/ppermute | solution.py:127
  126.7 16.0 %collective-permute-start.21 = (bf16[128,1024]{1,0:T(8,128)(2,1)S(1)}, bf16[128,1024]{1,0:T(8,128)(2,1)}, u32[]{:S(2)}, u32[]{:S(2)}) collective-permute-start(bf16[128,1024]{1,0:T(8,128)(2,1)S(1)} %get-tuple-element.31), channel_id=1, source_target_pairs={{0,1},{4,5},{8,9},{12,13},{16,17},{20,21},{24,25},{28,29}} | collective-permute-start | bytes 786440 | tf_op jit(solution)/shard_map/ppermute | solution.py:128
  128.1 14.7 %collective-permute-start.19 = (bf16[128,1024]{1,0:T(8,128)(2,1)S(1)}, bf16[128,1024]{1,0:T(8,128)(2,1)S(1)}, u32[]{:S(2)}, u32[]{:S(2)}) collective-permute-start(bf16[128,1024]{1,0:T(8,128)(2,1)S(1)} %add_convert_fusion.4), channel_id=1, source_target_pairs={{2,1},{3,2},{6,5},{7,6},{10,9},{11,10},{14,13},{15,14},{18,17},{19... | collective-permute-start | bytes 786440 | tf_op jit(solution)/shard_map/ppermute | solution.py:127
  138.8 11.7 %collective-permute-start.16 = (bf16[128,1024]{1,0:T(8,128)(2,1)}, bf16[128,1024]{1,0:T(8,128)(2,1)S(1)}, u32[]{:S(2)}, u32[]{:S(2)}) collective-permute-start(bf16[128,1024]{1,0:T(8,128)(2,1)} %get-tuple-element.25), channel_id=1, source_target_pairs={{0,1},{1,2},{4,5},{5,6},{8,9},{9,10},{12,13},{13,14},{16,17},{17,1... | collective-permute-start | bytes 786440 | tf_op jit(solution)/shard_map/ppermute | solution.py:128
  144.6 13.6 %collective-permute-start.22 = (bf16[128,1024]{1,0:T(8,128)(2,1)}, bf16[128,1024]{1,0:T(8,128)(2,1)S(1)}, u32[]{:S(2)}, u32[]{:S(2)}) collective-permute-start(bf16[128,1024]{1,0:T(8,128)(2,1)} %get-tuple-element.29), channel_id=1, source_target_pairs={{0,1},{1,2},{4,5},{5,6},{8,9},{9,10},{12,13},{13,14},{16,17},{17,1... | collective-permute-start | bytes 786440 | tf_op jit(solution)/shard_map/ppermute | solution.py:128
  147.1 14.3 %collective-permute-start.14 = (bf16[128,1024]{1,0:T(8,128)(2,1)}, bf16[128,1024]{1,0:T(8,128)(2,1)S(1)}, u32[]{:S(2)}, u32[]{:S(2)}) collective-permute-start(bf16[128,1024]{1,0:T(8,128)(2,1)} %get-tuple-element.24), channel_id=1, source_target_pairs={{1,0},{2,1},{3,2},{5,4},{6,5},{7,6},{9,8},{10,9},{11,10},{13,12},{... | collective-permute-start | bytes 786440 | tf_op jit(solution)/shard_map/ppermute | solution.py:127
  152.3 9.1 %collective-permute-start.17 = (bf16[128,1024]{1,0:T(8,128)(2,1)}, bf16[128,1024]{1,0:T(8,128)(2,1)S(1)}, u32[]{:S(2)}, u32[]{:S(2)}) collective-permute-start(bf16[128,1024]{1,0:T(8,128)(2,1)} %add_convert_fusion.6), channel_id=1, source_target_pairs={{0,1},{1,2},{2,3},{4,5},{5,6},{6,7},{8,9},{9,10},{10,11},{12,13},{... | collective-permute-start | bytes 786440 | tf_op jit(solution)/shard_map/ppermute | solution.py:128
  154.7 8.8 %collective-permute-start.20 = (bf16[128,1024]{1,0:T(8,128)(2,1)}, bf16[128,1024]{1,0:T(8,128)(2,1)S(1)}, u32[]{:S(2)}, u32[]{:S(2)}) collective-permute-start(bf16[128,1024]{1,0:T(8,128)(2,1)} %get-tuple-element.28), channel_id=1, source_target_pairs={{1,0},{2,1},{3,2},{5,4},{6,5},{7,6},{9,8},{10,9},{11,10},{13,12},{... | collective-permute-start | bytes 786440 | tf_op jit(solution)/shard_map/ppermute | solution.py:127
  (12 other events, 85.6 us)

commit v15 on v14

--- a/solution.py
+++ b/solution.py
@@ -22,19 +22,20 @@
     k = jnp.concatenate([kw_ref[...], kb_ref[...]], axis=0)
     v = jnp.concatenate([vw_ref[...], vb_ref[...]], axis=0)
     key_count = k.shape[0]
-    stacked = rows * group_size
-    row = lax.rem(lax.broadcasted_iota(jnp.int32, (stacked, key_count), 0), rows) + head_id * rows
-    col = lax.broadcasted_iota(jnp.int32, (stacked, key_count), 1)
+    row = lax.broadcasted_iota(jnp.int32, (rows, key_count), 0) + head_id * rows
+    col = lax.broadcasted_iota(jnp.int32, (rows, key_count), 1)
     in_window = col < window
     visible = (in_window & (row >= col)) | (
         jnp.logical_not(in_window) & (col < window + shard_id * per_shard)
     )
+    hidden = jnp.where(visible, 0.0, NEG_FILL).astype(jnp.float32)
+    hidden = jnp.concatenate([hidden] * group_size, axis=0)
     nt = (((1,), (1,)), ((), ()))
     tn = (((0,), (0,)), ((), ()))
     q = jnp.concatenate([q_ref[:, g * HD:(g + 1) * HD] for g in range(group_size)], axis=0)
     do = jnp.concatenate([g_ref[:, g * HD:(g + 1) * HD] for g in range(group_size)], axis=0)
     scores = lax.dot_general(q, k, nt, preferred_element_type=jnp.float32) * scaling
-    scores = jnp.where(visible, scores, NEG_FILL)
+    scores = scores + hidden
     row_max = jnp.max(scores, axis=1, keepdims=True)
     weights = jnp.exp(scores - row_max)
     probs = weights / jnp.sum(weights, axis=1, keepdims=True)

time: 173 us -> 173 us (level)
  no operation moved by 1% of the time
where the time goes in v15:
time: 173 us; the launch traced here: 170 us
  starting transfers between devices  75.6 us (44%)
  waiting for transfers between devices  37.3 us (22%)
  Pallas kernels  23.8 us (14%)
  other arithmetic  16.3 us (9%)
  local copies, waits for them, and re-layouts  15.8 us (9%)
    pallas_call x2, Pallas kernels, attend_all(): pl.pallas_call(kernel, grid_spec=pltpu.PrefetchScalarGridSpec(num_scalar_...  23.8 us
    ppermute x6, starting transfers between devices, head_gather(): lax.ppermute(from_left[-1], axis, [(j, j + 1) for j in range(step - 1, co...  15.7 us
    ppermute x6, starting transfers between devices, head_gather(): lax.ppermute(from_right[-1], axis, [(j + 1, j) for j in range(count - ste...  15.5 us
    ppermute x6, starting transfers between devices, head_reduce(): lax.ppermute(send_right, axis, [(j, j + 1) for j in range(0, min(step, co...  13.7 us
    ppermute x6, starting transfers between devices, head_reduce(): lax.ppermute(send_left, axis, [(j, j - 1) for j in range(max(1, count - s...  11.5 us
    all_to_all x2, waiting for transfers between devices, local_part(): lax.all_to_all(jnp.broadcast_to(own_beacon_rows[None], (ctx_axis,) + own_...  10.4 us
    all_to_all x2, starting transfers between devices, local_part(): lax.all_to_all(beacon_grads.reshape(ctx_axis, per_shard, 2 * kv_width), '...  9.97 us
    all_to_all x2, starting transfers between devices, local_part(): lax.all_to_all(jnp.broadcast_to(own_beacon_rows[None], (ctx_axis,) + own_...  9.23 us
  transfers between devices with their start and end apart: 28, of which 11 were waited for; matrix products, arithmetic and copies ran while one was open for 15% of the time, Pallas kernels for 14%

profile of v15, /device:TPU:10, one launch (start us, length us, event | category | flops | bytes accessed | tf_op | source)
XLA Modules:
  0.0 170.1 jit_solution(9637442778558452236)
XLA Ops:
  2.7 3.5 %collective-permute-start = (bf16[128,1024]{1,0:T(8,128)(2,1)S(1)}, bf16[128,1024]{1,0:T(8,128)(2,1)S(1)}, u32[]{:S(2)}, u32[]{:S(2)}) collective-permute-start(bf16[128,1024]{1,0:T(8,128)(2,1)S(1)} %pad_maximum_fusion.2), channel_id=1, source_target_pairs={{0,1},{1,2},{2,3},{4,5},{5,6},{6,7},{8,9},{9,10},{10,11},{12,13},{... | collective-permute-start | bytes 786440 | tf_op jit(solution)/shard_map/ppermute | solution.py:103
  8.6 3.5 %collective-permute-start.6 = (bf16[128,1024]{1,0:T(8,128)(2,1)S(1)}, bf16[128,1024]{1,0:T(8,128)(2,1)S(1)}, u32[]{:S(2)}, u32[]{:S(2)}) collective-permute-start(bf16[128,1024]{1,0:T(8,128)(2,1)S(1)} %pad_maximum_fusion.3), channel_id=1, source_target_pairs={{0,1},{1,2},{2,3},{4,5},{5,6},{6,7},{8,9},{9,10},{10,11},{12,13},{... | collective-permute-start | bytes 786440 | tf_op jit(solution)/shard_map/ppermute | solution.py:103
  14.6 3.5 %collective-permute-start.1 = (bf16[128,1024]{1,0:T(8,128)(2,1)S(1)}, bf16[128,1024]{1,0:T(8,128)(2,1)S(1)}, u32[]{:S(2)}, u32[]{:S(2)}) collective-permute-start(bf16[128,1024]{1,0:T(8,128)(2,1)S(1)} %collective-permute-done), channel_id=1, source_target_pairs={{1,2},{2,3},{5,6},{6,7},{9,10},{10,11},{13,14},{14,15},{17,18},{18... | collective-permute-start | bytes 786440 | tf_op jit(solution)/shard_map/ppermute | solution.py:103
  20.0 3.9 %collective-permute-start.7 = (bf16[128,1024]{1,0:T(8,128)(2,1)S(1)}, bf16[128,1024]{1,0:T(8,128)(2,1)S(1)}, u32[]{:S(2)}, u32[]{:S(2)}) collective-permute-start(bf16[128,1024]{1,0:T(8,128)(2,1)S(1)} %collective-permute-done.6), channel_id=1, source_target_pairs={{1,2},{2,3},{5,6},{6,7},{9,10},{10,11},{13,14},{14,15},{17,18},{18... | collective-permute-start | bytes 786440 | tf_op jit(solution)/shard_map/ppermute | solution.py:103
  27.7 2.5 %collective-permute-start.5 = (bf16[128,1024]{1,0:T(8,128)(2,1)S(1)}, bf16[128,1024]{1,0:T(8,128)(2,1)S(1)}, u32[]{:S(2)}, u32[]{:S(2)}) collective-permute-start(bf16[128,1024]{1,0:T(8,128)(2,1)S(1)} %collective-permute-done.4), channel_id=1, source_target_pairs={{1,0},{5,4},{9,8},{13,12},{17,16},{21,20},{25,24},{29,28}} | collective-permute-start | bytes 786440 | tf_op jit(solution)/shard_map/ppermute | solution.py:106
  32.7 4.4 %collective-permute-start.11 = (bf16[128,1024]{1,0:T(8,128)(2,1)S(1)}, bf16[128,1024]{1,0:T(8,128)(2,1)S(1)}, u32[]{:S(2)}, u32[]{:S(2)}) collective-permute-start(bf16[128,1024]{1,0:T(8,128)(2,1)S(1)} %collective-permute-done.10), channel_id=1, source_target_pairs={{1,0},{5,4},{9,8},{13,12},{17,16},{21,20},{25,24},{29,28}} | collective-permute-start | bytes 786440 | tf_op jit(solution)/shard_map/ppermute | solution.py:106
  37.2 4.7 %collective-permute-done.11 = bf16[128,1024]{1,0:T(8,128)(2,1)S(1)} collective-permute-done((bf16[128,1024]{1,0:T(8,128)(2,1)S(1)}, bf16[128,1024]{1,0:T(8,128)(2,1)S(1)}, u32[]{:S(2)}, u32[]{:S(2)}) %collective-permute-start.11) | collective-permute-done | bytes 262176 | tf_op jit(solution)/shard_map/ppermute | solution.py:106
  43.9 4.3 %all-to-all-start.1 = ((bf16[8,64,1024]{2,1,0:T(8,128)(2,1)}), bf16[8,64,1024]{2,1,0:T(8,128)(2,1)S(1)}, u32[]{:S(2)}, u32[]{:S(2)}) async-start(bf16[8,64,1024]{2,1,0:T(8,128)(2,1)} %broadcast_in_dim.5), calls=%async_computation.1 | async-start | bytes 2097152 | tf_op jit(solution)/shard_map/all_to_all | solution.py:140
  53.1 9.0 %all-to-all-done.1 = bf16[8,64,1024]{2,1,0:T(8,128)(2,1)S(1)} async-done(((bf16[8,64,1024]{2,1,0:T(8,128)(2,1)}), bf16[8,64,1024]{2,1,0:T(8,128)(2,1)S(1)}, u32[]{:S(2)}, u32[]{:S(2)}) %all-to-all-start.1) | async-done | bytes 1048608 | tf_op jit(solution)/shard_map/all_to_all | solution.py:140
  63.3 5.0 %all-to-all-start = ((bf16[8,64,1024]{2,1,0:T(8,128)(2,1)}), bf16[8,64,1024]{2,1,0:T(8,128)(2,1)S(1)}, u32[]{:S(2)}, u32[]{:S(2)}) async-start(bf16[8,64,1024]{2,1,0:T(8,128)(2,1)} %broadcast_in_dim.4), calls=%async_computation | async-start | bytes 2097152 | tf_op jit(solution)/shard_map/all_to_all | solution.py:140
  68.9 11.9 %shard_map.84 = (f32[512,1024]{1,0:T(8,128)}, bf16[512,1024]{1,0:T(8,128)(2,1)}, bf16[128,4096]{1,0:T(8,128)(2,1)}, bf16[128,4096]{1,0:T(8,128)(2,1)}) custom-call(s32[2]{0:T(128)} %pad_add_fusion.ids_ref, bf16[128,4096]{1,0:T(8,128)(2,1)} %q_ref.3, bf16[128,4096]{1,0:T(8,128)(2,1)} %g_ref.3, bf16[512,1024]{1,0:T(8,128)(2,1)} %copy-done, ...), custom_call_target="tpu_custom_call" | custom-call | tf_op jit(solution)/shard_map/pallas_call | solution.py:79
  82.2 5.0 %all-to-all-start.2 = ((bf16[8,64,1024]{2,1,0:T(8,128)(2,1)}), bf16[8,64,1024]{2,1,0:T(8,128)(2,1)S(1)}, u32[]{:S(2)}, u32[]{:S(2)}) async-start(bf16[8,64,1024]{2,1,0:T(8,128)(2,1)} %bitcast.63), calls=%async_computation.2 | async-start | bytes 2097152 | tf_op jit(solution)/shard_map/all_to_all | solution.py:147
  87.2 11.9 %shard_map.85 = (f32[512,1024]{1,0:T(8,128)}, bf16[512,1024]{1,0:T(8,128)(2,1)}, bf16[128,4096]{1,0:T(8,128)(2,1)}, bf16[128,4096]{1,0:T(8,128)(2,1)}) custom-call(s32[2]{0:T(128)} %pad_add_fusion.ids_ref, bf16[128,4096]{1,0:T(8,128)(2,1)} %q_ref.3, bf16[128,4096]{1,0:T(8,128)(2,1)} %g_ref.3, ...), custom_call_target="tpu_custom_call", output_to_operand_aliasing={{2}: (7, {}), {3}: (8, {})} | custom-call | tf_op jit(solution)/shard_map/pallas_call | solution.py:79
  101.1 5.0 %all-to-all-start.3 = ((bf16[8,64,1024]{2,1,0:T(8,128)(2,1)}), bf16[8,64,1024]{2,1,0:T(8,128)(2,1)S(1)}, u32[]{:S(2)}, u32[]{:S(2)}) async-start(bf16[8,64,1024]{2,1,0:T(8,128)(2,1)} %bitcast.62), calls=%async_computation.3 | async-start | bytes 2097152 | tf_op jit(solution)/shard_map/all_to_all | solution.py:147
  106.3 4.0 %scatter_fusion = f32[512,1024]{1,0:T(8,128)} fusion(f32[512,1024]{1,0:T(8,128)} %get-tuple-element.16, s32[64]{0:T(128)S(1)} %fusion, f32[64,1024]{1,0:T(8,128)S(1)} %convert_reduce_fusion.1), kind=kCustom, calls=%fused_computation.2 | custom fusion | flops 65536 | bytes 786688 | tf_op jit(solution)/shard_map/scatter-add | solution.py:151
  113.8 6.2 %all-to-all-done.3 = bf16[8,64,1024]{2,1,0:T(8,128)(2,1)S(1)} async-done(((bf16[8,64,1024]{2,1,0:T(8,128)(2,1)}), bf16[8,64,1024]{2,1,0:T(8,128)(2,1)S(1)}, u32[]{:S(2)}, u32[]{:S(2)}) %all-to-all-start.3) | async-done | bytes 1048608 | tf_op jit(solution)/shard_map/all_to_all | solution.py:147
  129.4 4.6 %collective-permute-done.15 = bf16[128,1024]{1,0:T(8,128)(2,1)} collective-permute-done((bf16[128,1024]{1,0:T(8,128)(2,1)S(1)}, bf16[128,1024]{1,0:T(8,128)(2,1)}, u32[]{:S(2)}, u32[]{:S(2)}) %collective-permute-start.15) | collective-permute-done | bytes 262176 | tf_op jit(solution)/shard_map/ppermute | solution.py:129
  134.0 2.5 %collective-permute-done.13 = bf16[128,1024]{1,0:T(8,128)(2,1)} collective-permute-done((bf16[128,1024]{1,0:T(8,128)(2,1)S(1)}, bf16[128,1024]{1,0:T(8,128)(2,1)}, u32[]{:S(2)}, u32[]{:S(2)}) %collective-permute-start.13) | collective-permute-done | bytes 262176 | tf_op jit(solution)/shard_map/ppermute | solution.py:128
  138.8 3.9 %collective-permute-start.16 = (bf16[128,1024]{1,0:T(8,128)(2,1)}, bf16[128,1024]{1,0:T(8,128)(2,1)S(1)}, u32[]{:S(2)}, u32[]{:S(2)}) collective-permute-start(bf16[128,1024]{1,0:T(8,128)(2,1)} %get-tuple-element.25), channel_id=1, source_target_pairs={{0,1},{1,2},{4,5},{5,6},{8,9},{9,10},{12,13},{13,14},{16,17},{17,1... | collective-permute-start | bytes 786440 | tf_op jit(solution)/shard_map/ppermute | solution.py:129
  144.6 2.4 %collective-permute-start.22 = (bf16[128,1024]{1,0:T(8,128)(2,1)}, bf16[128,1024]{1,0:T(8,128)(2,1)S(1)}, u32[]{:S(2)}, u32[]{:S(2)}) collective-permute-start(bf16[128,1024]{1,0:T(8,128)(2,1)} %get-tuple-element.29), channel_id=1, source_target_pairs={{0,1},{1,2},{4,5},{5,6},{8,9},{9,10},{12,13},{13,14},{16,17},{17,1... | collective-permute-start | bytes 786440 | tf_op jit(solution)/shard_map/ppermute | solution.py:129
  147.1 3.4 %collective-permute-start.14 = (bf16[128,1024]{1,0:T(8,128)(2,1)}, bf16[128,1024]{1,0:T(8,128)(2,1)S(1)}, u32[]{:S(2)}, u32[]{:S(2)}) collective-permute-start(bf16[128,1024]{1,0:T(8,128)(2,1)} %get-tuple-element.24), channel_id=1, source_target_pairs={{1,0},{2,1},{3,2},{5,4},{6,5},{7,6},{9,8},{10,9},{11,10},{13,12},{... | collective-permute-start | bytes 786440 | tf_op jit(solution)/shard_map/ppermute | solution.py:128
  152.3 2.4 %collective-permute-start.17 = (bf16[128,1024]{1,0:T(8,128)(2,1)}, bf16[128,1024]{1,0:T(8,128)(2,1)S(1)}, u32[]{:S(2)}, u32[]{:S(2)}) collective-permute-start(bf16[128,1024]{1,0:T(8,128)(2,1)} %add_convert_fusion.6), channel_id=1, source_target_pairs={{0,1},{1,2},{2,3},{4,5},{5,6},{6,7},{8,9},{9,10},{10,11},{12,13},{... | collective-permute-start | bytes 786440 | tf_op jit(solution)/shard_map/ppermute | solution.py:129
  154.7 3.4 %collective-permute-start.20 = (bf16[128,1024]{1,0:T(8,128)(2,1)}, bf16[128,1024]{1,0:T(8,128)(2,1)S(1)}, u32[]{:S(2)}, u32[]{:S(2)}) collective-permute-start(bf16[128,1024]{1,0:T(8,128)(2,1)} %get-tuple-element.28), channel_id=1, source_target_pairs={{1,0},{2,1},{3,2},{5,4},{6,5},{7,6},{9,8},{10,9},{11,10},{13,12},{... | collective-permute-start | bytes 786440 | tf_op jit(solution)/shard_map/ppermute | solution.py:128
  163.6 3.8 %collective-permute-done.23 = bf16[128,1024]{1,0:T(8,128)(2,1)S(1)} collective-permute-done((bf16[128,1024]{1,0:T(8,128)(2,1)}, bf16[128,1024]{1,0:T(8,128)(2,1)S(1)}, u32[]{:S(2)}, u32[]{:S(2)}) %collective-permute-start.23) | collective-permute-done | bytes 262176 | tf_op jit(solution)/shard_map/ppermute | solution.py:129
  (104 shorter events, 54.2 us)
Async XLA Ops:
  2.7 11.9 %collective-permute-start = (bf16[128,1024]{1,0:T(8,128)(2,1)S(1)}, bf16[128,1024]{1,0:T(8,128)(2,1)S(1)}, u32[]{:S(2)}, u32[]{:S(2)}) collective-permute-start(bf16[128,1024]{1,0:T(8,128)(2,1)S(1)} %pad_maximum_fusion.2), channel_id=1, source_target_pairs={{0,1},{1,2},{2,3},{4,5},{5,6},{6,7},{8,9},{9,10},{10,11},{12,13},{... | collective-permute-start | bytes 786440 | tf_op jit(solution)/shard_map/ppermute | solution.py:103
  6.1 11.9 %collective-permute-start.3 = (bf16[128,1024]{1,0:T(8,128)(2,1)S(1)}, bf16[128,1024]{1,0:T(8,128)(2,1)S(1)}, u32[]{:S(2)}, u32[]{:S(2)}) collective-permute-start(bf16[128,1024]{1,0:T(8,128)(2,1)S(1)} %pad_maximum_fusion.2), channel_id=1, source_target_pairs={{1,0},{2,1},{3,2},{5,4},{6,5},{7,6},{9,8},{10,9},{11,10},{13,12},{... | collective-permute-start | bytes 786440 | tf_op jit(solution)/shard_map/ppermute | solution.py:106
  8.6 11.4 %collective-permute-start.6 = (bf16[128,1024]{1,0:T(8,128)(2,1)S(1)}, bf16[128,1024]{1,0:T(8,128)(2,1)S(1)}, u32[]{:S(2)}, u32[]{:S(2)}) collective-permute-start(bf16[128,1024]{1,0:T(8,128)(2,1)S(1)} %pad_maximum_fusion.3), channel_id=1, source_target_pairs={{0,1},{1,2},{2,3},{4,5},{5,6},{6,7},{8,9},{9,10},{10,11},{12,13},{... | collective-permute-start | bytes 786440 | tf_op jit(solution)/shard_map/ppermute | solution.py:103
  12.0 11.9 %collective-permute-start.9 = (bf16[128,1024]{1,0:T(8,128)(2,1)S(1)}, bf16[128,1024]{1,0:T(8,128)(2,1)S(1)}, u32[]{:S(2)}, u32[]{:S(2)}) collective-permute-start(bf16[128,1024]{1,0:T(8,128)(2,1)S(1)} %pad_maximum_fusion.3), channel_id=1, source_target_pairs={{1,0},{2,1},{3,2},{5,4},{6,5},{7,6},{9,8},{10,9},{11,10},{13,12},{... | collective-permute-start | bytes 786440 | tf_op jit(solution)/shard_map/ppermute | solution.py:106
  14.6 11.4 %collective-permute-start.1 = (bf16[128,1024]{1,0:T(8,128)(2,1)S(1)}, bf16[128,1024]{1,0:T(8,128)(2,1)S(1)}, u32[]{:S(2)}, u32[]{:S(2)}) collective-permute-start(bf16[128,1024]{1,0:T(8,128)(2,1)S(1)} %collective-permute-done), channel_id=1, source_target_pairs={{1,2},{2,3},{5,6},{6,7},{9,10},{10,11},{13,14},{14,15},{17,18},{18... | collective-permute-start | bytes 786440 | tf_op jit(solution)/shard_map/ppermute | solution.py:103
  18.1 9.6 %collective-permute-start.4 = (bf16[128,1024]{1,0:T(8,128)(2,1)S(1)}, bf16[128,1024]{1,0:T(8,128)(2,1)S(1)}, u32[]{:S(2)}, u32[]{:S(2)}) collective-permute-start(bf16[128,1024]{1,0:T(8,128)(2,1)S(1)} %collective-permute-done.3), channel_id=1, source_target_pairs={{1,0},{2,1},{5,4},{6,5},{9,8},{10,9},{13,12},{14,13},{17,16},{18,1... | collective-permute-start | bytes 786440 | tf_op jit(solution)/shard_map/ppermute | solution.py:106
  20.0 10.3 %collective-permute-start.7 = (bf16[128,1024]{1,0:T(8,128)(2,1)S(1)}, bf16[128,1024]{1,0:T(8,128)(2,1)S(1)}, u32[]{:S(2)}, u32[]{:S(2)}) collective-permute-start(bf16[128,1024]{1,0:T(8,128)(2,1)S(1)} %collective-permute-done.6), channel_id=1, source_target_pairs={{1,2},{2,3},{5,6},{6,7},{9,10},{10,11},{13,14},{14,15},{17,18},{18... | collective-permute-start | bytes 786440 | tf_op jit(solution)/shard_map/ppermute | solution.py:103
  26.0 22.2 %collective-permute-start.2 = (bf16[128,1024]{1,0:T(8,128)(2,1)S(1)}, bf16[128,1024]{1,0:T(8,128)(2,1)S(1)}, u32[]{:S(2)}, u32[]{:S(2)}) collective-permute-start(bf16[128,1024]{1,0:T(8,128)(2,1)S(1)} %collective-permute-done.1), channel_id=1, source_target_pairs={{2,3},{6,7},{10,11},{14,15},{18,19},{22,23},{26,27},{30,31}} | collective-permute-start | bytes 786440 | tf_op jit(solution)/shard_map/ppermute | solution.py:103
  27.7 22.6 %collective-permute-start.5 = (bf16[128,1024]{1,0:T(8,128)(2,1)S(1)}, bf16[128,1024]{1,0:T(8,128)(2,1)S(1)}, u32[]{:S(2)}, u32[]{:S(2)}) collective-permute-start(bf16[128,1024]{1,0:T(8,128)(2,1)S(1)} %collective-permute-done.4), channel_id=1, source_target_pairs={{1,0},{5,4},{9,8},{13,12},{17,16},{21,20},{25,24},{29,28}} | collective-permute-start | bytes 786440 | tf_op jit(solution)/shard_map/ppermute | solution.py:106
  32.7 9.2 %collective-permute-start.11 = (bf16[128,1024]{1,0:T(8,128)(2,1)S(1)}, bf16[128,1024]{1,0:T(8,128)(2,1)S(1)}, u32[]{:S(2)}, u32[]{:S(2)}) collective-permute-start(bf16[128,1024]{1,0:T(8,128)(2,1)S(1)} %collective-permute-done.10), channel_id=1, source_target_pairs={{1,0},{5,4},{9,8},{13,12},{17,16},{21,20},{25,24},{29,28}} | collective-permute-start | bytes 786440 | tf_op jit(solution)/shard_map/ppermute | solution.py:106
  43.9 18.2 %all-to-all-start.1 = ((bf16[8,64,1024]{2,1,0:T(8,128)(2,1)}), bf16[8,64,1024]{2,1,0:T(8,128)(2,1)S(1)}, u32[]{:S(2)}, u32[]{:S(2)}) async-start(bf16[8,64,1024]{2,1,0:T(8,128)(2,1)} %broadcast_in_dim.5), calls=%async_computation.1 | async-start | bytes 2097152 | tf_op jit(solution)/shard_map/all_to_all | solution.py:140
  63.3 18.9 %all-to-all-start = ((bf16[8,64,1024]{2,1,0:T(8,128)(2,1)}), bf16[8,64,1024]{2,1,0:T(8,128)(2,1)S(1)}, u32[]{:S(2)}, u32[]{:S(2)}) async-start(bf16[8,64,1024]{2,1,0:T(8,128)(2,1)} %broadcast_in_dim.4), calls=%async_computation | async-start | bytes 2097152 | tf_op jit(solution)/shard_map/all_to_all | solution.py:140
  82.2 18.9 %all-to-all-start.2 = ((bf16[8,64,1024]{2,1,0:T(8,128)(2,1)}), bf16[8,64,1024]{2,1,0:T(8,128)(2,1)S(1)}, u32[]{:S(2)}, u32[]{:S(2)}) async-start(bf16[8,64,1024]{2,1,0:T(8,128)(2,1)} %bitcast.63), calls=%async_computation.2 | async-start | bytes 2097152 | tf_op jit(solution)/shard_map/all_to_all | solution.py:147
  101.1 18.9 %all-to-all-start.3 = ((bf16[8,64,1024]{2,1,0:T(8,128)(2,1)}), bf16[8,64,1024]{2,1,0:T(8,128)(2,1)S(1)}, u32[]{:S(2)}, u32[]{:S(2)}) async-start(bf16[8,64,1024]{2,1,0:T(8,128)(2,1)} %bitcast.62), calls=%async_computation.3 | async-start | bytes 2097152 | tf_op jit(solution)/shard_map/all_to_all | solution.py:147
  112.5 11.7 %collective-permute-start.12 = (bf16[128,1024]{1,0:T(8,128)(2,1)}, bf16[128,1024]{1,0:T(8,128)(2,1)}, u32[]{:S(2)}, u32[]{:S(2)}) collective-permute-start(bf16[128,1024]{1,0:T(8,128)(2,1)} %get-tuple-element.26), channel_id=1, source_target_pairs={{3,2},{7,6},{11,10},{15,14},{19,18},{23,22},{27,26},{31,30}} | collective-permute-start | bytes 786440 | tf_op jit(solution)/shard_map/ppermute | solution.py:128
  122.9 11.1 %collective-permute-start.15 = (bf16[128,1024]{1,0:T(8,128)(2,1)S(1)}, bf16[128,1024]{1,0:T(8,128)(2,1)}, u32[]{:S(2)}, u32[]{:S(2)}) collective-permute-start(bf16[128,1024]{1,0:T(8,128)(2,1)S(1)} %copy-done.6), channel_id=1, source_target_pairs={{0,1},{4,5},{8,9},{12,13},{16,17},{20,21},{24,25},{28,29}} | collective-permute-start | bytes 786440 | tf_op jit(solution)/shard_map/ppermute | solution.py:129
  125.4 11.2 %collective-permute-start.13 = (bf16[128,1024]{1,0:T(8,128)(2,1)S(1)}, bf16[128,1024]{1,0:T(8,128)(2,1)}, u32[]{:S(2)}, u32[]{:S(2)}) collective-permute-start(bf16[128,1024]{1,0:T(8,128)(2,1)S(1)} %add_convert_fusion.9), channel_id=1, source_target_pairs={{2,1},{3,2},{6,5},{7,6},{10,9},{11,10},{14,13},{15,14},{18,17},{19... | collective-permute-start | bytes 786440 | tf_op jit(solution)/shard_map/ppermute | solution.py:128
  126.7 16.0 %collective-permute-start.21 = (bf16[128,1024]{1,0:T(8,128)(2,1)S(1)}, bf16[128,1024]{1,0:T(8,128)(2,1)}, u32[]{:S(2)}, u32[]{:S(2)}) collective-permute-start(bf16[128,1024]{1,0:T(8,128)(2,1)S(1)} %get-tuple-element.31), channel_id=1, source_target_pairs={{0,1},{4,5},{8,9},{12,13},{16,17},{20,21},{24,25},{28,29}} | collective-permute-start | bytes 786440 | tf_op jit(solution)/shard_map/ppermute | solution.py:129
  128.1 14.7 %collective-permute-start.19 = (bf16[128,1024]{1,0:T(8,128)(2,1)S(1)}, bf16[128,1024]{1,0:T(8,128)(2,1)S(1)}, u32[]{:S(2)}, u32[]{:S(2)}) collective-permute-start(bf16[128,1024]{1,0:T(8,128)(2,1)S(1)} %add_convert_fusion.4), channel_id=1, source_target_pairs={{2,1},{3,2},{6,5},{7,6},{10,9},{11,10},{14,13},{15,14},{18,17},{19... | collective-permute-start | bytes 786440 | tf_op jit(solution)/shard_map/ppermute | solution.py:128
  138.8 11.7 %collective-permute-start.16 = (bf16[128,1024]{1,0:T(8,128)(2,1)}, bf16[128,1024]{1,0:T(8,128)(2,1)S(1)}, u32[]{:S(2)}, u32[]{:S(2)}) collective-permute-start(bf16[128,1024]{1,0:T(8,128)(2,1)} %get-tuple-element.25), channel_id=1, source_target_pairs={{0,1},{1,2},{4,5},{5,6},{8,9},{9,10},{12,13},{13,14},{16,17},{17,1... | collective-permute-start | bytes 786440 | tf_op jit(solution)/shard_map/ppermute | solution.py:129
  144.6 13.6 %collective-permute-start.22 = (bf16[128,1024]{1,0:T(8,128)(2,1)}, bf16[128,1024]{1,0:T(8,128)(2,1)S(1)}, u32[]{:S(2)}, u32[]{:S(2)}) collective-permute-start(bf16[128,1024]{1,0:T(8,128)(2,1)} %get-tuple-element.29), channel_id=1, source_target_pairs={{0,1},{1,2},{4,5},{5,6},{8,9},{9,10},{12,13},{13,14},{16,17},{17,1... | collective-permute-start | bytes 786440 | tf_op jit(solution)/shard_map/ppermute | solution.py:129
  147.1 14.3 %collective-permute-start.14 = (bf16[128,1024]{1,0:T(8,128)(2,1)}, bf16[128,1024]{1,0:T(8,128)(2,1)S(1)}, u32[]{:S(2)}, u32[]{:S(2)}) collective-permute-start(bf16[128,1024]{1,0:T(8,128)(2,1)} %get-tuple-element.24), channel_id=1, source_target_pairs={{1,0},{2,1},{3,2},{5,4},{6,5},{7,6},{9,8},{10,9},{11,10},{13,12},{... | collective-permute-start | bytes 786440 | tf_op jit(solution)/shard_map/ppermute | solution.py:128
  152.3 9.1 %collective-permute-start.17 = (bf16[128,1024]{1,0:T(8,128)(2,1)}, bf16[128,1024]{1,0:T(8,128)(2,1)S(1)}, u32[]{:S(2)}, u32[]{:S(2)}) collective-permute-start(bf16[128,1024]{1,0:T(8,128)(2,1)} %add_convert_fusion.6), channel_id=1, source_target_pairs={{0,1},{1,2},{2,3},{4,5},{5,6},{6,7},{8,9},{9,10},{10,11},{12,13},{... | collective-permute-start | bytes 786440 | tf_op jit(solution)/shard_map/ppermute | solution.py:129
  154.7 8.8 %collective-permute-start.20 = (bf16[128,1024]{1,0:T(8,128)(2,1)}, bf16[128,1024]{1,0:T(8,128)(2,1)S(1)}, u32[]{:S(2)}, u32[]{:S(2)}) collective-permute-start(bf16[128,1024]{1,0:T(8,128)(2,1)} %get-tuple-element.28), channel_id=1, source_target_pairs={{1,0},{2,1},{3,2},{5,4},{6,5},{7,6},{9,8},{10,9},{11,10},{13,12},{... | collective-permute-start | bytes 786440 | tf_op jit(solution)/shard_map/ppermute | solution.py:128
  (12 other events, 85.6 us)

commit v16 on v15

--- a/solution.py
+++ b/solution.py
@@ -136,10 +136,9 @@
     kv_rows = jnp.concatenate([keys, values], axis=1)
     kv_window = head_gather(kv_rows, "head", heads_axis)
     window = kv_window.shape[0]
-    own_beacon_rows = kv_window[positions]
+    own_beacon_rows = kv_window[jnp.tile(positions, ctx_axis)]
     kv_beacons = lax.all_to_all(
-        jnp.broadcast_to(own_beacon_rows[None], (ctx_axis,) + own_beacon_rows.shape),
-        "ctx", 0, 0, tiled=True,
+        own_beacon_rows.reshape(ctx_axis, per_shard, 2 * kv_width), "ctx", 0, 0, tiled=True,
     ).reshape(ctx_axis * per_shard, 2 * kv_width)
     window_grads, beacon_grads, attended_out, query_out = attend_all(
         ids, queries, out_grad, kv_window, kv_beacons, per_shard, part, parts, earlier

time: 173 us -> 174 us (level)
    gather x2, local copies, waits for them, and re-layouts: 1.42 us -> 5.57 us  [local_part(): own_beacon_rows = kv_window[jnp.tile(positions, ctx_axis)]]
    broadcast_in_dim x2 -> x0, local copies, waits for them, and re-layouts: 2.34 us -> none  [local_part(): jnp.broadcast_to(own_beacon_rows[None], (ctx_axis,) + own_beacon_rows.shape)]
    ppermute x6, starting transfers between devices: 15.7 us -> 17.8 us  [head_gather(): lax.ppermute(from_left[-1], axis, [(j, j + 1) for j in range(step - 1, co...]
    unnamed x32 -> x30, local copies, waits for them, and re-layouts: 4.64 us -> 5.39 us
  transfers between devices with their start and end apart: 28 -> 28, of which waited for: 11 -> 10; matrix products, arithmetic and copies ran while one was open for 15% -> 17% of each run, Pallas kernels for 14% -> 14%
where the time goes in v16:
time: 174 us; the launch traced here: 171 us
  starting transfers between devices  76 us (44%)
  waiting for transfers between devices  35.8 us (21%)
  Pallas kernels  23.8 us (14%)
  other arithmetic  17.7 us (10%)
  local copies, waits for them, and re-layouts  16.6 us (10%)
    pallas_call x2, Pallas kernels, attend_all(): pl.pallas_call(kernel, grid_spec=pltpu.PrefetchScalarGridSpec(num_scalar_...  23.8 us
    ppermute x6, starting transfers between devices, head_gather(): lax.ppermute(from_left[-1], axis, [(j, j + 1) for j in range(step - 1, co...  17.8 us
    ppermute x6, starting transfers between devices, head_gather(): lax.ppermute(from_right[-1], axis, [(j + 1, j) for j in range(count - ste...  14.3 us
    ppermute x6, starting transfers between devices, head_reduce(): lax.ppermute(send_right, axis, [(j, j + 1) for j in range(0, min(step, co...  13.4 us
    ppermute x6, starting transfers between devices, head_reduce(): lax.ppermute(send_left, axis, [(j, j - 1) for j in range(max(1, count - s...  11.3 us
    all_to_all x2, waiting for transfers between devices, local_part(): lax.all_to_all(own_beacon_rows.reshape(ctx_axis, per_shard, 2 * kv_width)...  10.3 us
    all_to_all x2, starting transfers between devices, local_part(): lax.all_to_all(beacon_grads.reshape(ctx_axis, per_shard, 2 * kv_width), '...  9.97 us
    all_to_all x2, starting transfers between devices, local_part(): lax.all_to_all(own_beacon_rows.reshape(ctx_axis, per_shard, 2 * kv_width)...  9.23 us
  transfers between devices with their start and end apart: 28, of which 10 were waited for; matrix products, arithmetic and copies ran while one was open for 17% of the time, Pallas kernels for 14%

profile of v16, /device:TPU:10, one launch (start us, length us, event | category | flops | bytes accessed | tf_op | source)
XLA Modules:
  0.0 171.1 jit_solution(12825794612122916012)
XLA Ops:
  3.4 3.5 %collective-permute-start = (bf16[128,1024]{1,0:T(8,128)(2,1)}, bf16[128,1024]{1,0:T(8,128)(2,1)S(1)}, u32[]{:S(2)}, u32[]{:S(2)}) collective-permute-start(bf16[128,1024]{1,0:T(8,128)(2,1)} %pad_maximum_fusion.2), channel_id=1, source_target_pairs={{0,1},{1,2},{2,3},{4,5},{5,6},{6,7},{8,9},{9,10},{10,11},{12,13},{... | collective-permute-start | bytes 786440 | tf_op jit(solution)/shard_map/ppermute | solution.py:103
  9.9 3.5 %collective-permute-start.6 = (bf16[128,1024]{1,0:T(8,128)(2,1)}, bf16[128,1024]{1,0:T(8,128)(2,1)S(1)}, u32[]{:S(2)}, u32[]{:S(2)}) collective-permute-start(bf16[128,1024]{1,0:T(8,128)(2,1)} %pad_maximum_fusion.3), channel_id=1, source_target_pairs={{0,1},{1,2},{2,3},{4,5},{5,6},{6,7},{8,9},{9,10},{10,11},{12,13},{... | collective-permute-start | bytes 786440 | tf_op jit(solution)/shard_map/ppermute | solution.py:103
  16.0 4.2 %collective-permute-start.1 = (bf16[128,1024]{1,0:T(8,128)(2,1)S(1)}, bf16[128,1024]{1,0:T(8,128)(2,1)}, u32[]{:S(2)}, u32[]{:S(2)}) collective-permute-start(bf16[128,1024]{1,0:T(8,128)(2,1)S(1)} %collective-permute-done), channel_id=1, source_target_pairs={{1,2},{2,3},{5,6},{6,7},{9,10},{10,11},{13,14},{14,15},{17,18},{18... | collective-permute-start | bytes 786440 | tf_op jit(solution)/shard_map/ppermute | solution.py:103
  22.1 4.6 %collective-permute-start.7 = (bf16[128,1024]{1,0:T(8,128)(2,1)S(1)}, bf16[128,1024]{1,0:T(8,128)(2,1)S(1)}, u32[]{:S(2)}, u32[]{:S(2)}) collective-permute-start(bf16[128,1024]{1,0:T(8,128)(2,1)S(1)} %collective-permute-done.6), channel_id=1, source_target_pairs={{1,2},{2,3},{5,6},{6,7},{9,10},{10,11},{13,14},{14,15},{17,18},{18... | collective-permute-start | bytes 786440 | tf_op jit(solution)/shard_map/ppermute | solution.py:103
  32.1 3.1 %collective-permute-done.10 = bf16[128,1024]{1,0:T(8,128)(2,1)S(1)} collective-permute-done((bf16[128,1024]{1,0:T(8,128)(2,1)S(1)}, bf16[128,1024]{1,0:T(8,128)(2,1)S(1)}, u32[]{:S(2)}, u32[]{:S(2)}) %collective-permute-start.10) | collective-permute-done | bytes 262176 | tf_op jit(solution)/shard_map/ppermute | solution.py:106
  35.2 4.4 %collective-permute-start.11 = (bf16[128,1024]{1,0:T(8,128)(2,1)S(1)}, bf16[128,1024]{1,0:T(8,128)(2,1)S(1)}, u32[]{:S(2)}, u32[]{:S(2)}) collective-permute-start(bf16[128,1024]{1,0:T(8,128)(2,1)S(1)} %collective-permute-done.10), channel_id=1, source_target_pairs={{1,0},{5,4},{9,8},{13,12},{17,16},{21,20},{25,24},{29,28}} | collective-permute-start | bytes 786440 | tf_op jit(solution)/shard_map/ppermute | solution.py:106
  40.7 3.1 %collective-permute-done.11 = bf16[128,1024]{1,0:T(8,128)(2,1)S(1)} collective-permute-done((bf16[128,1024]{1,0:T(8,128)(2,1)S(1)}, bf16[128,1024]{1,0:T(8,128)(2,1)S(1)}, u32[]{:S(2)}, u32[]{:S(2)}) %collective-permute-start.11) | collective-permute-done | bytes 262176 | tf_op jit(solution)/shard_map/ppermute | solution.py:106
  44.0 2.8 %gather_fusion.1 = bf16[512,1024]{1,0:T(8,128)(2,1)} fusion(bf16[512,1024]{1,0:T(8,128)(2,1)S(1)} %pad_maximum_fusion.1.kw_ref.vw_ref, s32[1024]{0:T(1024)S(1)} %pad_clamp_fusion), kind=kCustom, calls=%fused_computation.1 | custom fusion | bytes 2099200 | tf_op jit(solution)/shard_map/gather | solution.py:139
  46.8 4.3 %all-to-all-start.1 = ((bf16[8,64,1024]{2,1,0:T(8,128)(2,1)}), bf16[8,64,1024]{2,1,0:T(8,128)(2,1)S(1)}, u32[]{:S(2)}, u32[]{:S(2)}) async-start(bf16[8,64,1024]{2,1,0:T(8,128)(2,1)} %bitcast.28), calls=%async_computation.1 | async-start | bytes 2097152 | tf_op jit(solution)/shard_map/all_to_all | solution.py:140
  53.2 2.8 %gather_fusion = bf16[512,1024]{1,0:T(8,128)(2,1)} fusion(bf16[512,1024]{1,0:T(8,128)(2,1)S(1)} %pad_maximum_fusion.kw_ref.vw_ref, s32[1024]{0:T(1024)S(1)} %pad_clamp_fusion), kind=kCustom, calls=%fused_computation | custom fusion | bytes 2099200 | tf_op jit(solution)/shard_map/gather | solution.py:139
  56.0 8.9 %all-to-all-done.1 = bf16[8,64,1024]{2,1,0:T(8,128)(2,1)S(1)} async-done(((bf16[8,64,1024]{2,1,0:T(8,128)(2,1)}), bf16[8,64,1024]{2,1,0:T(8,128)(2,1)S(1)}, u32[]{:S(2)}, u32[]{:S(2)}) %all-to-all-start.1) | async-done | bytes 1048608 | tf_op jit(solution)/shard_map/all_to_all | solution.py:140
  64.9 5.0 %all-to-all-start = ((bf16[8,64,1024]{2,1,0:T(8,128)(2,1)}), bf16[8,64,1024]{2,1,0:T(8,128)(2,1)S(1)}, u32[]{:S(2)}, u32[]{:S(2)}) async-start(bf16[8,64,1024]{2,1,0:T(8,128)(2,1)} %bitcast.15), calls=%async_computation | async-start | bytes 2097152 | tf_op jit(solution)/shard_map/all_to_all | solution.py:140
  70.5 11.9 %shard_map.84 = (f32[512,1024]{1,0:T(8,128)}, bf16[512,1024]{1,0:T(8,128)(2,1)}, bf16[128,4096]{1,0:T(8,128)(2,1)}, bf16[128,4096]{1,0:T(8,128)(2,1)}) custom-call(s32[2]{0:T(128)} %pad_add_fusion.ids_ref, bf16[128,4096]{1,0:T(8,128)(2,1)} %q_ref.3, bf16[128,4096]{1,0:T(8,128)(2,1)} %g_ref.3, bf16[512,1024]{1,0:T(8,128)(2,1)} %copy-done, ...), custom_call_target="tpu_custom_call" | custom-call | tf_op jit(solution)/shard_map/pallas_call | solution.py:79
  83.8 5.0 %all-to-all-start.2 = ((bf16[8,64,1024]{2,1,0:T(8,128)(2,1)}), bf16[8,64,1024]{2,1,0:T(8,128)(2,1)S(1)}, u32[]{:S(2)}, u32[]{:S(2)}) async-start(bf16[8,64,1024]{2,1,0:T(8,128)(2,1)} %bitcast.67), calls=%async_computation.2 | async-start | bytes 2097152 | tf_op jit(solution)/shard_map/all_to_all | solution.py:146
  88.8 11.9 %shard_map.85 = (f32[512,1024]{1,0:T(8,128)}, bf16[512,1024]{1,0:T(8,128)(2,1)}, bf16[128,4096]{1,0:T(8,128)(2,1)}, bf16[128,4096]{1,0:T(8,128)(2,1)}) custom-call(s32[2]{0:T(128)} %pad_add_fusion.ids_ref, bf16[128,4096]{1,0:T(8,128)(2,1)} %q_ref.3, bf16[128,4096]{1,0:T(8,128)(2,1)} %g_ref.3, ...), custom_call_target="tpu_custom_call", output_to_operand_aliasing={{2}: (7, {}), {3}: (8, {})} | custom-call | tf_op jit(solution)/shard_map/pallas_call | solution.py:79
  102.7 5.0 %all-to-all-start.3 = ((bf16[8,64,1024]{2,1,0:T(8,128)(2,1)}), bf16[8,64,1024]{2,1,0:T(8,128)(2,1)S(1)}, u32[]{:S(2)}, u32[]{:S(2)}) async-start(bf16[8,64,1024]{2,1,0:T(8,128)(2,1)} %bitcast.66), calls=%async_computation.3 | async-start | bytes 2097152 | tf_op jit(solution)/shard_map/all_to_all | solution.py:146
  107.9 4.0 %scatter_fusion = f32[512,1024]{1,0:T(8,128)} fusion(f32[512,1024]{1,0:T(8,128)} %get-tuple-element.16, s32[64]{0:T(128)S(1)} %fusion, f32[64,1024]{1,0:T(8,128)S(1)} %convert_reduce_fusion.1), kind=kCustom, calls=%fused_computation.2 | custom fusion | flops 65536 | bytes 786688 | tf_op jit(solution)/shard_map/scatter-add | solution.py:150
  115.5 6.1 %all-to-all-done.3 = bf16[8,64,1024]{2,1,0:T(8,128)(2,1)S(1)} async-done(((bf16[8,64,1024]{2,1,0:T(8,128)(2,1)}), bf16[8,64,1024]{2,1,0:T(8,128)(2,1)S(1)}, u32[]{:S(2)}, u32[]{:S(2)}) %all-to-all-start.3) | async-done | bytes 1048608 | tf_op jit(solution)/shard_map/all_to_all | solution.py:146
  131.0 4.6 %collective-permute-done.15 = bf16[128,1024]{1,0:T(8,128)(2,1)} collective-permute-done((bf16[128,1024]{1,0:T(8,128)(2,1)S(1)}, bf16[128,1024]{1,0:T(8,128)(2,1)}, u32[]{:S(2)}, u32[]{:S(2)}) %collective-permute-start.15) | collective-permute-done | bytes 262176 | tf_op jit(solution)/shard_map/ppermute | solution.py:129
  140.3 3.3 %collective-permute-start.16 = (bf16[128,1024]{1,0:T(8,128)(2,1)S(1)}, bf16[128,1024]{1,0:T(8,128)(2,1)S(1)}, u32[]{:S(2)}, u32[]{:S(2)}) collective-permute-start(bf16[128,1024]{1,0:T(8,128)(2,1)S(1)} %get-tuple-element.25), channel_id=1, source_target_pairs={{0,1},{1,2},{4,5},{5,6},{8,9},{9,10},{12,13},{13,14},{16,17},{17,1... | collective-permute-start | bytes 786440 | tf_op jit(solution)/shard_map/ppermute | solution.py:129
  145.6 2.5 %collective-permute-start.22 = (bf16[128,1024]{1,0:T(8,128)(2,1)}, bf16[128,1024]{1,0:T(8,128)(2,1)S(1)}, u32[]{:S(2)}, u32[]{:S(2)}) collective-permute-start(bf16[128,1024]{1,0:T(8,128)(2,1)} %get-tuple-element.29), channel_id=1, source_target_pairs={{0,1},{1,2},{4,5},{5,6},{8,9},{9,10},{12,13},{13,14},{16,17},{17,1... | collective-permute-start | bytes 786440 | tf_op jit(solution)/shard_map/ppermute | solution.py:129
  148.1 3.3 %collective-permute-start.14 = (bf16[128,1024]{1,0:T(8,128)(2,1)}, bf16[128,1024]{1,0:T(8,128)(2,1)S(1)}, u32[]{:S(2)}, u32[]{:S(2)}) collective-permute-start(bf16[128,1024]{1,0:T(8,128)(2,1)} %get-tuple-element.24), channel_id=1, source_target_pairs={{1,0},{2,1},{3,2},{5,4},{6,5},{7,6},{9,8},{10,9},{11,10},{13,12},{... | collective-permute-start | bytes 786440 | tf_op jit(solution)/shard_map/ppermute | solution.py:128
  155.8 3.3 %collective-permute-start.20 = (bf16[128,1024]{1,0:T(8,128)(2,1)}, bf16[128,1024]{1,0:T(8,128)(2,1)S(1)}, u32[]{:S(2)}, u32[]{:S(2)}) collective-permute-start(bf16[128,1024]{1,0:T(8,128)(2,1)} %get-tuple-element.28), channel_id=1, source_target_pairs={{1,0},{2,1},{3,2},{5,4},{6,5},{7,6},{9,8},{10,9},{11,10},{13,12},{... | collective-permute-start | bytes 786440 | tf_op jit(solution)/shard_map/ppermute | solution.py:128
  164.6 3.7 %collective-permute-done.23 = bf16[128,1024]{1,0:T(8,128)(2,1)S(1)} collective-permute-done((bf16[128,1024]{1,0:T(8,128)(2,1)}, bf16[128,1024]{1,0:T(8,128)(2,1)S(1)}, u32[]{:S(2)}, u32[]{:S(2)}) %collective-permute-start.23) | collective-permute-done | bytes 262176 | tf_op jit(solution)/shard_map/ppermute | solution.py:129
  (103 shorter events, 55.1 us)
Async XLA Ops:
  3.4 12.6 %collective-permute-start = (bf16[128,1024]{1,0:T(8,128)(2,1)}, bf16[128,1024]{1,0:T(8,128)(2,1)S(1)}, u32[]{:S(2)}, u32[]{:S(2)}) collective-permute-start(bf16[128,1024]{1,0:T(8,128)(2,1)} %pad_maximum_fusion.2), channel_id=1, source_target_pairs={{0,1},{1,2},{2,3},{4,5},{5,6},{6,7},{8,9},{9,10},{10,11},{12,13},{... | collective-permute-start | bytes 786440 | tf_op jit(solution)/shard_map/ppermute | solution.py:103
  6.8 13.3 %collective-permute-start.3 = (bf16[128,1024]{1,0:T(8,128)(2,1)}, bf16[128,1024]{1,0:T(8,128)(2,1)S(1)}, u32[]{:S(2)}, u32[]{:S(2)}) collective-permute-start(bf16[128,1024]{1,0:T(8,128)(2,1)} %pad_maximum_fusion.2), channel_id=1, source_target_pairs={{1,0},{2,1},{3,2},{5,4},{6,5},{7,6},{9,8},{10,9},{11,10},{13,12},{... | collective-permute-start | bytes 786440 | tf_op jit(solution)/shard_map/ppermute | solution.py:106
  9.9 12.1 %collective-permute-start.6 = (bf16[128,1024]{1,0:T(8,128)(2,1)}, bf16[128,1024]{1,0:T(8,128)(2,1)S(1)}, u32[]{:S(2)}, u32[]{:S(2)}) collective-permute-start(bf16[128,1024]{1,0:T(8,128)(2,1)} %pad_maximum_fusion.3), channel_id=1, source_target_pairs={{0,1},{1,2},{2,3},{4,5},{5,6},{6,7},{8,9},{9,10},{10,11},{12,13},{... | collective-permute-start | bytes 786440 | tf_op jit(solution)/shard_map/ppermute | solution.py:103
  13.4 13.3 %collective-permute-start.9 = (bf16[128,1024]{1,0:T(8,128)(2,1)}, bf16[128,1024]{1,0:T(8,128)(2,1)S(1)}, u32[]{:S(2)}, u32[]{:S(2)}) collective-permute-start(bf16[128,1024]{1,0:T(8,128)(2,1)} %pad_maximum_fusion.3), channel_id=1, source_target_pairs={{1,0},{2,1},{3,2},{5,4},{6,5},{7,6},{9,8},{10,9},{11,10},{13,12},{... | collective-permute-start | bytes 786440 | tf_op jit(solution)/shard_map/ppermute | solution.py:106
  16.0 12.7 %collective-permute-start.1 = (bf16[128,1024]{1,0:T(8,128)(2,1)S(1)}, bf16[128,1024]{1,0:T(8,128)(2,1)}, u32[]{:S(2)}, u32[]{:S(2)}) collective-permute-start(bf16[128,1024]{1,0:T(8,128)(2,1)S(1)} %collective-permute-done), channel_id=1, source_target_pairs={{1,2},{2,3},{5,6},{6,7},{9,10},{10,11},{13,14},{14,15},{17,18},{18... | collective-permute-start | bytes 786440 | tf_op jit(solution)/shard_map/ppermute | solution.py:103
  20.2 9.9 %collective-permute-start.4 = (bf16[128,1024]{1,0:T(8,128)(2,1)S(1)}, bf16[128,1024]{1,0:T(8,128)(2,1)}, u32[]{:S(2)}, u32[]{:S(2)}) collective-permute-start(bf16[128,1024]{1,0:T(8,128)(2,1)S(1)} %collective-permute-done.3), channel_id=1, source_target_pairs={{1,0},{2,1},{5,4},{6,5},{9,8},{10,9},{13,12},{14,13},{17,16},{18,1... | collective-permute-start | bytes 786440 | tf_op jit(solution)/shard_map/ppermute | solution.py:106
  22.1 9.3 %collective-permute-start.7 = (bf16[128,1024]{1,0:T(8,128)(2,1)S(1)}, bf16[128,1024]{1,0:T(8,128)(2,1)S(1)}, u32[]{:S(2)}, u32[]{:S(2)}) collective-permute-start(bf16[128,1024]{1,0:T(8,128)(2,1)S(1)} %collective-permute-done.6), channel_id=1, source_target_pairs={{1,2},{2,3},{5,6},{6,7},{9,10},{10,11},{13,14},{14,15},{17,18},{18... | collective-permute-start | bytes 786440 | tf_op jit(solution)/shard_map/ppermute | solution.py:103
  28.7 22.3 %collective-permute-start.2 = (bf16[128,1024]{1,0:T(8,128)(2,1)}, bf16[128,1024]{1,0:T(8,128)(2,1)}, u32[]{:S(2)}, u32[]{:S(2)}) collective-permute-start(bf16[128,1024]{1,0:T(8,128)(2,1)} %collective-permute-done.1), channel_id=1, source_target_pairs={{2,3},{6,7},{10,11},{14,15},{18,19},{22,23},{26,27},{30,31}} | collective-permute-start | bytes 786440 | tf_op jit(solution)/shard_map/ppermute | solution.py:103
  30.1 22.9 %collective-permute-start.5 = (bf16[128,1024]{1,0:T(8,128)(2,1)}, bf16[128,1024]{1,0:T(8,128)(2,1)S(1)}, u32[]{:S(2)}, u32[]{:S(2)}) collective-permute-start(bf16[128,1024]{1,0:T(8,128)(2,1)} %collective-permute-done.4), channel_id=1, source_target_pairs={{1,0},{5,4},{9,8},{13,12},{17,16},{21,20},{25,24},{29,28}} | collective-permute-start | bytes 786440 | tf_op jit(solution)/shard_map/ppermute | solution.py:106
  31.4 9.2 %collective-permute-start.8 = (bf16[128,1024]{1,0:T(8,128)(2,1)S(1)}, bf16[128,1024]{1,0:T(8,128)(2,1)S(1)}, u32[]{:S(2)}, u32[]{:S(2)}) collective-permute-start(bf16[128,1024]{1,0:T(8,128)(2,1)S(1)} %collective-permute-done.7), channel_id=1, source_target_pairs={{2,3},{6,7},{10,11},{14,15},{18,19},{22,23},{26,27},{30,31}} | collective-permute-start | bytes 786440 | tf_op jit(solution)/shard_map/ppermute | solution.py:103
  46.8 18.2 %all-to-all-start.1 = ((bf16[8,64,1024]{2,1,0:T(8,128)(2,1)}), bf16[8,64,1024]{2,1,0:T(8,128)(2,1)S(1)}, u32[]{:S(2)}, u32[]{:S(2)}) async-start(bf16[8,64,1024]{2,1,0:T(8,128)(2,1)} %bitcast.28), calls=%async_computation.1 | async-start | bytes 2097152 | tf_op jit(solution)/shard_map/all_to_all | solution.py:140
  64.9 18.9 %all-to-all-start = ((bf16[8,64,1024]{2,1,0:T(8,128)(2,1)}), bf16[8,64,1024]{2,1,0:T(8,128)(2,1)S(1)}, u32[]{:S(2)}, u32[]{:S(2)}) async-start(bf16[8,64,1024]{2,1,0:T(8,128)(2,1)} %bitcast.15), calls=%async_computation | async-start | bytes 2097152 | tf_op jit(solution)/shard_map/all_to_all | solution.py:140
  83.8 18.9 %all-to-all-start.2 = ((bf16[8,64,1024]{2,1,0:T(8,128)(2,1)}), bf16[8,64,1024]{2,1,0:T(8,128)(2,1)S(1)}, u32[]{:S(2)}, u32[]{:S(2)}) async-start(bf16[8,64,1024]{2,1,0:T(8,128)(2,1)} %bitcast.67), calls=%async_computation.2 | async-start | bytes 2097152 | tf_op jit(solution)/shard_map/all_to_all | solution.py:146
  102.7 18.9 %all-to-all-start.3 = ((bf16[8,64,1024]{2,1,0:T(8,128)(2,1)}), bf16[8,64,1024]{2,1,0:T(8,128)(2,1)S(1)}, u32[]{:S(2)}, u32[]{:S(2)}) async-start(bf16[8,64,1024]{2,1,0:T(8,128)(2,1)} %bitcast.66), calls=%async_computation.3 | async-start | bytes 2097152 | tf_op jit(solution)/shard_map/all_to_all | solution.py:146
  114.1 11.7 %collective-permute-start.12 = (bf16[128,1024]{1,0:T(8,128)(2,1)}, bf16[128,1024]{1,0:T(8,128)(2,1)}, u32[]{:S(2)}, u32[]{:S(2)}) collective-permute-start(bf16[128,1024]{1,0:T(8,128)(2,1)} %get-tuple-element.26), channel_id=1, source_target_pairs={{3,2},{7,6},{11,10},{15,14},{19,18},{23,22},{27,26},{31,30}} | collective-permute-start | bytes 786440 | tf_op jit(solution)/shard_map/ppermute | solution.py:128
  124.5 11.1 %collective-permute-start.15 = (bf16[128,1024]{1,0:T(8,128)(2,1)S(1)}, bf16[128,1024]{1,0:T(8,128)(2,1)}, u32[]{:S(2)}, u32[]{:S(2)}) collective-permute-start(bf16[128,1024]{1,0:T(8,128)(2,1)S(1)} %copy-done.5), channel_id=1, source_target_pairs={{0,1},{4,5},{8,9},{12,13},{16,17},{20,21},{24,25},{28,29}} | collective-permute-start | bytes 786440 | tf_op jit(solution)/shard_map/ppermute | solution.py:129
  127.0 11.2 %collective-permute-start.13 = (bf16[128,1024]{1,0:T(8,128)(2,1)S(1)}, bf16[128,1024]{1,0:T(8,128)(2,1)}, u32[]{:S(2)}, u32[]{:S(2)}) collective-permute-start(bf16[128,1024]{1,0:T(8,128)(2,1)S(1)} %add_convert_fusion.9), channel_id=1, source_target_pairs={{2,1},{3,2},{6,5},{7,6},{10,9},{11,10},{14,13},{15,14},{18,17},{19... | collective-permute-start | bytes 786440 | tf_op jit(solution)/shard_map/ppermute | solution.py:128
  128.3 15.4 %collective-permute-start.21 = (bf16[128,1024]{1,0:T(8,128)(2,1)S(1)}, bf16[128,1024]{1,0:T(8,128)(2,1)}, u32[]{:S(2)}, u32[]{:S(2)}) collective-permute-start(bf16[128,1024]{1,0:T(8,128)(2,1)S(1)} %get-tuple-element.31), channel_id=1, source_target_pairs={{0,1},{4,5},{8,9},{12,13},{16,17},{20,21},{24,25},{28,29}} | collective-permute-start | bytes 786440 | tf_op jit(solution)/shard_map/ppermute | solution.py:129
  129.7 14.0 %collective-permute-start.19 = (bf16[128,1024]{1,0:T(8,128)(2,1)S(1)}, bf16[128,1024]{1,0:T(8,128)(2,1)S(1)}, u32[]{:S(2)}, u32[]{:S(2)}) collective-permute-start(bf16[128,1024]{1,0:T(8,128)(2,1)S(1)} %add_convert_fusion.4), channel_id=1, source_target_pairs={{2,1},{3,2},{6,5},{7,6},{10,9},{11,10},{14,13},{15,14},{18,17},{19... | collective-permute-start | bytes 786440 | tf_op jit(solution)/shard_map/ppermute | solution.py:128
  140.3 11.1 %collective-permute-start.16 = (bf16[128,1024]{1,0:T(8,128)(2,1)S(1)}, bf16[128,1024]{1,0:T(8,128)(2,1)S(1)}, u32[]{:S(2)}, u32[]{:S(2)}) collective-permute-start(bf16[128,1024]{1,0:T(8,128)(2,1)S(1)} %get-tuple-element.25), channel_id=1, source_target_pairs={{0,1},{1,2},{4,5},{5,6},{8,9},{9,10},{12,13},{13,14},{16,17},{17,1... | collective-permute-start | bytes 786440 | tf_op jit(solution)/shard_map/ppermute | solution.py:129
  145.6 13.5 %collective-permute-start.22 = (bf16[128,1024]{1,0:T(8,128)(2,1)}, bf16[128,1024]{1,0:T(8,128)(2,1)S(1)}, u32[]{:S(2)}, u32[]{:S(2)}) collective-permute-start(bf16[128,1024]{1,0:T(8,128)(2,1)} %get-tuple-element.29), channel_id=1, source_target_pairs={{0,1},{1,2},{4,5},{5,6},{8,9},{9,10},{12,13},{13,14},{16,17},{17,1... | collective-permute-start | bytes 786440 | tf_op jit(solution)/shard_map/ppermute | solution.py:129
  148.1 14.3 %collective-permute-start.14 = (bf16[128,1024]{1,0:T(8,128)(2,1)}, bf16[128,1024]{1,0:T(8,128)(2,1)S(1)}, u32[]{:S(2)}, u32[]{:S(2)}) collective-permute-start(bf16[128,1024]{1,0:T(8,128)(2,1)} %get-tuple-element.24), channel_id=1, source_target_pairs={{1,0},{2,1},{3,2},{5,4},{6,5},{7,6},{9,8},{10,9},{11,10},{13,12},{... | collective-permute-start | bytes 786440 | tf_op jit(solution)/shard_map/ppermute | solution.py:128
  153.3 9.2 %collective-permute-start.17 = (bf16[128,1024]{1,0:T(8,128)(2,1)}, bf16[128,1024]{1,0:T(8,128)(2,1)S(1)}, u32[]{:S(2)}, u32[]{:S(2)}) collective-permute-start(bf16[128,1024]{1,0:T(8,128)(2,1)} %add_convert_fusion.6), channel_id=1, source_target_pairs={{0,1},{1,2},{2,3},{4,5},{5,6},{6,7},{8,9},{9,10},{10,11},{12,13},{... | collective-permute-start | bytes 786440 | tf_op jit(solution)/shard_map/ppermute | solution.py:129
  155.8 8.8 %collective-permute-start.20 = (bf16[128,1024]{1,0:T(8,128)(2,1)}, bf16[128,1024]{1,0:T(8,128)(2,1)S(1)}, u32[]{:S(2)}, u32[]{:S(2)}) collective-permute-start(bf16[128,1024]{1,0:T(8,128)(2,1)} %get-tuple-element.28), channel_id=1, source_target_pairs={{1,0},{2,1},{3,2},{5,4},{6,5},{7,6},{9,8},{10,9},{11,10},{13,12},{... | collective-permute-start | bytes 786440 | tf_op jit(solution)/shard_map/ppermute | solution.py:128
  (11 other events, 75.2 us)
